TPU v7x, 512 devices: a whole 4x4x16 slice. The times are simulated.
512 devices in a mesh: sec: 2 (over core), lat: 8 (over y_hi, x), lon: 32 (over z, y_lo).
Axes of the slice: x: 4, y: 4 (y_hi: 2, y_lo: 2; y = y_hi * 2 + y_lo), z: 16, core: 2. Of those that a mesh axis runs over, the one named last changes fastest.
Arguments:
- state: float32 [2, 2, 60, 128, 4096], P('sec', None, None, 'lat', 'lon'), may hold values from -6 to 6
- zonal: float32 [2, 60, 128, 4096], P('sec', None, 'lat', 'lon'), may hold values from -0.45 to 0.45
- meridional: float32 [2, 60, 128, 4096], P('sec', None, 'lat', 'lon'), may hold values from -0.35 to 0.35
- mixing: float32 [2, 60, 128, 4096], P('sec', None, 'lat', 'lon'), may hold values from 0.005 to 0.05
- exchange_rate: float32 [2, 128, 4096], P('sec', 'lat', 'lon'), may hold values from 0.02 to 0.1
- sea_mask: int32 [2, 128, 4096], P('sec', 'lat', 'lon'), may hold values 0 or 1
- regrid_map: int32 [2, 4, 128, 4096], P('sec', None, 'lat', 'lon'), may hold values from 0 to 2047, as said below
Outputs:
- final_state: float32 [2, 2, 60, 128, 4096], P('sec', None, None, 'lat', 'lon')
- surface_flux: float32 [2, 2, 128, 4096], P('sec', None, 'lat', 'lon')
Inputs may be any that keep to these rules, and one draw needn't show every extreme that they name: regrid_map[s, t, cell] is the local number of a cell of the same block, at most 2 rows and 3 columns away (columns wrapping inside the block, rows clamped to it); entry t = 0 names the cell's own position.
All inputs are finite; a program needn't handle non-finite values. No bound on the sum of `sea_mask` on one device may be relied on, other than what follows from the above.
Results may differ from a plain program's by a relative error of at most 0.00002.
Values sent between devices are 32-bit elements; how exact they have to be, the bound alone decides.
No kernel may reach another device: no remote copies, remote signals or barrier semaphores. Data moves between devices by JAX's collectives and lax.ppermute only.
A program may use at most 128 MiB of HBM per device.

v0:
```python
import jax
import jax.numpy as jnp
from jax import lax
from jax.sharding import PartitionSpec as P

TAPS = 4
SUB = 4


def extended_2(x, sides, width):
    for axis, dim in sides:
        devices, length = (lax.axis_size(axis), x.shape[dim])
        up = [(i, (i + 1) % devices) for i in range(devices)]
        down = [(j, i) for i, j in up]
        last = lax.slice_in_dim(x, length - width, length, axis=dim)
        leading = lax.slice_in_dim(x, 0, width, axis=dim)
        before = lax.ppermute(last, axis, up)
        after = lax.ppermute(leading, axis, down)
        x = jnp.concatenate([before, x, after], axis=dim)
    return x


def swapped(block, axis, apart):
    count = lax.axis_size(axis)
    route = []
    for low in range(count):
        high = low | 1 << apart
        if high != low and high < count:
            route += [(low, high), (high, low)]
    return lax.ppermute(block, axis, route)


def extend(block, width):
    return extended_2(block, (("lat", 1), ("lon", 2)), width)


def inside_rows(rows_local, width):
    row_block = lax.axis_index("lat")
    blocks_total = lax.axis_size("lat")
    rows = jnp.arange(rows_local + 2 * width, dtype=jnp.int32) + row_block * rows_local - width
    valid = jnp.logical_and(rows >= 0, rows < rows_local * blocks_total)
    return valid.astype(jnp.float32)[:, None]


def advance(extended, wet_ext, zonal, meridional, mixing, flux):
    center = extended[..., 1:-1, 1:-1]
    west = extended[..., 1:-1, :-2]
    east = extended[..., 1:-1, 2:]
    south = extended[..., :-2, 1:-1]
    north = extended[..., 2:, 1:-1]
    wet_c = wet_ext[1:-1, 1:-1]
    wet_w = wet_ext[1:-1, :-2]
    wet_e = wet_ext[1:-1, 2:]
    wet_s = wet_ext[:-2, 1:-1]
    wet_n = wet_ext[2:, 1:-1]
    horiz = (
        wet_w * jnp.maximum(zonal, 0.0) * (west - center)
        + wet_e * jnp.maximum(-zonal, 0.0) * (east - center)
        + wet_s * jnp.maximum(meridional, 0.0) * (south - center)
        + wet_n * jnp.maximum(-meridional, 0.0) * (north - center)
    )
    down = mixing[:-1] * (center[:, 1:] - center[:, :-1])
    vert = jnp.pad(down, ((0, 0), (0, 1), (0, 0), (0, 0))) - jnp.pad(
        down, ((0, 0), (1, 0), (0, 0), (0, 0))
    )
    updated = center + wet_c * (horiz + vert)
    return jnp.concatenate([updated[:, :1] + flux[:, None], updated[:, 1:]], axis=1)


def shards(state, zonal, meridional, mixing, exchange_rate, sea_mask, regrid_map):
    tracers = state[0]
    fields, levels, rows_local, cols_local = tracers.shape
    section = lax.axis_index("sec")
    sea = sea_mask[0].astype(jnp.float32)
    wet = jnp.where(section == 1, sea, jnp.ones_like(sea))
    surface = tracers[:, 0]
    partner = swapped(surface, "sec", 0)
    flat = partner.reshape(fields, rows_local * cols_local)
    table = regrid_map[0].reshape(TAPS, rows_local * cols_local)
    picked = jnp.take(flat, table, axis=1)
    total = jnp.zeros((fields, rows_local * cols_local), jnp.float32)
    for tap in range(TAPS):
        total = total + picked[:, tap]
    regridded = (total / TAPS).reshape(fields, rows_local, cols_local)
    flux = exchange_rate[0] * sea * (regridded - surface)
    wet_ext = extend(wet[None], 1)[0] * inside_rows(rows_local, 1)
    current = tracers
    for step in range(SUB):
        extended = extend(current.reshape(fields * levels, rows_local, cols_local), 1)
        extended = extended.reshape(fields, levels, rows_local + 2, cols_local + 2)
        current = advance(extended, wet_ext, zonal[0], meridional[0], mixing[0], flux)
    return (current[None], flux[None])


def solution(mesh):
    return jax.shard_map(
        shards,
        mesh=mesh,
        in_specs=(
            P("sec", None, None, "lat", "lon"),
            P("sec", None, "lat", "lon"),
            P("sec", None, "lat", "lon"),
            P("sec", None, "lat", "lon"),
            P("sec", "lat", "lon"),
            P("sec", "lat", "lon"),
            P("sec", None, "lat", "lon"),
        ),
        out_specs=(P("sec", None, None, "lat", "lon"), P("sec", None, "lat", "lon")),
        check_vma=False,
    )
```

profile of v0, /device:TPU:6, one launch (start us, length us, event | category | flops | bytes accessed | tf_op | source)
XLA Modules:
  0.0 198.8 jit_solution(17998053284127792982)
XLA Ops:
  1.4 5.0 %collective-permute-start.4 = (f32[1,1,128]{2,1,0:T(1,128)S(1)}, f32[1,1,128]{2,1,0:T(1,128)S(1)}, u32[]{:S(2)}, u32[]{:S(2)}) collective-permute-start(f32[1,1,128]{2,1,0:T(1,128)S(1)} %get-tuple-element.35), channel_id=1, source_target_pairs={{0,32},{32,64},{64,96},{96,128},{128,160},{160,192},{192,224},{224... | collective-permute-start | bytes 1544 | tf_op jit(solution)/shard_map/ppermute | solution.py:17
  6.5 1.9 collective-permute-start.5
  8.4 1.6 copy.86
  10.1 7.5 %collective-permute-start = (f32[120,1,128]{0,2,1:T(8,128)S(1)}, f32[120,1,128]{0,2,1:T(8,128)S(1)}, u32[]{:S(2)}, u32[]{:S(2)}) collective-permute-start(f32[120,1,128]{0,2,1:T(8,128)S(1)} %get-tuple-element.14), channel_id=1, source_target_pairs={{0,32},{32,64},{64,96},{96,128},{128,160},{160,192},{192,224},{224... | collective-permute-start | bytes 184328 | tf_op jit(solution)/shard_map/ppermute | solution.py:17
  17.6 1.9 collective-permute-start.1
  20.3 1.9 collective-permute-start.8
  23.2 2.6 %collective-permute-start.6 = (f32[1,18,1]{2,1,0:T(8,128)S(1)}, f32[1,18,1]{2,1,0:T(8,128)S(1)}, u32[]{:S(2)}, u32[]{:S(2)}) collective-permute-start(f32[1,18,1]{2,1,0:T(8,128)S(1)} %get-tuple-element.31), channel_id=1, source_target_pairs={{0,1},{1,2},{2,3},{3,4},{4,5},{5,6},{6,7},{7,8},{8,9},{9,10},{10,1... | collective-permute-start | bytes 224 | tf_op jit(solution)/shard_map/ppermute | solution.py:17
  25.8 10.9 %collective-permute-start.7 = (f32[1,18,1]{2,1,0:T(8,128)S(1)}, f32[1,18,1]{2,1,0:T(8,128)S(1)}, u32[]{:S(2)}, u32[]{:S(2)}) collective-permute-start(f32[1,18,1]{2,1,0:T(8,128)S(1)} %get-tuple-element.32), channel_id=1, source_target_pairs={{1,0},{2,1},{3,2},{4,3},{5,4},{6,5},{7,6},{8,7},{9,8},{10,9},{11,1... | collective-permute-start | bytes 224 | tf_op jit(solution)/shard_map/ppermute | solution.py:18
  36.7 1.4 collective-permute-done.7
  39.8 27.9 %gather_fusion = f32[8192,2]{1,0:T(8,128)} fusion(f32[2,2048]{0,1:T(8,128)S(1)} %bitcast.66, s32[8192]{0:T(1024)S(1)} %broadcast_clamp_fusion), kind=kCustom, calls=%fused_computation | custom fusion | bytes 163840 | tf_op jit(solution)/shard_map/jit(_take)/gather | solution.py:80
  67.7 2.8 %copy.97 = f32[4,2048,2]{1,0,2:T(4,128)S(1)} copy(f32[4,2048,2]{2,1,0:T(8,128)} %bitcast.65) | data formatting | bytes 131072 | tf_op jit(solution)/shard_map/jit(_take)/gather | solution.py:80
  70.6 1.9 collective-permute-start.2
  72.5 6.3 %collective-permute-start.3 = (f32[120,18,1]{0,2,1:T(1,128)S(1)}, f32[120,18,1]{0,2,1:T(1,128)S(1)}, u32[]{:S(2)}, u32[]{:S(2)}) collective-permute-start(f32[120,18,1]{0,2,1:T(1,128)S(1)} %get-tuple-element.13), channel_id=1, source_target_pairs={{1,0},{2,1},{3,2},{4,3},{5,4},{6,5},{7,6},{8,7},{9,8},{10,9},{11,1... | collective-permute-start | bytes 25928 | tf_op jit(solution)/shard_map/ppermute | solution.py:18
  78.9 1.3 collective-permute-done.3
  80.2 1.2 pad_maximum_fusion.3
  81.4 4.3 %copy.128 = f32[120,18,130]{2,1,0:T(8,128)S(1)} copy(f32[120,18,130]{0,2,1:T(8,128)} %pad_maximum_fusion.3) | data formatting | bytes 2246400 | tf_op jit(solution)/shard_map/reshape | solution.py:90
  85.8 1.7 fusion.43
  89.6 1.9 collective-permute-start.10
  91.5 8.1 %collective-permute-start.9 = (f32[120,1,128]{2,1,0:T(1,128)S(1)}, f32[120,1,128]{2,1,0:T(1,128)S(1)}, u32[]{:S(2)}, u32[]{:S(2)}) collective-permute-start(f32[120,1,128]{2,1,0:T(1,128)S(1)} %get-tuple-element.20), channel_id=1, source_target_pairs={{0,32},{32,64},{64,96},{96,128},{128,160},{160,192},{192,224},{224... | collective-permute-start | bytes 184328 | tf_op jit(solution)/shard_map/ppermute | solution.py:17
  100.0 1.6 collective-permute-done.9
  101.8 1.6 fusion.50
  103.4 1.7 copy.98
  105.1 1.9 collective-permute-start.11
  107.4 6.0 %collective-permute-start.12 = (f32[120,18,1]{0,2,1:T(1,128)S(1)}, f32[120,18,1]{0,2,1:T(1,128)S(1)}, u32[]{:S(2)}, u32[]{:S(2)}) collective-permute-start(f32[120,18,1]{0,2,1:T(1,128)S(1)} %copy.99), channel_id=1, source_target_pairs={{1,0},{2,1},{3,2},{4,3},{5,4},{6,5},{7,6},{8,7},{9,8},{10,9},{11,1... | collective-permute-start | bytes 25928 | tf_op jit(solution)/shard_map/ppermute | solution.py:18
  114.8 1.2 pad_maximum_fusion.4
  116.1 4.3 %copy.129 = f32[120,18,130]{2,1,0:T(8,128)S(1)} copy(f32[120,18,130]{0,2,1:T(8,128)} %pad_maximum_fusion.4) | data formatting | bytes 2246400 | tf_op jit(solution)/shard_map/reshape | solution.py:90
  120.4 1.7 fusion.42
  123.5 8.1 %collective-permute-start.13 = (f32[120,1,128]{2,1,0:T(1,128)S(1)}, f32[120,1,128]{2,1,0:T(1,128)S(1)}, u32[]{:S(2)}, u32[]{:S(2)}) collective-permute-start(f32[120,1,128]{2,1,0:T(1,128)S(1)} %get-tuple-element.18), channel_id=1, source_target_pairs={{0,32},{32,64},{64,96},{96,128},{128,160},{160,192},{192,224},{224... | collective-permute-start | bytes 184328 | tf_op jit(solution)/shard_map/ppermute | solution.py:17
  131.7 1.9 collective-permute-start.14
  133.6 7.8 %collective-permute-done.14 = f32[120,1,128]{2,1,0:T(1,128)S(1)} collective-permute-done((f32[120,1,128]{2,1,0:T(1,128)S(1)}, f32[120,1,128]{2,1,0:T(1,128)S(1)}, u32[]{:S(2)}, u32[]{:S(2)}) %collective-permute-start.14) | collective-permute-done | bytes 61472 | tf_op jit(solution)/shard_map/ppermute | solution.py:18
  141.6 1.6 fusion.49
  143.3 1.7 copy.108
  145.0 2.1 %collective-permute-start.15 = (f32[120,18,1]{0,2,1:T(1,128)S(1)}, f32[120,18,1]{0,2,1:T(1,128)S(1)}, u32[]{:S(2)}, u32[]{:S(2)}) collective-permute-start(f32[120,18,1]{0,2,1:T(1,128)S(1)} %copy.108), channel_id=1, source_target_pairs={{0,1},{1,2},{2,3},{3,4},{4,5},{5,6},{6,7},{7,8},{8,9},{9,10},{10,1... | collective-permute-start | bytes 25928 | tf_op jit(solution)/shard_map/ppermute | solution.py:17
  147.5 6.0 %collective-permute-start.16 = (f32[120,18,1]{0,2,1:T(1,128)S(1)}, f32[120,18,1]{0,2,1:T(1,128)S(1)}, u32[]{:S(2)}, u32[]{:S(2)}) collective-permute-start(f32[120,18,1]{0,2,1:T(1,128)S(1)} %copy.109), channel_id=1, source_target_pairs={{1,0},{2,1},{3,2},{4,3},{5,4},{6,5},{7,6},{8,7},{9,8},{10,9},{11,1... | collective-permute-start | bytes 25928 | tf_op jit(solution)/shard_map/ppermute | solution.py:18
  154.9 1.2 pad_maximum_fusion.5
  156.1 4.3 %copy.130 = f32[120,18,130]{2,1,0:T(8,128)S(1)} copy(f32[120,18,130]{0,2,1:T(8,128)} %pad_maximum_fusion.5) | data formatting | bytes 2246400 | tf_op jit(solution)/shard_map/reshape | solution.py:90
  160.4 1.7 fusion.41
  163.6 1.9 collective-permute-start.17
  165.5 3.9 %collective-permute-start.18 = (f32[120,1,128]{2,1,0:T(1,128)S(1)}, f32[120,1,128]{2,1,0:T(1,128)S(1)}, u32[]{:S(2)}, u32[]{:S(2)}) collective-permute-start(f32[120,1,128]{2,1,0:T(1,128)S(1)} %get-tuple-element.17), channel_id=1, source_target_pairs={{32,0},{64,32},{96,64},{128,96},{160,128},{192,160},{224,192},{0,2... | collective-permute-start | bytes 184328 | tf_op jit(solution)/shard_map/ppermute | solution.py:18
  169.7 5.5 %collective-permute-done.18 = f32[120,1,128]{2,1,0:T(1,128)S(1)} collective-permute-done((f32[120,1,128]{2,1,0:T(1,128)S(1)}, f32[120,1,128]{2,1,0:T(1,128)S(1)}, u32[]{:S(2)}, u32[]{:S(2)}) %collective-permute-start.18) | collective-permute-done | bytes 61472 | tf_op jit(solution)/shard_map/ppermute | solution.py:18
  175.5 1.6 fusion.48
  177.1 1.7 copy.118
  178.8 1.9 collective-permute-start.19
  181.1 6.4 %collective-permute-start.20 = (f32[120,18,1]{0,2,1:T(1,128)S(1)}, f32[120,18,1]{0,2,1:T(1,128)S(1)}, u32[]{:S(2)}, u32[]{:S(2)}) collective-permute-start(f32[120,18,1]{0,2,1:T(1,128)S(1)} %copy.119), channel_id=1, source_target_pairs={{1,0},{2,1},{3,2},{4,3},{5,4},{6,5},{7,6},{8,7},{9,8},{10,9},{11,1... | collective-permute-start | bytes 25928 | tf_op jit(solution)/shard_map/ppermute | solution.py:18
  187.5 1.3 fusion.47
  189.3 1.2 pad_maximum_fusion.6
  190.5 4.3 %copy.131 = f32[120,18,130]{2,1,0:T(8,128)S(1)} copy(f32[120,18,130]{0,2,1:T(8,128)} %pad_maximum_fusion.6) | data formatting | bytes 2246400 | tf_op jit(solution)/shard_map/reshape | solution.py:90
  194.8 1.7 fusion.40
  (96 shorter events, 16.8 us)
Async XLA Ops:
  0.6 21.5 %copy-start.15 = (s32[1,4,16,128]{3,2,1,0:T(8,128)S(1)}, s32[1,4,16,128]{3,2,1,0:T(8,128)}, u32[]{:S(2)}) copy-start(s32[1,4,16,128]{3,2,1,0:T(8,128)} %param.13) | copy-start | bytes 98308
  0.6 21.6 %copy-start.14 = (f32[1,60,16,128]{3,2,1,0:T(8,128)S(1)}, f32[1,60,16,128]{3,2,1,0:T(8,128)}, u32[]{:S(2)}) copy-start(f32[1,60,16,128]{3,2,1,0:T(8,128)} %param.10) | copy-start | bytes 1474564
  1.4 21.7 %collective-permute-start.4 = (f32[1,1,128]{2,1,0:T(1,128)S(1)}, f32[1,1,128]{2,1,0:T(1,128)S(1)}, u32[]{:S(2)}, u32[]{:S(2)}) collective-permute-start(f32[1,1,128]{2,1,0:T(1,128)S(1)} %get-tuple-element.35), channel_id=1, source_target_pairs={{0,32},{32,64},{64,96},{96,128},{128,160},{160,192},{192,224},{224... | collective-permute-start | bytes 1544 | tf_op jit(solution)/shard_map/ppermute | solution.py:17
  6.5 16.7 %collective-permute-start.5 = (f32[1,1,128]{2,1,0:T(1,128)S(1)}, f32[1,1,128]{2,1,0:T(1,128)S(1)}, u32[]{:S(2)}, u32[]{:S(2)}) collective-permute-start(f32[1,1,128]{2,1,0:T(1,128)S(1)} %get-tuple-element.36), channel_id=1, source_target_pairs={{32,0},{64,32},{96,64},{128,96},{160,128},{192,160},{224,192},{0,2... | collective-permute-start | bytes 1544 | tf_op jit(solution)/shard_map/ppermute | solution.py:18
  8.4 29.9 %copy-start.12 = (f32[1,60,16,128]{3,2,1,0:T(8,128)S(1)}, f32[1,60,16,128]{3,2,1,0:T(8,128)}, u32[]{:S(2)}) copy-start(f32[1,60,16,128]{3,2,1,0:T(8,128)} %param.9) | copy-start | bytes 1474564
  8.4 29.8 %copy-start.13 = (f32[1,60,16,128]{3,2,1,0:T(8,128)S(1)}, f32[1,60,16,128]{3,2,1,0:T(8,128)}, u32[]{:S(2)}) copy-start(f32[1,60,16,128]{3,2,1,0:T(8,128)} %param.8) | copy-start | bytes 1474564
  10.1 60.5 %collective-permute-start = (f32[120,1,128]{0,2,1:T(8,128)S(1)}, f32[120,1,128]{0,2,1:T(8,128)S(1)}, u32[]{:S(2)}, u32[]{:S(2)}) collective-permute-start(f32[120,1,128]{0,2,1:T(8,128)S(1)} %get-tuple-element.14), channel_id=1, source_target_pairs={{0,32},{32,64},{64,96},{96,128},{128,160},{160,192},{192,224},{224... | collective-permute-start | bytes 184328 | tf_op jit(solution)/shard_map/ppermute | solution.py:17
  17.6 53.0 %collective-permute-start.1 = (f32[120,1,128]{0,2,1:T(8,128)S(1)}, f32[120,1,128]{0,2,1:T(8,128)S(1)}, u32[]{:S(2)}, u32[]{:S(2)}) collective-permute-start(f32[120,1,128]{0,2,1:T(8,128)S(1)} %get-tuple-element.15), channel_id=1, source_target_pairs={{32,0},{64,32},{96,64},{128,96},{160,128},{192,160},{224,192},{0,2... | collective-permute-start | bytes 184328 | tf_op jit(solution)/shard_map/ppermute | solution.py:18
  20.3 19.1 %collective-permute-start.8 = (f32[2,16,128]{2,1,0:T(8,128)S(1)}, f32[2,16,128]{2,1,0:T(8,128)S(1)}, u32[]{:S(2)}, u32[]{:S(2)}) collective-permute-start(f32[2,16,128]{2,1,0:T(8,128)S(1)} %slice_bitcast_fusion.1), channel_id=1, source_target_pairs={{0,256},{256,0},{1,257},{257,1},{2,258},{258,2},{3,259},{259,3},{4... | collective-permute-start | bytes 49160 | tf_op jit(solution)/shard_map/ppermute | solution.py:30
  23.2 13.4 %collective-permute-start.6 = (f32[1,18,1]{2,1,0:T(8,128)S(1)}, f32[1,18,1]{2,1,0:T(8,128)S(1)}, u32[]{:S(2)}, u32[]{:S(2)}) collective-permute-start(f32[1,18,1]{2,1,0:T(8,128)S(1)} %get-tuple-element.31), channel_id=1, source_target_pairs={{0,1},{1,2},{2,3},{3,4},{4,5},{5,6},{6,7},{7,8},{8,9},{9,10},{10,1... | collective-permute-start | bytes 224 | tf_op jit(solution)/shard_map/ppermute | solution.py:17
  25.8 12.2 %collective-permute-start.7 = (f32[1,18,1]{2,1,0:T(8,128)S(1)}, f32[1,18,1]{2,1,0:T(8,128)S(1)}, u32[]{:S(2)}, u32[]{:S(2)}) collective-permute-start(f32[1,18,1]{2,1,0:T(8,128)S(1)} %get-tuple-element.32), channel_id=1, source_target_pairs={{1,0},{2,1},{3,2},{4,3},{5,4},{6,5},{7,6},{8,7},{9,8},{10,9},{11,1... | collective-permute-start | bytes 224 | tf_op jit(solution)/shard_map/ppermute | solution.py:18
  70.6 8.3 %collective-permute-start.2 = (f32[120,18,1]{0,2,1:T(1,128)S(1)}, f32[120,18,1]{0,2,1:T(1,128)S(1)}, u32[]{:S(2)}, u32[]{:S(2)}) collective-permute-start(f32[120,18,1]{0,2,1:T(1,128)S(1)} %get-tuple-element.12), channel_id=1, source_target_pairs={{0,1},{1,2},{2,3},{3,4},{4,5},{5,6},{6,7},{7,8},{8,9},{9,10},{10,1... | collective-permute-start | bytes 25928 | tf_op jit(solution)/shard_map/ppermute | solution.py:17
  72.5 7.7 %collective-permute-start.3 = (f32[120,18,1]{0,2,1:T(1,128)S(1)}, f32[120,18,1]{0,2,1:T(1,128)S(1)}, u32[]{:S(2)}, u32[]{:S(2)}) collective-permute-start(f32[120,18,1]{0,2,1:T(1,128)S(1)} %get-tuple-element.13), channel_id=1, source_target_pairs={{1,0},{2,1},{3,2},{4,3},{5,4},{6,5},{7,6},{8,7},{9,8},{10,9},{11,1... | collective-permute-start | bytes 25928 | tf_op jit(solution)/shard_map/ppermute | solution.py:18
  85.7 1.7 copy-start
  85.7 1.7 copy-start.4
  85.8 1.7 copy-start.8
  89.6 10.3 %collective-permute-start.10 = (f32[120,1,128]{2,1,0:T(1,128)S(1)}, f32[120,1,128]{2,1,0:T(1,128)S(1)}, u32[]{:S(2)}, u32[]{:S(2)}) collective-permute-start(f32[120,1,128]{2,1,0:T(1,128)S(1)} %get-tuple-element.21), channel_id=1, source_target_pairs={{32,0},{64,32},{96,64},{128,96},{160,128},{192,160},{224,192},{0,2... | collective-permute-start | bytes 184328 | tf_op jit(solution)/shard_map/ppermute | solution.py:18
  91.5 10.0 %collective-permute-start.9 = (f32[120,1,128]{2,1,0:T(1,128)S(1)}, f32[120,1,128]{2,1,0:T(1,128)S(1)}, u32[]{:S(2)}, u32[]{:S(2)}) collective-permute-start(f32[120,1,128]{2,1,0:T(1,128)S(1)} %get-tuple-element.20), channel_id=1, source_target_pairs={{0,32},{32,64},{64,96},{96,128},{128,160},{160,192},{192,224},{224... | collective-permute-start | bytes 184328 | tf_op jit(solution)/shard_map/ppermute | solution.py:17
  105.1 8.8 %collective-permute-start.11 = (f32[120,18,1]{0,2,1:T(1,128)S(1)}, f32[120,18,1]{0,2,1:T(1,128)S(1)}, u32[]{:S(2)}, u32[]{:S(2)}) collective-permute-start(f32[120,18,1]{0,2,1:T(1,128)S(1)} %copy.98), channel_id=1, source_target_pairs={{0,1},{1,2},{2,3},{3,4},{4,5},{5,6},{6,7},{7,8},{8,9},{9,10},{10,1... | collective-permute-start | bytes 25928 | tf_op jit(solution)/shard_map/ppermute | solution.py:17
  107.4 7.4 %collective-permute-start.12 = (f32[120,18,1]{0,2,1:T(1,128)S(1)}, f32[120,18,1]{0,2,1:T(1,128)S(1)}, u32[]{:S(2)}, u32[]{:S(2)}) collective-permute-start(f32[120,18,1]{0,2,1:T(1,128)S(1)} %copy.99), channel_id=1, source_target_pairs={{1,0},{2,1},{3,2},{4,3},{5,4},{6,5},{7,6},{8,7},{9,8},{10,9},{11,1... | collective-permute-start | bytes 25928 | tf_op jit(solution)/shard_map/ppermute | solution.py:18
  120.4 1.7 copy-start.1
  120.4 1.7 copy-start.5
  120.4 1.7 copy-start.9
  123.5 10.1 %collective-permute-start.13 = (f32[120,1,128]{2,1,0:T(1,128)S(1)}, f32[120,1,128]{2,1,0:T(1,128)S(1)}, u32[]{:S(2)}, u32[]{:S(2)}) collective-permute-start(f32[120,1,128]{2,1,0:T(1,128)S(1)} %get-tuple-element.18), channel_id=1, source_target_pairs={{0,32},{32,64},{64,96},{96,128},{128,160},{160,192},{192,224},{224... | collective-permute-start | bytes 184328 | tf_op jit(solution)/shard_map/ppermute | solution.py:17
  131.7 9.7 %collective-permute-start.14 = (f32[120,1,128]{2,1,0:T(1,128)S(1)}, f32[120,1,128]{2,1,0:T(1,128)S(1)}, u32[]{:S(2)}, u32[]{:S(2)}) collective-permute-start(f32[120,1,128]{2,1,0:T(1,128)S(1)} %get-tuple-element.19), channel_id=1, source_target_pairs={{32,0},{64,32},{96,64},{128,96},{160,128},{192,160},{224,192},{0,2... | collective-permute-start | bytes 184328 | tf_op jit(solution)/shard_map/ppermute | solution.py:18
  145.0 8.9 %collective-permute-start.15 = (f32[120,18,1]{0,2,1:T(1,128)S(1)}, f32[120,18,1]{0,2,1:T(1,128)S(1)}, u32[]{:S(2)}, u32[]{:S(2)}) collective-permute-start(f32[120,18,1]{0,2,1:T(1,128)S(1)} %copy.108), channel_id=1, source_target_pairs={{0,1},{1,2},{2,3},{3,4},{4,5},{5,6},{6,7},{7,8},{8,9},{9,10},{10,1... | collective-permute-start | bytes 25928 | tf_op jit(solution)/shard_map/ppermute | solution.py:17
  147.5 7.4 %collective-permute-start.16 = (f32[120,18,1]{0,2,1:T(1,128)S(1)}, f32[120,18,1]{0,2,1:T(1,128)S(1)}, u32[]{:S(2)}, u32[]{:S(2)}) collective-permute-start(f32[120,18,1]{0,2,1:T(1,128)S(1)} %copy.109), channel_id=1, source_target_pairs={{1,0},{2,1},{3,2},{4,3},{5,4},{6,5},{7,6},{8,7},{9,8},{10,9},{11,1... | collective-permute-start | bytes 25928 | tf_op jit(solution)/shard_map/ppermute | solution.py:18
  160.4 1.7 copy-start.2
  160.4 1.7 copy-start.6
  160.4 1.7 copy-start.10
  163.6 6.1 %collective-permute-start.17 = (f32[120,1,128]{2,1,0:T(1,128)S(1)}, f32[120,1,128]{2,1,0:T(1,128)S(1)}, u32[]{:S(2)}, u32[]{:S(2)}) collective-permute-start(f32[120,1,128]{2,1,0:T(1,128)S(1)} %get-tuple-element.16), channel_id=1, source_target_pairs={{0,32},{32,64},{64,96},{96,128},{128,160},{160,192},{192,224},{224... | collective-permute-start | bytes 184328 | tf_op jit(solution)/shard_map/ppermute | solution.py:17
  165.5 9.7 %collective-permute-start.18 = (f32[120,1,128]{2,1,0:T(1,128)S(1)}, f32[120,1,128]{2,1,0:T(1,128)S(1)}, u32[]{:S(2)}, u32[]{:S(2)}) collective-permute-start(f32[120,1,128]{2,1,0:T(1,128)S(1)} %get-tuple-element.17), channel_id=1, source_target_pairs={{32,0},{64,32},{96,64},{128,96},{160,128},{192,160},{224,192},{0,2... | collective-permute-start | bytes 184328 | tf_op jit(solution)/shard_map/ppermute | solution.py:18
  178.8 10.5 %collective-permute-start.19 = (f32[120,18,1]{0,2,1:T(1,128)S(1)}, f32[120,18,1]{0,2,1:T(1,128)S(1)}, u32[]{:S(2)}, u32[]{:S(2)}) collective-permute-start(f32[120,18,1]{0,2,1:T(1,128)S(1)} %copy.118), channel_id=1, source_target_pairs={{0,1},{1,2},{2,3},{3,4},{4,5},{5,6},{6,7},{7,8},{8,9},{9,10},{10,1... | collective-permute-start | bytes 25928 | tf_op jit(solution)/shard_map/ppermute | solution.py:17
  181.1 8.2 %collective-permute-start.20 = (f32[120,18,1]{0,2,1:T(1,128)S(1)}, f32[120,18,1]{0,2,1:T(1,128)S(1)}, u32[]{:S(2)}, u32[]{:S(2)}) collective-permute-start(f32[120,18,1]{0,2,1:T(1,128)S(1)} %copy.119), channel_id=1, source_target_pairs={{1,0},{2,1},{3,2},{4,3},{5,4},{6,5},{7,6},{8,7},{9,8},{10,9},{11,1... | collective-permute-start | bytes 25928 | tf_op jit(solution)/shard_map/ppermute | solution.py:18
  194.8 1.7 copy-start.3
  194.8 1.7 copy-start.7
  194.8 1.7 copy-start.11
where the time goes:
time: 200 us; the launch traced here: 199 us
  starting transfers between devices  90.4 us (45%)
  local copies, waits for them, and re-layouts  64.5 us (32%)
  other arithmetic  22.5 us (11%)
  waiting for transfers between devices  20 us (10%)
    ppermute x10, starting transfers between devices, extended_2(): after = lax.ppermute(leading, axis, down)  47.3 us
    ppermute x10, starting transfers between devices, extended_2(): before = lax.ppermute(last, axis, up)  41.2 us
    gather x2, local copies, waits for them, and re-layouts, shards(): picked = jnp.take(flat, table, axis=1)  30.7 us
    ppermute x10, waiting for transfers between devices, extended_2(): after = lax.ppermute(leading, axis, down)  18.1 us
    reshape x4, local copies, waits for them, and re-layouts, shards(): extended = extended.reshape(fields, levels, rows_local + 2, cols_local + 2)  17.2 us
    slice x12, local copies, waits for them, and re-layouts, extended_2(): last = lax.slice_in_dim(x, length - width, length, axis=dim)  10.3 us
    mul x4, other arithmetic, advance(): down = mixing[:-1] * (center[:, 1:] - center[:, :-1])  6.8 us
    concatenate x8, other arithmetic, extended_2(): x = jnp.concatenate([before, x, after], axis=dim)  5.68 us
  transfers between devices with their start and end apart: 21, of which 9 were waited for; matrix products, arithmetic and copies ran while one was open for 20% of the time, Pallas kernels for 0%

commit v1 on v0

v1 whole, which is shorter than its diff:
```python
import jax
import jax.numpy as jnp
from jax import lax
from jax.sharding import PartitionSpec as P

TAPS = 4
SUB = 4
ROW_REACH = 2
COL_REACH = 3


def shifted(x, da, db):
    n_lat = lax.axis_size("lat")
    n_lon = lax.axis_size("lon")
    pairs = []
    for a in range(n_lat):
        for b in range(n_lon):
            src = a * n_lon + b
            dst = ((a + da) % n_lat) * n_lon + (b + db) % n_lon
            pairs.append((src, dst))
    flat = x.reshape(-1)
    return lax.ppermute(flat, ("lat", "lon"), pairs).reshape(x.shape)


def halo8(x, w):
    top = shifted(x[..., -w:, :], 1, 0)
    bottom = shifted(x[..., :w, :], -1, 0)
    left = shifted(x[..., :, -w:], 0, 1)
    right = shifted(x[..., :, :w], 0, -1)
    top_left = shifted(x[..., -w:, -w:], 1, 1)
    top_right = shifted(x[..., -w:, :w], 1, -1)
    bottom_left = shifted(x[..., :w, -w:], -1, 1)
    bottom_right = shifted(x[..., :w, :w], -1, -1)
    upper = jnp.concatenate([top_left, top, top_right], axis=-1)
    middle = jnp.concatenate([left, x, right], axis=-1)
    lower = jnp.concatenate([bottom_left, bottom, bottom_right], axis=-1)
    return jnp.concatenate([upper, middle, lower], axis=-2)


def regrid(partner, table):
    fields, rows, cols = partner.shape
    row = lax.broadcasted_iota(jnp.int32, (rows, cols), 0)
    col = lax.broadcasted_iota(jnp.int32, (rows, cols), 1)
    d_row = table // cols - row
    d_col = table % cols - col
    d_col = jnp.where(d_col > cols // 2, d_col - cols, d_col)
    d_col = jnp.where(d_col < -(cols // 2), d_col + cols, d_col)
    padded = jnp.concatenate(
        [jnp.repeat(partner[:, :1], ROW_REACH, axis=1), partner, jnp.repeat(partner[:, -1:], ROW_REACH, axis=1)],
        axis=1,
    )
    moved = {}
    for a in range(-ROW_REACH, ROW_REACH + 1):
        rows_a = padded[:, ROW_REACH + a : ROW_REACH + a + rows]
        for b in range(-COL_REACH, COL_REACH + 1):
            moved[a, b] = jnp.roll(rows_a, -b, axis=2)
    total = None
    for tap in range(TAPS):
        picked = moved[0, 0]
        for (a, b), values in moved.items():
            hit = jnp.logical_and(d_row[tap] == a, d_col[tap] == b)
            picked = jnp.where(hit[None], values, picked)
        total = picked if total is None else total + picked
    return total / TAPS


def advance(q, wet, zonal, meridional, mixing, flux):
    center = q[..., 1:-1, 1:-1]
    west = q[..., 1:-1, :-2]
    east = q[..., 1:-1, 2:]
    south = q[..., :-2, 1:-1]
    north = q[..., 2:, 1:-1]
    wet_c = wet[1:-1, 1:-1]
    wet_w = wet[1:-1, :-2]
    wet_e = wet[1:-1, 2:]
    wet_s = wet[:-2, 1:-1]
    wet_n = wet[2:, 1:-1]
    horiz = (
        (wet_w * jnp.maximum(zonal, 0.0)) * (west - center)
        + (wet_e * jnp.maximum(-zonal, 0.0)) * (east - center)
        + (wet_s * jnp.maximum(meridional, 0.0)) * (south - center)
        + (wet_n * jnp.maximum(-meridional, 0.0)) * (north - center)
    )
    down = mixing[:-1] * (center[:, 1:] - center[:, :-1])
    vert = jnp.pad(down, ((0, 0), (0, 1), (0, 0), (0, 0))) - jnp.pad(
        down, ((0, 0), (1, 0), (0, 0), (0, 0))
    )
    updated = center + wet_c * (horiz + vert)
    return jnp.concatenate([updated[:, :1] + flux[:, None], updated[:, 1:]], axis=1)


def crop(x, e):
    if e == 0:
        return x
    return x[..., e:-e, e:-e]


def shards(state, zonal, meridional, mixing, exchange_rate, sea_mask, regrid_map):
    tracers = state[0]
    fields, levels, rows, cols = tracers.shape
    section = lax.axis_index("sec")
    sea = sea_mask[0].astype(jnp.float32)
    wet = jnp.where(section == 1, sea, jnp.ones_like(sea))
    surface = tracers[:, 0]
    partner = lax.ppermute(surface, "sec", [(0, 1), (1, 0)])

    width = SUB
    stack = jnp.concatenate(
        [tracers.reshape(fields * levels, rows, cols), zonal[0], meridional[0], mixing[0], wet[None]], axis=0
    )
    ext = halo8(stack, width)
    n_q = fields * levels
    q = ext[:n_q].reshape(fields, levels, rows + 2 * width, cols + 2 * width)
    zonal_x = ext[n_q : n_q + levels]
    meridional_x = ext[n_q + levels : n_q + 2 * levels]
    mixing_x = ext[n_q + 2 * levels : n_q + 3 * levels]
    wet_x = ext[n_q + 3 * levels]
    row_block = lax.axis_index("lat")
    global_row = jnp.arange(rows + 2 * width, dtype=jnp.int32) + row_block * rows - width
    inside = jnp.logical_and(global_row >= 0, global_row < rows * lax.axis_size("lat"))
    wet_x = wet_x * inside.astype(jnp.float32)[:, None]

    regridded = regrid(partner, regrid_map[0])
    flux = exchange_rate[0] * sea * (regridded - surface)
    flux_x = halo8(flux, width - 1)

    for step in range(SUB):
        e = width - 1 - step
        q = advance(
            q,
            crop(wet_x, width - 1 - e),
            crop(zonal_x, width - e),
            crop(meridional_x, width - e),
            crop(mixing_x, width - e),
            crop(flux_x, width - 1 - e),
        )
    return (q[None], flux[None])


def solution(mesh):
    return jax.shard_map(
        shards,
        mesh=mesh,
        in_specs=(
            P("sec", None, None, "lat", "lon"),
            P("sec", None, "lat", "lon"),
            P("sec", None, "lat", "lon"),
            P("sec", None, "lat", "lon"),
            P("sec", "lat", "lon"),
            P("sec", "lat", "lon"),
            P("sec", None, "lat", "lon"),
        ),
        out_specs=(P("sec", None, None, "lat", "lon"), P("sec", None, "lat", "lon")),
        check_vma=False,
    )
```

time: 200 us -> 176 us (0.88)
  the two profiles are of different devices: /device:TPU:6 before, /device:TPU:16 now
where the time goes in v1:
time: 176 us; the launch traced here: 175 us
  starting transfers between devices  77.8 us (44%)
  local copies, waits for them, and re-layouts  56.8 us (32%)
  other arithmetic  37.3 us (21%)
    ppermute x16, starting transfers between devices, shifted(): return lax.ppermute(flat, ('lat', 'lon'), pairs).reshape(x.shape)  75.9 us
    reshape x16, local copies, waits for them, and re-layouts, shifted(): return lax.ppermute(flat, ('lat', 'lon'), pairs).reshape(x.shape)  18.4 us
    reshape x16, local copies, waits for them, and re-layouts, shifted(): flat = x.reshape(-1)  17.2 us
    add x4, other arithmetic, advance(): updated = center + wet_c * (horiz + vert)  12.6 us
    concatenate x1, other arithmetic, halo8(): return jnp.concatenate([upper, middle, lower], axis=-2)  9.12 us
    unnamed x47, local copies, waits for them, and re-layouts  9.07 us
    mul x4, other arithmetic, advance(): down = mixing[:-1] * (center[:, 1:] - center[:, :-1])  5.55 us
    slice x4, local copies, waits for them, and re-layouts, advance(): down = mixing[:-1] * (center[:, 1:] - center[:, :-1])  4.47 us
  transfers between devices with their start and end apart: 17, of which 1 were waited for; matrix products, arithmetic and copies ran while one was open for 25% of the time, Pallas kernels for 0%

profile of v1, /device:TPU:16, one launch (start us, length us, event | category | flops | bytes accessed | tf_op | source)
XLA Modules:
  0.0 174.8 jit_solution(12286276045262323378)
XLA Ops:
  0.7 1.3 constant_dynamic-update-slice_fusion.1
  3.1 1.1 bitcast_dynamic-update-slice_fusion
  4.3 1.3 fusion.162
  5.6 2.2 %reshape.163 = f32[154112]{0:T(1024)} reshape(f32[301,4,128]{2,1,0:T(4,128)} %get-tuple-element.120) | data formatting | bytes 1232896 | tf_op jit(solution)/shard_map/reshape | solution.py:21
  7.7 3.4 %collective-permute-start.1 = (f32[154112]{0:T(1024)}, f32[154112]{0:T(1024)}, u32[]{:S(2)}, u32[]{:S(2)}) collective-permute-start(f32[154112]{0:T(1024)} %reshape.163), channel_id=1, source_target_pairs={{0,32},{1,33},{2,34},{3,35},{4,36},{5,37},{6,38},{7,39},{8,40},{9,... | collective-permute-start | bytes 1849352 | tf_op jit(solution)/shard_map/ppermute | solution.py:22
  11.1 2.1 %reshape.173 = f32[154112]{0:T(1024)} reshape(f32[301,4,128]{2,1,0:T(4,128)} %get-tuple-element.121) | data formatting | bytes 1232896 | tf_op jit(solution)/shard_map/reshape | solution.py:21
  13.3 6.0 %collective-permute-start.6 = (f32[154112]{0:T(1024)}, f32[154112]{0:T(1024)}, u32[]{:S(2)}, u32[]{:S(2)}) collective-permute-start(f32[154112]{0:T(1024)} %reshape.173), channel_id=1, source_target_pairs={{0,224},{1,225},{2,226},{3,227},{4,228},{5,229},{6,230},{7,231},{8... | collective-permute-start | bytes 1849352 | tf_op jit(solution)/shard_map/ppermute | solution.py:22
  20.4 1.9 %collective-permute-start.8 = (f32[2,16,128]{2,1,0:T(8,128)S(1)}, f32[2,16,128]{2,1,0:T(8,128)S(1)}, u32[]{:S(2)}, u32[]{:S(2)}) collective-permute-start(f32[2,16,128]{2,1,0:T(8,128)S(1)} %slice_bitcast_fusion.3), channel_id=1, source_target_pairs={{0,256},{256,0},{1,257},{257,1},{2,258},{258,2},{3,259},{259,3},{4... | collective-permute-start | bytes 49160 | tf_op jit(solution)/shard_map/ppermute | solution.py:105
  22.3 2.0 %fusion.161 = (f32[301,4,4]{2,1,0:T(4,128)}, f32[301,4,4]{2,1,0:T(4,128)S(1)}, f32[301,4,4]{2,1,0:T(4,128)}, f32[301,4,4]{2,1,0:T(4,128)}) fusion(f32[301,16,128]{2,1,0:T(8,128)S(1)} %get-tuple-element.365), kind=kLoop, calls=%fused_computation.551 | loop fusion | bytes 154112 | tf_op jit(solution)/shard_map/slice | solution.py:30
  24.3 3.0 %fusion.163 = (f32[301,16,4]{2,1,0:T(8,128)}, f32[301,16,4]{2,1,0:T(8,128)}) fusion(f32[301,16,128]{2,1,0:T(8,128)S(1)} %get-tuple-element.365), kind=kLoop, calls=%fused_computation.553 | loop fusion | bytes 308224 | tf_op jit(solution)/shard_map/slice | solution.py:28
  29.8 1.6 reshape.161
  31.4 1.6 reshape.165
  33.0 1.6 reshape.171
  35.9 2.0 %subtract_multiply_fusion = f32[2,16,128]{2,1,0:T(8,128)S(1)} fusion(f32[2,16,128]{2,1,0:T(8,128)S(1)} %collective-permute-done.8, f32[2,2,128]{2,1,0:T(2,128)S(1)} %reshape.179, f32[2,16,3]{2,1,0:T(8,128)S(1)} %get-tuple-element.269, f32[2,16,3]{2,1,0:T(8,128)S(1)} %get-tuple-element.336, f32[2,16,125]{2,1,0:T(8,128)S(1)} %get-tuple-element.332, ...), kind=kLoop, calls=%fused_computation.337 | loop fusion | flops 745472 | bytes 807680 | tf_op jit(solution)/shard_map/mul | solution.py:124
  38.2 3.2 %collective-permute-start.12 = (f32[96]{0:T(128)S(1)}, f32[96]{0:T(128)S(1)}, u32[]{:S(2)}, u32[]{:S(2)}) collective-permute-start(f32[96]{0:T(128)S(1)} %reshape.186), channel_id=1, source_target_pairs={{0,1},{1,2},{2,3},{3,4},{4,5},{5,6},{6,7},{7,8},{8,9},{9,10},{10,1... | collective-permute-start | bytes 1160 | tf_op jit(solution)/shard_map/ppermute | solution.py:22
  41.6 1.9 %collective-permute-start.9 = (f32[18]{0:T(128)S(1)}, f32[18]{0:T(128)S(1)}, u32[]{:S(2)}, u32[]{:S(2)}) collective-permute-start(f32[18]{0:T(128)S(1)} %reshape.180), channel_id=1, source_target_pairs={{0,33},{1,34},{2,35},{3,36},{4,37},{5,38},{6,39},{7,40},{8,41},{9,... | collective-permute-start | bytes 224 | tf_op jit(solution)/shard_map/ppermute | solution.py:22
  43.6 8.2 %collective-permute-start.11 = (f32[18]{0:T(128)S(1)}, f32[18]{0:T(128)S(1)}, u32[]{:S(2)}, u32[]{:S(2)}) collective-permute-start(f32[18]{0:T(128)S(1)} %reshape.184), channel_id=1, source_target_pairs={{0,63},{1,32},{2,33},{3,34},{4,35},{5,36},{6,37},{7,38},{8,39},{9,... | collective-permute-start | bytes 224 | tf_op jit(solution)/shard_map/ppermute | solution.py:22
  52.0 1.9 %collective-permute-start.14 = (f32[18]{0:T(128)S(1)}, f32[18]{0:T(128)S(1)}, u32[]{:S(2)}, u32[]{:S(2)}) collective-permute-start(f32[18]{0:T(128)S(1)} %reshape.190), channel_id=1, source_target_pairs={{0,225},{1,226},{2,227},{3,228},{4,229},{5,230},{6,231},{7,232},{8... | collective-permute-start | bytes 224 | tf_op jit(solution)/shard_map/ppermute | solution.py:22
  53.9 8.7 %collective-permute-start.16 = (f32[18]{0:T(128)S(1)}, f32[18]{0:T(128)S(1)}, u32[]{:S(2)}, u32[]{:S(2)}) collective-permute-start(f32[18]{0:T(128)S(1)} %reshape.194), channel_id=1, source_target_pairs={{0,255},{1,224},{2,225},{3,226},{4,227},{5,228},{6,229},{7,230},{8... | collective-permute-start | bytes 224 | tf_op jit(solution)/shard_map/ppermute | solution.py:22
  62.6 1.9 %collective-permute-start = (f32[4816]{0:T(1024)S(1)}, f32[4816]{0:T(1024)S(1)}, u32[]{:S(2)}, u32[]{:S(2)}) collective-permute-start(f32[4816]{0:T(1024)S(1)} %reshape.161), channel_id=1, source_target_pairs={{0,33},{1,34},{2,35},{3,36},{4,37},{5,38},{6,39},{7,40},{8,41},{9,... | collective-permute-start | bytes 57800 | tf_op jit(solution)/shard_map/ppermute | solution.py:22
  64.6 7.6 %collective-permute-start.2 = (f32[4816]{0:T(1024)S(1)}, f32[4816]{0:T(1024)S(1)}, u32[]{:S(2)}, u32[]{:S(2)}) collective-permute-start(f32[4816]{0:T(1024)S(1)} %reshape.165), channel_id=1, source_target_pairs={{0,63},{1,32},{2,33},{3,34},{4,35},{5,36},{6,37},{7,38},{8,39},{9,... | collective-permute-start | bytes 57800 | tf_op jit(solution)/shard_map/ppermute | solution.py:22
  72.2 4.5 %collective-permute-start.13 = (f32[96]{0:T(128)S(1)}, f32[96]{0:T(128)S(1)}, u32[]{:S(2)}, u32[]{:S(2)}) collective-permute-start(f32[96]{0:T(128)S(1)} %reshape.188), channel_id=1, source_target_pairs={{0,31},{1,0},{2,1},{3,2},{4,3},{5,4},{6,5},{7,6},{8,7},{9,8},{10,9... | collective-permute-start | bytes 1160 | tf_op jit(solution)/shard_map/ppermute | solution.py:22
  76.8 1.2 collective-permute-done.13
  78.0 6.6 %collective-permute-start.5 = (f32[4816]{0:T(1024)S(1)}, f32[4816]{0:T(1024)S(1)}, u32[]{:S(2)}, u32[]{:S(2)}) collective-permute-start(f32[4816]{0:T(1024)S(1)} %reshape.171), channel_id=1, source_target_pairs={{0,225},{1,226},{2,227},{3,228},{4,229},{5,230},{6,231},{7,232},{8... | collective-permute-start | bytes 57800 | tf_op jit(solution)/shard_map/ppermute | solution.py:22
  84.7 4.3 %collective-permute-start.7 = (f32[4816]{0:T(1024)S(1)}, f32[4816]{0:T(1024)S(1)}, u32[]{:S(2)}, u32[]{:S(2)}) collective-permute-start(f32[4816]{0:T(1024)S(1)} %reshape.175), channel_id=1, source_target_pairs={{0,255},{1,224},{2,225},{3,226},{4,227},{5,228},{6,229},{7,230},{8... | collective-permute-start | bytes 57800 | tf_op jit(solution)/shard_map/ppermute | solution.py:22
  89.0 6.0 %collective-permute-start.10 = (f32[768]{0:T(1024)S(1)}, f32[768]{0:T(1024)S(1)}, u32[]{:S(2)}, u32[]{:S(2)}) collective-permute-start(f32[768]{0:T(1024)S(1)} %reshape.182), channel_id=1, source_target_pairs={{0,32},{1,33},{2,34},{3,35},{4,36},{5,37},{6,38},{7,39},{8,40},{9,... | collective-permute-start | bytes 9224 | tf_op jit(solution)/shard_map/ppermute | solution.py:22
  95.8 3.5 %reshape.167 = f32[19264]{0:T(1024)S(1)} reshape(f32[301,16,4]{2,1,0:T(8,128)} %get-tuple-element.122) | data formatting | bytes 154112 | tf_op jit(solution)/shard_map/reshape | solution.py:21
  99.3 3.5 %reshape.169 = f32[19264]{0:T(1024)S(1)} reshape(f32[301,16,4]{2,1,0:T(8,128)} %get-tuple-element.123) | data formatting | bytes 154112 | tf_op jit(solution)/shard_map/reshape | solution.py:21
  102.8 1.9 %collective-permute-start.3 = (f32[19264]{0:T(1024)S(1)}, f32[19264]{0:T(1024)S(1)}, u32[]{:S(2)}, u32[]{:S(2)}) collective-permute-start(f32[19264]{0:T(1024)S(1)} %reshape.167), channel_id=1, source_target_pairs={{0,1},{1,2},{2,3},{3,4},{4,5},{5,6},{6,7},{7,8},{8,9},{9,10},{10,1... | collective-permute-start | bytes 231176 | tf_op jit(solution)/shard_map/ppermute | solution.py:22
  104.8 6.0 %collective-permute-start.4 = (f32[19264]{0:T(1024)S(1)}, f32[19264]{0:T(1024)S(1)}, u32[]{:S(2)}, u32[]{:S(2)}) collective-permute-start(f32[19264]{0:T(1024)S(1)} %reshape.169), channel_id=1, source_target_pairs={{0,31},{1,0},{2,1},{3,2},{4,3},{5,4},{6,5},{7,6},{8,7},{9,8},{10,9... | collective-permute-start | bytes 231176 | tf_op jit(solution)/shard_map/ppermute | solution.py:22
  110.8 3.7 %collective-permute-start.15 = (f32[768]{0:T(1024)S(1)}, f32[768]{0:T(1024)S(1)}, u32[]{:S(2)}, u32[]{:S(2)}) collective-permute-start(f32[768]{0:T(1024)S(1)} %reshape.192), channel_id=1, source_target_pairs={{0,224},{1,225},{2,226},{3,227},{4,228},{5,229},{6,230},{7,231},{8... | collective-permute-start | bytes 9224 | tf_op jit(solution)/shard_map/ppermute | solution.py:22
  116.3 1.7 reshape.166
  118.0 1.6 reshape.172
  119.6 1.6 reshape.176
  121.3 4.0 %reshape.168 = f32[301,16,4]{2,1,0:T(8,128)} reshape(f32[19264]{0:T(1024)S(1)} %collective-permute-done.3) | data formatting | bytes 154112 | tf_op jit(solution)/shard_map/reshape | solution.py:22
  125.3 4.0 %reshape.170 = f32[301,16,4]{2,1,0:T(8,128)} reshape(f32[19264]{0:T(1024)S(1)} %collective-permute-done.4) | data formatting | bytes 154112 | tf_op jit(solution)/shard_map/reshape | solution.py:22
  129.3 2.1 %reshape.164 = f32[301,4,128]{2,1,0:T(4,128)} reshape(f32[154112]{0:T(1024)} %collective-permute-done.1) | data formatting | bytes 1232896 | tf_op jit(solution)/shard_map/reshape | solution.py:22
  131.4 2.1 %reshape.174 = f32[301,4,128]{2,1,0:T(4,128)} reshape(f32[154112]{0:T(1024)} %collective-permute-done.6) | data formatting | bytes 1232896 | tf_op jit(solution)/shard_map/reshape | solution.py:22
  133.5 9.1 %maximum_maximum_fusion = f32[301,24,136]{2,1,0:T(8,128)S(1)} fusion(f32[301,4,4]{2,1,0:T(4,128)} %reshape.176, f32[301,4,128]{2,1,0:T(4,128)} %reshape.174, f32[301,4,4]{2,1,0:T(4,128)} %reshape.172, f32[301,16,4]{2,1,0:T(8,128)} %reshape.170, f32[301,16,128]{2,1,0:T(8,128)S(1)} %get-tuple-element.365, f32[301,16,4]{2,1,0:T(8,128)} %reshape.168, ...), kind=kLoop, calls=%fused_computation.15 | loop fusion | flops 7859712 | bytes 7859712 | tf_op jit(solution)/shard_map/concatenate | solution.py:37
  143.3 1.6 slice.1228
  146.7 1.6 slice.1250
  148.4 1.6 fusion.52
  151.0 3.5 %fusion.42 = f32[2,60,22,134]{3,2,1,0:T(8,128)S(1)} fusion(f32[2,60,24,136]{3,2,1,0:T(8,128)S(1)} %bitcast.375, f32[2,59,22,134]{3,2,1,0:T(8,128)S(1)} %fusion.52, f32[60,22,134]{2,1,0:T(8,128)S(1)} %get-tuple-element.114, f32[60,22,134]{2,1,0:T(8,128)S(1)} %get-tuple-element.115, f32[60,22,134]{2,1,0:T(8,128)S(1)} %get-tuple-element.113, ...), kind=kLoop, calls=%fused_computation.59 | loop fusion | flops 5306400 | bytes 12723568 | tf_op jit(solution)/shard_map/add | solution.py:88
  155.9 1.7 fusion.51
  158.6 4.0 %fusion.25 = f32[2,60,20,132]{3,2,1,0:T(8,128)S(1)} fusion(f32[2,1,22,134]{3,2,1,0:T(8,128)S(1)} %get-tuple-element.10, f32[2,59,22,134]{3,2,1,0:T(8,128)S(1)} %slice.1210, f32[2,59,20,132]{3,2,1,0:T(8,128)S(1)} %fusion.51, f32[60,20,132]{2,1,0:T(8,128)S(1)} %get-tuple-element.110, f32[60,20,132]{2,1,0:T(8,128)S(1)} %get-tuple-element.111, ...), kind=kLoop, calls=%fused_computation.41 | loop fusion | flops 6336000 | bytes 6473280 | tf_op jit(solution)/shard_map/add | solution.py:88
  164.0 1.7 fusion.49
  166.7 3.9 %fusion.6 = f32[2,60,18,130]{3,2,1,0:T(8,128)S(1)} fusion(f32[2,1,20,132]{3,2,1,0:T(8,128)S(1)} %fusion.81, f32[2,59,20,132]{3,2,1,0:T(8,128)S(1)} %slice.1232, f32[2,59,18,130]{3,2,1,0:T(8,128)S(1)} %fusion.49, f32[60,18,130]{2,1,0:T(8,128)S(1)} %get-tuple-element.106, f32[60,18,130]{2,1,0:T(8,128)S(1)} %get-tuple-element.107, ...), kind=kLoop, calls=%fused_computation.22 | loop fusion | flops 5616000 | bytes 5750640 | tf_op jit(solution)/shard_map/add | solution.py:88
  172.5 1.1 fusion.59
  (125 shorter events, 20.4 us)
Async XLA Ops:
  0.6 2.4 %copy-start.11 = (f32[1,60,16,128]{3,2,1,0:T(8,128)S(1)}, f32[1,60,16,128]{3,2,1,0:T(8,128)}, u32[]{:S(2)}) copy-start(f32[1,60,16,128]{3,2,1,0:T(8,128)} %param.9) | copy-start | bytes 1474564
  0.6 3.6 %copy-start.18 = (f32[1,16,128]{2,1,0:T(8,128)S(1)}, f32[1,16,128]{2,1,0:T(8,128)}, u32[]{:S(2)}) copy-start(f32[1,16,128]{2,1,0:T(8,128)} %param.11) | copy-start | bytes 24580
  0.7 3.6 %copy-start.19 = (s32[1,16,128]{2,1,0:T(8,128)S(1)}, s32[1,16,128]{2,1,0:T(8,128)}, u32[]{:S(2)}) copy-start(s32[1,16,128]{2,1,0:T(8,128)} %param.12) | copy-start | bytes 24580
  3.1 16.2 %copy-start.9 = (f32[1,2,60,16,128]{4,3,2,1,0:T(8,128)S(1)}, f32[1,2,60,16,128]{4,3,2,1,0:T(8,128)}, u32[]{:S(2)}) copy-start(f32[1,2,60,16,128]{4,3,2,1,0:T(8,128)} %param.7) | copy-start | bytes 2949124
  7.7 121.5 %collective-permute-start.1 = (f32[154112]{0:T(1024)}, f32[154112]{0:T(1024)}, u32[]{:S(2)}, u32[]{:S(2)}) collective-permute-start(f32[154112]{0:T(1024)} %reshape.163), channel_id=1, source_target_pairs={{0,32},{1,33},{2,34},{3,35},{4,36},{5,37},{6,38},{7,39},{8,40},{9,... | collective-permute-start | bytes 1849352 | tf_op jit(solution)/shard_map/ppermute | solution.py:22
  13.3 118.1 %collective-permute-start.6 = (f32[154112]{0:T(1024)}, f32[154112]{0:T(1024)}, u32[]{:S(2)}, u32[]{:S(2)}) collective-permute-start(f32[154112]{0:T(1024)} %reshape.173), channel_id=1, source_target_pairs={{0,224},{1,225},{2,226},{3,227},{4,228},{5,229},{6,230},{7,231},{8... | collective-permute-start | bytes 1849352 | tf_op jit(solution)/shard_map/ppermute | solution.py:22
  19.5 1.0 copy-start.15
  20.4 14.8 %collective-permute-start.8 = (f32[2,16,128]{2,1,0:T(8,128)S(1)}, f32[2,16,128]{2,1,0:T(8,128)S(1)}, u32[]{:S(2)}, u32[]{:S(2)}) collective-permute-start(f32[2,16,128]{2,1,0:T(8,128)S(1)} %slice_bitcast_fusion.3), channel_id=1, source_target_pairs={{0,256},{256,0},{1,257},{257,1},{2,258},{258,2},{3,259},{259,3},{4... | collective-permute-start | bytes 49160 | tf_op jit(solution)/shard_map/ppermute | solution.py:105
  24.3 3.0 %copy-start.17 = (s32[1,4,16,128]{3,2,1,0:T(8,128)S(1)}, s32[1,4,16,128]{3,2,1,0:T(8,128)}, u32[]{:S(2)}) copy-start(s32[1,4,16,128]{3,2,1,0:T(8,128)} %param.13) | copy-start | bytes 98308
  35.2 59.7 %copy-start.13 = (f32[1,60,16,128]{3,2,1,0:T(8,128)S(1)}, f32[1,60,16,128]{3,2,1,0:T(8,128)}, u32[]{:S(2)}) copy-start(f32[1,60,16,128]{3,2,1,0:T(8,128)} %param.10) | copy-start | bytes 1474564
  38.0 135.7 %copy-start.16 = (f32[2,16,128]{2,1,0:T(8,128)}, f32[2,16,128]{2,1,0:T(8,128)S(1)}, u32[]{:S(2)}) copy-start(f32[2,16,128]{2,1,0:T(8,128)S(1)} %subtract_multiply_fusion) | copy-start | bytes 49156
  38.2 34.0 %collective-permute-start.12 = (f32[96]{0:T(128)S(1)}, f32[96]{0:T(128)S(1)}, u32[]{:S(2)}, u32[]{:S(2)}) collective-permute-start(f32[96]{0:T(128)S(1)} %reshape.186), channel_id=1, source_target_pairs={{0,1},{1,2},{2,3},{3,4},{4,5},{5,6},{6,7},{7,8},{8,9},{9,10},{10,1... | collective-permute-start | bytes 1160 | tf_op jit(solution)/shard_map/ppermute | solution.py:22
  41.6 10.3 %collective-permute-start.9 = (f32[18]{0:T(128)S(1)}, f32[18]{0:T(128)S(1)}, u32[]{:S(2)}, u32[]{:S(2)}) collective-permute-start(f32[18]{0:T(128)S(1)} %reshape.180), channel_id=1, source_target_pairs={{0,33},{1,34},{2,35},{3,36},{4,37},{5,38},{6,39},{7,40},{8,41},{9,... | collective-permute-start | bytes 224 | tf_op jit(solution)/shard_map/ppermute | solution.py:22
  43.6 10.3 %collective-permute-start.11 = (f32[18]{0:T(128)S(1)}, f32[18]{0:T(128)S(1)}, u32[]{:S(2)}, u32[]{:S(2)}) collective-permute-start(f32[18]{0:T(128)S(1)} %reshape.184), channel_id=1, source_target_pairs={{0,63},{1,32},{2,33},{3,34},{4,35},{5,36},{6,37},{7,38},{8,39},{9,... | collective-permute-start | bytes 224 | tf_op jit(solution)/shard_map/ppermute | solution.py:22
  52.0 10.7 %collective-permute-start.14 = (f32[18]{0:T(128)S(1)}, f32[18]{0:T(128)S(1)}, u32[]{:S(2)}, u32[]{:S(2)}) collective-permute-start(f32[18]{0:T(128)S(1)} %reshape.190), channel_id=1, source_target_pairs={{0,225},{1,226},{2,227},{3,228},{4,229},{5,230},{6,231},{7,232},{8... | collective-permute-start | bytes 224 | tf_op jit(solution)/shard_map/ppermute | solution.py:22
  53.9 10.7 %collective-permute-start.16 = (f32[18]{0:T(128)S(1)}, f32[18]{0:T(128)S(1)}, u32[]{:S(2)}, u32[]{:S(2)}) collective-permute-start(f32[18]{0:T(128)S(1)} %reshape.194), channel_id=1, source_target_pairs={{0,255},{1,224},{2,225},{3,226},{4,227},{5,228},{6,229},{7,230},{8... | collective-permute-start | bytes 224 | tf_op jit(solution)/shard_map/ppermute | solution.py:22
  62.6 22.0 %collective-permute-start = (f32[4816]{0:T(1024)S(1)}, f32[4816]{0:T(1024)S(1)}, u32[]{:S(2)}, u32[]{:S(2)}) collective-permute-start(f32[4816]{0:T(1024)S(1)} %reshape.161), channel_id=1, source_target_pairs={{0,33},{1,34},{2,35},{3,36},{4,37},{5,38},{6,39},{7,40},{8,41},{9,... | collective-permute-start | bytes 57800 | tf_op jit(solution)/shard_map/ppermute | solution.py:22
  64.6 24.4 %collective-permute-start.2 = (f32[4816]{0:T(1024)S(1)}, f32[4816]{0:T(1024)S(1)}, u32[]{:S(2)}, u32[]{:S(2)}) collective-permute-start(f32[4816]{0:T(1024)S(1)} %reshape.165), channel_id=1, source_target_pairs={{0,63},{1,32},{2,33},{3,34},{4,35},{5,36},{6,37},{7,38},{8,39},{9,... | collective-permute-start | bytes 57800 | tf_op jit(solution)/shard_map/ppermute | solution.py:22
  72.2 5.8 %collective-permute-start.13 = (f32[96]{0:T(128)S(1)}, f32[96]{0:T(128)S(1)}, u32[]{:S(2)}, u32[]{:S(2)}) collective-permute-start(f32[96]{0:T(128)S(1)} %reshape.188), channel_id=1, source_target_pairs={{0,31},{1,0},{2,1},{3,2},{4,3},{5,4},{6,5},{7,6},{8,7},{9,8},{10,9... | collective-permute-start | bytes 1160 | tf_op jit(solution)/shard_map/ppermute | solution.py:22
  78.0 24.8 %collective-permute-start.5 = (f32[4816]{0:T(1024)S(1)}, f32[4816]{0:T(1024)S(1)}, u32[]{:S(2)}, u32[]{:S(2)}) collective-permute-start(f32[4816]{0:T(1024)S(1)} %reshape.171), channel_id=1, source_target_pairs={{0,225},{1,226},{2,227},{3,228},{4,229},{5,230},{6,231},{7,232},{8... | collective-permute-start | bytes 57800 | tf_op jit(solution)/shard_map/ppermute | solution.py:22
  84.7 20.1 %collective-permute-start.7 = (f32[4816]{0:T(1024)S(1)}, f32[4816]{0:T(1024)S(1)}, u32[]{:S(2)}, u32[]{:S(2)}) collective-permute-start(f32[4816]{0:T(1024)S(1)} %reshape.175), channel_id=1, source_target_pairs={{0,255},{1,224},{2,225},{3,226},{4,227},{5,228},{6,229},{7,230},{8... | collective-permute-start | bytes 57800 | tf_op jit(solution)/shard_map/ppermute | solution.py:22
  89.0 21.8 %collective-permute-start.10 = (f32[768]{0:T(1024)S(1)}, f32[768]{0:T(1024)S(1)}, u32[]{:S(2)}, u32[]{:S(2)}) collective-permute-start(f32[768]{0:T(1024)S(1)} %reshape.182), channel_id=1, source_target_pairs={{0,32},{1,33},{2,34},{3,35},{4,36},{5,37},{6,38},{7,39},{8,40},{9,... | collective-permute-start | bytes 9224 | tf_op jit(solution)/shard_map/ppermute | solution.py:22
  102.8 18.5 %collective-permute-start.3 = (f32[19264]{0:T(1024)S(1)}, f32[19264]{0:T(1024)S(1)}, u32[]{:S(2)}, u32[]{:S(2)}) collective-permute-start(f32[19264]{0:T(1024)S(1)} %reshape.167), channel_id=1, source_target_pairs={{0,1},{1,2},{2,3},{3,4},{4,5},{5,6},{6,7},{7,8},{8,9},{9,10},{10,1... | collective-permute-start | bytes 231176 | tf_op jit(solution)/shard_map/ppermute | solution.py:22
  104.8 20.5 %collective-permute-start.4 = (f32[19264]{0:T(1024)S(1)}, f32[19264]{0:T(1024)S(1)}, u32[]{:S(2)}, u32[]{:S(2)}) collective-permute-start(f32[19264]{0:T(1024)S(1)} %reshape.169), channel_id=1, source_target_pairs={{0,31},{1,0},{2,1},{3,2},{4,3},{5,4},{6,5},{7,6},{8,7},{9,8},{10,9... | collective-permute-start | bytes 231176 | tf_op jit(solution)/shard_map/ppermute | solution.py:22
  110.8 10.5 %collective-permute-start.15 = (f32[768]{0:T(1024)S(1)}, f32[768]{0:T(1024)S(1)}, u32[]{:S(2)}, u32[]{:S(2)}) collective-permute-start(f32[768]{0:T(1024)S(1)} %reshape.192), channel_id=1, source_target_pairs={{0,224},{1,225},{2,226},{3,227},{4,228},{5,229},{6,230},{7,231},{8... | collective-permute-start | bytes 9224 | tf_op jit(solution)/shard_map/ppermute | solution.py:22
  142.6 2.3 %copy-start.5 = (f32[301,4,4]{2,1,0:T(4,128)S(1)}, f32[301,4,4]{2,1,0:T(4,128)}, u32[]{:S(2)}) copy-start(f32[301,4,4]{2,1,0:T(4,128)} %reshape.172) | copy-start | bytes 57796
  142.6 2.3 %copy-start.6 = (f32[301,4,4]{2,1,0:T(4,128)S(1)}, f32[301,4,4]{2,1,0:T(4,128)}, u32[]{:S(2)}) copy-start(f32[301,4,4]{2,1,0:T(4,128)} %reshape.176) | copy-start | bytes 57796
  142.6 2.3 %copy-start.7 = (f32[301,4,128]{2,1,0:T(4,128)S(1)}, f32[301,4,128]{2,1,0:T(4,128)}, u32[]{:S(2)}) copy-start(f32[301,4,128]{2,1,0:T(4,128)} %reshape.164) | copy-start | bytes 1849348
  142.6 2.3 %copy-start.8 = (f32[301,4,128]{2,1,0:T(4,128)S(1)}, f32[301,4,128]{2,1,0:T(4,128)}, u32[]{:S(2)}) copy-start(f32[301,4,128]{2,1,0:T(4,128)} %reshape.174) | copy-start | bytes 1849348
  142.8 2.8 %copy-start = (f32[301,16,4]{2,1,0:T(8,128)S(1)}, f32[301,16,4]{2,1,0:T(8,128)}, u32[]{:S(2)}) copy-start(f32[301,16,4]{2,1,0:T(8,128)} %reshape.168) | copy-start | bytes 231172
  142.8 3.5 %copy-start.1 = (f32[301,16,4]{2,1,0:T(8,128)S(1)}, f32[301,16,4]{2,1,0:T(8,128)}, u32[]{:S(2)}) copy-start(f32[301,16,4]{2,1,0:T(8,128)} %reshape.170) | copy-start | bytes 231172
  142.9 3.6 %copy-start.4 = (f32[301,4,4]{2,1,0:T(4,128)S(1)}, f32[301,4,4]{2,1,0:T(4,128)}, u32[]{:S(2)}) copy-start(f32[301,4,4]{2,1,0:T(4,128)} %reshape.166) | copy-start | bytes 57796
  142.9 3.6 %copy-start.20 = (f32[24]{0:T(128)S(1)}, f32[24]{0:T(128)}, u32[]{:S(2)}) copy-start(f32[24]{0:T(128)} %and_convert_fusion) | copy-start | bytes 292
  154.6 1.4 copy-start.3
  162.6 1.4 copy-start.2
  170.6 1.0 copy-start.14
  170.9 1.5 copy-start.10
  170.9 1.5 copy-start.12

commit v2 on v1

--- a/solution.py
+++ b/solution.py
@@ -9,32 +9,18 @@
 COL_REACH = 3
 
 
-def shifted(x, da, db):
-    n_lat = lax.axis_size("lat")
-    n_lon = lax.axis_size("lon")
-    pairs = []
-    for a in range(n_lat):
-        for b in range(n_lon):
-            src = a * n_lon + b
-            dst = ((a + da) % n_lat) * n_lon + (b + db) % n_lon
-            pairs.append((src, dst))
-    flat = x.reshape(-1)
-    return lax.ppermute(flat, ("lat", "lon"), pairs).reshape(x.shape)
+def shifted(x, axis, step):
+    count = lax.axis_size(axis)
+    return lax.ppermute(x, axis, [(i, (i + step) % count) for i in range(count)])
 
 
-def halo8(x, w):
-    top = shifted(x[..., -w:, :], 1, 0)
-    bottom = shifted(x[..., :w, :], -1, 0)
-    left = shifted(x[..., :, -w:], 0, 1)
-    right = shifted(x[..., :, :w], 0, -1)
-    top_left = shifted(x[..., -w:, -w:], 1, 1)
-    top_right = shifted(x[..., -w:, :w], 1, -1)
-    bottom_left = shifted(x[..., :w, -w:], -1, 1)
-    bottom_right = shifted(x[..., :w, :w], -1, -1)
-    upper = jnp.concatenate([top_left, top, top_right], axis=-1)
-    middle = jnp.concatenate([left, x, right], axis=-1)
-    lower = jnp.concatenate([bottom_left, bottom, bottom_right], axis=-1)
-    return jnp.concatenate([upper, middle, lower], axis=-2)
+def halo2(x, w):
+    top = shifted(x[:, -w:, :], "lat", 1)
+    bottom = shifted(x[:, :w, :], "lat", -1)
+    x = jnp.concatenate([top, x, bottom], axis=1)
+    left = shifted(x[:, :, -w:], "lon", 1)
+    right = shifted(x[:, :, :w], "lon", -1)
+    return jnp.concatenate([left, x, right], axis=2)
 
 
 def regrid(partner, table):
@@ -104,25 +90,25 @@
     surface = tracers[:, 0]
     partner = lax.ppermute(surface, "sec", [(0, 1), (1, 0)])
 
+    regridded = regrid(partner, regrid_map[0])
+    flux = exchange_rate[0] * sea * (regridded - surface)
+
     width = SUB
     stack = jnp.concatenate(
-        [tracers.reshape(fields * levels, rows, cols), zonal[0], meridional[0], mixing[0], wet[None]], axis=0
+        [tracers.reshape(fields * levels, rows, cols), zonal[0], meridional[0], mixing[0], wet[None], flux], axis=0
     )
-    ext = halo8(stack, width)
+    ext = halo2(stack, width)
     n_q = fields * levels
     q = ext[:n_q].reshape(fields, levels, rows + 2 * width, cols + 2 * width)
     zonal_x = ext[n_q : n_q + levels]
     meridional_x = ext[n_q + levels : n_q + 2 * levels]
     mixing_x = ext[n_q + 2 * levels : n_q + 3 * levels]
     wet_x = ext[n_q + 3 * levels]
+    flux_x = ext[n_q + 3 * levels + 1 :]
     row_block = lax.axis_index("lat")
     global_row = jnp.arange(rows + 2 * width, dtype=jnp.int32) + row_block * rows - width
     inside = jnp.logical_and(global_row >= 0, global_row < rows * lax.axis_size("lat"))
     wet_x = wet_x * inside.astype(jnp.float32)[:, None]
-
-    regridded = regrid(partner, regrid_map[0])
-    flux = exchange_rate[0] * sea * (regridded - surface)
-    flux_x = halo8(flux, width - 1)
 
     for step in range(SUB):
         e = width - 1 - step
@@ -132,7 +118,7 @@
             crop(zonal_x, width - e),
             crop(meridional_x, width - e),
             crop(mixing_x, width - e),
-            crop(flux_x, width - 1 - e),
+            crop(flux_x, width - e),
         )
     return (q[None], flux[None])
 

time: 176 us -> 153 us (0.87)
  the two profiles are of different devices: /device:TPU:16 before, /device:TPU:1 now
where the time goes in v2:
time: 153 us; the launch traced here: 152 us
  other arithmetic  55.1 us (36%)
  local copies, waits for them, and re-layouts  51 us (33%)
  starting transfers between devices  26.7 us (17%)
  waiting for transfers between devices  18 us (12%)
    ppermute x4, waiting for transfers between devices, shifted(): lax.ppermute(x, axis, [(i, (i + step) % count) for i in range(count)])  18 us
    ppermute x4, starting transfers between devices, shifted(): lax.ppermute(x, axis, [(i, (i + step) % count) for i in range(count)])  17.9 us
    add x4, other arithmetic, advance(): updated = center + wet_c * (horiz + vert)  17.2 us
    mul x4, other arithmetic, advance(): wet_w * jnp.maximum(zonal, 0.0)  13 us
    slice x5, local copies, waits for them, and re-layouts, advance(): down = mixing[:-1] * (center[:, 1:] - center[:, :-1])  11.4 us
    concatenate x1, other arithmetic, halo2(): return jnp.concatenate([left, x, right], axis=2)  9.51 us
    ppermute x2, local copies, waits for them, and re-layouts, shifted(): lax.ppermute(x, axis, [(i, (i + step) % count) for i in range(count)])  8.9 us
    ppermute x1, starting transfers between devices, shards(): partner = lax.ppermute(surface, 'sec', [(0, 1), (1, 0)])  8.73 us
  transfers between devices with their start and end apart: 5, of which 3 were waited for; matrix products, arithmetic and copies ran while one was open for 9% of the time, Pallas kernels for 0%

profile of v2, /device:TPU:1, one launch (start us, length us, event | category | flops | bytes accessed | tf_op | source)
XLA Modules:
  0.0 151.9 jit_solution(14392745425054736784)
XLA Ops:
  0.7 1.4 copy.102
  2.1 0.6 slice_bitcast_fusion.1
  2.7 8.7 %collective-permute-start = (f32[2,16,128]{2,1,0:T(8,128)}, f32[2,16,128]{2,1,0:T(8,128)S(1)}, u32[]{:S(2)}, u32[]{:S(2)}) collective-permute-start(f32[2,16,128]{2,1,0:T(8,128)} %slice_bitcast_fusion.1), channel_id=1, source_target_pairs={{0,256},{256,0},{1,257},{257,1},{2,258},{258,2},{3,259},{259,3},{4... | collective-permute-start | bytes 49160 | tf_op jit(solution)/shard_map/ppermute | solution.py:91
  11.5 1.3 constant_dynamic-update-slice_fusion.2
  12.7 0.8 compare_select_fusion
  13.6 1.1 bitcast_dynamic-update-slice_fusion
  15.1 0.7 multiply_bitcast_fusion
  16.5 2.3 %constant_dynamic-update-slice_fusion = (f32[303,16,128]{2,1,0:T(8,128)S(1)}, f32[2,16,128]{2,1,0:T(8,128)}) fusion(f32[303,16,128]{2,1,0:T(8,128)S(1)} %get-tuple-element.344, f32[2,60,16,128]{3,2,0,1:T(8,128)} %bitcast.369, f32[2,16,128]{2,1,0:T(8,128)S(1)} %collective-permute-done, pred[16,128]{1,0:T(8,128)(4,1)S(1)} %get-tuple-element.437, ...), kind=kLoop, calls=%fused_computation.361 | loop fusion | flops 745472 | bytes 1314816 | tf_op jit(solution)/shard_map/concatenate | solution.py:97
  19.0 1.9 %collective-permute-start.2 = (f32[303,4,128]{2,1,0:T(4,128)S(1)}, f32[303,4,128]{2,1,0:T(4,128)S(1)}, u32[]{:S(2)}, u32[]{:S(2)}) collective-permute-start(f32[303,4,128]{2,1,0:T(4,128)S(1)} %get-tuple-element.120), channel_id=1, source_target_pairs={{0,224},{32,0},{64,32},{96,64},{128,96},{160,128},{192,160},{224,1... | collective-permute-start | bytes 1861640 | tf_op jit(solution)/shard_map/ppermute | solution.py:14
  20.9 3.4 %collective-permute-start.1 = (f32[303,4,128]{2,1,0:T(4,128)S(1)}, f32[303,4,128]{2,1,0:T(4,128)}, u32[]{:S(2)}, u32[]{:S(2)}) collective-permute-start(f32[303,4,128]{2,1,0:T(4,128)S(1)} %get-tuple-element.119), channel_id=1, source_target_pairs={{0,32},{32,64},{64,96},{96,128},{128,160},{160,192},{192,224},{224... | collective-permute-start | bytes 1861640 | tf_op jit(solution)/shard_map/ppermute | solution.py:14
  24.3 12.2 %collective-permute-done.2 = f32[303,4,128]{2,1,0:T(4,128)S(1)} collective-permute-done((f32[303,4,128]{2,1,0:T(4,128)S(1)}, f32[303,4,128]{2,1,0:T(4,128)S(1)}, u32[]{:S(2)}, u32[]{:S(2)}) %collective-permute-start.2) | collective-permute-done | bytes 620576 | tf_op jit(solution)/shard_map/ppermute | solution.py:14
  36.5 5.5 %collective-permute-done.1 = f32[303,4,128]{2,1,0:T(4,128)} collective-permute-done((f32[303,4,128]{2,1,0:T(4,128)S(1)}, f32[303,4,128]{2,1,0:T(4,128)}, u32[]{:S(2)}, u32[]{:S(2)}) %collective-permute-start.1) | collective-permute-done | bytes 620576 | tf_op jit(solution)/shard_map/ppermute | solution.py:14
  42.0 1.7 %pad_maximum_fusion.1 = f32[303,24,128]{2,1,0:T(8,128)S(1)} fusion(f32[303,4,128]{2,1,0:T(4,128)S(1)} %collective-permute-done.2, f32[303,16,128]{2,1,0:T(8,128)S(1)} %get-tuple-element.4, f32[303,4,128]{2,1,0:T(4,128)} %collective-permute-done.1), kind=kLoop, calls=%fused_computation.16 | loop fusion | flops 1861632 | bytes 7446528 | tf_op jit(solution)/shard_map/concatenate | solution.py:20
  43.7 4.2 %fusion.162 = (f32[303,24,4]{2,1,0:T(8,128)}, f32[303,24,4]{2,1,0:T(8,128)}) fusion(f32[303,24,128]{2,1,0:T(8,128)S(1)} %pad_maximum_fusion.1), kind=kLoop, calls=%fused_computation.554 | loop fusion | bytes 465408 | tf_op jit(solution)/shard_map/slice | solution.py:21
  47.9 4.2 %copy.41 = f32[303,24,4]{0,1,2:T(8,128)S(1)} copy(f32[303,24,4]{2,1,0:T(8,128)} %get-tuple-element.111) | data formatting | bytes 232704 | tf_op jit(solution)/shard_map/slice | solution.py:22
  52.0 10.7 %collective-permute-start.4 = (f32[303,24,4]{0,1,2:T(8,128)S(1)}, f32[303,24,4]{0,1,2:T(8,128)S(1)}, u32[]{:S(2)}, u32[]{:S(2)}) collective-permute-start(f32[303,24,4]{0,1,2:T(8,128)S(1)} %copy.41), channel_id=1, source_target_pairs={{0,31},{1,0},{2,1},{3,2},{4,3},{5,4},{6,5},{7,6},{8,7},{9,8},{10,9... | collective-permute-start | bytes 349064 | tf_op jit(solution)/shard_map/ppermute | solution.py:14
  62.8 4.2 %copy.40 = f32[303,24,4]{0,1,2:T(8,128)S(1)} copy(f32[303,24,4]{2,1,0:T(8,128)} %get-tuple-element.110) | data formatting | bytes 232704 | tf_op jit(solution)/shard_map/slice | solution.py:21
  67.0 1.9 %collective-permute-start.3 = (f32[303,24,4]{0,1,2:T(8,128)S(1)}, f32[303,24,4]{0,1,2:T(8,128)}, u32[]{:S(2)}, u32[]{:S(2)}) collective-permute-start(f32[303,24,4]{0,1,2:T(8,128)S(1)} %copy.40), channel_id=1, source_target_pairs={{0,1},{1,2},{2,3},{3,4},{4,5},{5,6},{6,7},{7,8},{8,9},{9,10},{10,1... | collective-permute-start | bytes 349064 | tf_op jit(solution)/shard_map/ppermute | solution.py:14
  68.9 1.8 %slice_bitcast_fusion = f32[59,16,128]{2,1,0:T(8,128)} fusion(f32[1,60,16,128]{3,2,1,0:T(8,128)} %param.10), kind=kLoop, calls=%fused_computation.132 | loop fusion | bytes 966656 | tf_op jit(solution)/shard_map/slice | solution.py:70
  70.8 4.1 %copy.43 = f32[303,24,4]{2,1,0:T(8,128)} copy(f32[303,24,4]{0,1,2:T(8,128)S(1)} %collective-permute-done.4) | data formatting | bytes 232704 | tf_op jit(solution)/shard_map/ppermute | solution.py:14
  74.9 0.2 collective-permute-done.3
  75.1 4.8 %copy.42 = f32[303,24,4]{2,1,0:T(8,128)} copy(f32[303,24,4]{0,1,2:T(8,128)} %collective-permute-done.3) | data formatting | bytes 232704 | tf_op jit(solution)/shard_map/ppermute | solution.py:14
  79.9 9.5 %pad_maximum_fusion = f32[303,24,136]{2,1,0:T(8,128)} fusion(f32[303,24,4]{2,1,0:T(8,128)} %copy.43, f32[303,4,128]{2,1,0:T(4,128)S(1)} %collective-permute-done.2, f32[303,16,128]{2,1,0:T(8,128)S(1)} %get-tuple-element.4, f32[303,4,128]{2,1,0:T(4,128)} %collective-permute-done.1, f32[303,24,4]{2,1,0:T(8,128)} %copy.42), kind=kLoop, calls=%fused_computation.15 | loop fusion | flops 3955968 | bytes 7911936 | tf_op jit(solution)/shard_map/concatenate | solution.py:23
  89.4 2.0 %slice.1145 = f32[120,24,136]{2,1,0:T(8,128)S(1)} slice(f32[303,24,136]{2,1,0:T(8,128)} %pad_maximum_fusion), slice={[0:120], [0:24], [0:136]} | slice | bytes 3133440 | tf_op jit(solution)/shard_map/slice | solution.py:102
  91.4 8.5 %fusion.164 = (f32[2,60,22,134]{3,2,1,0:T(8,128)}, f32[2,60,22,134]{3,2,1,0:T(8,128)}, f32[2,60,22,134]{3,2,1,0:T(8,128)}, f32[2,60,22,134]{3,2,1,0:T(8,128)}, f32[2,60,22,134]{3,2,1,0:T(8,128)}) fusion(f32[2,60,24,136]{3,2,1,0:T(8,128)S(1)} %bitcast.365), kind=kLoop, calls=%fused_computation.556 | loop fusion | bytes 14150400 | tf_op jit(solution)/shard_map/slice | solution.py:54
  99.9 1.6 %fusion.163 = (f32[2,59,22,134]{3,2,1,0:T(8,128)S(1)}, f32[2,59,22,134]{3,2,1,0:T(8,128)S(1)}) fusion(f32[2,60,24,136]{3,2,1,0:T(8,128)S(1)} %bitcast.366), kind=kLoop, calls=%fused_computation.555 | loop fusion | bytes 5565824 | tf_op jit(solution)/shard_map/slice | solution.py:70
  101.5 2.1 %slice.1158 = f32[59,22,134]{2,1,0:T(8,128)S(1)} slice(f32[303,24,136]{2,1,0:T(8,128)} %pad_maximum_fusion), slice={[240:299], [1:23], [1:135]} | slice | bytes 1391456 | tf_op jit(solution)/shard_map/slice | solution.py:70
  103.6 3.0 %slice.1180 = f32[59,20,132]{2,1,0:T(8,128)} slice(f32[303,24,136]{2,1,0:T(8,128)} %pad_maximum_fusion), slice={[240:299], [2:22], [2:134]} | slice | bytes 1246080 | tf_op jit(solution)/shard_map/slice | solution.py:70
  106.6 0.8 fusion.87
  107.6 2.9 %slice.1201 = f32[59,18,130]{2,1,0:T(8,128)} slice(f32[303,24,136]{2,1,0:T(8,128)} %pad_maximum_fusion), slice={[240:299], [3:21], [3:133]} | slice | bytes 1104480 | tf_op jit(solution)/shard_map/slice | solution.py:70
  110.7 0.5 fusion.52
  111.2 5.1 %maximum_multiply_fusion.11 = (f32[60,22,134]{2,1,0:T(8,128)S(1)}, f32[60,22,134]{2,1,0:T(8,128)}, f32[60,22,134]{2,1,0:T(8,128)}, f32[60,22,134]{2,1,0:T(8,128)}) fusion(f32[303,24,136]{2,1,0:T(8,128)} %pad_maximum_fusion, f32[22,134]{1,0:T(8,128)S(1)} %get-tuple-element.259, f32[22,134]{1,0:T(8,128)S(1)} %get-tuple-element.258, ...), kind=kLoop, calls=%fused_computation.93 | loop fusion | flops 1768800 | bytes 4292288 | tf_op jit(solution)/shard_map/mul | solution.py:65
  116.3 6.0 %fusion.42 = f32[2,60,22,134]{3,2,0,1:T(8,128)S(1)} fusion(f32[2,60,22,134]{3,2,1,0:T(8,128)S(1)} %copy-done.7, f32[2,60,22,134]{3,2,1,0:T(8,128)} %get-tuple-element.116, f32[2,60,22,134]{3,2,1,0:T(8,128)} %get-tuple-element.117, f32[2,60,22,134]{3,2,1,0:T(8,128)} %get-tuple-element.118, f32[2,60,22,134]{3,2,1,0:T(8,128)S(1)} %copy-done.6, ...), kind=kLoop, calls=%fused_computation.60 | loop fusion | flops 5306400 | bytes 12723568 | tf_op jit(solution)/shard_map/add | solution.py:74
  122.5 0.9 fusion.82
  123.4 0.5 copy-done.9
  123.8 1.6 %fusion.51 = f32[2,59,20,132]{3,2,0,1:T(8,128)S(1)} fusion(f32[2,59,22,134]{3,2,0,1:T(8,128)S(1)} %slice.1162, f32[2,1,22,134]{3,2,0,1:T(8,128)S(1)} %fusion.82, f32[2,60,22,134]{3,2,0,1:T(8,128)S(1)} %fusion.42, f32[59,20,132]{2,1,0:T(8,128)S(1)} %copy-done.9), kind=kLoop, calls=%fused_computation.74 | loop fusion | flops 934560 | bytes 4530240 | tf_op jit(solution)/shard_map/mul | solution.py:70
  125.5 3.9 %maximum_multiply_fusion.7 = (f32[60,20,132]{2,1,0:T(8,128)S(1)}, f32[60,20,132]{2,1,0:T(8,128)S(1)}, f32[60,20,132]{2,1,0:T(8,128)S(1)}, f32[60,20,132]{2,1,0:T(8,128)}) fusion(f32[303,24,136]{2,1,0:T(8,128)} %pad_maximum_fusion, f32[20,132]{1,0:T(8,128)S(1)} %get-tuple-element.254, f32[20,132]{1,0:T(8,128)S(1)} %get-tuple-element.253, ...), kind=kLoop, calls=%fused_computation.89 | loop fusion | flops 1584000 | bytes 3843840 | tf_op jit(solution)/shard_map/mul | solution.py:65
  129.4 5.0 %fusion.25 = f32[2,60,20,132]{3,2,0,1:T(8,128)S(1)} fusion(f32[2,1,22,134]{3,2,0,1:T(8,128)S(1)} %fusion.82, f32[2,59,22,134]{3,2,0,1:T(8,128)S(1)} %slice.1162, f32[2,59,20,132]{3,2,0,1:T(8,128)S(1)} %fusion.51, f32[60,20,132]{2,1,0:T(8,128)S(1)} %get-tuple-element.104, f32[60,20,132]{2,1,0:T(8,128)} %get-tuple-element.105, ...), kind=kLoop, calls=%fused_computation.42 | loop fusion | flops 6336000 | bytes 6473280 | tf_op jit(solution)/shard_map/add | solution.py:74
  134.6 0.9 fusion.81
  135.5 0.5 copy-done.8
  136.0 1.6 %fusion.49 = f32[2,59,18,130]{3,2,0,1:T(8,128)S(1)} fusion(f32[2,59,20,132]{3,2,0,1:T(8,128)S(1)} %slice.1183, f32[2,1,20,132]{3,2,0,1:T(8,128)S(1)} %fusion.81, f32[2,60,20,132]{3,2,0,1:T(8,128)S(1)} %fusion.25, f32[59,18,130]{2,1,0:T(8,128)S(1)} %copy-done.8), kind=kLoop, calls=%fused_computation.71 | loop fusion | flops 828360 | bytes 4028400 | tf_op jit(solution)/shard_map/mul | solution.py:70
  137.6 4.0 %maximum_multiply_fusion.3 = (f32[60,18,130]{2,1,0:T(8,128)S(1)}, f32[60,18,130]{2,1,0:T(8,128)S(1)}, f32[60,18,130]{2,1,0:T(8,128)S(1)}, f32[60,18,130]{2,1,0:T(8,128)}) fusion(f32[303,24,136]{2,1,0:T(8,128)} %pad_maximum_fusion, f32[18,130]{1,0:T(8,128)S(1)} %get-tuple-element.249, f32[18,130]{1,0:T(8,128)S(1)} %get-tuple-element.248, ...), kind=kLoop, calls=%fused_computation.85 | loop fusion | flops 1404000 | bytes 3407040 | tf_op jit(solution)/shard_map/mul | solution.py:65
  141.6 5.0 %fusion.6 = f32[2,60,18,130]{3,2,0,1:T(8,128)S(1)} fusion(f32[2,1,20,132]{3,2,0,1:T(8,128)S(1)} %fusion.81, f32[2,59,20,132]{3,2,0,1:T(8,128)S(1)} %slice.1183, f32[2,59,18,130]{3,2,0,1:T(8,128)S(1)} %fusion.49, f32[60,18,130]{2,1,0:T(8,128)S(1)} %get-tuple-element.100, f32[60,18,130]{2,1,0:T(8,128)} %get-tuple-element.101, ...), kind=kLoop, calls=%fused_computation.23 | loop fusion | flops 5616000 | bytes 5750640 | tf_op jit(solution)/shard_map/add | solution.py:74
  146.8 0.8 copy-done.11
  147.9 0.8 fusion.80
  148.9 0.6 fusion.73
  149.6 1.2 fusion.59
  150.9 1.0 copy_bitcast_fusion
  (67 shorter events, 2.7 us)
Async XLA Ops:
  0.6 12.9 %copy-start.12 = (f32[1,60,16,128]{3,2,1,0:T(8,128)S(1)}, f32[1,60,16,128]{3,2,1,0:T(8,128)}, u32[]{:S(2)}) copy-start(f32[1,60,16,128]{3,2,1,0:T(8,128)} %param.8) | copy-start | bytes 1474564
  0.6 13.0 %copy-start.10 = (f32[1,60,16,128]{3,2,1,0:T(8,128)S(1)}, f32[1,60,16,128]{3,2,1,0:T(8,128)}, u32[]{:S(2)}) copy-start(f32[1,60,16,128]{3,2,1,0:T(8,128)} %param.9) | copy-start | bytes 1474564
  2.1 9.4 %copy-start.15 = (f32[1,2,60,16,128]{4,3,1,2,0:T(8,128)}, f32[1,2,60,16,128]{4,3,1,2,0:T(8,128)S(1)}, u32[]{:S(2)}) copy-start(f32[1,2,60,16,128]{4,3,1,2,0:T(8,128)S(1)} %copy.102) | copy-start | bytes 2949124
  2.1 13.0 %copy-start.17 = (f32[1,16,128]{2,1,0:T(8,128)S(1)}, f32[1,16,128]{2,1,0:T(8,128)}, u32[]{:S(2)}) copy-start(f32[1,16,128]{2,1,0:T(8,128)} %param.11) | copy-start | bytes 24580
  2.7 13.1 %collective-permute-start = (f32[2,16,128]{2,1,0:T(8,128)}, f32[2,16,128]{2,1,0:T(8,128)S(1)}, u32[]{:S(2)}, u32[]{:S(2)}) collective-permute-start(f32[2,16,128]{2,1,0:T(8,128)} %slice_bitcast_fusion.1), channel_id=1, source_target_pairs={{0,256},{256,0},{1,257},{257,1},{2,258},{258,2},{3,259},{259,3},{4... | collective-permute-start | bytes 49160 | tf_op jit(solution)/shard_map/ppermute | solution.py:91
  18.8 61.1 %copy-start.2 = (f32[303,16,128]{2,1,0:T(8,128)}, f32[303,16,128]{2,1,0:T(8,128)S(1)}, u32[]{:S(2)}) copy-start(f32[303,16,128]{2,1,0:T(8,128)S(1)} %get-tuple-element.4) | copy-start | bytes 7446532
  19.0 17.5 %collective-permute-start.2 = (f32[303,4,128]{2,1,0:T(4,128)S(1)}, f32[303,4,128]{2,1,0:T(4,128)S(1)}, u32[]{:S(2)}, u32[]{:S(2)}) collective-permute-start(f32[303,4,128]{2,1,0:T(4,128)S(1)} %get-tuple-element.120), channel_id=1, source_target_pairs={{0,224},{32,0},{64,32},{96,64},{128,96},{160,128},{192,160},{224,1... | collective-permute-start | bytes 1861640 | tf_op jit(solution)/shard_map/ppermute | solution.py:14
  20.9 21.1 %collective-permute-start.1 = (f32[303,4,128]{2,1,0:T(4,128)S(1)}, f32[303,4,128]{2,1,0:T(4,128)}, u32[]{:S(2)}, u32[]{:S(2)}) collective-permute-start(f32[303,4,128]{2,1,0:T(4,128)S(1)} %get-tuple-element.119), channel_id=1, source_target_pairs={{0,32},{32,64},{64,96},{96,128},{128,160},{160,192},{192,224},{224... | collective-permute-start | bytes 1861640 | tf_op jit(solution)/shard_map/ppermute | solution.py:14
  36.5 43.4 %copy-start.4 = (f32[303,4,128]{2,1,0:T(4,128)}, f32[303,4,128]{2,1,0:T(4,128)S(1)}, u32[]{:S(2)}) copy-start(f32[303,4,128]{2,1,0:T(4,128)S(1)} %collective-permute-done.2) | copy-start | bytes 1861636
  52.0 18.7 %collective-permute-start.4 = (f32[303,24,4]{0,1,2:T(8,128)S(1)}, f32[303,24,4]{0,1,2:T(8,128)S(1)}, u32[]{:S(2)}, u32[]{:S(2)}) collective-permute-start(f32[303,24,4]{0,1,2:T(8,128)S(1)} %copy.41), channel_id=1, source_target_pairs={{0,31},{1,0},{2,1},{3,2},{4,3},{5,4},{6,5},{7,6},{8,7},{9,8},{10,9... | collective-permute-start | bytes 349064 | tf_op jit(solution)/shard_map/ppermute | solution.py:14
  67.0 8.1 %collective-permute-start.3 = (f32[303,24,4]{0,1,2:T(8,128)S(1)}, f32[303,24,4]{0,1,2:T(8,128)}, u32[]{:S(2)}, u32[]{:S(2)}) collective-permute-start(f32[303,24,4]{0,1,2:T(8,128)S(1)} %copy.40), channel_id=1, source_target_pairs={{0,1},{1,2},{2,3},{3,4},{4,5},{5,6},{6,7},{7,8},{8,9},{9,10},{10,1... | collective-permute-start | bytes 349064 | tf_op jit(solution)/shard_map/ppermute | solution.py:14
  99.9 6.7 %copy-start.1 = (f32[303,24,4]{2,1,0:T(8,128)S(1)}, f32[303,24,4]{2,1,0:T(8,128)}, u32[]{:S(2)}) copy-start(f32[303,24,4]{2,1,0:T(8,128)} %copy.42) | copy-start | bytes 349060
  99.9 6.7 %copy-start.3 = (f32[303,16,128]{2,1,0:T(8,128)S(1)}, f32[303,16,128]{2,1,0:T(8,128)}, u32[]{:S(2)}) copy-start(f32[303,16,128]{2,1,0:T(8,128)} %copy-done.2) | copy-start | bytes 7446532
  101.5 5.1 %copy-start = (f32[303,24,4]{2,1,0:T(8,128)S(1)}, f32[303,24,4]{2,1,0:T(8,128)}, u32[]{:S(2)}) copy-start(f32[303,24,4]{2,1,0:T(8,128)} %copy.43) | copy-start | bytes 349060
  101.5 5.1 %copy-start.5 = (f32[303,4,128]{2,1,0:T(4,128)S(1)}, f32[303,4,128]{2,1,0:T(4,128)}, u32[]{:S(2)}) copy-start(f32[303,4,128]{2,1,0:T(4,128)} %copy-done.4) | copy-start | bytes 1861636
  111.2 5.1 %copy-start.6 = (f32[2,60,22,134]{3,2,1,0:T(8,128)S(1)}, f32[2,60,22,134]{3,2,1,0:T(8,128)}, u32[]{:S(2)}) copy-start(f32[2,60,22,134]{3,2,1,0:T(8,128)} %get-tuple-element.114) | copy-start | bytes 4245124
  111.2 5.1 %copy-start.7 = (f32[2,60,22,134]{3,2,1,0:T(8,128)S(1)}, f32[2,60,22,134]{3,2,1,0:T(8,128)}, u32[]{:S(2)}) copy-start(f32[2,60,22,134]{3,2,1,0:T(8,128)} %get-tuple-element.115) | copy-start | bytes 4245124
  122.5 1.4 copy-start.9
  134.6 1.4 copy-start.8
  146.6 1.0 copy-start.11
  146.6 1.2 copy-start.13
  147.9 1.0 copy-start.14
  149.6 1.3 copy-start.16

commit v3 on v2

v3 whole, which is shorter than its diff:
```python
import functools

import jax
import jax.numpy as jnp
from jax import lax
from jax.experimental import pallas as pl
from jax.experimental.pallas import tpu as pltpu
from jax.sharding import PartitionSpec as P

TAPS = 4
SUB = 4
ROW_REACH = 2
COL_REACH = 3
LANES = 128
HALF = 64
COL_PAD = 8
INTERPRET = False


def shifted(x, axis, step):
    count = lax.axis_size(axis)
    return lax.ppermute(x, axis, [(i, (i + step) % count) for i in range(count)])


def regrid(partner, table):
    fields, rows, cols = partner.shape
    row = lax.broadcasted_iota(jnp.int32, (rows, cols), 0)
    col = lax.broadcasted_iota(jnp.int32, (rows, cols), 1)
    d_row = table // cols - row
    d_col = table % cols - col
    d_col = jnp.where(d_col > cols // 2, d_col - cols, d_col)
    d_col = jnp.where(d_col < -(cols // 2), d_col + cols, d_col)
    padded = jnp.concatenate(
        [jnp.repeat(partner[:, :1], ROW_REACH, axis=1), partner, jnp.repeat(partner[:, -1:], ROW_REACH, axis=1)],
        axis=1,
    )
    moved = {}
    for a in range(-ROW_REACH, ROW_REACH + 1):
        rows_a = padded[:, ROW_REACH + a : ROW_REACH + a + rows]
        for b in range(-COL_REACH, COL_REACH + 1):
            moved[a, b] = jnp.roll(rows_a, -b, axis=2)
    total = None
    for tap in range(TAPS):
        picked = moved[0, 0]
        for (a, b), values in moved.items():
            hit = jnp.logical_and(d_row[tap] == a, d_col[tap] == b)
            picked = jnp.where(hit[None], values, picked)
        total = picked if total is None else total + picked
    return total / TAPS


def steps_kernel(x_ref, top_ref, bot_ref, left_ref, right_ref, o_ref,
                 s_ref, qa_ref, qb_ref, cw_ref, ce_ref, cs_ref, cn_ref, wc_ref, mx_ref, fl_ref, *, levels, width):
    rows, cols = x_ref.shape[0], x_ref.shape[1]
    ext_rows = rows + 2 * width
    ext_cols = cols + 2 * COL_PAD
    s_ref[width : width + rows, COL_PAD : COL_PAD + cols, :] = x_ref[...]
    s_ref[0:width, COL_PAD : COL_PAD + cols, :] = top_ref[...]
    s_ref[width + rows :, COL_PAD : COL_PAD + cols, :] = bot_ref[...]
    s_ref[:, 0:COL_PAD, :] = left_ref[...]
    s_ref[:, COL_PAD + cols :, :] = right_ref[...]

    lane = lax.broadcasted_iota(jnp.int32, (ext_cols, LANES), 1)
    low = lane < HALF
    level = lane % HALF
    down_ok = level < levels - 1
    level0 = level == 0

    def swap_halves(v):
        return pltpu.roll(v, HALF, 1)

    def wet_of(v):
        return jnp.where(low, swap_halves(v), v)

    def coef_row(r, carry):
        v1 = s_ref[r, :, LANES : 2 * LANES]
        v2 = s_ref[r, :, 2 * LANES : 3 * LANES]
        zon = jnp.where(low, v1, swap_halves(v1))
        mer = jnp.where(low, swap_halves(v1), v1)
        mix = jnp.where(low, v2, swap_halves(v2))
        wet_c = wet_of(v2)
        wet_s = wet_of(s_ref[r - 1, :, 2 * LANES : 3 * LANES])
        wet_n = wet_of(s_ref[r + 1, :, 2 * LANES : 3 * LANES])
        wet_w = pltpu.roll(wet_c, 1, 0)
        wet_e = pltpu.roll(wet_c, ext_cols - 1, 0)
        cw_ref[r] = wet_w * jnp.maximum(zon, 0.0)
        ce_ref[r] = wet_e * jnp.maximum(-zon, 0.0)
        cs_ref[r] = wet_s * jnp.maximum(mer, 0.0)
        cn_ref[r] = wet_n * jnp.maximum(-mer, 0.0)
        wc_ref[r] = wet_c
        mx_ref[r] = mix
        fl_ref[r] = pltpu.roll(s_ref[r, :, 0:LANES], LANES - levels, 1)
        return carry

    lax.fori_loop(1, ext_rows - 1, coef_row, 0)
    qa_ref[...] = s_ref[:, :, 0:LANES]

    def step(src, dst):
        def body(r, carry):
            qc = src[r]
            qs = src[r - 1]
            qn = src[r + 1]
            qw = pltpu.roll(qc, 1, 0)
            qe = pltpu.roll(qc, ext_cols - 1, 0)
            horiz = (
                cw_ref[r] * (qw - qc)
                + ce_ref[r] * (qe - qc)
                + cs_ref[r] * (qs - qc)
                + cn_ref[r] * (qn - qc)
            )
            up = pltpu.roll(qc, LANES - 1, 1)
            down = jnp.where(down_ok, mx_ref[r] * (up - qc), 0.0)
            vert = down - pltpu.roll(down, 1, 1)
            updated = qc + wc_ref[r] * (horiz + vert)
            dst[r] = jnp.where(level0, updated + fl_ref[r], updated)
            return carry

        lax.fori_loop(1, ext_rows - 1, body, 0)

    for k in range(SUB):
        if k % 2 == 0:
            step(qa_ref, qb_ref)
        else:
            step(qb_ref, qa_ref)
    final = qa_ref if SUB % 2 == 0 else qb_ref
    o_ref[...] = final[width : width + rows, COL_PAD : COL_PAD + cols, :]


def run_steps(x, top, bot, left, right, levels, width):
    rows, cols, _ = x.shape
    ext = (rows + 2 * width, cols + 2 * COL_PAD, LANES)
    scratch = [pltpu.VMEM((rows + 2 * width, cols + 2 * COL_PAD, 3 * LANES), jnp.float32)]
    scratch += [pltpu.VMEM(ext, jnp.float32) for _ in range(9)]
    return pl.pallas_call(
        functools.partial(steps_kernel, levels=levels, width=width),
        out_shape=jax.ShapeDtypeStruct((rows, cols, LANES), jnp.float32),
        scratch_shapes=scratch,
        compiler_params=pltpu.CompilerParams(vmem_limit_bytes=60 * 1024 * 1024),
        interpret=INTERPRET,
    )(x, top, bot, left, right)


def to_lanes(x, fill):
    return jnp.concatenate([jnp.transpose(x, (1, 2, 0)), fill], axis=-1)


def shards(state, zonal, meridional, mixing, exchange_rate, sea_mask, regrid_map):
    tracers = state[0]
    fields, levels, rows, cols = tracers.shape
    section = lax.axis_index("sec")
    sea = sea_mask[0].astype(jnp.float32)
    wet = jnp.where(section == 1, sea, jnp.ones_like(sea))
    surface = tracers[:, 0]
    partner = lax.ppermute(surface, "sec", [(0, 1), (1, 0)])

    regridded = regrid(partner, regrid_map[0])
    flux = exchange_rate[0] * sea * (regridded - surface)

    pad = HALF - levels
    zeros = jnp.zeros((rows, cols, pad), jnp.float32)
    flux_pad = [jnp.concatenate([flux[f][:, :, None], zeros[:, :, 1:]], axis=-1) for f in range(fields)]
    x = jnp.concatenate(
        [to_lanes(tracers[0], flux_pad[0]), to_lanes(tracers[1], flux_pad[1]),
         to_lanes(zonal[0], zeros), to_lanes(meridional[0], zeros),
         to_lanes(mixing[0], zeros), jnp.broadcast_to(wet[:, :, None], (rows, cols, HALF))],
        axis=-1,
    )

    width = SUB
    top = shifted(x[-width:], "lat", 1)
    bot = shifted(x[:width], "lat", -1)
    row_block = lax.axis_index("lat")
    wet_lane = lax.broadcasted_iota(jnp.int32, (1, 1, 3 * LANES), 2) >= 2 * LANES + HALF
    top = jnp.where(jnp.logical_and(wet_lane, row_block == 0), 0.0, top)
    bot = jnp.where(jnp.logical_and(wet_lane, row_block == lax.axis_size("lat") - 1), 0.0, bot)
    left = shifted(jnp.concatenate([top[:, -COL_PAD:], x[:, -COL_PAD:], bot[:, -COL_PAD:]], axis=0), "lon", 1)
    right = shifted(jnp.concatenate([top[:, :COL_PAD], x[:, :COL_PAD], bot[:, :COL_PAD]], axis=0), "lon", -1)

    out = run_steps(x, top, bot, left, right, levels, width)
    q = out.reshape(rows, cols, fields, HALF)[..., :levels]
    q = jnp.transpose(q, (2, 3, 0, 1))
    return (q[None], flux[None])


def solution(mesh):
    return jax.shard_map(
        shards,
        mesh=mesh,
        in_specs=(
            P("sec", None, None, "lat", "lon"),
            P("sec", None, "lat", "lon"),
            P("sec", None, "lat", "lon"),
            P("sec", None, "lat", "lon"),
            P("sec", "lat", "lon"),
            P("sec", "lat", "lon"),
            P("sec", None, "lat", "lon"),
        ),
        out_specs=(P("sec", None, None, "lat", "lon"), P("sec", None, "lat", "lon")),
        check_vma=False,
    )
```

time: 153 us -> 120 us (0.78)
  other arithmetic: 55.1 us -> 9.16 us
  Pallas kernels: 0 us -> 22.1 us
  local copies, waits for them, and re-layouts: 51 us -> 30.5 us
  waiting for transfers between devices: 18 us -> 29.3 us
    slice x19 -> x5, local copies, waits for them, and re-layouts: 35.6 us -> 2.69 us  [the longest x1 1.4 us: shards(): bot = shifted(x[:width], 'lat', -1)]
    pallas_call x0 -> x1, Pallas kernels: none -> 22.1 us  [run_steps(): pl.pallas_call(functools.partial(steps_kernel, levels=levels, width=width...]
    add x8 -> x0, other arithmetic: 19.9 us -> none  [the longest x4 17.2 us: advance(): updated = center + wet_c * (horiz + vert)]
    mul x10 -> x0, other arithmetic: 18.3 us -> none  [the longest x4 13 us: advance(): wet_w * jnp.maximum(zonal, 0.0)]
    concatenate x3 -> x2, other arithmetic: 13.4 us -> 0.04 us  [the longest x1 0.02 us: shards(): jnp.concatenate([top[:, -COL_PAD:], x[:, -COL_PAD:], bot[:, -COL_PAD:]],...]
    ppermute x4, waiting for transfers between devices: 18 us -> 29.3 us  [shifted(): lax.ppermute(x, axis, [(i, (i + step) % count) for i in range(count)])]
    ppermute x2 -> x0, local copies, waits for them, and re-layouts: 8.9 us -> none  [shifted(): lax.ppermute(x, axis, [(i, (i + step) % count) for i in range(count)])]
    concatenate x0 -> x1, local copies, waits for them, and re-layouts: none -> 8.38 us  [shards(): jnp.concatenate([to_lanes(tracers[0], flux_pad[0]), to_lanes(tracers[1],...]
  transfers between devices with their start and end apart: 5 -> 5, of which waited for: 3 -> 4; matrix products, arithmetic and copies ran while one was open for 9% -> 12% of each run, Pallas kernels for 0% -> 0%
where the time goes in v3:
time: 120 us
  local copies, waits for them, and re-layouts  30.5 us (25%)
  waiting for transfers between devices  29.3 us (24%)
  starting transfers between devices  26.8 us (22%)
  Pallas kernels  22.1 us (18%)
  other arithmetic  9.16 us (8%)
  between operations  1.56 us (1%)
    ppermute x4, waiting for transfers between devices, shifted(): lax.ppermute(x, axis, [(i, (i + step) % count) for i in range(count)])  29.3 us
    pallas_call x1, Pallas kernels, run_steps(): pl.pallas_call(functools.partial(steps_kernel, levels=levels, width=width...  22.1 us
    ppermute x4, starting transfers between devices, shifted(): lax.ppermute(x, axis, [(i, (i + step) % count) for i in range(count)])  17.9 us
    unnamed x103, local copies, waits for them, and re-layouts  11.5 us
    ppermute x1, starting transfers between devices, shards(): partner = lax.ppermute(surface, 'sec', [(0, 1), (1, 0)])  8.88 us
    concatenate x1, local copies, waits for them, and re-layouts, shards(): jnp.concatenate([to_lanes(tracers[0], flux_pad[0]), to_lanes(tracers[1],...  8.38 us
    broadcast_in_dim x8, other arithmetic, regrid(): picked = jnp.where(hit[None], values, picked)  4.39 us
    another operation x3, local copies, waits for them, and re-layouts, shards(): flux[f][:, :, None]  2.82 us
  transfers between devices with their start and end apart: 5, of which 4 were waited for; matrix products, arithmetic and copies ran while one was open for 12% of the time, Pallas kernels for 0%

profile of v3, /device:TPU:1, one launch (start us, length us, event | category | flops | bytes accessed | tf_op | source)
XLA Modules:
  0.0 119.5 jit_solution(8191231072419209060)
XLA Ops:
  0.6 1.3 %copy.39 = f32[1,2,60,16,128]{4,3,1,2,0:T(8,128)S(1)} copy(f32[1,2,60,16,128]{4,3,2,1,0:T(8,128)} %param.7) | data formatting | bytes 1966080 | tf_op args[0]
  2.0 0.0 copy-start.3
  2.0 8.9 %collective-permute-start = (f32[2,16,128]{2,1,0:T(8,128)S(1)}, f32[2,16,128]{2,1,0:T(8,128)S(1)}, u32[]{:S(2)}, u32[]{:S(2)}) collective-permute-start(f32[2,16,128]{2,1,0:T(8,128)S(1)} %slice_bitcast_fusion.1), channel_id=1, source_target_pairs={{0,256},{256,0},{1,257},{257,1},{2,258},{258,2},{3,259},{259,3},{4... | collective-permute-start | bytes 49160 | tf_op jit(solution)/shard_map/ppermute | solution.py:154
  10.9 1.2 %fusion.82 = (f32[1,1,60,16,128]{4,3,2,1,0:T(8,128)S(1)}, f32[1,1,60,16,128]{4,3,2,1,0:T(8,128)S(1)}) fusion(f32[1,2,60,16,128]{4,3,2,1,0:T(8,128)} %param.7), kind=kLoop, calls=%fused_computation.422 | loop fusion | bytes 1966080 | tf_op jit(solution)/shard_map/slice | solution.py:163
  12.3 0.7 and_bitcast_fusion.132
  13.0 0.7 and_bitcast_fusion.27
  13.7 0.7 and_bitcast_fusion.131
  14.4 0.7 and_bitcast_fusion.96
  15.1 0.7 and_bitcast_fusion.61
  15.9 0.0 copy-start.5
  15.9 0.7 and_bitcast_fusion.26
  16.7 0.7 select_bitcast_fusion
  17.4 1.4 %copy.36 = f32[1,1,60,16,128]{2,4,3,1,0:T(8,128)} copy(f32[1,1,60,16,128]{4,3,2,1,0:T(8,128)S(1)} %get-tuple-element.103) | data formatting | bytes 983040
  18.8 1.4 %copy.37 = f32[1,1,60,16,128]{2,4,3,1,0:T(8,128)} copy(f32[1,1,60,16,128]{4,3,2,1,0:T(8,128)S(1)} %get-tuple-element.102) | data formatting | bytes 983040
  20.5 1.4 %copy.29 = f32[1,60,16,128]{1,3,2,0:T(8,128)} copy(f32[1,60,16,128]{3,2,1,0:T(8,128)S(1)} %copy-done.3) | data formatting | bytes 983040 | tf_op args[1]
  21.9 1.4 %copy.30 = f32[1,60,16,128]{1,3,2,0:T(8,128)} copy(f32[1,60,16,128]{3,2,1,0:T(8,128)S(1)} %copy-done.4) | data formatting | bytes 983040 | tf_op args[2]
  23.2 1.4 %copy.31 = f32[1,60,16,128]{1,3,2,0:T(8,128)} copy(f32[1,60,16,128]{3,2,1,0:T(8,128)S(1)} %copy-done.5) | data formatting | bytes 983040 | tf_op args[3]
  24.6 0.1 fusion.8
  24.8 0.1 fusion.9
  24.9 0.1 fusion.10
  25.0 0.1 fusion.11
  25.1 0.1 fusion.7
  25.2 0.1 fusion.6
  25.7 2.1 %subtract_multiply_fusion = f32[2,16,128]{2,1,0:T(8,128)S(1)} fusion(f32[2,16,128]{2,1,0:T(8,128)S(1)} %collective-permute-done, f32[2,2,128]{2,1,0:T(2,128)S(1)} %reshape.40, f32[2,16,3]{2,1,0:T(8,128)S(1)} %get-tuple-element.229, f32[2,16,3]{2,1,0:T(8,128)S(1)} %get-tuple-element.290, f32[2,16,125]{2,1,0:T(8,128)S(1)} %get-tuple-element.286, ...), kind=kLoop, calls=%fused_computation.203 | loop fusion | flops 745472 | bytes 807680 | tf_op jit(solution)/shard_map/mul | solution.py:157
  27.8 1.4 %copy.32 = f32[16,128,1]{2,1,0:T(8,128)} copy(f32[16,128,1]{1,0,2:T(8,128)S(1)} %get-tuple-element.270) | data formatting | bytes 16384 | tf_op jit(solution)/shard_map/broadcast_in_dim;squeeze | solution.py:161
  29.2 1.4 %copy.33 = f32[16,128,1]{2,1,0:T(8,128)} copy(f32[16,128,1]{1,0,2:T(8,128)S(1)} %get-tuple-element.269) | data formatting | bytes 16384 | tf_op jit(solution)/shard_map/broadcast_in_dim;squeeze | solution.py:161
  30.6 1.3 %broadcast_in_dim.1446 = f32[16,128,64]{2,1,0:T(8,128)} broadcast(f32[16,128]{1,0:T(8,128)S(1)} %get-tuple-element.318), dimensions={0,1} | broadcast | bytes 532480 | tf_op jit(solution)/shard_map/broadcast_in_dim | solution.py:165
  31.9 1.1 broadcast.366
  33.1 1.1 broadcast_in_dim.1444
  34.1 8.4 %concatenate.146.x_ref = f32[16,128,384]{2,1,0:T(8,128)S(1)} concatenate(f32[16,128,60]{2,1,0:T(8,128)} %bitcast.344, f32[16,128,1]{2,1,0:T(8,128)} %copy.32, f32[16,128,3]{2,1,0:T(8,128)} %broadcast.366, f32[16,128,60]{2,1,0:T(8,128)} %bitcast.345, f32[16,128,1]{2,1,0:T(8,128)} %copy.33, f32[16,128,3]{2,1,0:T(8,128)} %broadcast.366, f32[16,128,60]{2,1,0:T(8,128)} %bitcast.346, ...), dimensions={2} | concatenate | bytes 6291456 | tf_op jit(solution)/shard_map/concatenate | solution.py:162
  42.5 1.4 %fusion.81 = (f32[4,128,384]{2,1,0:T(8,128)}, f32[4,128,384]{2,1,0:T(8,128)}) fusion(f32[16,128,384]{2,1,0:T(8,128)S(1)} %concatenate.146.x_ref), kind=kLoop, calls=%fused_computation.421 | loop fusion | bytes 3145728 | tf_op jit(solution)/shard_map/slice | solution.py:171
  43.9 1.9 %collective-permute-start.2 = (f32[4,128,384]{2,1,0:T(8,128)}, f32[4,128,384]{2,1,0:T(8,128)}, u32[]{:S(2)}, u32[]{:S(2)}) collective-permute-start(f32[4,128,384]{2,1,0:T(8,128)} %get-tuple-element.100), channel_id=1, source_target_pairs={{0,224},{32,0},{64,32},{96,64},{128,96},{160,128},{192,160},{224,1... | collective-permute-start | bytes 2359304 | tf_op jit(solution)/shard_map/ppermute | solution.py:22
  45.9 3.4 %collective-permute-start.1 = (f32[4,128,384]{2,1,0:T(8,128)}, f32[4,128,384]{2,1,0:T(8,128)S(1)}, u32[]{:S(2)}, u32[]{:S(2)}) collective-permute-start(f32[4,128,384]{2,1,0:T(8,128)} %get-tuple-element.101), channel_id=1, source_target_pairs={{0,32},{32,64},{64,96},{96,128},{128,160},{160,192},{192,224},{224... | collective-permute-start | bytes 2359304 | tf_op jit(solution)/shard_map/ppermute | solution.py:22
  49.3 15.9 %collective-permute-done.2 = f32[4,128,384]{2,1,0:T(8,128)} collective-permute-done((f32[4,128,384]{2,1,0:T(8,128)}, f32[4,128,384]{2,1,0:T(8,128)}, u32[]{:S(2)}, u32[]{:S(2)}) %collective-permute-start.2) | collective-permute-done | bytes 786464 | tf_op jit(solution)/shard_map/ppermute | solution.py:22
  65.2 1.2 broadcast_select_fusion.bot_ref
  66.4 4.2 %collective-permute-done.1 = f32[4,128,384]{2,1,0:T(8,128)S(1)} collective-permute-done((f32[4,128,384]{2,1,0:T(8,128)}, f32[4,128,384]{2,1,0:T(8,128)S(1)}, u32[]{:S(2)}, u32[]{:S(2)}) %collective-permute-start.1) | collective-permute-done | bytes 786464 | tf_op jit(solution)/shard_map/ppermute | solution.py:22
  70.6 0.1 broadcast_select_fusion.1.top_ref
  70.7 0.0 copy-start.2
  70.7 0.8 copy-done.2
  71.6 10.7 %collective-permute-start.4 = (f32[24,8,384]{2,1,0:T(8,128)S(1)}, f32[24,8,384]{2,1,0:T(8,128)S(1)}, u32[]{:S(2)}, u32[]{:S(2)}) collective-permute-start(f32[24,8,384]{2,1,0:T(8,128)S(1)} %pad_maximum_fusion.1), channel_id=1, source_target_pairs={{0,31},{1,0},{2,1},{3,2},{4,3},{5,4},{6,5},{7,6},{8,7},{9,8},{10,9... | collective-permute-start | bytes 884744 | tf_op jit(solution)/shard_map/ppermute | solution.py:22
  82.4 1.9 %collective-permute-start.3 = (f32[24,8,384]{2,1,0:T(8,128)S(1)}, f32[24,8,384]{2,1,0:T(8,128)S(1)}, u32[]{:S(2)}, u32[]{:S(2)}) collective-permute-start(f32[24,8,384]{2,1,0:T(8,128)S(1)} %pad_maximum_fusion), channel_id=1, source_target_pairs={{0,1},{1,2},{2,3},{3,4},{4,5},{5,6},{6,7},{7,8},{8,9},{9,10},{10,1... | collective-permute-start | bytes 884744 | tf_op jit(solution)/shard_map/ppermute | solution.py:22
  84.3 3.3 %collective-permute-done.4.right_ref = f32[24,8,384]{2,1,0:T(8,128)S(1)} collective-permute-done((f32[24,8,384]{2,1,0:T(8,128)S(1)}, f32[24,8,384]{2,1,0:T(8,128)S(1)}, u32[]{:S(2)}, u32[]{:S(2)}) %collective-permute-start.4) | collective-permute-done | bytes 294944 | tf_op jit(solution)/shard_map/ppermute | solution.py:22
  87.6 5.9 %collective-permute-done.3.left_ref = f32[24,8,384]{2,1,0:T(8,128)S(1)} collective-permute-done((f32[24,8,384]{2,1,0:T(8,128)S(1)}, f32[24,8,384]{2,1,0:T(8,128)S(1)}, u32[]{:S(2)}, u32[]{:S(2)}) %collective-permute-start.3) | collective-permute-done | bytes 294944 | tf_op jit(solution)/shard_map/ppermute | solution.py:22
  93.5 0.7 copy-done.7
  94.2 22.1 %shard_map.86 = f32[16,128,128]{2,1,0:T(8,128)} custom-call(f32[16,128,384]{2,1,0:T(8,128)} %copy-done, f32[4,128,384]{2,1,0:T(8,128)} %copy-done.2, f32[4,128,384]{2,1,0:T(8,128)} %copy-done.1, f32[24,8,384]{2,1,0:T(8,128)} %copy-done.7, f32[24,8,384]{2,1,0:T(8,128)} %copy-done.6), custom_call_target="tpu_custom_call" | custom-call | tf_op jit(solution)/shard_map/pallas_call | solution.py:134
  116.4 1.6 %copy.34 = f32[16,128,128]{1,2,0:T(8,128)S(1)} copy(f32[16,128,128]{2,1,0:T(8,128)} %shard_map.86) | data formatting | bytes 2097152 | tf_op jit(solution)/shard_map/pallas_call | solution.py:134
  117.9 0.1 slice_bitcast_fusion
  118.0 1.5 %copy.35 = f32[1,2,60,16,128]{4,3,2,1,0:T(8,128)} copy(f32[1,2,60,16,128]{4,2,1,3,0:T(8,128)S(1)} %slice_bitcast_fusion) | data formatting | bytes 1966080
  (107 shorter events, 0.4 us)
Async XLA Ops:
  0.6 11.5 %copy-start.9 = (s32[1,4,16,128]{3,2,1,0:T(8,128)S(1)}, s32[1,4,16,128]{3,2,1,0:T(8,128)}, u32[]{:S(2)}) copy-start(s32[1,4,16,128]{3,2,1,0:T(8,128)} %param.13) | copy-start | bytes 98308
  2.0 18.2 %copy-start.3 = (f32[1,60,16,128]{3,2,1,0:T(8,128)S(1)}, f32[1,60,16,128]{3,2,1,0:T(8,128)}, u32[]{:S(2)}) copy-start(f32[1,60,16,128]{3,2,1,0:T(8,128)} %param.8) | copy-start | bytes 1474564
  2.0 22.6 %collective-permute-start = (f32[2,16,128]{2,1,0:T(8,128)S(1)}, f32[2,16,128]{2,1,0:T(8,128)S(1)}, u32[]{:S(2)}, u32[]{:S(2)}) collective-permute-start(f32[2,16,128]{2,1,0:T(8,128)S(1)} %slice_bitcast_fusion.1), channel_id=1, source_target_pairs={{0,256},{256,0},{1,257},{257,1},{2,258},{258,2},{3,259},{259,3},{4... | collective-permute-start | bytes 49160 | tf_op jit(solution)/shard_map/ppermute | solution.py:154
  12.2 9.7 %copy-start.4 = (f32[1,60,16,128]{3,2,1,0:T(8,128)S(1)}, f32[1,60,16,128]{3,2,1,0:T(8,128)}, u32[]{:S(2)}) copy-start(f32[1,60,16,128]{3,2,1,0:T(8,128)} %param.9) | copy-start | bytes 1474564
  15.9 7.3 %copy-start.5 = (f32[1,60,16,128]{3,2,1,0:T(8,128)S(1)}, f32[1,60,16,128]{3,2,1,0:T(8,128)}, u32[]{:S(2)}) copy-start(f32[1,60,16,128]{3,2,1,0:T(8,128)} %param.10) | copy-start | bytes 1474564
  20.1 5.2 %copy-start.11 = (pred[16,128]{1,0:T(8,128)(4,1)S(1)}, pred[16,128]{1,0:T(8,128)(4,1)}, u32[]{:S(2)}) copy-start(pred[16,128]{1,0:T(8,128)(4,1)} %get-tuple-element.117) | copy-start | bytes 6148
  20.1 5.2 %copy-start.12 = (pred[16,128]{1,0:T(8,128)(4,1)S(1)}, pred[16,128]{1,0:T(8,128)(4,1)}, u32[]{:S(2)}) copy-start(pred[16,128]{1,0:T(8,128)(4,1)} %get-tuple-element.119) | copy-start | bytes 6148
  20.1 5.2 %copy-start.13 = (pred[16,128]{1,0:T(8,128)(4,1)S(1)}, pred[16,128]{1,0:T(8,128)(4,1)}, u32[]{:S(2)}) copy-start(pred[16,128]{1,0:T(8,128)(4,1)} %get-tuple-element.121) | copy-start | bytes 6148
  20.2 5.2 %copy-start.14 = (pred[16,128]{1,0:T(8,128)(4,1)S(1)}, pred[16,128]{1,0:T(8,128)(4,1)}, u32[]{:S(2)}) copy-start(pred[16,128]{1,0:T(8,128)(4,1)} %get-tuple-element.181) | copy-start | bytes 6148
  20.2 5.2 %copy-start.15 = (pred[16,128]{1,0:T(8,128)(4,1)S(1)}, pred[16,128]{1,0:T(8,128)(4,1)}, u32[]{:S(2)}) copy-start(pred[16,128]{1,0:T(8,128)(4,1)} %get-tuple-element.183) | copy-start | bytes 6148
  20.2 5.2 %copy-start.16 = (pred[16,128]{1,0:T(8,128)(4,1)S(1)}, pred[16,128]{1,0:T(8,128)(4,1)}, u32[]{:S(2)}) copy-start(pred[16,128]{1,0:T(8,128)(4,1)} %get-tuple-element.185) | copy-start | bytes 6148
  20.2 5.2 %copy-start.17 = (pred[16,128]{1,0:T(8,128)(4,1)S(1)}, pred[16,128]{1,0:T(8,128)(4,1)}, u32[]{:S(2)}) copy-start(pred[16,128]{1,0:T(8,128)(4,1)} %get-tuple-element.187) | copy-start | bytes 6148
  20.2 5.2 %copy-start.18 = (pred[16,128]{1,0:T(8,128)(4,1)S(1)}, pred[16,128]{1,0:T(8,128)(4,1)}, u32[]{:S(2)}) copy-start(pred[16,128]{1,0:T(8,128)(4,1)} %get-tuple-element.189) | copy-start | bytes 6148
  20.2 5.2 %copy-start.19 = (pred[16,128]{1,0:T(8,128)(4,1)S(1)}, pred[16,128]{1,0:T(8,128)(4,1)}, u32[]{:S(2)}) copy-start(pred[16,128]{1,0:T(8,128)(4,1)} %get-tuple-element.191) | copy-start | bytes 6148
  20.2 5.2 %copy-start.20 = (pred[16,128]{1,0:T(8,128)(4,1)S(1)}, pred[16,128]{1,0:T(8,128)(4,1)}, u32[]{:S(2)}) copy-start(pred[16,128]{1,0:T(8,128)(4,1)} %get-tuple-element.193) | copy-start | bytes 6148
  20.2 5.2 %copy-start.21 = (pred[16,128]{1,0:T(8,128)(4,1)S(1)}, pred[16,128]{1,0:T(8,128)(4,1)}, u32[]{:S(2)}) copy-start(pred[16,128]{1,0:T(8,128)(4,1)} %get-tuple-element.195) | copy-start | bytes 6148
  20.2 5.2 %copy-start.22 = (pred[16,128]{1,0:T(8,128)(4,1)S(1)}, pred[16,128]{1,0:T(8,128)(4,1)}, u32[]{:S(2)}) copy-start(pred[16,128]{1,0:T(8,128)(4,1)} %get-tuple-element.90) | copy-start | bytes 6148
  20.2 5.2 %copy-start.23 = (pred[16,128]{1,0:T(8,128)(4,1)S(1)}, pred[16,128]{1,0:T(8,128)(4,1)}, u32[]{:S(2)}) copy-start(pred[16,128]{1,0:T(8,128)(4,1)} %get-tuple-element.165) | copy-start | bytes 6148
  20.3 5.2 %copy-start.24 = (pred[16,128]{1,0:T(8,128)(4,1)S(1)}, pred[16,128]{1,0:T(8,128)(4,1)}, u32[]{:S(2)}) copy-start(pred[16,128]{1,0:T(8,128)(4,1)} %get-tuple-element.167) | copy-start | bytes 6148
  20.3 5.2 %copy-start.25 = (pred[16,128]{1,0:T(8,128)(4,1)S(1)}, pred[16,128]{1,0:T(8,128)(4,1)}, u32[]{:S(2)}) copy-start(pred[16,128]{1,0:T(8,128)(4,1)} %get-tuple-element.169) | copy-start | bytes 6148
  20.3 5.2 %copy-start.26 = (pred[16,128]{1,0:T(8,128)(4,1)S(1)}, pred[16,128]{1,0:T(8,128)(4,1)}, u32[]{:S(2)}) copy-start(pred[16,128]{1,0:T(8,128)(4,1)} %get-tuple-element.416) | copy-start | bytes 6148
  20.3 5.2 %copy-start.27 = (pred[16,128]{1,0:T(8,128)(4,1)S(1)}, pred[16,128]{1,0:T(8,128)(4,1)}, u32[]{:S(2)}) copy-start(pred[16,128]{1,0:T(8,128)(4,1)} %get-tuple-element.418) | copy-start | bytes 6148
  20.3 5.2 %copy-start.28 = (pred[16,128]{1,0:T(8,128)(4,1)S(1)}, pred[16,128]{1,0:T(8,128)(4,1)}, u32[]{:S(2)}) copy-start(pred[16,128]{1,0:T(8,128)(4,1)} %get-tuple-element.420) | copy-start | bytes 6148
  20.3 5.2 %copy-start.29 = (pred[16,128]{1,0:T(8,128)(4,1)S(1)}, pred[16,128]{1,0:T(8,128)(4,1)}, u32[]{:S(2)}) copy-start(pred[16,128]{1,0:T(8,128)(4,1)} %get-tuple-element.422) | copy-start | bytes 6148
  20.3 5.2 %copy-start.30 = (pred[16,128]{1,0:T(8,128)(4,1)S(1)}, pred[16,128]{1,0:T(8,128)(4,1)}, u32[]{:S(2)}) copy-start(pred[16,128]{1,0:T(8,128)(4,1)} %get-tuple-element.424) | copy-start | bytes 6148
  20.3 5.2 %copy-start.31 = (pred[16,128]{1,0:T(8,128)(4,1)S(1)}, pred[16,128]{1,0:T(8,128)(4,1)}, u32[]{:S(2)}) copy-start(pred[16,128]{1,0:T(8,128)(4,1)} %get-tuple-element.426) | copy-start | bytes 6148
  20.3 5.2 %copy-start.32 = (pred[16,128]{1,0:T(8,128)(4,1)S(1)}, pred[16,128]{1,0:T(8,128)(4,1)}, u32[]{:S(2)}) copy-start(pred[16,128]{1,0:T(8,128)(4,1)} %get-tuple-element.428) | copy-start | bytes 6148
  20.4 5.2 %copy-start.33 = (pred[16,128]{1,0:T(8,128)(4,1)S(1)}, pred[16,128]{1,0:T(8,128)(4,1)}, u32[]{:S(2)}) copy-start(pred[16,128]{1,0:T(8,128)(4,1)} %get-tuple-element.430) | copy-start | bytes 6148
  20.4 5.2 %copy-start.34 = (pred[16,128]{1,0:T(8,128)(4,1)S(1)}, pred[16,128]{1,0:T(8,128)(4,1)}, u32[]{:S(2)}) copy-start(pred[16,128]{1,0:T(8,128)(4,1)} %get-tuple-element.432) | copy-start | bytes 6148
  20.4 5.2 %copy-start.35 = (pred[16,128]{1,0:T(8,128)(4,1)S(1)}, pred[16,128]{1,0:T(8,128)(4,1)}, u32[]{:S(2)}) copy-start(pred[16,128]{1,0:T(8,128)(4,1)} %get-tuple-element.434) | copy-start | bytes 6148
  20.4 5.2 %copy-start.36 = (pred[16,128]{1,0:T(8,128)(4,1)S(1)}, pred[16,128]{1,0:T(8,128)(4,1)}, u32[]{:S(2)}) copy-start(pred[16,128]{1,0:T(8,128)(4,1)} %get-tuple-element.436) | copy-start | bytes 6148
  20.4 5.2 %copy-start.37 = (pred[16,128]{1,0:T(8,128)(4,1)S(1)}, pred[16,128]{1,0:T(8,128)(4,1)}, u32[]{:S(2)}) copy-start(pred[16,128]{1,0:T(8,128)(4,1)} %get-tuple-element.438) | copy-start | bytes 6148
  20.4 5.2 %copy-start.38 = (pred[16,128]{1,0:T(8,128)(4,1)S(1)}, pred[16,128]{1,0:T(8,128)(4,1)}, u32[]{:S(2)}) copy-start(pred[16,128]{1,0:T(8,128)(4,1)} %get-tuple-element.320) | copy-start | bytes 6148
  20.4 5.2 %copy-start.39 = (pred[16,128]{1,0:T(8,128)(4,1)S(1)}, pred[16,128]{1,0:T(8,128)(4,1)}, u32[]{:S(2)}) copy-start(pred[16,128]{1,0:T(8,128)(4,1)} %get-tuple-element.321) | copy-start | bytes 6148
  20.4 5.2 %copy-start.40 = (pred[16,128]{1,0:T(8,128)(4,1)S(1)}, pred[16,128]{1,0:T(8,128)(4,1)}, u32[]{:S(2)}) copy-start(pred[16,128]{1,0:T(8,128)(4,1)} %get-tuple-element.322) | copy-start | bytes 6148
  20.4 5.2 %copy-start.41 = (pred[16,128]{1,0:T(8,128)(4,1)S(1)}, pred[16,128]{1,0:T(8,128)(4,1)}, u32[]{:S(2)}) copy-start(pred[16,128]{1,0:T(8,128)(4,1)} %get-tuple-element.323) | copy-start | bytes 6148
  20.4 5.2 %copy-start.42 = (pred[16,128]{1,0:T(8,128)(4,1)S(1)}, pred[16,128]{1,0:T(8,128)(4,1)}, u32[]{:S(2)}) copy-start(pred[16,128]{1,0:T(8,128)(4,1)} %get-tuple-element.324) | copy-start | bytes 6148
  20.5 5.2 %copy-start.43 = (pred[16,128]{1,0:T(8,128)(4,1)S(1)}, pred[16,128]{1,0:T(8,128)(4,1)}, u32[]{:S(2)}) copy-start(pred[16,128]{1,0:T(8,128)(4,1)} %get-tuple-element.325) | copy-start | bytes 6148
  20.5 5.2 %copy-start.44 = (pred[16,128]{1,0:T(8,128)(4,1)S(1)}, pred[16,128]{1,0:T(8,128)(4,1)}, u32[]{:S(2)}) copy-start(pred[16,128]{1,0:T(8,128)(4,1)} %get-tuple-element.326) | copy-start | bytes 6148
  20.5 5.2 %copy-start.45 = (pred[16,128]{1,0:T(8,128)(4,1)S(1)}, pred[16,128]{1,0:T(8,128)(4,1)}, u32[]{:S(2)}) copy-start(pred[16,128]{1,0:T(8,128)(4,1)} %get-tuple-element.327) | copy-start | bytes 6148
  20.5 5.2 %copy-start.46 = (pred[16,128]{1,0:T(8,128)(4,1)S(1)}, pred[16,128]{1,0:T(8,128)(4,1)}, u32[]{:S(2)}) copy-start(pred[16,128]{1,0:T(8,128)(4,1)} %get-tuple-element.328) | copy-start | bytes 6148
  27.8 14.7 %copy-start.8 = (f32[2,16,128]{2,1,0:T(8,128)}, f32[2,16,128]{2,1,0:T(8,128)S(1)}, u32[]{:S(2)}) copy-start(f32[2,16,128]{2,1,0:T(8,128)S(1)} %subtract_multiply_fusion) | copy-start | bytes 49156
  42.5 28.2 %copy-start = (f32[16,128,384]{2,1,0:T(8,128)}, f32[16,128,384]{2,1,0:T(8,128)S(1)}, u32[]{:S(2)}) copy-start(f32[16,128,384]{2,1,0:T(8,128)S(1)} %concatenate.146.x_ref) | copy-start | bytes 9437188
  43.9 21.3 %collective-permute-start.2 = (f32[4,128,384]{2,1,0:T(8,128)}, f32[4,128,384]{2,1,0:T(8,128)}, u32[]{:S(2)}, u32[]{:S(2)}) collective-permute-start(f32[4,128,384]{2,1,0:T(8,128)} %get-tuple-element.100), channel_id=1, source_target_pairs={{0,224},{32,0},{64,32},{96,64},{128,96},{160,128},{192,160},{224,1... | collective-permute-start | bytes 2359304 | tf_op jit(solution)/shard_map/ppermute | solution.py:22
  45.9 24.8 %collective-permute-start.1 = (f32[4,128,384]{2,1,0:T(8,128)}, f32[4,128,384]{2,1,0:T(8,128)S(1)}, u32[]{:S(2)}, u32[]{:S(2)}) collective-permute-start(f32[4,128,384]{2,1,0:T(8,128)} %get-tuple-element.101), channel_id=1, source_target_pairs={{0,32},{32,64},{64,96},{96,128},{128,160},{160,192},{192,224},{224... | collective-permute-start | bytes 2359304 | tf_op jit(solution)/shard_map/ppermute | solution.py:22
  71.6 16.0 %collective-permute-start.4 = (f32[24,8,384]{2,1,0:T(8,128)S(1)}, f32[24,8,384]{2,1,0:T(8,128)S(1)}, u32[]{:S(2)}, u32[]{:S(2)}) collective-permute-start(f32[24,8,384]{2,1,0:T(8,128)S(1)} %pad_maximum_fusion.1), channel_id=1, source_target_pairs={{0,31},{1,0},{2,1},{3,2},{4,3},{5,4},{6,5},{7,6},{8,7},{9,8},{10,9... | collective-permute-start | bytes 884744 | tf_op jit(solution)/shard_map/ppermute | solution.py:22
  82.4 11.1 %collective-permute-start.3 = (f32[24,8,384]{2,1,0:T(8,128)S(1)}, f32[24,8,384]{2,1,0:T(8,128)S(1)}, u32[]{:S(2)}, u32[]{:S(2)}) collective-permute-start(f32[24,8,384]{2,1,0:T(8,128)S(1)} %pad_maximum_fusion), channel_id=1, source_target_pairs={{0,1},{1,2},{2,3},{3,4},{4,5},{5,6},{6,7},{7,8},{8,9},{9,10},{10,1... | collective-permute-start | bytes 884744 | tf_op jit(solution)/shard_map/ppermute | solution.py:22
  87.6 5.9 %copy-start.6 = (f32[24,8,384]{2,1,0:T(8,128)}, f32[24,8,384]{2,1,0:T(8,128)S(1)}, u32[]{:S(2)}) copy-start(f32[24,8,384]{2,1,0:T(8,128)S(1)} %collective-permute-done.4.right_ref) | copy-start | bytes 884740
  (5 other events, 13.5 us)

commit v4 on v3

--- a/solution.py
+++ b/solution.py
@@ -49,16 +49,20 @@
     return total / TAPS
 
 
-def steps_kernel(x_ref, top_ref, bot_ref, left_ref, right_ref, o_ref,
-                 s_ref, qa_ref, qb_ref, cw_ref, ce_ref, cs_ref, cn_ref, wc_ref, mx_ref, fl_ref, *, levels, width):
-    rows, cols = x_ref.shape[0], x_ref.shape[1]
+def steps_kernel(xq_ref, topq_ref, botq_ref, leftq_ref, rightq_ref, xv_ref, topv_ref, botv_ref, leftv_ref, rightv_ref,
+                 o_ref, s_ref, qa_ref, qb_ref, cw_ref, ce_ref, cs_ref, cn_ref, wc_ref, mx_ref, fl_ref, *, levels, width):
+    rows, cols = xq_ref.shape[0], xq_ref.shape[1]
     ext_rows = rows + 2 * width
     ext_cols = cols + 2 * COL_PAD
-    s_ref[width : width + rows, COL_PAD : COL_PAD + cols, :] = x_ref[...]
-    s_ref[0:width, COL_PAD : COL_PAD + cols, :] = top_ref[...]
-    s_ref[width + rows :, COL_PAD : COL_PAD + cols, :] = bot_ref[...]
-    s_ref[:, 0:COL_PAD, :] = left_ref[...]
-    s_ref[:, COL_PAD + cols :, :] = right_ref[...]
+    for lo, hi, x_ref, top_ref, bot_ref, left_ref, right_ref in (
+        (0, LANES, xq_ref, topq_ref, botq_ref, leftq_ref, rightq_ref),
+        (LANES, 3 * LANES, xv_ref, topv_ref, botv_ref, leftv_ref, rightv_ref),
+    ):
+        s_ref[width : width + rows, COL_PAD : COL_PAD + cols, lo:hi] = x_ref[...]
+        s_ref[0:width, COL_PAD : COL_PAD + cols, lo:hi] = top_ref[...]
+        s_ref[width + rows :, COL_PAD : COL_PAD + cols, lo:hi] = bot_ref[...]
+        s_ref[:, 0:COL_PAD, lo:hi] = left_ref[...]
+        s_ref[:, COL_PAD + cols :, lo:hi] = right_ref[...]
 
     lane = lax.broadcasted_iota(jnp.int32, (ext_cols, LANES), 1)
     low = lane < HALF
@@ -95,7 +99,7 @@
     lax.fori_loop(1, ext_rows - 1, coef_row, 0)
     qa_ref[...] = s_ref[:, :, 0:LANES]
 
-    def step(src, dst):
+    def step(src, dst, k):
         def body(r, carry):
             qc = src[r]
             qs = src[r - 1]
@@ -115,19 +119,19 @@
             dst[r] = jnp.where(level0, updated + fl_ref[r], updated)
             return carry
 
-        lax.fori_loop(1, ext_rows - 1, body, 0)
+        lax.fori_loop(k + 1, ext_rows - 1 - k, body, 0)
 
     for k in range(SUB):
         if k % 2 == 0:
-            step(qa_ref, qb_ref)
+            step(qa_ref, qb_ref, k)
         else:
-            step(qb_ref, qa_ref)
+            step(qb_ref, qa_ref, k)
     final = qa_ref if SUB % 2 == 0 else qb_ref
     o_ref[...] = final[width : width + rows, COL_PAD : COL_PAD + cols, :]
 
 
-def run_steps(x, top, bot, left, right, levels, width):
-    rows, cols, _ = x.shape
+def run_steps(q_parts, v_parts, levels, width):
+    rows, cols, _ = q_parts[0].shape
     ext = (rows + 2 * width, cols + 2 * COL_PAD, LANES)
     scratch = [pltpu.VMEM((rows + 2 * width, cols + 2 * COL_PAD, 3 * LANES), jnp.float32)]
     scratch += [pltpu.VMEM(ext, jnp.float32) for _ in range(9)]
@@ -137,11 +141,23 @@
         scratch_shapes=scratch,
         compiler_params=pltpu.CompilerParams(vmem_limit_bytes=60 * 1024 * 1024),
         interpret=INTERPRET,
-    )(x, top, bot, left, right)
-
-
-def to_lanes(x, fill):
-    return jnp.concatenate([jnp.transpose(x, (1, 2, 0)), fill], axis=-1)
+    )(*q_parts, *v_parts)
+
+
+def lanes_last(planes):
+    return jnp.transpose(jnp.concatenate(planes, axis=0), (1, 2, 0))
+
+
+def halo_parts(x, width, mask=None):
+    top = shifted(x[-width:], "lat", 1)
+    bot = shifted(x[:width], "lat", -1)
+    if mask is not None:
+        row_block = lax.axis_index("lat")
+        top = jnp.where(jnp.logical_and(mask, row_block == 0), 0.0, top)
+        bot = jnp.where(jnp.logical_and(mask, row_block == lax.axis_size("lat") - 1), 0.0, bot)
+    left = shifted(jnp.concatenate([top[:, -COL_PAD:], x[:, -COL_PAD:], bot[:, -COL_PAD:]], axis=0), "lon", 1)
+    right = shifted(jnp.concatenate([top[:, :COL_PAD], x[:, :COL_PAD], bot[:, :COL_PAD]], axis=0), "lon", -1)
+    return (x, top, bot, left, right)
 
 
 def shards(state, zonal, meridional, mixing, exchange_rate, sea_mask, regrid_map):
@@ -150,35 +166,26 @@
     section = lax.axis_index("sec")
     sea = sea_mask[0].astype(jnp.float32)
     wet = jnp.where(section == 1, sea, jnp.ones_like(sea))
+    width = SUB
+    gap = jnp.zeros((HALF - levels, rows, cols), jnp.float32)
+
+    xv = lanes_last([zonal[0], gap, meridional[0], gap, mixing[0], gap, jnp.broadcast_to(wet, (HALF, rows, cols))])
+    wet_lane = lax.broadcasted_iota(jnp.int32, (1, 1, 2 * LANES), 2) >= LANES + HALF
+    v_parts = halo_parts(xv, width, wet_lane)
+
     surface = tracers[:, 0]
     partner = lax.ppermute(surface, "sec", [(0, 1), (1, 0)])
-
     regridded = regrid(partner, regrid_map[0])
     flux = exchange_rate[0] * sea * (regridded - surface)
 
-    pad = HALF - levels
-    zeros = jnp.zeros((rows, cols, pad), jnp.float32)
-    flux_pad = [jnp.concatenate([flux[f][:, :, None], zeros[:, :, 1:]], axis=-1) for f in range(fields)]
-    x = jnp.concatenate(
-        [to_lanes(tracers[0], flux_pad[0]), to_lanes(tracers[1], flux_pad[1]),
-         to_lanes(zonal[0], zeros), to_lanes(meridional[0], zeros),
-         to_lanes(mixing[0], zeros), jnp.broadcast_to(wet[:, :, None], (rows, cols, HALF))],
-        axis=-1,
-    )
-
-    width = SUB
-    top = shifted(x[-width:], "lat", 1)
-    bot = shifted(x[:width], "lat", -1)
-    row_block = lax.axis_index("lat")
-    wet_lane = lax.broadcasted_iota(jnp.int32, (1, 1, 3 * LANES), 2) >= 2 * LANES + HALF
-    top = jnp.where(jnp.logical_and(wet_lane, row_block == 0), 0.0, top)
-    bot = jnp.where(jnp.logical_and(wet_lane, row_block == lax.axis_size("lat") - 1), 0.0, bot)
-    left = shifted(jnp.concatenate([top[:, -COL_PAD:], x[:, -COL_PAD:], bot[:, -COL_PAD:]], axis=0), "lon", 1)
-    right = shifted(jnp.concatenate([top[:, :COL_PAD], x[:, :COL_PAD], bot[:, :COL_PAD]], axis=0), "lon", -1)
-
-    out = run_steps(x, top, bot, left, right, levels, width)
-    q = out.reshape(rows, cols, fields, HALF)[..., :levels]
-    q = jnp.transpose(q, (2, 3, 0, 1))
+    planes = []
+    for f in range(fields):
+        planes += [tracers[f], flux[f][None], gap[1:]]
+    xq = lanes_last(planes)
+    q_parts = halo_parts(xq, width)
+
+    out = run_steps(q_parts, v_parts, levels, width)
+    q = jnp.transpose(out, (2, 0, 1)).reshape(fields, HALF, rows, cols)[:, :levels]
     return (q[None], flux[None])
 
 

time: 120 us -> 251 us (2.09)
  the two profiles are of different devices: /device:TPU:1 before, /device:TPU:6 now
where the time goes in v4:
time: 251 us; the launch traced here: 248 us
  local copies, waits for them, and re-layouts  138 us (55%)
  starting transfers between devices  39.7 us (16%)
  other arithmetic  31.5 us (13%)
  Pallas kernels  20.1 us (8%)
  waiting for transfers between devices  17.2 us (7%)
    slice x52, local copies, waits for them, and re-layouts, regrid(): moved[a, b] = jnp.roll(rows_a, -b, axis=2)  70.1 us
    unnamed x149, local copies, waits for them, and re-layouts  38.8 us
    ppermute x8, starting transfers between devices, shifted(): lax.ppermute(x, axis, [(i, (i + step) % count) for i in range(count)])  37.8 us
    pallas_call x1, Pallas kernels, run_steps(): pl.pallas_call(functools.partial(steps_kernel, levels=levels, width=width...  20.1 us
    ppermute x8, waiting for transfers between devices, shifted(): lax.ppermute(x, axis, [(i, (i + step) % count) for i in range(count)])  17.2 us
    concatenate x7, other arithmetic, regrid(): jnp.concatenate([jnp.repeat(partner[:, :1], ROW_REACH, axis=1), partner,...  14.9 us
    concatenate x2, local copies, waits for them, and re-layouts, lanes_last(): return jnp.transpose(jnp.concatenate(planes, axis=0), (1, 2, 0))  9.83 us
    select_n x4, local copies, waits for them, and re-layouts, regrid(): picked = jnp.where(hit[None], values, picked)  7.56 us
  transfers between devices with their start and end apart: 9, of which 3 were waited for; matrix products, arithmetic and copies ran while one was open for 54% of the time, Pallas kernels for 0%

profile of v4, /device:TPU:6, one launch (start us, length us, event | category | flops | bytes accessed | tf_op | source)
XLA Modules:
  0.0 248.4 jit_solution(4515938170854119025)
XLA Ops:
  0.6 29.3 %copy.476 = f32[1,2,60,16,128]{1,4,3,2,0:T(8,128)} copy(f32[1,2,60,16,128]{4,3,2,1,0:T(8,128)} %param.7) | data formatting | bytes 1966080 | tf_op args[0]
  31.7 1.9 collective-permute-start
  39.8 5.8 %concatenate.158 = f32[256,16,128]{0,2,1:T(8,128)S(1)} concatenate(f32[60,16,128]{0,2,1:T(8,128)} %bitcast.340, f32[4,16,128]{0,2,1:T(8,128)S(1)} %broadcast_in_dim.1441, f32[60,16,128]{0,2,1:T(8,128)} %bitcast.341, f32[4,16,128]{0,2,1:T(8,128)S(1)} %broadcast_in_dim.1441, f32[60,16,128]{0,2,1:T(8,128)} %bitcast.342, f32[4,16,128]{0,2,1:T(8,128)S(1)} %broadcast_in_dim.1441, ...), dimensions={0} | concatenate | bytes 4194304 | tf_op jit(solution)/shard_map/concatenate | solution.py:148
  46.7 5.0 %collective-permute-start.5 = (f32[4,128,256]{2,1,0:T(8,128)}, f32[4,128,256]{2,1,0:T(8,128)}, u32[]{:S(2)}, u32[]{:S(2)}) collective-permute-start(f32[4,128,256]{2,1,0:T(8,128)} %get-tuple-element.107), channel_id=1, source_target_pairs={{0,32},{32,64},{64,96},{96,128},{128,160},{160,192},{192,224},{224... | collective-permute-start | bytes 1572872 | tf_op jit(solution)/shard_map/ppermute | solution.py:22
  51.8 1.9 collective-permute-start.6
  64.1 4.1 %fusion.11 = (f32[2,16,127]{0,2,1:T(8,128)}, f32[2,16,127]{0,2,1:T(8,128)}, f32[2,16,127]{0,2,1:T(8,128)}, f32[2,16,127]{0,2,1:T(8,128)}, f32[2,16,127]{0,2,1:T(...) fusion(f32[2,16,128]{0,2,1:T(8,128)S(1)} %copy.479, f32[2,2,128]{0,2,1:T(8,128)S(1)} %reshape.34, ...), kind=kLoop, calls=%fused_computation.111 | loop fusion | flops 32512 | bytes 150528 | tf_op jit(solution)/shard_map/concatenate | solution.py:33
  68.8 4.0 %fusion.12 = (f32[2,16,126]{0,2,1:T(8,128)}, f32[2,16,126]{0,2,1:T(8,128)}, f32[2,16,126]{0,2,1:T(8,128)}, f32[2,16,126]{0,2,1:T(8,128)}, f32[2,16,126]{0,2,1:T(...) fusion(f32[2,16,128]{0,2,1:T(8,128)S(1)} %copy.479, f32[2,2,128]{0,2,1:T(8,128)S(1)} %reshape.34, ...), kind=kLoop, calls=%fused_computation.112 | loop fusion | flops 32256 | bytes 149504 | tf_op jit(solution)/shard_map/concatenate | solution.py:33
  73.5 3.3 %fusion.7 = (f32[2,16,125]{0,2,1:T(8,128)}, f32[2,16,125]{0,2,1:T(8,128)}, f32[2,16,125]{0,2,1:T(8,128)}, f32[2,16,125]{0,2,1:T(8,128)}, f32[2,16,125]{0,2,1:T(8...) fusion(f32[2,16,128]{0,2,1:T(8,128)S(1)} %copy.479, f32[2,2,128]{0,2,1:T(8,128)S(1)} %reshape.34, ...), kind=kLoop, calls=%fused_computation.107 | loop fusion | flops 28000 | bytes 132480 | tf_op jit(solution)/shard_map/concatenate | solution.py:33
  78.3 3.5 %fusion.30 = (f32[2,16,128]{0,2,1:T(8,128)}, f32[2,16,128]{0,2,1:T(8,128)}, f32[2,16,128]{0,2,1:T(8,128)}, f32[2,16,128]{0,2,1:T(8,128)}, f32[2,16,128]{0,2,1:T(8,128)}) fusion(f32[2,16,128]{0,2,1:T(8,128)S(1)} %copy.479, f32[2,2,128]{0,2,1:T(8,128)S(1)} %reshape.34, f32[2,16,3]{0,2,1:T(4,128)S(1)} %get-tuple-element.135, ...), kind=kLoop, calls=%fused_computation.133 | loop fusion | flops 28672 | bytes 108928 | tf_op jit(solution)/shard_map/jit(_where)/select_n | solution.py:47
  81.8 2.2 copy.530
  85.0 2.2 copy.570
  87.2 2.1 copy.610
  90.3 2.3 copy.484
  92.6 2.2 copy.487
  95.7 2.3 copy.499
  98.0 2.2 copy.510
  101.1 2.3 copy.522
  103.4 2.2 copy.525
  118.4 2.3 copy.489
  120.6 2.2 copy.494
  123.7 2.3 copy.508
  126.0 2.2 copy.515
  129.1 2.3 copy.527
  135.9 1.5 copy.500
  141.9 1.5 copy.526
  143.4 1.5 copy.481
  145.0 1.6 copy.490
  146.5 1.5 copy.493
  151.2 1.6 copy.480
  153.2 1.7 copy.492
  154.9 1.6 copy.503
  156.8 1.7 copy.517
  158.5 1.6 copy.518
  162.3 2.3 add_multiply_fusion
  165.0 1.6 subtract_multiply_fusion
  166.6 1.7 fusion.66
  168.4 4.1 %concatenate.155 = f32[128,16,128]{0,2,1:T(8,128)S(1)} concatenate(f32[60,16,128]{0,2,1:T(8,128)} %bitcast.338, f32[1,16,128]{0,2,1:T(8,128)} %get-tuple-element.167, f32[3,16,128]{0,2,1:T(8,128)S(1)} %broadcast.358, f32[60,16,128]{0,2,1:T(8,128)} %bitcast.339, f32[1,16,128]{0,2,1:T(8,128)} %get-tuple-element.166, f32[3,16,128]{0,2,1:T(8,128)S(1)} %broadcast.358), dimensions={0} | concatenate | bytes 2097152 | tf_op jit(solution)/shard_map/concatenate | solution.py:148
  172.5 7.5 %collective-permute-start.1 = (f32[4,128,128]{2,1,0:T(8,128)S(1)}, f32[4,128,128]{2,1,0:T(8,128)S(1)}, u32[]{:S(2)}, u32[]{:S(2)}) collective-permute-start(f32[4,128,128]{2,1,0:T(8,128)S(1)} %get-tuple-element.165), channel_id=1, source_target_pairs={{0,32},{32,64},{64,96},{96,128},{128,160},{160,192},{192,224},{224... | collective-permute-start | bytes 786440 | tf_op jit(solution)/shard_map/ppermute | solution.py:22
  180.0 1.9 collective-permute-start.2
  182.0 3.7 %collective-permute-done.1.topq_ref = f32[4,128,128]{2,1,0:T(8,128)S(1)} collective-permute-done((f32[4,128,128]{2,1,0:T(8,128)S(1)}, f32[4,128,128]{2,1,0:T(8,128)S(1)}, u32[]{:S(2)}, u32[]{:S(2)}) %collective-permute-start.1) | collective-permute-done | bytes 262176 | tf_op jit(solution)/shard_map/ppermute | solution.py:22
  185.7 7.7 %collective-permute-done.2.botq_ref = f32[4,128,128]{2,1,0:T(8,128)S(1)} collective-permute-done((f32[4,128,128]{2,1,0:T(8,128)S(1)}, f32[4,128,128]{2,1,0:T(8,128)S(1)}, u32[]{:S(2)}, u32[]{:S(2)}) %collective-permute-start.2) | collective-permute-done | bytes 262176 | tf_op jit(solution)/shard_map/ppermute | solution.py:22
  193.4 11.5 %collective-permute-start.4 = (f32[24,8,128]{2,1,0:T(8,128)S(1)}, f32[24,8,128]{2,1,0:T(8,128)}, u32[]{:S(2)}, u32[]{:S(2)}) collective-permute-start(f32[24,8,128]{2,1,0:T(8,128)S(1)} %pad_maximum_fusion.5), channel_id=1, source_target_pairs={{0,31},{1,0},{2,1},{3,2},{4,3},{5,4},{6,5},{7,6},{8,7},{9,8},{10,9... | collective-permute-start | bytes 294920 | tf_op jit(solution)/shard_map/ppermute | solution.py:22
  207.5 1.9 collective-permute-start.7
  209.4 6.0 %collective-permute-start.8 = (f32[24,8,256]{2,1,0:T(8,128)S(1)}, f32[24,8,256]{2,1,0:T(8,128)S(1)}, u32[]{:S(2)}, u32[]{:S(2)}) collective-permute-start(f32[24,8,256]{2,1,0:T(8,128)S(1)} %pad_maximum_fusion.3), channel_id=1, source_target_pairs={{0,31},{1,0},{2,1},{3,2},{4,3},{5,4},{6,5},{7,6},{8,7},{9,8},{10,9... | collective-permute-start | bytes 589832 | tf_op jit(solution)/shard_map/ppermute | solution.py:22
  215.5 1.9 collective-permute-start.3
  218.3 5.8 %collective-permute-done.3.leftq_ref = f32[24,8,128]{2,1,0:T(8,128)S(1)} collective-permute-done((f32[24,8,128]{2,1,0:T(8,128)S(1)}, f32[24,8,128]{2,1,0:T(8,128)S(1)}, u32[]{:S(2)}, u32[]{:S(2)}) %collective-permute-start.3) | collective-permute-done | bytes 98336 | tf_op jit(solution)/shard_map/ppermute | solution.py:22
  225.5 20.1 %shard_map.86 = f32[16,128,128]{2,1,0:T(8,128)} custom-call(f32[16,128,128]{2,1,0:T(8,128)} %bitcast.337, f32[4,128,128]{2,1,0:T(8,128)} %copy-done.18, f32[4,128,128]{2,1,0:T(8,128)} %copy-done.19, f32[24,8,128]{2,1,0:T(8,128)} %copy-done.22, f32[24,8,128]{2,1,0:T(8,128)} %collective-permute-done.4.rightq_ref, f32[16,128,256]{2,1,0:T(8,128)} %bitcast.334, ...), custom_call_target="tpu_custom_call" | custom-call | tf_op jit(solution)/shard_map/pallas_call | solution.py:138
  245.6 1.7 copy.693
  (234 shorter events, 61.4 us)
Async XLA Ops:
  30.0 3.6 %copy-start.15 = (f32[1,60,16,128]{3,2,1,0:T(8,128)S(1)}, f32[1,60,16,128]{3,2,1,0:T(8,128)}, u32[]{:S(2)}) copy-start(f32[1,60,16,128]{3,2,1,0:T(8,128)} %param.8) | copy-start | bytes 1474564
  31.3 3.7 %copy-start.16 = (f32[1,60,16,128]{3,2,1,0:T(8,128)S(1)}, f32[1,60,16,128]{3,2,1,0:T(8,128)}, u32[]{:S(2)}) copy-start(f32[1,60,16,128]{3,2,1,0:T(8,128)} %param.9) | copy-start | bytes 1474564
  31.7 31.1 %collective-permute-start = (f32[2,16,128]{2,1,0:T(8,128)S(1)}, f32[2,16,128]{2,1,0:T(8,128)S(1)}, u32[]{:S(2)}, u32[]{:S(2)}) collective-permute-start(f32[2,16,128]{2,1,0:T(8,128)S(1)} %copy.477), channel_id=1, source_target_pairs={{0,256},{256,0},{1,257},{257,1},{2,258},{258,2},{3,259},{259,3},{4... | collective-permute-start | bytes 49160 | tf_op jit(solution)/shard_map/ppermute | solution.py:177
  33.6 2.8 %copy-start.17 = (f32[1,60,16,128]{3,2,1,0:T(8,128)S(1)}, f32[1,60,16,128]{3,2,1,0:T(8,128)}, u32[]{:S(2)}) copy-start(f32[1,60,16,128]{3,2,1,0:T(8,128)} %param.10) | copy-start | bytes 1474564
  35.0 2.8 %copy-start.68 = (s32[1,16,128]{2,1,0:T(8,128)S(1)}, s32[1,16,128]{2,1,0:T(8,128)}, u32[]{:S(2)}) copy-start(s32[1,16,128]{2,1,0:T(8,128)} %param.12) | copy-start | bytes 24580
  35.0 2.8 %copy-start.69 = (f32[1,16,128]{2,1,0:T(8,128)S(1)}, f32[1,16,128]{2,1,0:T(8,128)}, u32[]{:S(2)}) copy-start(f32[1,16,128]{2,1,0:T(8,128)} %param.11) | copy-start | bytes 24580
  45.6 8.2 %copy-start = (f32[256,16,128]{0,2,1:T(8,128)}, f32[256,16,128]{0,2,1:T(8,128)S(1)}, u32[]{:S(2)}) copy-start(f32[256,16,128]{0,2,1:T(8,128)S(1)} %concatenate.158) | copy-start | bytes 6291460
  45.6 8.1 %copy-start.12 = (f32[1,2,60,16,128]{4,3,2,1,0:T(8,128)S(1)}, f32[1,2,60,16,128]{4,3,2,1,0:T(8,128)}, u32[]{:S(2)}) copy-start(f32[1,2,60,16,128]{4,3,2,1,0:T(8,128)} %param.7) | copy-start | bytes 2949124
  46.7 158.2 %collective-permute-start.5 = (f32[4,128,256]{2,1,0:T(8,128)}, f32[4,128,256]{2,1,0:T(8,128)}, u32[]{:S(2)}, u32[]{:S(2)}) collective-permute-start(f32[4,128,256]{2,1,0:T(8,128)} %get-tuple-element.107), channel_id=1, source_target_pairs={{0,32},{32,64},{64,96},{96,128},{128,160},{160,192},{192,224},{224... | collective-permute-start | bytes 1572872 | tf_op jit(solution)/shard_map/ppermute | solution.py:22
  51.7 2.1 copy-start.63
  51.8 154.4 %collective-permute-start.6 = (f32[4,128,256]{2,1,0:T(8,128)}, f32[4,128,256]{2,1,0:T(8,128)}, u32[]{:S(2)}, u32[]{:S(2)}) collective-permute-start(f32[4,128,256]{2,1,0:T(8,128)} %get-tuple-element.106), channel_id=1, source_target_pairs={{0,224},{32,0},{64,32},{96,64},{128,96},{160,128},{192,160},{224,1... | collective-permute-start | bytes 1572872 | tf_op jit(solution)/shard_map/ppermute | solution.py:22
  81.8 2.2 copy-start.11
  85.0 4.4 %copy-start.10 = (f32[2,16,128]{0,2,1:T(8,128)S(1)}, f32[2,16,128]{0,2,1:T(8,128)}, u32[]{:S(2)}) copy-start(f32[2,16,128]{0,2,1:T(8,128)} %get-tuple-element.109) | copy-start | bytes 49156
  90.3 4.4 %copy-start.9 = (f32[2,16,127]{0,2,1:T(8,128)S(1)}, f32[2,16,127]{0,2,1:T(8,128)}, u32[]{:S(2)}) copy-start(f32[2,16,127]{0,2,1:T(8,128)} %get-tuple-element.180) | copy-start | bytes 48772
  95.7 4.4 %copy-start.8 = (f32[2,16,127]{0,2,1:T(8,128)S(1)}, f32[2,16,127]{0,2,1:T(8,128)}, u32[]{:S(2)}) copy-start(f32[2,16,127]{0,2,1:T(8,128)} %get-tuple-element.127) | copy-start | bytes 48772
  101.1 16.3 %copy-start.7 = (f32[2,16,126]{0,2,1:T(8,128)S(1)}, f32[2,16,126]{0,2,1:T(8,128)}, u32[]{:S(2)}) copy-start(f32[2,16,126]{0,2,1:T(8,128)} %get-tuple-element.174) | copy-start | bytes 48388
  118.4 4.4 %copy-start.6 = (f32[2,16,126]{0,2,1:T(8,128)S(1)}, f32[2,16,126]{0,2,1:T(8,128)}, u32[]{:S(2)}) copy-start(f32[2,16,126]{0,2,1:T(8,128)} %get-tuple-element.175) | copy-start | bytes 48388
  123.7 4.4 %copy-start.5 = (f32[2,16,126]{0,2,1:T(8,128)S(1)}, f32[2,16,126]{0,2,1:T(8,128)}, u32[]{:S(2)}) copy-start(f32[2,16,126]{0,2,1:T(8,128)} %get-tuple-element.119) | copy-start | bytes 48388
  129.1 23.7 %copy-start.4 = (f32[2,16,125]{0,2,1:T(8,128)S(1)}, f32[2,16,125]{0,2,1:T(8,128)}, u32[]{:S(2)}) copy-start(f32[2,16,125]{0,2,1:T(8,128)} %get-tuple-element.185) | copy-start | bytes 48004
  153.2 3.3 %copy-start.3 = (f32[2,16,125]{0,2,1:T(8,128)S(1)}, f32[2,16,125]{0,2,1:T(8,128)}, u32[]{:S(2)}) copy-start(f32[2,16,125]{0,2,1:T(8,128)} %get-tuple-element.131) | copy-start | bytes 48004
  156.8 3.3 %copy-start.2 = (f32[2,16,128]{0,2,1:T(8,128)S(1)}, f32[2,16,128]{0,2,1:T(8,128)}, u32[]{:S(2)}) copy-start(f32[2,16,128]{0,2,1:T(8,128)} %get-tuple-element.192) | copy-start | bytes 49156
  160.4 1.5 copy-start.26
  160.4 1.5 copy-start.27
  160.4 1.5 copy-start.28
  160.5 1.5 copy-start.29
  160.5 1.5 copy-start.30
  160.5 1.5 copy-start.31
  160.5 1.5 copy-start.32
  160.5 1.5 copy-start.33
  160.5 1.5 copy-start.34
  160.5 1.5 copy-start.35
  160.5 1.5 copy-start.36
  160.5 1.5 copy-start.37
  160.5 1.5 copy-start.38
  160.6 1.5 copy-start.39
  160.6 1.5 copy-start.40
  172.4 33.7 %copy-start.1 = (f32[128,16,128]{0,2,1:T(8,128)}, f32[128,16,128]{0,2,1:T(8,128)S(1)}, u32[]{:S(2)}) copy-start(f32[128,16,128]{0,2,1:T(8,128)S(1)} %concatenate.155) | copy-start | bytes 3145732
  172.4 32.5 %copy-start.70 = (pred[256]{0:T(512)(128)(4,1)S(1)}, pred[256]{0:T(512)(128)(4,1)}, u32[]{:S(2)}) copy-start(pred[256]{0:T(512)(128)(4,1)} %fusion.61) | copy-start | bytes 772
  172.5 13.2 %collective-permute-start.1 = (f32[4,128,128]{2,1,0:T(8,128)S(1)}, f32[4,128,128]{2,1,0:T(8,128)S(1)}, u32[]{:S(2)}, u32[]{:S(2)}) collective-permute-start(f32[4,128,128]{2,1,0:T(8,128)S(1)} %get-tuple-element.165), channel_id=1, source_target_pairs={{0,32},{32,64},{64,96},{96,128},{128,160},{160,192},{192,224},{224... | collective-permute-start | bytes 786440 | tf_op jit(solution)/shard_map/ppermute | solution.py:22
  180.0 13.4 %collective-permute-start.2 = (f32[4,128,128]{2,1,0:T(8,128)S(1)}, f32[4,128,128]{2,1,0:T(8,128)S(1)}, u32[]{:S(2)}, u32[]{:S(2)}) collective-permute-start(f32[4,128,128]{2,1,0:T(8,128)S(1)} %get-tuple-element.164), channel_id=1, source_target_pairs={{0,224},{32,0},{64,32},{96,64},{128,96},{160,128},{192,160},{224,1... | collective-permute-start | bytes 786440 | tf_op jit(solution)/shard_map/ppermute | solution.py:22
  185.7 21.7 %copy-start.18 = (f32[4,128,128]{2,1,0:T(8,128)}, f32[4,128,128]{2,1,0:T(8,128)S(1)}, u32[]{:S(2)}) copy-start(f32[4,128,128]{2,1,0:T(8,128)S(1)} %collective-permute-done.1.topq_ref) | copy-start | bytes 786436
  193.4 14.0 %copy-start.19 = (f32[4,128,128]{2,1,0:T(8,128)}, f32[4,128,128]{2,1,0:T(8,128)S(1)}, u32[]{:S(2)}) copy-start(f32[4,128,128]{2,1,0:T(8,128)S(1)} %collective-permute-done.2.botq_ref) | copy-start | bytes 786436
  193.4 24.9 %collective-permute-start.4 = (f32[24,8,128]{2,1,0:T(8,128)S(1)}, f32[24,8,128]{2,1,0:T(8,128)}, u32[]{:S(2)}, u32[]{:S(2)}) collective-permute-start(f32[24,8,128]{2,1,0:T(8,128)S(1)} %pad_maximum_fusion.5), channel_id=1, source_target_pairs={{0,31},{1,0},{2,1},{3,2},{4,3},{5,4},{6,5},{7,6},{8,7},{9,8},{10,9... | collective-permute-start | bytes 294920 | tf_op jit(solution)/shard_map/ppermute | solution.py:22
  206.1 12.2 %copy-start.13 = (f32[4,128,256]{2,1,0:T(8,128)}, f32[4,128,256]{2,1,0:T(8,128)S(1)}, u32[]{:S(2)}) copy-start(f32[4,128,256]{2,1,0:T(8,128)S(1)} %broadcast_select_fusion.1.topv_ref) | copy-start | bytes 1572868
  207.4 16.7 %copy-start.14 = (f32[4,128,256]{2,1,0:T(8,128)}, f32[4,128,256]{2,1,0:T(8,128)S(1)}, u32[]{:S(2)}) copy-start(f32[4,128,256]{2,1,0:T(8,128)S(1)} %broadcast_select_fusion.botv_ref) | copy-start | bytes 1572868
  207.5 16.6 %collective-permute-start.7 = (f32[24,8,256]{2,1,0:T(8,128)S(1)}, f32[24,8,256]{2,1,0:T(8,128)S(1)}, u32[]{:S(2)}, u32[]{:S(2)}) collective-permute-start(f32[24,8,256]{2,1,0:T(8,128)S(1)} %pad_maximum_fusion.2), channel_id=1, source_target_pairs={{0,1},{1,2},{2,3},{3,4},{4,5},{5,6},{6,7},{7,8},{8,9},{9,10},{10,1... | collective-permute-start | bytes 589832 | tf_op jit(solution)/shard_map/ppermute | solution.py:22
  209.4 14.7 %collective-permute-start.8 = (f32[24,8,256]{2,1,0:T(8,128)S(1)}, f32[24,8,256]{2,1,0:T(8,128)S(1)}, u32[]{:S(2)}, u32[]{:S(2)}) collective-permute-start(f32[24,8,256]{2,1,0:T(8,128)S(1)} %pad_maximum_fusion.3), channel_id=1, source_target_pairs={{0,31},{1,0},{2,1},{3,2},{4,3},{5,4},{6,5},{7,6},{8,7},{9,8},{10,9... | collective-permute-start | bytes 589832 | tf_op jit(solution)/shard_map/ppermute | solution.py:22
  215.5 8.6 %collective-permute-start.3 = (f32[24,8,128]{2,1,0:T(8,128)S(1)}, f32[24,8,128]{2,1,0:T(8,128)S(1)}, u32[]{:S(2)}, u32[]{:S(2)}) collective-permute-start(f32[24,8,128]{2,1,0:T(8,128)S(1)} %pad_maximum_fusion.4), channel_id=1, source_target_pairs={{0,1},{1,2},{2,3},{3,4},{4,5},{5,6},{6,7},{7,8},{8,9},{9,10},{10,1... | collective-permute-start | bytes 294920 | tf_op jit(solution)/shard_map/ppermute | solution.py:22
  (32 other events, 45.4 us)

commit v5 on v3

--- a/solution.py
+++ b/solution.py
@@ -20,6 +20,15 @@
 def shifted(x, axis, step):
     count = lax.axis_size(axis)
     return lax.ppermute(x, axis, [(i, (i + step) % count) for i in range(count)])
+
+
+def shifted2(x, da, db):
+    n_lat = lax.axis_size("lat")
+    n_lon = lax.axis_size("lon")
+    pairs = [
+        (a * n_lon + b, ((a + da) % n_lat) * n_lon + (b + db) % n_lon) for a in range(n_lat) for b in range(n_lon)
+    ]
+    return lax.ppermute(x, ("lat", "lon"), pairs)
 
 
 def regrid(partner, table):
@@ -167,14 +176,20 @@
     )
 
     width = SUB
-    top = shifted(x[-width:], "lat", 1)
-    bot = shifted(x[:width], "lat", -1)
     row_block = lax.axis_index("lat")
     wet_lane = lax.broadcasted_iota(jnp.int32, (1, 1, 3 * LANES), 2) >= 2 * LANES + HALF
-    top = jnp.where(jnp.logical_and(wet_lane, row_block == 0), 0.0, top)
-    bot = jnp.where(jnp.logical_and(wet_lane, row_block == lax.axis_size("lat") - 1), 0.0, bot)
-    left = shifted(jnp.concatenate([top[:, -COL_PAD:], x[:, -COL_PAD:], bot[:, -COL_PAD:]], axis=0), "lon", 1)
-    right = shifted(jnp.concatenate([top[:, :COL_PAD], x[:, :COL_PAD], bot[:, :COL_PAD]], axis=0), "lon", -1)
+    top_mask = jnp.logical_and(wet_lane, row_block == 0)
+    bot_mask = jnp.logical_and(wet_lane, row_block == lax.axis_size("lat") - 1)
+    top = jnp.where(top_mask, 0.0, shifted2(x[-width:], 1, 0))
+    bot = jnp.where(bot_mask, 0.0, shifted2(x[:width], -1, 0))
+    mid_left = shifted2(x[:, -COL_PAD:], 0, 1)
+    mid_right = shifted2(x[:, :COL_PAD], 0, -1)
+    top_left = jnp.where(top_mask, 0.0, shifted2(x[-width:, -COL_PAD:], 1, 1))
+    top_right = jnp.where(top_mask, 0.0, shifted2(x[-width:, :COL_PAD], 1, -1))
+    bot_left = jnp.where(bot_mask, 0.0, shifted2(x[:width, -COL_PAD:], -1, 1))
+    bot_right = jnp.where(bot_mask, 0.0, shifted2(x[:width, :COL_PAD], -1, -1))
+    left = jnp.concatenate([top_left, mid_left, bot_left], axis=0)
+    right = jnp.concatenate([top_right, mid_right, bot_right], axis=0)
 
     out = run_steps(x, top, bot, left, right, levels, width)
     q = out.reshape(rows, cols, fields, HALF)[..., :levels]

time: 120 us -> 125 us (1.042)
  the two profiles are of different devices: /device:TPU:1 before, /device:TPU:9 now
where the time goes in v5:
time: 125 us; the launch traced here: 124 us
  starting transfers between devices  37.4 us (30%)
  local copies, waits for them, and re-layouts  27.9 us (22%)
  waiting for transfers between devices  23.3 us (19%)
  Pallas kernels  22.1 us (18%)
  other arithmetic  11.7 us (9%)
  between operations  1.63 us (1%)
    ppermute x8, starting transfers between devices, shifted2(): return lax.ppermute(x, ('lat', 'lon'), pairs)  34.6 us
    ppermute x8, waiting for transfers between devices, shifted2(): return lax.ppermute(x, ('lat', 'lon'), pairs)  23.3 us
    pallas_call x1, Pallas kernels, run_steps(): pl.pallas_call(functools.partial(steps_kernel, levels=levels, width=width...  22.1 us
    unnamed x103, local copies, waits for them, and re-layouts  9.97 us
    concatenate x1, local copies, waits for them, and re-layouts, shards(): jnp.concatenate([to_lanes(tracers[0], flux_pad[0]), to_lanes(tracers[1],...  8.55 us
    broadcast_in_dim x8, other arithmetic, regrid(): picked = jnp.where(hit[None], values, picked)  4.39 us
    another operation x3, local copies, waits for them, and re-layouts, shards(): flux[f][:, :, None]  2.81 us
    ppermute x1, starting transfers between devices, shards(): partner = lax.ppermute(surface, 'sec', [(0, 1), (1, 0)])  2.72 us
  transfers between devices with their start and end apart: 9, of which 2 were waited for; matrix products, arithmetic and copies ran while one was open for 13% of the time, Pallas kernels for 0%

profile of v5, /device:TPU:9, one launch (start us, length us, event | category | flops | bytes accessed | tf_op | source)
XLA Modules:
  0.0 124.0 jit_solution(6861633045928907454)
XLA Ops:
  0.7 1.3 %copy.39 = f32[1,2,60,16,128]{4,3,1,2,0:T(8,128)S(1)} copy(f32[1,2,60,16,128]{4,3,2,1,0:T(8,128)} %param.7) | data formatting | bytes 1966080 | tf_op args[0]
  2.0 2.7 %collective-permute-start = (f32[2,16,128]{2,1,0:T(8,128)S(1)}, f32[2,16,128]{2,1,0:T(8,128)S(1)}, u32[]{:S(2)}, u32[]{:S(2)}) collective-permute-start(f32[2,16,128]{2,1,0:T(8,128)S(1)} %slice_bitcast_fusion.1), channel_id=1, source_target_pairs={{0,256},{256,0},{1,257},{257,1},{2,258},{258,2},{3,259},{259,3},{4... | collective-permute-start | bytes 49160 | tf_op jit(solution)/shard_map/ppermute | solution.py:163
  4.8 1.2 %fusion.83 = (f32[1,1,60,16,128]{4,3,2,1,0:T(8,128)S(1)}, f32[1,1,60,16,128]{4,3,2,1,0:T(8,128)S(1)}) fusion(f32[1,2,60,16,128]{4,3,2,1,0:T(8,128)} %param.7), kind=kLoop, calls=%fused_computation.427 | loop fusion | bytes 1966080 | tf_op jit(solution)/shard_map/slice | solution.py:172
  6.1 0.5 fusion.79
  6.7 0.6 and_bitcast_fusion.132
  7.3 0.7 and_bitcast_fusion.27
  8.1 0.7 and_bitcast_fusion.131
  8.8 0.8 and_bitcast_fusion.96
  9.6 0.7 and_bitcast_fusion.61
  10.3 0.8 and_bitcast_fusion.26
  11.1 0.5 fusion.78
  11.6 1.4 %copy.36 = f32[1,1,60,16,128]{2,4,3,1,0:T(8,128)} copy(f32[1,1,60,16,128]{4,3,2,1,0:T(8,128)S(1)} %get-tuple-element.107) | data formatting | bytes 983040
  13.0 1.4 %copy.37 = f32[1,1,60,16,128]{2,4,3,1,0:T(8,128)} copy(f32[1,1,60,16,128]{4,3,2,1,0:T(8,128)S(1)} %get-tuple-element.106) | data formatting | bytes 983040
  14.7 1.4 %copy.29 = f32[1,60,16,128]{1,3,2,0:T(8,128)} copy(f32[1,60,16,128]{3,2,1,0:T(8,128)S(1)} %copy-done.1) | data formatting | bytes 983040 | tf_op args[1]
  16.1 1.4 %copy.30 = f32[1,60,16,128]{1,3,2,0:T(8,128)} copy(f32[1,60,16,128]{3,2,1,0:T(8,128)S(1)} %copy-done.2) | data formatting | bytes 983040 | tf_op args[2]
  17.5 1.4 %copy.31 = f32[1,60,16,128]{1,3,2,0:T(8,128)} copy(f32[1,60,16,128]{3,2,1,0:T(8,128)S(1)} %copy-done.3) | data formatting | bytes 983040 | tf_op args[3]
  18.9 0.1 fusion.8
  19.0 0.1 fusion.9
  19.1 0.1 fusion.10
  19.2 0.1 fusion.11
  19.3 0.1 fusion.7
  19.4 0.1 fusion.6
  19.9 2.1 %subtract_multiply_fusion = f32[2,16,128]{2,1,0:T(8,128)S(1)} fusion(f32[2,16,128]{2,1,0:T(8,128)S(1)} %collective-permute-done, f32[2,2,128]{2,1,0:T(2,128)S(1)} %reshape.40, f32[2,16,3]{2,1,0:T(8,128)S(1)} %get-tuple-element.229, f32[2,16,3]{2,1,0:T(8,128)S(1)} %get-tuple-element.290, f32[2,16,125]{2,1,0:T(8,128)S(1)} %get-tuple-element.286, ...), kind=kLoop, calls=%fused_computation.207 | loop fusion | flops 745472 | bytes 807680 | tf_op jit(solution)/shard_map/mul | solution.py:166
  22.1 1.4 %copy.32 = f32[16,128,1]{2,1,0:T(8,128)} copy(f32[16,128,1]{1,0,2:T(8,128)S(1)} %get-tuple-element.270) | data formatting | bytes 16384 | tf_op jit(solution)/shard_map/broadcast_in_dim;squeeze | solution.py:170
  23.4 1.4 %copy.33 = f32[16,128,1]{2,1,0:T(8,128)} copy(f32[16,128,1]{1,0,2:T(8,128)S(1)} %get-tuple-element.269) | data formatting | bytes 16384 | tf_op jit(solution)/shard_map/broadcast_in_dim;squeeze | solution.py:170
  24.9 1.3 %broadcast_in_dim.1472 = f32[16,128,64]{2,1,0:T(8,128)} broadcast(f32[16,128]{1,0:T(8,128)S(1)} %get-tuple-element.318), dimensions={0,1} | broadcast | bytes 532480 | tf_op jit(solution)/shard_map/broadcast_in_dim | solution.py:174
  26.2 1.2 broadcast.366
  27.3 1.1 broadcast_in_dim.1470
  28.4 8.6 %concatenate.146.x_ref = f32[16,128,384]{2,1,0:T(8,128)S(1)} concatenate(f32[16,128,60]{2,1,0:T(8,128)} %bitcast.344, f32[16,128,1]{2,1,0:T(8,128)} %copy.32, f32[16,128,3]{2,1,0:T(8,128)} %broadcast.366, f32[16,128,60]{2,1,0:T(8,128)} %bitcast.345, f32[16,128,1]{2,1,0:T(8,128)} %copy.33, f32[16,128,3]{2,1,0:T(8,128)} %broadcast.366, f32[16,128,60]{2,1,0:T(8,128)} %bitcast.346, ...), dimensions={2} | concatenate | bytes 6291456 | tf_op jit(solution)/shard_map/concatenate | solution.py:171
  37.1 0.1 fusion.82
  37.2 4.4 %collective-permute-start.3 = (f32[4,8,384]{2,1,0:T(8,128)S(1)}, f32[4,8,384]{2,1,0:T(8,128)S(1)}, u32[]{:S(2)}, u32[]{:S(2)}) collective-permute-start(f32[4,8,384]{2,1,0:T(8,128)S(1)} %get-tuple-element.101), channel_id=1, source_target_pairs={{0,33},{1,34},{2,35},{3,36},{4,37},{5,38},{6,39},{7,40},{8,41},{9,... | collective-permute-start | bytes 147464 | tf_op jit(solution)/shard_map/ppermute | solution.py:31
  41.5 2.8 %collective-permute-start.6 = (f32[4,8,384]{2,1,0:T(8,128)S(1)}, f32[4,8,384]{2,1,0:T(8,128)S(1)}, u32[]{:S(2)}, u32[]{:S(2)}) collective-permute-start(f32[4,8,384]{2,1,0:T(8,128)S(1)} %get-tuple-element.98), channel_id=1, source_target_pairs={{0,63},{1,32},{2,33},{3,34},{4,35},{5,36},{6,37},{7,38},{8,39},{9,... | collective-permute-start | bytes 147464 | tf_op jit(solution)/shard_map/ppermute | solution.py:31
  44.3 8.0 %collective-permute-start.2 = (f32[4,128,384]{2,1,0:T(8,128)S(1)}, f32[4,128,384]{2,1,0:T(8,128)S(1)}, u32[]{:S(2)}, u32[]{:S(2)}) collective-permute-start(f32[4,128,384]{2,1,0:T(8,128)S(1)} %get-tuple-element.104), channel_id=1, source_target_pairs={{0,224},{1,225},{2,226},{3,227},{4,228},{5,229},{6,230},{7,231},{8... | collective-permute-start | bytes 2359304 | tf_op jit(solution)/shard_map/ppermute | solution.py:31
  52.4 1.9 %collective-permute-start.5 = (f32[4,8,384]{2,1,0:T(8,128)S(1)}, f32[4,8,384]{2,1,0:T(8,128)S(1)}, u32[]{:S(2)}, u32[]{:S(2)}) collective-permute-start(f32[4,8,384]{2,1,0:T(8,128)S(1)} %get-tuple-element.100), channel_id=1, source_target_pairs={{0,225},{1,226},{2,227},{3,228},{4,229},{5,230},{6,231},{7,232},{8... | collective-permute-start | bytes 147464 | tf_op jit(solution)/shard_map/ppermute | solution.py:31
  54.3 7.1 %collective-permute-start.8 = (f32[4,8,384]{2,1,0:T(8,128)S(1)}, f32[4,8,384]{2,1,0:T(8,128)S(1)}, u32[]{:S(2)}, u32[]{:S(2)}) collective-permute-start(f32[4,8,384]{2,1,0:T(8,128)S(1)} %get-tuple-element.99), channel_id=1, source_target_pairs={{0,255},{1,224},{2,225},{3,226},{4,227},{5,228},{6,229},{7,230},{8... | collective-permute-start | bytes 147464 | tf_op jit(solution)/shard_map/ppermute | solution.py:31
  61.4 6.3 %collective-permute-start.7 = (f32[16,8,384]{2,1,0:T(8,128)S(1)}, f32[16,8,384]{2,1,0:T(8,128)S(1)}, u32[]{:S(2)}, u32[]{:S(2)}) collective-permute-start(f32[16,8,384]{2,1,0:T(8,128)S(1)} %get-tuple-element.102), channel_id=1, source_target_pairs={{0,31},{1,0},{2,1},{3,2},{4,3},{5,4},{6,5},{7,6},{8,7},{9,8},{10,9... | collective-permute-start | bytes 589832 | tf_op jit(solution)/shard_map/ppermute | solution.py:31
  67.8 2.2 %collective-permute-start.1 = (f32[4,128,384]{2,1,0:T(8,128)S(1)}, f32[4,128,384]{2,1,0:T(8,128)S(1)}, u32[]{:S(2)}, u32[]{:S(2)}) collective-permute-start(f32[4,128,384]{2,1,0:T(8,128)S(1)} %get-tuple-element.105), channel_id=1, source_target_pairs={{0,32},{1,33},{2,34},{3,35},{4,36},{5,37},{6,38},{7,39},{8,40},{9,... | collective-permute-start | bytes 2359304 | tf_op jit(solution)/shard_map/ppermute | solution.py:31
  70.0 4.9 %collective-permute-done.5 = f32[4,8,384]{2,1,0:T(8,128)S(1)} collective-permute-done((f32[4,8,384]{2,1,0:T(8,128)S(1)}, f32[4,8,384]{2,1,0:T(8,128)S(1)}, u32[]{:S(2)}, u32[]{:S(2)}) %collective-permute-start.5) | collective-permute-done | bytes 49184 | tf_op jit(solution)/shard_map/ppermute | solution.py:31
  74.9 1.9 %collective-permute-start.4 = (f32[16,8,384]{2,1,0:T(8,128)S(1)}, f32[16,8,384]{2,1,0:T(8,128)S(1)}, u32[]{:S(2)}, u32[]{:S(2)}) collective-permute-start(f32[16,8,384]{2,1,0:T(8,128)S(1)} %get-tuple-element.103), channel_id=1, source_target_pairs={{0,1},{1,2},{2,3},{3,4},{4,5},{5,6},{6,7},{7,8},{8,9},{9,10},{10,1... | collective-permute-start | bytes 589832 | tf_op jit(solution)/shard_map/ppermute | solution.py:31
  76.9 0.7 pad_maximum_fusion.1.right_ref
  77.6 18.4 %collective-permute-done.4 = f32[16,8,384]{2,1,0:T(8,128)S(1)} collective-permute-done((f32[16,8,384]{2,1,0:T(8,128)S(1)}, f32[16,8,384]{2,1,0:T(8,128)S(1)}, u32[]{:S(2)}, u32[]{:S(2)}) %collective-permute-start.4) | collective-permute-done | bytes 196640 | tf_op jit(solution)/shard_map/ppermute | solution.py:31
  96.0 0.7 pad_maximum_fusion.left_ref
  96.7 1.0 broadcast_select_fusion.bot_ref
  97.7 0.9 broadcast_select_fusion.1.top_ref
  98.7 22.1 %shard_map.86 = f32[16,128,128]{2,1,0:T(8,128)} custom-call(f32[16,128,384]{2,1,0:T(8,128)} %copy-done, f32[4,128,384]{2,1,0:T(8,128)} %broadcast_select_fusion.1.top_ref, f32[4,128,384]{2,1,0:T(8,128)} %broadcast_select_fusion.bot_ref, f32[24,8,384]{2,1,0:T(8,128)} %pad_maximum_fusion.left_ref, f32[24,8,384]{2,1,0:T(8,128)} %pad_maximum_fusion.1.right_ref), custom_call_target="tpu_custom_call" | custom-call | tf_op jit(solution)/shard_map/pallas_call | solution.py:143
  120.8 1.6 %copy.34 = f32[16,128,128]{1,2,0:T(8,128)S(1)} copy(f32[16,128,128]{2,1,0:T(8,128)} %shard_map.86) | data formatting | bytes 2097152 | tf_op jit(solution)/shard_map/pallas_call | solution.py:143
  122.4 0.1 slice_bitcast_fusion
  122.5 1.5 %copy.35 = f32[1,2,60,16,128]{4,3,2,1,0:T(8,128)} copy(f32[1,2,60,16,128]{4,2,1,3,0:T(8,128)S(1)} %slice_bitcast_fusion) | data formatting | bytes 1966080
  (116 shorter events, 0.4 us)
Async XLA Ops:
  0.6 5.4 %copy-start.5 = (s32[1,4,16,128]{3,2,1,0:T(8,128)S(1)}, s32[1,4,16,128]{3,2,1,0:T(8,128)}, u32[]{:S(2)}) copy-start(s32[1,4,16,128]{3,2,1,0:T(8,128)} %param.13) | copy-start | bytes 98308
  0.6 7.4 %copy-start.45 = (f32[1,16,128]{2,1,0:T(8,128)S(1)}, f32[1,16,128]{2,1,0:T(8,128)}, u32[]{:S(2)}) copy-start(f32[1,16,128]{2,1,0:T(8,128)} %param.11) | copy-start | bytes 24580
  0.7 7.4 %copy-start.44 = (s32[1,16,128]{2,1,0:T(8,128)S(1)}, s32[1,16,128]{2,1,0:T(8,128)}, u32[]{:S(2)}) copy-start(s32[1,16,128]{2,1,0:T(8,128)} %param.12) | copy-start | bytes 24580
  2.0 12.3 %copy-start.1 = (f32[1,60,16,128]{3,2,1,0:T(8,128)S(1)}, f32[1,60,16,128]{3,2,1,0:T(8,128)}, u32[]{:S(2)}) copy-start(f32[1,60,16,128]{3,2,1,0:T(8,128)} %param.8) | copy-start | bytes 1474564
  2.0 16.8 %collective-permute-start = (f32[2,16,128]{2,1,0:T(8,128)S(1)}, f32[2,16,128]{2,1,0:T(8,128)S(1)}, u32[]{:S(2)}, u32[]{:S(2)}) collective-permute-start(f32[2,16,128]{2,1,0:T(8,128)S(1)} %slice_bitcast_fusion.1), channel_id=1, source_target_pairs={{0,256},{256,0},{1,257},{257,1},{2,258},{258,2},{3,259},{259,3},{4... | collective-permute-start | bytes 49160 | tf_op jit(solution)/shard_map/ppermute | solution.py:163
  6.0 10.1 %copy-start.2 = (f32[1,60,16,128]{3,2,1,0:T(8,128)S(1)}, f32[1,60,16,128]{3,2,1,0:T(8,128)}, u32[]{:S(2)}) copy-start(f32[1,60,16,128]{3,2,1,0:T(8,128)} %param.9) | copy-start | bytes 1474564
  9.6 7.9 %copy-start.3 = (f32[1,60,16,128]{3,2,1,0:T(8,128)S(1)}, f32[1,60,16,128]{3,2,1,0:T(8,128)}, u32[]{:S(2)}) copy-start(f32[1,60,16,128]{3,2,1,0:T(8,128)} %param.10) | copy-start | bytes 1474564
  14.4 5.2 %copy-start.9 = (pred[16,128]{1,0:T(8,128)(4,1)S(1)}, pred[16,128]{1,0:T(8,128)(4,1)}, u32[]{:S(2)}) copy-start(pred[16,128]{1,0:T(8,128)(4,1)} %get-tuple-element.121) | copy-start | bytes 6148
  14.4 5.2 %copy-start.10 = (pred[16,128]{1,0:T(8,128)(4,1)S(1)}, pred[16,128]{1,0:T(8,128)(4,1)}, u32[]{:S(2)}) copy-start(pred[16,128]{1,0:T(8,128)(4,1)} %get-tuple-element.181) | copy-start | bytes 6148
  14.4 5.2 %copy-start.11 = (pred[16,128]{1,0:T(8,128)(4,1)S(1)}, pred[16,128]{1,0:T(8,128)(4,1)}, u32[]{:S(2)}) copy-start(pred[16,128]{1,0:T(8,128)(4,1)} %get-tuple-element.183) | copy-start | bytes 6148
  14.4 5.2 %copy-start.12 = (pred[16,128]{1,0:T(8,128)(4,1)S(1)}, pred[16,128]{1,0:T(8,128)(4,1)}, u32[]{:S(2)}) copy-start(pred[16,128]{1,0:T(8,128)(4,1)} %get-tuple-element.185) | copy-start | bytes 6148
  14.4 5.2 %copy-start.13 = (pred[16,128]{1,0:T(8,128)(4,1)S(1)}, pred[16,128]{1,0:T(8,128)(4,1)}, u32[]{:S(2)}) copy-start(pred[16,128]{1,0:T(8,128)(4,1)} %get-tuple-element.187) | copy-start | bytes 6148
  14.4 5.2 %copy-start.14 = (pred[16,128]{1,0:T(8,128)(4,1)S(1)}, pred[16,128]{1,0:T(8,128)(4,1)}, u32[]{:S(2)}) copy-start(pred[16,128]{1,0:T(8,128)(4,1)} %get-tuple-element.189) | copy-start | bytes 6148
  14.4 5.2 %copy-start.15 = (pred[16,128]{1,0:T(8,128)(4,1)S(1)}, pred[16,128]{1,0:T(8,128)(4,1)}, u32[]{:S(2)}) copy-start(pred[16,128]{1,0:T(8,128)(4,1)} %get-tuple-element.191) | copy-start | bytes 6148
  14.4 5.2 %copy-start.16 = (pred[16,128]{1,0:T(8,128)(4,1)S(1)}, pred[16,128]{1,0:T(8,128)(4,1)}, u32[]{:S(2)}) copy-start(pred[16,128]{1,0:T(8,128)(4,1)} %get-tuple-element.193) | copy-start | bytes 6148
  14.4 5.2 %copy-start.17 = (pred[16,128]{1,0:T(8,128)(4,1)S(1)}, pred[16,128]{1,0:T(8,128)(4,1)}, u32[]{:S(2)}) copy-start(pred[16,128]{1,0:T(8,128)(4,1)} %get-tuple-element.195) | copy-start | bytes 6148
  14.4 5.2 %copy-start.18 = (pred[16,128]{1,0:T(8,128)(4,1)S(1)}, pred[16,128]{1,0:T(8,128)(4,1)}, u32[]{:S(2)}) copy-start(pred[16,128]{1,0:T(8,128)(4,1)} %get-tuple-element.90) | copy-start | bytes 6148
  14.5 5.2 %copy-start.19 = (pred[16,128]{1,0:T(8,128)(4,1)S(1)}, pred[16,128]{1,0:T(8,128)(4,1)}, u32[]{:S(2)}) copy-start(pred[16,128]{1,0:T(8,128)(4,1)} %get-tuple-element.165) | copy-start | bytes 6148
  14.5 5.2 %copy-start.20 = (pred[16,128]{1,0:T(8,128)(4,1)S(1)}, pred[16,128]{1,0:T(8,128)(4,1)}, u32[]{:S(2)}) copy-start(pred[16,128]{1,0:T(8,128)(4,1)} %get-tuple-element.167) | copy-start | bytes 6148
  14.5 5.2 %copy-start.21 = (pred[16,128]{1,0:T(8,128)(4,1)S(1)}, pred[16,128]{1,0:T(8,128)(4,1)}, u32[]{:S(2)}) copy-start(pred[16,128]{1,0:T(8,128)(4,1)} %get-tuple-element.169) | copy-start | bytes 6148
  14.5 5.2 %copy-start.22 = (pred[16,128]{1,0:T(8,128)(4,1)S(1)}, pred[16,128]{1,0:T(8,128)(4,1)}, u32[]{:S(2)}) copy-start(pred[16,128]{1,0:T(8,128)(4,1)} %get-tuple-element.420) | copy-start | bytes 6148
  14.5 5.2 %copy-start.23 = (pred[16,128]{1,0:T(8,128)(4,1)S(1)}, pred[16,128]{1,0:T(8,128)(4,1)}, u32[]{:S(2)}) copy-start(pred[16,128]{1,0:T(8,128)(4,1)} %get-tuple-element.422) | copy-start | bytes 6148
  14.5 5.2 %copy-start.24 = (pred[16,128]{1,0:T(8,128)(4,1)S(1)}, pred[16,128]{1,0:T(8,128)(4,1)}, u32[]{:S(2)}) copy-start(pred[16,128]{1,0:T(8,128)(4,1)} %get-tuple-element.424) | copy-start | bytes 6148
  14.5 5.2 %copy-start.25 = (pred[16,128]{1,0:T(8,128)(4,1)S(1)}, pred[16,128]{1,0:T(8,128)(4,1)}, u32[]{:S(2)}) copy-start(pred[16,128]{1,0:T(8,128)(4,1)} %get-tuple-element.426) | copy-start | bytes 6148
  14.5 5.2 %copy-start.26 = (pred[16,128]{1,0:T(8,128)(4,1)S(1)}, pred[16,128]{1,0:T(8,128)(4,1)}, u32[]{:S(2)}) copy-start(pred[16,128]{1,0:T(8,128)(4,1)} %get-tuple-element.428) | copy-start | bytes 6148
  14.5 5.2 %copy-start.27 = (pred[16,128]{1,0:T(8,128)(4,1)S(1)}, pred[16,128]{1,0:T(8,128)(4,1)}, u32[]{:S(2)}) copy-start(pred[16,128]{1,0:T(8,128)(4,1)} %get-tuple-element.430) | copy-start | bytes 6148
  14.6 5.2 %copy-start.28 = (pred[16,128]{1,0:T(8,128)(4,1)S(1)}, pred[16,128]{1,0:T(8,128)(4,1)}, u32[]{:S(2)}) copy-start(pred[16,128]{1,0:T(8,128)(4,1)} %get-tuple-element.432) | copy-start | bytes 6148
  14.6 5.2 %copy-start.29 = (pred[16,128]{1,0:T(8,128)(4,1)S(1)}, pred[16,128]{1,0:T(8,128)(4,1)}, u32[]{:S(2)}) copy-start(pred[16,128]{1,0:T(8,128)(4,1)} %get-tuple-element.434) | copy-start | bytes 6148
  14.6 5.2 %copy-start.30 = (pred[16,128]{1,0:T(8,128)(4,1)S(1)}, pred[16,128]{1,0:T(8,128)(4,1)}, u32[]{:S(2)}) copy-start(pred[16,128]{1,0:T(8,128)(4,1)} %get-tuple-element.436) | copy-start | bytes 6148
  14.6 5.2 %copy-start.31 = (pred[16,128]{1,0:T(8,128)(4,1)S(1)}, pred[16,128]{1,0:T(8,128)(4,1)}, u32[]{:S(2)}) copy-start(pred[16,128]{1,0:T(8,128)(4,1)} %get-tuple-element.438) | copy-start | bytes 6148
  14.6 5.2 %copy-start.32 = (pred[16,128]{1,0:T(8,128)(4,1)S(1)}, pred[16,128]{1,0:T(8,128)(4,1)}, u32[]{:S(2)}) copy-start(pred[16,128]{1,0:T(8,128)(4,1)} %get-tuple-element.440) | copy-start | bytes 6148
  14.6 5.2 %copy-start.33 = (pred[16,128]{1,0:T(8,128)(4,1)S(1)}, pred[16,128]{1,0:T(8,128)(4,1)}, u32[]{:S(2)}) copy-start(pred[16,128]{1,0:T(8,128)(4,1)} %get-tuple-element.442) | copy-start | bytes 6148
  14.6 5.2 %copy-start.34 = (pred[16,128]{1,0:T(8,128)(4,1)S(1)}, pred[16,128]{1,0:T(8,128)(4,1)}, u32[]{:S(2)}) copy-start(pred[16,128]{1,0:T(8,128)(4,1)} %get-tuple-element.320) | copy-start | bytes 6148
  14.6 5.2 %copy-start.35 = (pred[16,128]{1,0:T(8,128)(4,1)S(1)}, pred[16,128]{1,0:T(8,128)(4,1)}, u32[]{:S(2)}) copy-start(pred[16,128]{1,0:T(8,128)(4,1)} %get-tuple-element.321) | copy-start | bytes 6148
  14.6 5.2 %copy-start.36 = (pred[16,128]{1,0:T(8,128)(4,1)S(1)}, pred[16,128]{1,0:T(8,128)(4,1)}, u32[]{:S(2)}) copy-start(pred[16,128]{1,0:T(8,128)(4,1)} %get-tuple-element.322) | copy-start | bytes 6148
  14.6 5.2 %copy-start.37 = (pred[16,128]{1,0:T(8,128)(4,1)S(1)}, pred[16,128]{1,0:T(8,128)(4,1)}, u32[]{:S(2)}) copy-start(pred[16,128]{1,0:T(8,128)(4,1)} %get-tuple-element.323) | copy-start | bytes 6148
  22.0 15.0 %copy-start.4 = (f32[2,16,128]{2,1,0:T(8,128)}, f32[2,16,128]{2,1,0:T(8,128)S(1)}, u32[]{:S(2)}) copy-start(f32[2,16,128]{2,1,0:T(8,128)S(1)} %subtract_multiply_fusion) | copy-start | bytes 49156
  37.0 60.7 %copy-start = (f32[16,128,384]{2,1,0:T(8,128)}, f32[16,128,384]{2,1,0:T(8,128)S(1)}, u32[]{:S(2)}) copy-start(f32[16,128,384]{2,1,0:T(8,128)S(1)} %concatenate.146.x_ref) | copy-start | bytes 9437188
  37.0 33.0 %copy-start.46 = (pred[384]{0:T(512)(128)(4,1)S(1)}, pred[384]{0:T(512)(128)(4,1)}, u32[]{:S(2)}) copy-start(pred[384]{0:T(512)(128)(4,1)} %fusion.79) | copy-start | bytes 1156
  37.0 39.8 %copy-start.47 = (pred[384]{0:T(512)(128)(4,1)S(1)}, pred[384]{0:T(512)(128)(4,1)}, u32[]{:S(2)}) copy-start(pred[384]{0:T(512)(128)(4,1)} %fusion.78) | copy-start | bytes 1156
  37.2 24.3 %collective-permute-start.3 = (f32[4,8,384]{2,1,0:T(8,128)S(1)}, f32[4,8,384]{2,1,0:T(8,128)S(1)}, u32[]{:S(2)}, u32[]{:S(2)}) collective-permute-start(f32[4,8,384]{2,1,0:T(8,128)S(1)} %get-tuple-element.101), channel_id=1, source_target_pairs={{0,33},{1,34},{2,35},{3,36},{4,37},{5,38},{6,39},{7,40},{8,41},{9,... | collective-permute-start | bytes 147464 | tf_op jit(solution)/shard_map/ppermute | solution.py:31
  41.5 26.2 %collective-permute-start.6 = (f32[4,8,384]{2,1,0:T(8,128)S(1)}, f32[4,8,384]{2,1,0:T(8,128)S(1)}, u32[]{:S(2)}, u32[]{:S(2)}) collective-permute-start(f32[4,8,384]{2,1,0:T(8,128)S(1)} %get-tuple-element.98), channel_id=1, source_target_pairs={{0,63},{1,32},{2,33},{3,34},{4,35},{5,36},{6,37},{7,38},{8,39},{9,... | collective-permute-start | bytes 147464 | tf_op jit(solution)/shard_map/ppermute | solution.py:31
  44.3 52.4 %collective-permute-start.2 = (f32[4,128,384]{2,1,0:T(8,128)S(1)}, f32[4,128,384]{2,1,0:T(8,128)S(1)}, u32[]{:S(2)}, u32[]{:S(2)}) collective-permute-start(f32[4,128,384]{2,1,0:T(8,128)S(1)} %get-tuple-element.104), channel_id=1, source_target_pairs={{0,224},{1,225},{2,226},{3,227},{4,228},{5,229},{6,230},{7,231},{8... | collective-permute-start | bytes 2359304 | tf_op jit(solution)/shard_map/ppermute | solution.py:31
  52.4 22.5 %collective-permute-start.5 = (f32[4,8,384]{2,1,0:T(8,128)S(1)}, f32[4,8,384]{2,1,0:T(8,128)S(1)}, u32[]{:S(2)}, u32[]{:S(2)}) collective-permute-start(f32[4,8,384]{2,1,0:T(8,128)S(1)} %get-tuple-element.100), channel_id=1, source_target_pairs={{0,225},{1,226},{2,227},{3,228},{4,229},{5,230},{6,231},{7,232},{8... | collective-permute-start | bytes 147464 | tf_op jit(solution)/shard_map/ppermute | solution.py:31
  54.3 22.5 %collective-permute-start.8 = (f32[4,8,384]{2,1,0:T(8,128)S(1)}, f32[4,8,384]{2,1,0:T(8,128)S(1)}, u32[]{:S(2)}, u32[]{:S(2)}) collective-permute-start(f32[4,8,384]{2,1,0:T(8,128)S(1)} %get-tuple-element.99), channel_id=1, source_target_pairs={{0,255},{1,224},{2,225},{3,226},{4,227},{5,228},{6,229},{7,230},{8... | collective-permute-start | bytes 147464 | tf_op jit(solution)/shard_map/ppermute | solution.py:31
  61.4 15.5 %collective-permute-start.7 = (f32[16,8,384]{2,1,0:T(8,128)S(1)}, f32[16,8,384]{2,1,0:T(8,128)S(1)}, u32[]{:S(2)}, u32[]{:S(2)}) collective-permute-start(f32[16,8,384]{2,1,0:T(8,128)S(1)} %get-tuple-element.102), channel_id=1, source_target_pairs={{0,31},{1,0},{2,1},{3,2},{4,3},{5,4},{6,5},{7,6},{8,7},{9,8},{10,9... | collective-permute-start | bytes 589832 | tf_op jit(solution)/shard_map/ppermute | solution.py:31
  67.8 30.0 %collective-permute-start.1 = (f32[4,128,384]{2,1,0:T(8,128)S(1)}, f32[4,128,384]{2,1,0:T(8,128)S(1)}, u32[]{:S(2)}, u32[]{:S(2)}) collective-permute-start(f32[4,128,384]{2,1,0:T(8,128)S(1)} %get-tuple-element.105), channel_id=1, source_target_pairs={{0,32},{1,33},{2,34},{3,35},{4,36},{5,37},{6,38},{7,39},{8,40},{9,... | collective-permute-start | bytes 2359304 | tf_op jit(solution)/shard_map/ppermute | solution.py:31
  74.9 21.1 %collective-permute-start.4 = (f32[16,8,384]{2,1,0:T(8,128)S(1)}, f32[16,8,384]{2,1,0:T(8,128)S(1)}, u32[]{:S(2)}, u32[]{:S(2)}) collective-permute-start(f32[16,8,384]{2,1,0:T(8,128)S(1)} %get-tuple-element.103), channel_id=1, source_target_pairs={{0,1},{1,2},{2,3},{3,4},{4,5},{5,6},{6,7},{7,8},{8,9},{9,10},{10,1... | collective-permute-start | bytes 589832 | tf_op jit(solution)/shard_map/ppermute | solution.py:31
  (9 other events, 44.0 us)

commit v6 on v3

--- a/solution.py
+++ b/solution.py
@@ -140,6 +140,51 @@
     )(x, top, bot, left, right)
 
 
+def pack_kernel(st_ref, zon_ref, mer_ref, mix_ref, wet_ref, flux_ref, o_ref, t0_ref, t1_ref, t2_ref, *, levels):
+    rows = wet_ref.shape[0]
+    for t_ref in (t0_ref, t1_ref, t2_ref):
+        t_ref[...] = jnp.zeros(t_ref.shape, jnp.float32)
+    sub = lax.broadcasted_iota(jnp.int32, (LANES, LANES), 0)
+
+    def body(r, carry):
+        levels_at = pl.ds(r, levels, stride=rows)
+        t0_ref[0:levels] = st_ref[0, levels_at, :]
+        t0_ref[HALF : HALF + levels] = st_ref[1, levels_at, :]
+        t1_ref[0:levels] = zon_ref[levels_at, :]
+        t1_ref[HALF : HALF + levels] = mer_ref[levels_at, :]
+        t2_ref[0:levels] = mix_ref[levels_at, :]
+        t2_ref[HALF:LANES] = jnp.broadcast_to(wet_ref[pl.ds(r, 1), :], (LANES - HALF, LANES))
+        f0 = jnp.broadcast_to(flux_ref[0, pl.ds(r, 1), :], (LANES, LANES))
+        f1 = jnp.broadcast_to(flux_ref[1, pl.ds(r, 1), :], (LANES, LANES))
+        t0 = t0_ref[...]
+        t0 = jnp.where(sub == levels, f0, t0)
+        t0 = jnp.where(sub == HALF + levels, f1, t0)
+        o_ref[r, :, 0:LANES] = jnp.transpose(t0)
+        o_ref[r, :, LANES : 2 * LANES] = jnp.transpose(t1_ref[...])
+        o_ref[r, :, 2 * LANES : 3 * LANES] = jnp.transpose(t2_ref[...])
+        return carry
+
+    for r in range(rows):
+        body(r, 0)
+
+
+def pack(tracers, zonal, meridional, mixing, wet, flux):
+    fields, levels, rows, cols = tracers.shape
+    return pl.pallas_call(
+        functools.partial(pack_kernel, levels=levels),
+        out_shape=jax.ShapeDtypeStruct((rows, cols, 3 * LANES), jnp.float32),
+        scratch_shapes=[pltpu.VMEM((LANES, LANES), jnp.float32) for _ in range(3)],
+        interpret=INTERPRET,
+    )(
+        tracers.reshape(fields, levels * rows, cols),
+        zonal.reshape(levels * rows, cols),
+        meridional.reshape(levels * rows, cols),
+        mixing.reshape(levels * rows, cols),
+        wet,
+        flux,
+    )
+
+
 def to_lanes(x, fill):
     return jnp.concatenate([jnp.transpose(x, (1, 2, 0)), fill], axis=-1)
 
@@ -156,15 +201,7 @@
     regridded = regrid(partner, regrid_map[0])
     flux = exchange_rate[0] * sea * (regridded - surface)
 
-    pad = HALF - levels
-    zeros = jnp.zeros((rows, cols, pad), jnp.float32)
-    flux_pad = [jnp.concatenate([flux[f][:, :, None], zeros[:, :, 1:]], axis=-1) for f in range(fields)]
-    x = jnp.concatenate(
-        [to_lanes(tracers[0], flux_pad[0]), to_lanes(tracers[1], flux_pad[1]),
-         to_lanes(zonal[0], zeros), to_lanes(meridional[0], zeros),
-         to_lanes(mixing[0], zeros), jnp.broadcast_to(wet[:, :, None], (rows, cols, HALF))],
-        axis=-1,
-    )
+    x = pack(tracers, zonal[0], meridional[0], mixing[0], wet, flux)
 
     width = SUB
     top = shifted(x[-width:], "lat", 1)

time: 120 us -> 93 us (0.78)
  local copies, waits for them, and re-layouts: 30.5 us -> 7.77 us
  Pallas kernels: 22.1 us -> 26.4 us
  other arithmetic: 9.16 us -> 5.01 us
  waiting for transfers between devices: 29.3 us -> 25.8 us
    concatenate x1 -> x0, local copies, waits for them, and re-layouts: 8.38 us -> none  [shards(): jnp.concatenate([to_lanes(tracers[0], flux_pad[0]), to_lanes(tracers[1],...]
    unnamed x103 -> x10, local copies, waits for them, and re-layouts: 11.5 us -> 3.58 us
    pallas_call x0 -> x1, Pallas kernels: none -> 4.26 us  [pack(): pl.pallas_call(functools.partial(pack_kernel, levels=levels), out_shape=j...]
    broadcast_in_dim x8, other arithmetic: 4.39 us -> 0.34 us  [regrid(): picked = jnp.where(hit[None], values, picked)]
    another operation x4 -> x0, local copies, waits for them, and re-layouts: 3.94 us -> none  [the longest x3 2.82 us: shards(): flux[f][:, :, None]]
    ppermute x4, waiting for transfers between devices: 29.3 us -> 25.8 us  [shifted(): lax.ppermute(x, axis, [(i, (i + step) % count) for i in range(count)])]
    broadcast_in_dim x2 -> x0, local copies, waits for them, and re-layouts: 2.38 us -> none  [the longest x1 1.32 us: shards(): jnp.broadcast_to(wet[:, :, None], (rows, cols, HALF))]
    slice x1 -> x0, local copies, waits for them, and re-layouts: 1.25 us -> none  [shards(): tracers[1]]
  transfers between devices with their start and end apart: 5 -> 5, of which waited for: 4 -> 4; matrix products, arithmetic and copies ran while one was open for 12% -> 4% of each run, Pallas kernels for 0% -> 0%
where the time goes in v6:
time: 93 us; the launch traced here: 92.5 us
  starting transfers between devices  26.7 us (29%)
  Pallas kernels  26.4 us (28%)
  waiting for transfers between devices  25.8 us (28%)
  local copies, waits for them, and re-layouts  7.77 us (8%)
  other arithmetic  5.01 us (5%)
  between operations  0.94 us (1%)
    ppermute x4, waiting for transfers between devices, shifted(): lax.ppermute(x, axis, [(i, (i + step) % count) for i in range(count)])  25.8 us
    pallas_call x1, Pallas kernels, run_steps(): pl.pallas_call(functools.partial(steps_kernel, levels=levels, width=width...  22.1 us
    ppermute x4, starting transfers between devices, shifted(): lax.ppermute(x, axis, [(i, (i + step) % count) for i in range(count)])  17.9 us
    ppermute x1, starting transfers between devices, shards(): partner = lax.ppermute(surface, 'sec', [(0, 1), (1, 0)])  8.75 us
    pallas_call x1, Pallas kernels, pack(): pl.pallas_call(functools.partial(pack_kernel, levels=levels), out_shape=j...  4.26 us
    unnamed x10, local copies, waits for them, and re-layouts  3.58 us
    mul x2, other arithmetic, shards(): flux = exchange_rate[0] * sea * (regridded - surface)  3.12 us
  transfers between devices with their start and end apart: 5, of which 4 were waited for; matrix products, arithmetic and copies ran while one was open for 4% of the time, Pallas kernels for 0%

profile of v6, /device:TPU:1, one launch (start us, length us, event | category | flops | bytes accessed | tf_op | source)
XLA Modules:
  0.0 92.5 jit_solution(8931516748741104825)
XLA Ops:
  0.6 1.3 %copy.15 = f32[1,2,60,16,128]{4,3,1,2,0:T(8,128)S(1)} copy(f32[1,2,60,16,128]{4,3,2,1,0:T(8,128)} %param.7) | data formatting | bytes 1966080 | tf_op args[0]
  2.0 8.7 %collective-permute-start = (f32[2,16,128]{2,1,0:T(8,128)S(1)}, f32[2,16,128]{2,1,0:T(8,128)S(1)}, u32[]{:S(2)}, u32[]{:S(2)}) collective-permute-start(f32[2,16,128]{2,1,0:T(8,128)S(1)} %slice_bitcast_fusion.1), channel_id=1, source_target_pairs={{0,256},{256,0},{1,257},{257,1},{2,258},{258,2},{3,259},{259,3},{4... | collective-permute-start | bytes 49160 | tf_op jit(solution)/shard_map/ppermute | solution.py:199
  10.7 0.8 compare_select_fusion
  11.6 0.1 and_bitcast_fusion.27
  11.9 1.3 %multiply_bitcast_fusion = (f32[16,128]{1,0:T(8,128)S(1)}, f32[16,128]{1,0:T(8,128)}) fusion(f32[1,16,128]{2,1,0:T(8,128)} %param.11, s32[1,16,128]{2,1,0:T(8,128)} %param.12, pred[]{:T(512)S(6)} %eq.667), kind=kLoop, calls=%fused_computation.225 | loop fusion | flops 6144 | bytes 32769 | tf_op jit(solution)/shard_map/mul | solution.py:202
  13.3 0.0 collective-permute-done
  13.3 0.1 fusion.6
  13.4 0.1 fusion.11
  13.5 0.1 fusion.10
  13.6 0.1 fusion.9
  13.7 0.1 fusion.8
  13.8 0.1 fusion.7
  13.9 1.8 %subtract_multiply_fusion.flux_ref = f32[2,16,128]{2,1,0:T(8,128)} fusion(f32[2,16,128]{2,1,0:T(8,128)S(1)} %collective-permute-done, f32[2,2,128]{2,1,0:T(2,128)S(1)} %reshape.30, f32[2,16,3]{2,1,0:T(8,128)S(1)} %get-tuple-element.225, f32[2,16,3]{2,1,0:T(8,128)S(1)} %get-tuple-element.284, f32[2,16,125]{2,1,0:T(8,128)S(1)} %get-tuple-element.280, ...), kind=kLoop, calls=%fused_computation.203 | loop fusion | flops 745472 | bytes 807680 | tf_op jit(solution)/shard_map/mul | solution.py:202
  15.7 4.3 %shard_map.86.x_ref = f32[16,128,384]{2,1,0:T(8,128)} custom-call(f32[2,960,128]{2,1,0:T(8,128)} %bitcast.330, f32[960,128]{1,0:T(8,128)} %bitcast.333, f32[960,128]{1,0:T(8,128)} %bitcast.334, f32[960,128]{1,0:T(8,128)} %bitcast.335, f32[16,128]{1,0:T(8,128)} %get-tuple-element.313.wet_ref, f32[2,16,128]{2,1,0:T(8,128)} %subtract_multiply_fusion.flux_ref), custom_call_target="tpu_custom_call" | custom-call | tf_op jit(solution)/shard_map/pallas_call | solution.py:173
  20.0 1.5 %fusion.81 = (f32[4,128,384]{2,1,0:T(8,128)S(1)}, f32[4,128,384]{2,1,0:T(8,128)S(1)}) fusion(f32[16,128,384]{2,1,0:T(8,128)} %shard_map.86.x_ref), kind=kLoop, calls=%fused_computation.419 | loop fusion | bytes 3145728 | tf_op jit(solution)/shard_map/slice | solution.py:208
  21.5 1.9 %collective-permute-start.2 = (f32[4,128,384]{2,1,0:T(8,128)S(1)}, f32[4,128,384]{2,1,0:T(8,128)S(1)}, u32[]{:S(2)}, u32[]{:S(2)}) collective-permute-start(f32[4,128,384]{2,1,0:T(8,128)S(1)} %get-tuple-element.98), channel_id=1, source_target_pairs={{0,224},{32,0},{64,32},{96,64},{128,96},{160,128},{192,160},{224,1... | collective-permute-start | bytes 2359304 | tf_op jit(solution)/shard_map/ppermute | solution.py:22
  23.4 3.4 %collective-permute-start.1 = (f32[4,128,384]{2,1,0:T(8,128)S(1)}, f32[4,128,384]{2,1,0:T(8,128)S(1)}, u32[]{:S(2)}, u32[]{:S(2)}) collective-permute-start(f32[4,128,384]{2,1,0:T(8,128)S(1)} %get-tuple-element.99), channel_id=1, source_target_pairs={{0,32},{32,64},{64,96},{96,128},{128,160},{160,192},{192,224},{224... | collective-permute-start | bytes 2359304 | tf_op jit(solution)/shard_map/ppermute | solution.py:22
  26.8 1.1 %fusion.80 = (f32[16,8,384]{2,1,0:T(8,128)S(1)}, f32[16,8,384]{2,1,0:T(8,128)S(1)}) fusion(f32[16,128,384]{2,1,0:T(8,128)} %shard_map.86.x_ref), kind=kLoop, calls=%fused_computation.418 | loop fusion | bytes 786432 | tf_op jit(solution)/shard_map/slice | solution.py:214
  27.9 14.6 %collective-permute-done.2 = f32[4,128,384]{2,1,0:T(8,128)S(1)} collective-permute-done((f32[4,128,384]{2,1,0:T(8,128)S(1)}, f32[4,128,384]{2,1,0:T(8,128)S(1)}, u32[]{:S(2)}, u32[]{:S(2)}) %collective-permute-start.2) | collective-permute-done | bytes 786464 | tf_op jit(solution)/shard_map/ppermute | solution.py:22
  42.4 0.1 broadcast_select_fusion.bot_ref
  42.5 0.0 copy-start
  42.5 5.4 %collective-permute-done.1 = f32[4,128,384]{2,1,0:T(8,128)S(1)} collective-permute-done((f32[4,128,384]{2,1,0:T(8,128)S(1)}, f32[4,128,384]{2,1,0:T(8,128)S(1)}, u32[]{:S(2)}, u32[]{:S(2)}) %collective-permute-start.1) | collective-permute-done | bytes 786464 | tf_op jit(solution)/shard_map/ppermute | solution.py:22
  48.0 0.1 broadcast_select_fusion.1.top_ref
  48.0 0.0 copy-start.1
  48.1 1.9 %collective-permute-start.3 = (f32[24,8,384]{2,1,0:T(8,128)S(1)}, f32[24,8,384]{2,1,0:T(8,128)S(1)}, u32[]{:S(2)}, u32[]{:S(2)}) collective-permute-start(f32[24,8,384]{2,1,0:T(8,128)S(1)} %pad_maximum_fusion), channel_id=1, source_target_pairs={{0,1},{1,2},{2,3},{3,4},{4,5},{5,6},{6,7},{7,8},{8,9},{9,10},{10,1... | collective-permute-start | bytes 884744 | tf_op jit(solution)/shard_map/ppermute | solution.py:22
  50.1 10.7 %collective-permute-start.4 = (f32[24,8,384]{2,1,0:T(8,128)S(1)}, f32[24,8,384]{2,1,0:T(8,128)S(1)}, u32[]{:S(2)}, u32[]{:S(2)}) collective-permute-start(f32[24,8,384]{2,1,0:T(8,128)S(1)} %pad_maximum_fusion.1), channel_id=1, source_target_pairs={{0,31},{1,0},{2,1},{3,2},{4,3},{5,4},{6,5},{7,6},{8,7},{9,8},{10,9... | collective-permute-start | bytes 884744 | tf_op jit(solution)/shard_map/ppermute | solution.py:22
  60.8 4.3 %collective-permute-done.3.left_ref = f32[24,8,384]{2,1,0:T(8,128)S(1)} collective-permute-done((f32[24,8,384]{2,1,0:T(8,128)S(1)}, f32[24,8,384]{2,1,0:T(8,128)S(1)}, u32[]{:S(2)}, u32[]{:S(2)}) %collective-permute-start.3) | collective-permute-done | bytes 294944 | tf_op jit(solution)/shard_map/ppermute | solution.py:22
  65.1 0.0 copy-start.2
  65.1 1.4 %collective-permute-done.4.right_ref = f32[24,8,384]{2,1,0:T(8,128)S(1)} collective-permute-done((f32[24,8,384]{2,1,0:T(8,128)S(1)}, f32[24,8,384]{2,1,0:T(8,128)S(1)}, u32[]{:S(2)}, u32[]{:S(2)}) %collective-permute-start.4) | collective-permute-done | bytes 294944 | tf_op jit(solution)/shard_map/ppermute | solution.py:22
  66.5 0.0 copy-done
  66.5 0.0 copy-done.1
  66.5 0.0 copy-done.2
  66.6 0.0 copy-start.3
  66.6 0.7 copy-done.3
  67.3 22.1 %shard_map.87 = f32[16,128,128]{2,1,0:T(8,128)} custom-call(f32[16,128,384]{2,1,0:T(8,128)} %shard_map.86.x_ref, f32[4,128,384]{2,1,0:T(8,128)} %copy-done.1, f32[4,128,384]{2,1,0:T(8,128)} %copy-done, f32[24,8,384]{2,1,0:T(8,128)} %copy-done.2, f32[24,8,384]{2,1,0:T(8,128)} %copy-done.3), custom_call_target="tpu_custom_call" | custom-call | tf_op jit(solution)/shard_map/pallas_call | solution.py:134
  89.4 1.6 %copy.12 = f32[16,128,128]{1,2,0:T(8,128)S(1)} copy(f32[16,128,128]{2,1,0:T(8,128)} %shard_map.87) | data formatting | bytes 2097152 | tf_op jit(solution)/shard_map/pallas_call | solution.py:134
  90.9 0.1 slice_bitcast_fusion
  91.0 1.5 %copy.13 = f32[1,2,60,16,128]{4,3,2,1,0:T(8,128)} copy(f32[1,2,60,16,128]{4,2,1,3,0:T(8,128)S(1)} %slice_bitcast_fusion) | data formatting | bytes 1966080
  (17 shorter events, 0.4 us)
Async XLA Ops:
  2.0 11.3 %collective-permute-start = (f32[2,16,128]{2,1,0:T(8,128)S(1)}, f32[2,16,128]{2,1,0:T(8,128)S(1)}, u32[]{:S(2)}, u32[]{:S(2)}) collective-permute-start(f32[2,16,128]{2,1,0:T(8,128)S(1)} %slice_bitcast_fusion.1), channel_id=1, source_target_pairs={{0,256},{256,0},{1,257},{257,1},{2,258},{258,2},{3,259},{259,3},{4... | collective-permute-start | bytes 49160 | tf_op jit(solution)/shard_map/ppermute | solution.py:199
  21.5 21.0 %collective-permute-start.2 = (f32[4,128,384]{2,1,0:T(8,128)S(1)}, f32[4,128,384]{2,1,0:T(8,128)S(1)}, u32[]{:S(2)}, u32[]{:S(2)}) collective-permute-start(f32[4,128,384]{2,1,0:T(8,128)S(1)} %get-tuple-element.98), channel_id=1, source_target_pairs={{0,224},{32,0},{64,32},{96,64},{128,96},{160,128},{192,160},{224,1... | collective-permute-start | bytes 2359304 | tf_op jit(solution)/shard_map/ppermute | solution.py:22
  23.4 24.6 %collective-permute-start.1 = (f32[4,128,384]{2,1,0:T(8,128)S(1)}, f32[4,128,384]{2,1,0:T(8,128)S(1)}, u32[]{:S(2)}, u32[]{:S(2)}) collective-permute-start(f32[4,128,384]{2,1,0:T(8,128)S(1)} %get-tuple-element.99), channel_id=1, source_target_pairs={{0,32},{32,64},{64,96},{96,128},{128,160},{160,192},{192,224},{224... | collective-permute-start | bytes 2359304 | tf_op jit(solution)/shard_map/ppermute | solution.py:22
  42.5 24.0 %copy-start = (f32[4,128,384]{2,1,0:T(8,128)}, f32[4,128,384]{2,1,0:T(8,128)S(1)}, u32[]{:S(2)}) copy-start(f32[4,128,384]{2,1,0:T(8,128)S(1)} %broadcast_select_fusion.bot_ref) | copy-start | bytes 2359300
  48.0 18.5 %copy-start.1 = (f32[4,128,384]{2,1,0:T(8,128)}, f32[4,128,384]{2,1,0:T(8,128)S(1)}, u32[]{:S(2)}) copy-start(f32[4,128,384]{2,1,0:T(8,128)S(1)} %broadcast_select_fusion.1.top_ref) | copy-start | bytes 2359300
  48.1 17.0 %collective-permute-start.3 = (f32[24,8,384]{2,1,0:T(8,128)S(1)}, f32[24,8,384]{2,1,0:T(8,128)S(1)}, u32[]{:S(2)}, u32[]{:S(2)}) collective-permute-start(f32[24,8,384]{2,1,0:T(8,128)S(1)} %pad_maximum_fusion), channel_id=1, source_target_pairs={{0,1},{1,2},{2,3},{3,4},{4,5},{5,6},{6,7},{7,8},{8,9},{9,10},{10,1... | collective-permute-start | bytes 884744 | tf_op jit(solution)/shard_map/ppermute | solution.py:22
  50.1 16.5 %collective-permute-start.4 = (f32[24,8,384]{2,1,0:T(8,128)S(1)}, f32[24,8,384]{2,1,0:T(8,128)S(1)}, u32[]{:S(2)}, u32[]{:S(2)}) collective-permute-start(f32[24,8,384]{2,1,0:T(8,128)S(1)} %pad_maximum_fusion.1), channel_id=1, source_target_pairs={{0,31},{1,0},{2,1},{3,2},{4,3},{5,4},{6,5},{7,6},{8,7},{9,8},{10,9... | collective-permute-start | bytes 884744 | tf_op jit(solution)/shard_map/ppermute | solution.py:22
  65.1 1.4 %copy-start.2 = (f32[24,8,384]{2,1,0:T(8,128)}, f32[24,8,384]{2,1,0:T(8,128)S(1)}, u32[]{:S(2)}) copy-start(f32[24,8,384]{2,1,0:T(8,128)S(1)} %collective-permute-done.3.left_ref) | copy-start | bytes 884740
  66.6 0.7 copy-start.3

commit v7 on v6

--- a/solution.py
+++ b/solution.py
@@ -17,9 +17,10 @@
 INTERPRET = False
 
 
-def shifted(x, axis, step):
+def shifted(x, axis, step, cyclic=True):
     count = lax.axis_size(axis)
-    return lax.ppermute(x, axis, [(i, (i + step) % count) for i in range(count)])
+    pairs = [(i, (i + step) % count) for i in range(count) if cyclic or 0 <= i + step < count]
+    return lax.ppermute(x, axis, pairs)
 
 
 def regrid(partner, table):
@@ -95,7 +96,7 @@
     lax.fori_loop(1, ext_rows - 1, coef_row, 0)
     qa_ref[...] = s_ref[:, :, 0:LANES]
 
-    def step(src, dst):
+    def step(src, dst, k):
         def body(r, carry):
             qc = src[r]
             qs = src[r - 1]
@@ -115,15 +116,18 @@
             dst[r] = jnp.where(level0, updated + fl_ref[r], updated)
             return carry
 
-        lax.fori_loop(1, ext_rows - 1, body, 0)
+        lax.fori_loop(k + 1, ext_rows - 1 - k, body, 0)
 
     for k in range(SUB):
         if k % 2 == 0:
-            step(qa_ref, qb_ref)
+            step(qa_ref, qb_ref, k)
         else:
-            step(qb_ref, qa_ref)
+            step(qb_ref, qa_ref, k)
     final = qa_ref if SUB % 2 == 0 else qb_ref
-    o_ref[...] = final[width : width + rows, COL_PAD : COL_PAD + cols, :]
+    for r in range(rows):
+        tile = jnp.transpose(final[width + r, COL_PAD : COL_PAD + cols, :])
+        for f in range(o_ref.shape[0]):
+            o_ref[f, pl.ds(r, levels, stride=rows), :] = tile[f * HALF : f * HALF + levels]
 
 
 def run_steps(x, top, bot, left, right, levels, width):
@@ -133,7 +137,7 @@
     scratch += [pltpu.VMEM(ext, jnp.float32) for _ in range(9)]
     return pl.pallas_call(
         functools.partial(steps_kernel, levels=levels, width=width),
-        out_shape=jax.ShapeDtypeStruct((rows, cols, LANES), jnp.float32),
+        out_shape=jax.ShapeDtypeStruct((LANES // HALF, levels * rows, cols), jnp.float32),
         scratch_shapes=scratch,
         compiler_params=pltpu.CompilerParams(vmem_limit_bytes=60 * 1024 * 1024),
         interpret=INTERPRET,
@@ -204,8 +208,8 @@
     x = pack(tracers, zonal[0], meridional[0], mixing[0], wet, flux)
 
     width = SUB
-    top = shifted(x[-width:], "lat", 1)
-    bot = shifted(x[:width], "lat", -1)
+    top = shifted(x[-width:], "lat", 1, cyclic=False)
+    bot = shifted(x[:width], "lat", -1, cyclic=False)
     row_block = lax.axis_index("lat")
     wet_lane = lax.broadcasted_iota(jnp.int32, (1, 1, 3 * LANES), 2) >= 2 * LANES + HALF
     top = jnp.where(jnp.logical_and(wet_lane, row_block == 0), 0.0, top)
@@ -214,8 +218,7 @@
     right = shifted(jnp.concatenate([top[:, :COL_PAD], x[:, :COL_PAD], bot[:, :COL_PAD]], axis=0), "lon", -1)
 
     out = run_steps(x, top, bot, left, right, levels, width)
-    q = out.reshape(rows, cols, fields, HALF)[..., :levels]
-    q = jnp.transpose(q, (2, 3, 0, 1))
+    q = out.reshape(fields, levels, rows, cols)
     return (q[None], flux[None])
 
 

time: 93 us -> 88.2 us (0.948)
  the two profiles are of different devices: /device:TPU:1 before, /device:TPU:16 now
where the time goes in v7:
time: 88.2 us; the launch traced here: 87.8 us
  waiting for transfers between devices  27 us (31%)
  starting transfers between devices  25.5 us (29%)
  Pallas kernels  24.7 us (28%)
  other arithmetic  5.01 us (6%)
  local copies, waits for them, and re-layouts  4.63 us (5%)
  between operations  0.91 us (1%)
    ppermute x4, waiting for transfers between devices, shifted(): return lax.ppermute(x, axis, pairs)  27 us
    ppermute x4, starting transfers between devices, shifted(): return lax.ppermute(x, axis, pairs)  23.6 us
    pallas_call x1, Pallas kernels, run_steps(): pl.pallas_call(functools.partial(steps_kernel, levels=levels, width=width...  20.4 us
    pallas_call x1, Pallas kernels, pack(): pl.pallas_call(functools.partial(pack_kernel, levels=levels), out_shape=j...  4.26 us
    mul x2, other arithmetic, shards(): flux = exchange_rate[0] * sea * (regridded - surface)  3.12 us
    unnamed x9, local copies, waits for them, and re-layouts  2.07 us
    ppermute x1, starting transfers between devices, shards(): partner = lax.ppermute(surface, 'sec', [(0, 1), (1, 0)])  1.92 us
  transfers between devices with their start and end apart: 5, of which 4 were waited for; matrix products, arithmetic and copies ran while one was open for 4% of the time, Pallas kernels for 0%

profile of v7, /device:TPU:16, one launch (start us, length us, event | category | flops | bytes accessed | tf_op | source)
XLA Modules:
  0.0 87.8 jit_solution(8941328466449136139)
XLA Ops:
  0.6 1.3 %copy.11 = f32[1,2,60,16,128]{4,3,1,2,0:T(8,128)S(1)} copy(f32[1,2,60,16,128]{4,3,2,1,0:T(8,128)} %param.7) | data formatting | bytes 1966080 | tf_op args[0]
  2.0 1.9 %collective-permute-start = (f32[2,16,128]{2,1,0:T(8,128)S(1)}, f32[2,16,128]{2,1,0:T(8,128)S(1)}, u32[]{:S(2)}, u32[]{:S(2)}) collective-permute-start(f32[2,16,128]{2,1,0:T(8,128)S(1)} %slice_bitcast_fusion), channel_id=1, source_target_pairs={{0,256},{256,0},{1,257},{257,1},{2,258},{258,2},{3,259},{259,3},{4... | collective-permute-start | bytes 49160 | tf_op jit(solution)/shard_map/ppermute | solution.py:203
  3.9 0.8 compare_select_fusion
  4.8 0.1 and_bitcast_fusion.27
  5.1 1.3 %multiply_bitcast_fusion = (f32[16,128]{1,0:T(8,128)S(1)}, f32[16,128]{1,0:T(8,128)}) fusion(f32[1,16,128]{2,1,0:T(8,128)} %param.11, s32[1,16,128]{2,1,0:T(8,128)} %param.12, pred[]{:T(512)S(6)} %eq.667), kind=kLoop, calls=%fused_computation.224 | loop fusion | flops 6144 | bytes 32769 | tf_op jit(solution)/shard_map/mul | solution.py:206
  6.4 0.0 collective-permute-done
  6.5 0.1 fusion.6
  6.6 0.1 fusion.11
  6.7 0.1 fusion.10
  6.8 0.1 fusion.9
  6.9 0.1 fusion.8
  7.0 0.1 fusion.7
  7.1 1.8 %subtract_multiply_fusion.flux_ref = f32[2,16,128]{2,1,0:T(8,128)} fusion(f32[2,16,128]{2,1,0:T(8,128)S(1)} %collective-permute-done, f32[2,2,128]{2,1,0:T(2,128)S(1)} %reshape.27, f32[2,16,3]{2,1,0:T(8,128)S(1)} %get-tuple-element.223, f32[2,16,3]{2,1,0:T(8,128)S(1)} %get-tuple-element.282, f32[2,16,125]{2,1,0:T(8,128)S(1)} %get-tuple-element.278, ...), kind=kLoop, calls=%fused_computation.202 | loop fusion | flops 745472 | bytes 807680 | tf_op jit(solution)/shard_map/mul | solution.py:206
  8.9 4.3 %shard_map.86.x_ref = f32[16,128,384]{2,1,0:T(8,128)} custom-call(f32[2,960,128]{2,1,0:T(8,128)} %bitcast.325, f32[960,128]{1,0:T(8,128)} %bitcast.329, f32[960,128]{1,0:T(8,128)} %bitcast.330, f32[960,128]{1,0:T(8,128)} %bitcast.331, f32[16,128]{1,0:T(8,128)} %get-tuple-element.311.wet_ref, f32[2,16,128]{2,1,0:T(8,128)} %subtract_multiply_fusion.flux_ref), custom_call_target="tpu_custom_call" | custom-call | tf_op jit(solution)/shard_map/pallas_call | solution.py:177
  13.2 1.5 %fusion.81 = (f32[4,128,384]{2,1,0:T(8,128)S(1)}, f32[4,128,384]{2,1,0:T(8,128)S(1)}) fusion(f32[16,128,384]{2,1,0:T(8,128)} %shard_map.86.x_ref), kind=kLoop, calls=%fused_computation.418 | loop fusion | bytes 3145728 | tf_op jit(solution)/shard_map/slice | solution.py:212
  14.6 4.4 %collective-permute-start.2 = (f32[4,128,384]{2,1,0:T(8,128)S(1)}, f32[4,128,384]{2,1,0:T(8,128)S(1)}, u32[]{:S(2)}, u32[]{:S(2)}) collective-permute-start(f32[4,128,384]{2,1,0:T(8,128)S(1)} %get-tuple-element.96), channel_id=1, source_target_pairs={{32,0},{64,32},{96,64},{128,96},{160,128},{192,160},{224,192},{33,... | collective-permute-start | bytes 2359304 | tf_op jit(solution)/shard_map/ppermute | solution.py:23
  19.1 1.9 %collective-permute-start.1 = (f32[4,128,384]{2,1,0:T(8,128)S(1)}, f32[4,128,384]{2,1,0:T(8,128)S(1)}, u32[]{:S(2)}, u32[]{:S(2)}) collective-permute-start(f32[4,128,384]{2,1,0:T(8,128)S(1)} %get-tuple-element.97), channel_id=1, source_target_pairs={{0,32},{32,64},{64,96},{96,128},{128,160},{160,192},{192,224},{1,3... | collective-permute-start | bytes 2359304 | tf_op jit(solution)/shard_map/ppermute | solution.py:23
  21.0 1.1 %fusion.80 = (f32[16,8,384]{2,1,0:T(8,128)S(1)}, f32[16,8,384]{2,1,0:T(8,128)S(1)}) fusion(f32[16,128,384]{2,1,0:T(8,128)} %shard_map.86.x_ref), kind=kLoop, calls=%fused_computation.417 | loop fusion | bytes 786432 | tf_op jit(solution)/shard_map/slice | solution.py:218
  22.1 14.4 %collective-permute-done.2 = f32[4,128,384]{2,1,0:T(8,128)S(1)} collective-permute-done((f32[4,128,384]{2,1,0:T(8,128)S(1)}, f32[4,128,384]{2,1,0:T(8,128)S(1)}, u32[]{:S(2)}, u32[]{:S(2)}) %collective-permute-start.2) | collective-permute-done | bytes 786464 | tf_op jit(solution)/shard_map/ppermute | solution.py:23
  36.5 0.1 broadcast_select_fusion.bot_ref
  36.6 0.0 copy-start
  36.6 7.7 %collective-permute-done.1 = f32[4,128,384]{2,1,0:T(8,128)S(1)} collective-permute-done((f32[4,128,384]{2,1,0:T(8,128)S(1)}, f32[4,128,384]{2,1,0:T(8,128)S(1)}, u32[]{:S(2)}, u32[]{:S(2)}) %collective-permute-start.1) | collective-permute-done | bytes 786464 | tf_op jit(solution)/shard_map/ppermute | solution.py:23
  44.3 0.1 broadcast_select_fusion.1.top_ref
  44.3 0.0 copy-start.1
  44.4 4.1 %collective-permute-start.3 = (f32[24,8,384]{2,1,0:T(8,128)S(1)}, f32[24,8,384]{2,1,0:T(8,128)S(1)}, u32[]{:S(2)}, u32[]{:S(2)}) collective-permute-start(f32[24,8,384]{2,1,0:T(8,128)S(1)} %pad_maximum_fusion), channel_id=1, source_target_pairs={{0,1},{1,2},{2,3},{3,4},{4,5},{5,6},{6,7},{7,8},{8,9},{9,10},{10,1... | collective-permute-start | bytes 884744 | tf_op jit(solution)/shard_map/ppermute | solution.py:23
  48.5 13.2 %collective-permute-start.4 = (f32[24,8,384]{2,1,0:T(8,128)S(1)}, f32[24,8,384]{2,1,0:T(8,128)S(1)}, u32[]{:S(2)}, u32[]{:S(2)}) collective-permute-start(f32[24,8,384]{2,1,0:T(8,128)S(1)} %pad_maximum_fusion.1), channel_id=1, source_target_pairs={{0,31},{1,0},{2,1},{3,2},{4,3},{5,4},{6,5},{7,6},{8,7},{9,8},{10,9... | collective-permute-start | bytes 884744 | tf_op jit(solution)/shard_map/ppermute | solution.py:23
  61.7 3.7 %collective-permute-done.3.left_ref = f32[24,8,384]{2,1,0:T(8,128)S(1)} collective-permute-done((f32[24,8,384]{2,1,0:T(8,128)S(1)}, f32[24,8,384]{2,1,0:T(8,128)S(1)}, u32[]{:S(2)}, u32[]{:S(2)}) %collective-permute-start.3) | collective-permute-done | bytes 294944 | tf_op jit(solution)/shard_map/ppermute | solution.py:23
  65.4 0.0 copy-start.2
  65.4 1.3 %collective-permute-done.4.right_ref = f32[24,8,384]{2,1,0:T(8,128)S(1)} collective-permute-done((f32[24,8,384]{2,1,0:T(8,128)S(1)}, f32[24,8,384]{2,1,0:T(8,128)S(1)}, u32[]{:S(2)}, u32[]{:S(2)}) %collective-permute-start.4) | collective-permute-done | bytes 294944 | tf_op jit(solution)/shard_map/ppermute | solution.py:23
  66.6 0.0 copy-done
  66.6 0.0 copy-done.1
  66.6 0.0 copy-done.2
  66.6 0.0 copy-start.3
  66.6 0.7 copy-done.3
  67.4 20.4 %shard_map.87 = f32[2,960,128]{2,1,0:T(8,128)} custom-call(f32[16,128,384]{2,1,0:T(8,128)} %shard_map.86.x_ref, f32[4,128,384]{2,1,0:T(8,128)} %copy-done.1, f32[4,128,384]{2,1,0:T(8,128)} %copy-done, f32[24,8,384]{2,1,0:T(8,128)} %copy-done.2, f32[24,8,384]{2,1,0:T(8,128)} %copy-done.3), custom_call_target="tpu_custom_call" | custom-call | tf_op jit(solution)/shard_map/pallas_call | solution.py:138
  (17 shorter events, 0.4 us)
Async XLA Ops:
  2.0 4.5 %collective-permute-start = (f32[2,16,128]{2,1,0:T(8,128)S(1)}, f32[2,16,128]{2,1,0:T(8,128)S(1)}, u32[]{:S(2)}, u32[]{:S(2)}) collective-permute-start(f32[2,16,128]{2,1,0:T(8,128)S(1)} %slice_bitcast_fusion), channel_id=1, source_target_pairs={{0,256},{256,0},{1,257},{257,1},{2,258},{258,2},{3,259},{259,3},{4... | collective-permute-start | bytes 49160 | tf_op jit(solution)/shard_map/ppermute | solution.py:203
  14.6 21.9 %collective-permute-start.2 = (f32[4,128,384]{2,1,0:T(8,128)S(1)}, f32[4,128,384]{2,1,0:T(8,128)S(1)}, u32[]{:S(2)}, u32[]{:S(2)}) collective-permute-start(f32[4,128,384]{2,1,0:T(8,128)S(1)} %get-tuple-element.96), channel_id=1, source_target_pairs={{32,0},{64,32},{96,64},{128,96},{160,128},{192,160},{224,192},{33,... | collective-permute-start | bytes 2359304 | tf_op jit(solution)/shard_map/ppermute | solution.py:23
  19.1 25.2 %collective-permute-start.1 = (f32[4,128,384]{2,1,0:T(8,128)S(1)}, f32[4,128,384]{2,1,0:T(8,128)S(1)}, u32[]{:S(2)}, u32[]{:S(2)}) collective-permute-start(f32[4,128,384]{2,1,0:T(8,128)S(1)} %get-tuple-element.97), channel_id=1, source_target_pairs={{0,32},{32,64},{64,96},{96,128},{128,160},{160,192},{192,224},{1,3... | collective-permute-start | bytes 2359304 | tf_op jit(solution)/shard_map/ppermute | solution.py:23
  36.6 30.0 %copy-start = (f32[4,128,384]{2,1,0:T(8,128)}, f32[4,128,384]{2,1,0:T(8,128)S(1)}, u32[]{:S(2)}) copy-start(f32[4,128,384]{2,1,0:T(8,128)S(1)} %broadcast_select_fusion.bot_ref) | copy-start | bytes 2359300
  44.3 22.3 %copy-start.1 = (f32[4,128,384]{2,1,0:T(8,128)}, f32[4,128,384]{2,1,0:T(8,128)S(1)}, u32[]{:S(2)}) copy-start(f32[4,128,384]{2,1,0:T(8,128)S(1)} %broadcast_select_fusion.1.top_ref) | copy-start | bytes 2359300
  44.4 21.0 %collective-permute-start.3 = (f32[24,8,384]{2,1,0:T(8,128)S(1)}, f32[24,8,384]{2,1,0:T(8,128)S(1)}, u32[]{:S(2)}, u32[]{:S(2)}) collective-permute-start(f32[24,8,384]{2,1,0:T(8,128)S(1)} %pad_maximum_fusion), channel_id=1, source_target_pairs={{0,1},{1,2},{2,3},{3,4},{4,5},{5,6},{6,7},{7,8},{8,9},{9,10},{10,1... | collective-permute-start | bytes 884744 | tf_op jit(solution)/shard_map/ppermute | solution.py:23
  48.5 18.1 %collective-permute-start.4 = (f32[24,8,384]{2,1,0:T(8,128)S(1)}, f32[24,8,384]{2,1,0:T(8,128)S(1)}, u32[]{:S(2)}, u32[]{:S(2)}) collective-permute-start(f32[24,8,384]{2,1,0:T(8,128)S(1)} %pad_maximum_fusion.1), channel_id=1, source_target_pairs={{0,31},{1,0},{2,1},{3,2},{4,3},{5,4},{6,5},{7,6},{8,7},{9,8},{10,9... | collective-permute-start | bytes 884744 | tf_op jit(solution)/shard_map/ppermute | solution.py:23
  65.4 1.3 %copy-start.2 = (f32[24,8,384]{2,1,0:T(8,128)}, f32[24,8,384]{2,1,0:T(8,128)S(1)}, u32[]{:S(2)}) copy-start(f32[24,8,384]{2,1,0:T(8,128)S(1)} %collective-permute-done.3.left_ref) | copy-start | bytes 884740
  66.6 0.7 copy-start.3

commit v8 on v4

--- a/solution.py
+++ b/solution.py
@@ -17,9 +17,10 @@
 INTERPRET = False
 
 
-def shifted(x, axis, step):
+def shifted(x, axis, step, cyclic=True):
     count = lax.axis_size(axis)
-    return lax.ppermute(x, axis, [(i, (i + step) % count) for i in range(count)])
+    pairs = [(i, (i + step) % count) for i in range(count) if cyclic or 0 <= i + step < count]
+    return lax.ppermute(x, axis, pairs)
 
 
 def regrid(partner, table):
@@ -50,19 +51,22 @@
 
 
 def steps_kernel(xq_ref, topq_ref, botq_ref, leftq_ref, rightq_ref, xv_ref, topv_ref, botv_ref, leftv_ref, rightv_ref,
-                 o_ref, s_ref, qa_ref, qb_ref, cw_ref, ce_ref, cs_ref, cn_ref, wc_ref, mx_ref, fl_ref, *, levels, width):
+                 o_ref, s_ref, qa_ref, qb_ref, cw_ref, ce_ref, cs_ref, cn_ref, wc_ref, mx_ref, fl_ref, wb_ref,
+                 *, levels, width):
     rows, cols = xq_ref.shape[0], xq_ref.shape[1]
     ext_rows = rows + 2 * width
     ext_cols = cols + 2 * COL_PAD
-    for lo, hi, x_ref, top_ref, bot_ref, left_ref, right_ref in (
-        (0, LANES, xq_ref, topq_ref, botq_ref, leftq_ref, rightq_ref),
-        (LANES, 3 * LANES, xv_ref, topv_ref, botv_ref, leftv_ref, rightv_ref),
+    inner = (COL_PAD, COL_PAD + cols)
+    for lo, hi, w, x_ref, top_ref, bot_ref, left_ref, right_ref in (
+        (0, LANES, width, xq_ref, topq_ref, botq_ref, leftq_ref, rightq_ref),
+        (LANES, 3 * LANES, width - 1, xv_ref, topv_ref, botv_ref, leftv_ref, rightv_ref),
     ):
-        s_ref[width : width + rows, COL_PAD : COL_PAD + cols, lo:hi] = x_ref[...]
-        s_ref[0:width, COL_PAD : COL_PAD + cols, lo:hi] = top_ref[...]
-        s_ref[width + rows :, COL_PAD : COL_PAD + cols, lo:hi] = bot_ref[...]
-        s_ref[:, 0:COL_PAD, lo:hi] = left_ref[...]
-        s_ref[:, COL_PAD + cols :, lo:hi] = right_ref[...]
+        r0 = width - w
+        s_ref[width : width + rows, inner[0] : inner[1], lo:hi] = x_ref[...]
+        s_ref[r0:width, inner[0] : inner[1], lo:hi] = top_ref[...]
+        s_ref[width + rows : width + rows + w, inner[0] : inner[1], lo:hi] = bot_ref[...]
+        s_ref[r0 : width + rows + w, 0:COL_PAD, lo:hi] = left_ref[...]
+        s_ref[r0 : width + rows + w, inner[1] :, lo:hi] = right_ref[...]
 
     lane = lax.broadcasted_iota(jnp.int32, (ext_cols, LANES), 1)
     low = lane < HALF
@@ -73,8 +77,16 @@
     def swap_halves(v):
         return pltpu.roll(v, HALF, 1)
 
-    def wet_of(v):
-        return jnp.where(low, swap_halves(v), v)
+    def wet_row(r, carry):
+        spread = jnp.where(lane == levels + 1, s_ref[r, :, 0:LANES], 0.0)
+        shift = 1
+        while shift < LANES:
+            spread = spread + pltpu.roll(spread, shift, 1)
+            shift *= 2
+        wb_ref[r] = spread
+        return carry
+
+    lax.fori_loop(0, ext_rows, wet_row, 0)
 
     def coef_row(r, carry):
         v1 = s_ref[r, :, LANES : 2 * LANES]
@@ -82,9 +94,9 @@
         zon = jnp.where(low, v1, swap_halves(v1))
         mer = jnp.where(low, swap_halves(v1), v1)
         mix = jnp.where(low, v2, swap_halves(v2))
-        wet_c = wet_of(v2)
-        wet_s = wet_of(s_ref[r - 1, :, 2 * LANES : 3 * LANES])
-        wet_n = wet_of(s_ref[r + 1, :, 2 * LANES : 3 * LANES])
+        wet_c = wb_ref[r]
+        wet_s = wb_ref[r - 1]
+        wet_n = wb_ref[r + 1]
         wet_w = pltpu.roll(wet_c, 1, 0)
         wet_e = pltpu.roll(wet_c, ext_cols - 1, 0)
         cw_ref[r] = wet_w * jnp.maximum(zon, 0.0)
@@ -127,30 +139,76 @@
         else:
             step(qb_ref, qa_ref, k)
     final = qa_ref if SUB % 2 == 0 else qb_ref
-    o_ref[...] = final[width : width + rows, COL_PAD : COL_PAD + cols, :]
+    for r in range(rows):
+        tile = jnp.transpose(final[width + r, inner[0] : inner[1], :])
+        for f in range(o_ref.shape[0]):
+            o_ref[f, pl.ds(r, levels, stride=rows), :] = tile[f * HALF : f * HALF + levels]
 
 
 def run_steps(q_parts, v_parts, levels, width):
     rows, cols, _ = q_parts[0].shape
     ext = (rows + 2 * width, cols + 2 * COL_PAD, LANES)
     scratch = [pltpu.VMEM((rows + 2 * width, cols + 2 * COL_PAD, 3 * LANES), jnp.float32)]
-    scratch += [pltpu.VMEM(ext, jnp.float32) for _ in range(9)]
+    scratch += [pltpu.VMEM(ext, jnp.float32) for _ in range(10)]
     return pl.pallas_call(
         functools.partial(steps_kernel, levels=levels, width=width),
-        out_shape=jax.ShapeDtypeStruct((rows, cols, LANES), jnp.float32),
+        out_shape=jax.ShapeDtypeStruct((LANES // HALF, levels * rows, cols), jnp.float32),
         scratch_shapes=scratch,
         compiler_params=pltpu.CompilerParams(vmem_limit_bytes=60 * 1024 * 1024),
         interpret=INTERPRET,
     )(*q_parts, *v_parts)
 
 
-def lanes_last(planes):
-    return jnp.transpose(jnp.concatenate(planes, axis=0), (1, 2, 0))
-
-
-def halo_parts(x, width, mask=None):
-    top = shifted(x[-width:], "lat", 1)
-    bot = shifted(x[:width], "lat", -1)
+def pack_q_kernel(st_ref, wet_ref, flux_ref, o_ref, t_ref, *, levels):
+    rows = wet_ref.shape[0]
+    t_ref[...] = jnp.zeros(t_ref.shape, jnp.float32)
+    sub = lax.broadcasted_iota(jnp.int32, (LANES, LANES), 0)
+    for r in range(rows):
+        levels_at = pl.ds(r, levels, stride=rows)
+        t_ref[0:levels] = st_ref[0, levels_at, :]
+        t_ref[HALF : HALF + levels] = st_ref[1, levels_at, :]
+        tile = t_ref[...]
+        tile = jnp.where(sub == levels, jnp.broadcast_to(flux_ref[0, pl.ds(r, 1), :], (LANES, LANES)), tile)
+        tile = jnp.where(sub == HALF + levels, jnp.broadcast_to(flux_ref[1, pl.ds(r, 1), :], (LANES, LANES)), tile)
+        tile = jnp.where(sub == levels + 1, jnp.broadcast_to(wet_ref[pl.ds(r, 1), :], (LANES, LANES)), tile)
+        o_ref[r] = jnp.transpose(tile)
+
+
+def pack_v_kernel(zon_ref, mer_ref, mix_ref, o_ref, t1_ref, t2_ref, *, levels, rows):
+    for t_ref in (t1_ref, t2_ref):
+        t_ref[...] = jnp.zeros(t_ref.shape, jnp.float32)
+    for r in range(rows):
+        levels_at = pl.ds(r, levels, stride=rows)
+        t1_ref[0:levels] = zon_ref[levels_at, :]
+        t1_ref[HALF : HALF + levels] = mer_ref[levels_at, :]
+        t2_ref[0:levels] = mix_ref[levels_at, :]
+        o_ref[r, :, 0:LANES] = jnp.transpose(t1_ref[...])
+        o_ref[r, :, LANES : 2 * LANES] = jnp.transpose(t2_ref[...])
+
+
+def pack_q(tracers, wet, flux):
+    fields, levels, rows, cols = tracers.shape
+    return pl.pallas_call(
+        functools.partial(pack_q_kernel, levels=levels),
+        out_shape=jax.ShapeDtypeStruct((rows, cols, LANES), jnp.float32),
+        scratch_shapes=[pltpu.VMEM((LANES, LANES), jnp.float32)],
+        interpret=INTERPRET,
+    )(tracers.reshape(fields, levels * rows, cols), wet, flux)
+
+
+def pack_v(zonal, meridional, mixing):
+    levels, rows, cols = zonal.shape
+    return pl.pallas_call(
+        functools.partial(pack_v_kernel, levels=levels, rows=rows),
+        out_shape=jax.ShapeDtypeStruct((rows, cols, 2 * LANES), jnp.float32),
+        scratch_shapes=[pltpu.VMEM((LANES, LANES), jnp.float32) for _ in range(2)],
+        interpret=INTERPRET,
+    )(zonal.reshape(levels * rows, cols), meridional.reshape(levels * rows, cols), mixing.reshape(levels * rows, cols))
+
+
+def halo_parts(x, w, mask=None):
+    top = shifted(x[-w:], "lat", 1, cyclic=False)
+    bot = shifted(x[:w], "lat", -1, cyclic=False)
     if mask is not None:
         row_block = lax.axis_index("lat")
         top = jnp.where(jnp.logical_and(mask, row_block == 0), 0.0, top)
@@ -163,29 +221,22 @@
 def shards(state, zonal, meridional, mixing, exchange_rate, sea_mask, regrid_map):
     tracers = state[0]
     fields, levels, rows, cols = tracers.shape
+    width = SUB
+    v_parts = halo_parts(pack_v(zonal[0], meridional[0], mixing[0]), width - 1)
+
     section = lax.axis_index("sec")
     sea = sea_mask[0].astype(jnp.float32)
     wet = jnp.where(section == 1, sea, jnp.ones_like(sea))
-    width = SUB
-    gap = jnp.zeros((HALF - levels, rows, cols), jnp.float32)
-
-    xv = lanes_last([zonal[0], gap, meridional[0], gap, mixing[0], gap, jnp.broadcast_to(wet, (HALF, rows, cols))])
-    wet_lane = lax.broadcasted_iota(jnp.int32, (1, 1, 2 * LANES), 2) >= LANES + HALF
-    v_parts = halo_parts(xv, width, wet_lane)
-
     surface = tracers[:, 0]
     partner = lax.ppermute(surface, "sec", [(0, 1), (1, 0)])
     regridded = regrid(partner, regrid_map[0])
     flux = exchange_rate[0] * sea * (regridded - surface)
 
-    planes = []
-    for f in range(fields):
-        planes += [tracers[f], flux[f][None], gap[1:]]
-    xq = lanes_last(planes)
-    q_parts = halo_parts(xq, width)
+    wet_lane = lax.broadcasted_iota(jnp.int32, (1, 1, LANES), 2) == levels + 1
+    q_parts = halo_parts(pack_q(tracers, wet, flux), width, wet_lane)
 
     out = run_steps(q_parts, v_parts, levels, width)
-    q = jnp.transpose(out, (2, 0, 1)).reshape(fields, HALF, rows, cols)[:, :levels]
+    q = out.reshape(fields, levels, rows, cols)
     return (q[None], flux[None])
 
 

time: 251 us -> 105 us (0.42)
  the two profiles are of different devices: /device:TPU:6 before, /device:TPU:16 now
where the time goes in v8:
time: 105 us; the launch traced here: 104 us
  starting transfers between devices  42 us (40%)
  Pallas kernels  37.5 us (36%)
  waiting for transfers between devices  13.2 us (13%)
  local copies, waits for them, and re-layouts  6.86 us (7%)
  other arithmetic  3.45 us (3%)
  between operations  1.14 us (1%)
    ppermute x8, starting transfers between devices, shifted(): return lax.ppermute(x, axis, pairs)  40.1 us
    pallas_call x1, Pallas kernels, run_steps(): pl.pallas_call(functools.partial(steps_kernel, levels=levels, width=width...  31.5 us
    ppermute x8, waiting for transfers between devices, shifted(): return lax.ppermute(x, axis, pairs)  13.2 us
    pallas_call x1, Pallas kernels, pack_v(): pl.pallas_call(functools.partial(pack_v_kernel, levels=levels, rows=rows)...  3.38 us
    unnamed x23, local copies, waits for them, and re-layouts  2.7 us
    pallas_call x1, Pallas kernels, pack_q(): pl.pallas_call(functools.partial(pack_q_kernel, levels=levels), out_shape...  2.61 us
    mul x2, other arithmetic, shards(): flux = exchange_rate[0] * sea * (regridded - surface)  2.4 us
    slice x2, local copies, waits for them, and re-layouts, halo_parts(): bot = shifted(x[:w], 'lat', -1, cyclic=False)  2.25 us
  transfers between devices with their start and end apart: 9, of which 3 were waited for; matrix products, arithmetic and copies ran while one was open for 7% of the time, Pallas kernels for 6%

profile of v8, /device:TPU:16, one launch (start us, length us, event | category | flops | bytes accessed | tf_op | source)
XLA Modules:
  0.0 104.2 jit_solution(17131671200394730231)
XLA Ops:
  0.6 1.3 %copy.11 = f32[1,2,60,16,128]{4,3,1,2,0:T(8,128)S(1)} copy(f32[1,2,60,16,128]{4,3,2,1,0:T(8,128)} %param.7) | data formatting | bytes 1966080 | tf_op args[0]
  2.0 1.9 %collective-permute-start = (f32[2,16,128]{2,1,0:T(8,128)S(1)}, f32[2,16,128]{2,1,0:T(8,128)S(1)}, u32[]{:S(2)}, u32[]{:S(2)}) collective-permute-start(f32[2,16,128]{2,1,0:T(8,128)S(1)} %slice_bitcast_fusion), channel_id=1, source_target_pairs={{0,256},{256,0},{1,257},{257,1},{2,258},{258,2},{3,259},{259,3},{4... | collective-permute-start | bytes 49160 | tf_op jit(solution)/shard_map/ppermute | solution.py:231
  3.9 0.0 copy-start.8
  3.9 0.0 copy-start.9
  3.9 0.0 copy-start.10
  3.9 3.4 %shard_map.87.xv_ref = f32[16,128,256]{2,1,0:T(8,128)} custom-call(f32[960,128]{1,0:T(8,128)} %bitcast.329, f32[960,128]{1,0:T(8,128)} %bitcast.330, f32[960,128]{1,0:T(8,128)} %bitcast.331), custom_call_target="tpu_custom_call" | custom-call | tf_op jit(solution)/shard_map/pallas_call | solution.py:201
  7.3 1.2 %fusion.79 = (f32[3,128,256]{2,1,0:T(8,128)S(1)}, f32[3,128,256]{2,1,0:T(8,128)S(1)}) fusion(f32[16,128,256]{2,1,0:T(8,128)} %shard_map.87.xv_ref), kind=kLoop, calls=%fused_computation.419 | loop fusion | bytes 1572864 | tf_op jit(solution)/shard_map/slice | solution.py:211
  8.5 4.4 %collective-permute-start.6 = (f32[3,128,256]{2,1,0:T(8,128)S(1)}, f32[3,128,256]{2,1,0:T(8,128)S(1)}, u32[]{:S(2)}, u32[]{:S(2)}) collective-permute-start(f32[3,128,256]{2,1,0:T(8,128)S(1)} %get-tuple-element.96), channel_id=1, source_target_pairs={{32,0},{64,32},{96,64},{128,96},{160,128},{192,160},{224,192},{33,... | collective-permute-start | bytes 1179656 | tf_op jit(solution)/shard_map/ppermute | solution.py:23
  13.0 1.9 %collective-permute-start.5 = (f32[3,128,256]{2,1,0:T(8,128)S(1)}, f32[3,128,256]{2,1,0:T(8,128)S(1)}, u32[]{:S(2)}, u32[]{:S(2)}) collective-permute-start(f32[3,128,256]{2,1,0:T(8,128)S(1)} %get-tuple-element.97), channel_id=1, source_target_pairs={{0,32},{32,64},{64,96},{96,128},{128,160},{160,192},{192,224},{1,3... | collective-permute-start | bytes 1179656 | tf_op jit(solution)/shard_map/ppermute | solution.py:23
  14.9 1.0 fusion.78
  15.9 0.0 copy-done.8
  16.0 0.0 copy-done.9
  16.0 0.0 copy-done.10
  16.0 0.6 multiply_bitcast_fusion
  17.0 0.0 collective-permute-done
  17.0 0.1 fusion.6
  17.1 0.1 fusion.11
  17.2 0.1 fusion.10
  17.3 0.1 fusion.9
  17.4 0.1 fusion.8
  17.6 0.1 fusion.7
  17.7 1.8 %subtract_multiply_fusion.flux_ref = f32[2,16,128]{2,1,0:T(8,128)} fusion(f32[2,16,128]{2,1,0:T(8,128)S(1)} %collective-permute-done, f32[2,2,128]{2,1,0:T(2,128)S(1)} %reshape.27, f32[2,16,3]{2,1,0:T(8,128)S(1)} %get-tuple-element.231, f32[2,16,3]{2,1,0:T(8,128)S(1)} %get-tuple-element.290, f32[2,16,125]{2,1,0:T(8,128)S(1)} %get-tuple-element.286, ...), kind=kLoop, calls=%fused_computation.204 | loop fusion | flops 745472 | bytes 807680 | tf_op jit(solution)/shard_map/mul | solution.py:233
  19.4 2.6 %shard_map.86.xq_ref = f32[16,128,128]{2,1,0:T(8,128)} custom-call(f32[2,960,128]{2,1,0:T(8,128)} %bitcast.325, f32[16,128]{1,0:T(8,128)} %get-tuple-element.319.wet_ref, f32[2,16,128]{2,1,0:T(8,128)} %subtract_multiply_fusion.flux_ref), custom_call_target="tpu_custom_call" | custom-call | tf_op jit(solution)/shard_map/pallas_call | solution.py:191
  22.1 1.1 %fusion.81 = (f32[4,128,128]{2,1,0:T(8,128)S(1)}, f32[4,128,128]{2,1,0:T(8,128)S(1)}) fusion(f32[16,128,128]{2,1,0:T(8,128)} %shard_map.86.xq_ref), kind=kLoop, calls=%fused_computation.421 | loop fusion | bytes 1048576 | tf_op jit(solution)/shard_map/slice | solution.py:211
  23.1 7.5 %collective-permute-start.2 = (f32[4,128,128]{2,1,0:T(8,128)S(1)}, f32[4,128,128]{2,1,0:T(8,128)S(1)}, u32[]{:S(2)}, u32[]{:S(2)}) collective-permute-start(f32[4,128,128]{2,1,0:T(8,128)S(1)} %get-tuple-element.100), channel_id=1, source_target_pairs={{32,0},{64,32},{96,64},{128,96},{160,128},{192,160},{224,192},{33,... | collective-permute-start | bytes 786440 | tf_op jit(solution)/shard_map/ppermute | solution.py:23
  30.7 1.9 %collective-permute-start.1 = (f32[4,128,128]{2,1,0:T(8,128)S(1)}, f32[4,128,128]{2,1,0:T(8,128)S(1)}, u32[]{:S(2)}, u32[]{:S(2)}) collective-permute-start(f32[4,128,128]{2,1,0:T(8,128)S(1)} %get-tuple-element.101), channel_id=1, source_target_pairs={{0,32},{32,64},{64,96},{96,128},{128,160},{160,192},{192,224},{1,3... | collective-permute-start | bytes 786440 | tf_op jit(solution)/shard_map/ppermute | solution.py:23
  32.6 0.9 fusion.80
  33.5 2.8 %collective-permute-done.2 = f32[4,128,128]{2,1,0:T(8,128)S(1)} collective-permute-done((f32[4,128,128]{2,1,0:T(8,128)S(1)}, f32[4,128,128]{2,1,0:T(8,128)S(1)}, u32[]{:S(2)}, u32[]{:S(2)}) %collective-permute-start.2) | collective-permute-done | bytes 262176 | tf_op jit(solution)/shard_map/ppermute | solution.py:23
  36.3 0.0 copy-start
  36.4 7.8 %collective-permute-done.1 = f32[4,128,128]{2,1,0:T(8,128)S(1)} collective-permute-done((f32[4,128,128]{2,1,0:T(8,128)S(1)}, f32[4,128,128]{2,1,0:T(8,128)S(1)}, u32[]{:S(2)}, u32[]{:S(2)}) %collective-permute-start.1) | collective-permute-done | bytes 262176 | tf_op jit(solution)/shard_map/ppermute | solution.py:23
  44.2 0.0 copy-start.1
  44.2 4.0 %collective-permute-start.3 = (f32[24,8,128]{2,1,0:T(8,128)S(1)}, f32[24,8,128]{2,1,0:T(8,128)S(1)}, u32[]{:S(2)}, u32[]{:S(2)}) collective-permute-start(f32[24,8,128]{2,1,0:T(8,128)S(1)} %pad_maximum_fusion.2), channel_id=1, source_target_pairs={{0,1},{1,2},{2,3},{3,4},{4,5},{5,6},{6,7},{7,8},{8,9},{9,10},{10,1... | collective-permute-start | bytes 294920 | tf_op jit(solution)/shard_map/ppermute | solution.py:23
  48.2 0.0 collective-permute-done.6.botv_ref
  48.2 0.0 copy-start.2
  48.3 0.0 collective-permute-done.5.topv_ref
  48.3 0.0 copy-start.3
  48.3 3.2 %collective-permute-start.7 = (f32[22,8,256]{2,1,0:T(8,128)S(1)}, f32[22,8,256]{2,1,0:T(8,128)S(1)}, u32[]{:S(2)}, u32[]{:S(2)}) collective-permute-start(f32[22,8,256]{2,1,0:T(8,128)S(1)} %pad_maximum_fusion), channel_id=1, source_target_pairs={{0,1},{1,2},{2,3},{3,4},{4,5},{5,6},{6,7},{7,8},{8,9},{9,10},{10,1... | collective-permute-start | bytes 540680 | tf_op jit(solution)/shard_map/ppermute | solution.py:23
  51.6 13.2 %collective-permute-start.8 = (f32[22,8,256]{2,1,0:T(8,128)S(1)}, f32[22,8,256]{2,1,0:T(8,128)S(1)}, u32[]{:S(2)}, u32[]{:S(2)}) collective-permute-start(f32[22,8,256]{2,1,0:T(8,128)S(1)} %pad_maximum_fusion.1), channel_id=1, source_target_pairs={{0,31},{1,0},{2,1},{3,2},{4,3},{5,4},{6,5},{7,6},{8,7},{9,8},{10,9... | collective-permute-start | bytes 540680 | tf_op jit(solution)/shard_map/ppermute | solution.py:23
  64.8 3.9 %collective-permute-start.4 = (f32[24,8,128]{2,1,0:T(8,128)S(1)}, f32[24,8,128]{2,1,0:T(8,128)S(1)}, u32[]{:S(2)}, u32[]{:S(2)}) collective-permute-start(f32[24,8,128]{2,1,0:T(8,128)S(1)} %pad_maximum_fusion.3), channel_id=1, source_target_pairs={{0,31},{1,0},{2,1},{3,2},{4,3},{5,4},{6,5},{7,6},{8,7},{9,8},{10,9... | collective-permute-start | bytes 294920 | tf_op jit(solution)/shard_map/ppermute | solution.py:23
  68.7 0.0 collective-permute-done.3.leftq_ref
  68.7 0.0 copy-start.6
  68.7 2.6 %collective-permute-done.4.rightq_ref = f32[24,8,128]{2,1,0:T(8,128)S(1)} collective-permute-done((f32[24,8,128]{2,1,0:T(8,128)S(1)}, f32[24,8,128]{2,1,0:T(8,128)S(1)}, u32[]{:S(2)}, u32[]{:S(2)}) %collective-permute-start.4) | collective-permute-done | bytes 98336 | tf_op jit(solution)/shard_map/ppermute | solution.py:23
  71.3 0.0 collective-permute-done.7.leftv_ref
  71.3 0.0 collective-permute-done.8.rightv_ref
  71.3 0.6 copy-done.7
  71.9 0.1 copy-done.4
  72.0 0.7 copy-done.5
  72.7 31.5 %shard_map.88 = f32[2,960,128]{2,1,0:T(8,128)} custom-call(f32[16,128,128]{2,1,0:T(8,128)} %shard_map.86.xq_ref, f32[4,128,128]{2,1,0:T(8,128)} %copy-done.1, f32[4,128,128]{2,1,0:T(8,128)} %copy-done, f32[24,8,128]{2,1,0:T(8,128)} %copy-done.6, f32[24,8,128]{2,1,0:T(8,128)} %copy-done.7, f32[16,128,256]{2,1,0:T(8,128)} %shard_map.87.xv_ref, ...), custom_call_target="tpu_custom_call" | custom-call | tf_op jit(solution)/shard_map/pallas_call | solution.py:153
  (33 shorter events, 0.5 us)
Async XLA Ops:
  2.0 15.0 %collective-permute-start = (f32[2,16,128]{2,1,0:T(8,128)S(1)}, f32[2,16,128]{2,1,0:T(8,128)S(1)}, u32[]{:S(2)}, u32[]{:S(2)}) collective-permute-start(f32[2,16,128]{2,1,0:T(8,128)S(1)} %slice_bitcast_fusion), channel_id=1, source_target_pairs={{0,256},{256,0},{1,257},{257,1},{2,258},{258,2},{3,259},{259,3},{4... | collective-permute-start | bytes 49160 | tf_op jit(solution)/shard_map/ppermute | solution.py:231
  3.9 12.0 %copy-start.8 = (s32[1,4,16,128]{3,2,1,0:T(8,128)S(1)}, s32[1,4,16,128]{3,2,1,0:T(8,128)}, u32[]{:S(2)}) copy-start(s32[1,4,16,128]{3,2,1,0:T(8,128)} %param.13) | copy-start | bytes 98308
  3.9 12.1 %copy-start.9 = (f32[1,16,128]{2,1,0:T(8,128)S(1)}, f32[1,16,128]{2,1,0:T(8,128)}, u32[]{:S(2)}) copy-start(f32[1,16,128]{2,1,0:T(8,128)} %param.11) | copy-start | bytes 24580
  3.9 12.1 %copy-start.10 = (s32[1,16,128]{2,1,0:T(8,128)S(1)}, s32[1,16,128]{2,1,0:T(8,128)}, u32[]{:S(2)}) copy-start(s32[1,16,128]{2,1,0:T(8,128)} %param.12) | copy-start | bytes 24580
  8.5 39.7 %collective-permute-start.6 = (f32[3,128,256]{2,1,0:T(8,128)S(1)}, f32[3,128,256]{2,1,0:T(8,128)S(1)}, u32[]{:S(2)}, u32[]{:S(2)}) collective-permute-start(f32[3,128,256]{2,1,0:T(8,128)S(1)} %get-tuple-element.96), channel_id=1, source_target_pairs={{32,0},{64,32},{96,64},{128,96},{160,128},{192,160},{224,192},{33,... | collective-permute-start | bytes 1179656 | tf_op jit(solution)/shard_map/ppermute | solution.py:23
  13.0 35.3 %collective-permute-start.5 = (f32[3,128,256]{2,1,0:T(8,128)S(1)}, f32[3,128,256]{2,1,0:T(8,128)S(1)}, u32[]{:S(2)}, u32[]{:S(2)}) collective-permute-start(f32[3,128,256]{2,1,0:T(8,128)S(1)} %get-tuple-element.97), channel_id=1, source_target_pairs={{0,32},{32,64},{64,96},{96,128},{128,160},{160,192},{192,224},{1,3... | collective-permute-start | bytes 1179656 | tf_op jit(solution)/shard_map/ppermute | solution.py:23
  23.1 13.2 %collective-permute-start.2 = (f32[4,128,128]{2,1,0:T(8,128)S(1)}, f32[4,128,128]{2,1,0:T(8,128)S(1)}, u32[]{:S(2)}, u32[]{:S(2)}) collective-permute-start(f32[4,128,128]{2,1,0:T(8,128)S(1)} %get-tuple-element.100), channel_id=1, source_target_pairs={{32,0},{64,32},{96,64},{128,96},{160,128},{192,160},{224,192},{33,... | collective-permute-start | bytes 786440 | tf_op jit(solution)/shard_map/ppermute | solution.py:23
  30.7 13.5 %collective-permute-start.1 = (f32[4,128,128]{2,1,0:T(8,128)S(1)}, f32[4,128,128]{2,1,0:T(8,128)S(1)}, u32[]{:S(2)}, u32[]{:S(2)}) collective-permute-start(f32[4,128,128]{2,1,0:T(8,128)S(1)} %get-tuple-element.101), channel_id=1, source_target_pairs={{0,32},{32,64},{64,96},{96,128},{128,160},{160,192},{192,224},{1,3... | collective-permute-start | bytes 786440 | tf_op jit(solution)/shard_map/ppermute | solution.py:23
  36.3 35.0 %copy-start = (f32[4,128,128]{2,1,0:T(8,128)}, f32[4,128,128]{2,1,0:T(8,128)S(1)}, u32[]{:S(2)}) copy-start(f32[4,128,128]{2,1,0:T(8,128)S(1)} %broadcast_select_fusion.botq_ref) | copy-start | bytes 786436
  44.2 27.1 %copy-start.1 = (f32[4,128,128]{2,1,0:T(8,128)}, f32[4,128,128]{2,1,0:T(8,128)S(1)}, u32[]{:S(2)}) copy-start(f32[4,128,128]{2,1,0:T(8,128)S(1)} %broadcast_select_fusion.1.topq_ref) | copy-start | bytes 786436
  44.2 24.5 %collective-permute-start.3 = (f32[24,8,128]{2,1,0:T(8,128)S(1)}, f32[24,8,128]{2,1,0:T(8,128)S(1)}, u32[]{:S(2)}, u32[]{:S(2)}) collective-permute-start(f32[24,8,128]{2,1,0:T(8,128)S(1)} %pad_maximum_fusion.2), channel_id=1, source_target_pairs={{0,1},{1,2},{2,3},{3,4},{4,5},{5,6},{6,7},{7,8},{8,9},{9,10},{10,1... | collective-permute-start | bytes 294920 | tf_op jit(solution)/shard_map/ppermute | solution.py:23
  48.2 23.1 %copy-start.2 = (f32[3,128,256]{2,1,0:T(8,128)}, f32[3,128,256]{2,1,0:T(8,128)S(1)}, u32[]{:S(2)}) copy-start(f32[3,128,256]{2,1,0:T(8,128)S(1)} %collective-permute-done.6.botv_ref) | copy-start | bytes 1179652
  48.3 23.1 %copy-start.3 = (f32[3,128,256]{2,1,0:T(8,128)}, f32[3,128,256]{2,1,0:T(8,128)S(1)}, u32[]{:S(2)}) copy-start(f32[3,128,256]{2,1,0:T(8,128)S(1)} %collective-permute-done.5.topv_ref) | copy-start | bytes 1179652
  48.3 23.0 %collective-permute-start.7 = (f32[22,8,256]{2,1,0:T(8,128)S(1)}, f32[22,8,256]{2,1,0:T(8,128)S(1)}, u32[]{:S(2)}, u32[]{:S(2)}) collective-permute-start(f32[22,8,256]{2,1,0:T(8,128)S(1)} %pad_maximum_fusion), channel_id=1, source_target_pairs={{0,1},{1,2},{2,3},{3,4},{4,5},{5,6},{6,7},{7,8},{8,9},{9,10},{10,1... | collective-permute-start | bytes 540680 | tf_op jit(solution)/shard_map/ppermute | solution.py:23
  51.6 19.7 %collective-permute-start.8 = (f32[22,8,256]{2,1,0:T(8,128)S(1)}, f32[22,8,256]{2,1,0:T(8,128)S(1)}, u32[]{:S(2)}, u32[]{:S(2)}) collective-permute-start(f32[22,8,256]{2,1,0:T(8,128)S(1)} %pad_maximum_fusion.1), channel_id=1, source_target_pairs={{0,31},{1,0},{2,1},{3,2},{4,3},{5,4},{6,5},{7,6},{8,7},{9,8},{10,9... | collective-permute-start | bytes 540680 | tf_op jit(solution)/shard_map/ppermute | solution.py:23
  64.8 6.5 %collective-permute-start.4 = (f32[24,8,128]{2,1,0:T(8,128)S(1)}, f32[24,8,128]{2,1,0:T(8,128)S(1)}, u32[]{:S(2)}, u32[]{:S(2)}) collective-permute-start(f32[24,8,128]{2,1,0:T(8,128)S(1)} %pad_maximum_fusion.3), channel_id=1, source_target_pairs={{0,31},{1,0},{2,1},{3,2},{4,3},{5,4},{6,5},{7,6},{8,7},{9,8},{10,9... | collective-permute-start | bytes 294920 | tf_op jit(solution)/shard_map/ppermute | solution.py:23
  68.7 2.6 %copy-start.6 = (f32[24,8,128]{2,1,0:T(8,128)}, f32[24,8,128]{2,1,0:T(8,128)S(1)}, u32[]{:S(2)}) copy-start(f32[24,8,128]{2,1,0:T(8,128)S(1)} %collective-permute-done.3.leftq_ref) | copy-start | bytes 294916
  71.3 0.7 copy-start.7
  71.3 0.7 copy-start.4
  72.0 0.7 copy-start.5

commit v9 on v8

--- a/solution.py
+++ b/solution.py
@@ -77,13 +77,10 @@
     def swap_halves(v):
         return pltpu.roll(v, HALF, 1)
 
+    pick = (lax.broadcasted_iota(jnp.int32, (LANES, LANES), 0) == levels + 1).astype(jnp.float32)
+
     def wet_row(r, carry):
-        spread = jnp.where(lane == levels + 1, s_ref[r, :, 0:LANES], 0.0)
-        shift = 1
-        while shift < LANES:
-            spread = spread + pltpu.roll(spread, shift, 1)
-            shift *= 2
-        wb_ref[r] = spread
+        wb_ref[r] = jnp.dot(s_ref[r, :, 0:LANES], pick, preferred_element_type=jnp.float32)
         return carry
 
     lax.fori_loop(0, ext_rows, wet_row, 0)

time: 105 us -> 95.8 us (0.912)
  Pallas kernels: 37.5 us -> 28.6 us
    pallas_call x1, Pallas kernels: 31.5 us -> 22.6 us  [run_steps(): pl.pallas_call(functools.partial(steps_kernel, levels=levels, width=width...]
  transfers between devices with their start and end apart: 9 -> 9, of which waited for: 3 -> 3; matrix products, arithmetic and copies ran while one was open for 7% -> 8% of each run, Pallas kernels for 6% -> 6%
where the time goes in v9:
time: 95.8 us; the launch traced here: 95.3 us
  starting transfers between devices  42 us (44%)
  Pallas kernels  28.6 us (30%)
  waiting for transfers between devices  13.2 us (14%)
  local copies, waits for them, and re-layouts  6.86 us (7%)
  other arithmetic  3.45 us (4%)
  between operations  1.14 us (1%)
    ppermute x8, starting transfers between devices, shifted(): return lax.ppermute(x, axis, pairs)  40.1 us
    pallas_call x1, Pallas kernels, run_steps(): pl.pallas_call(functools.partial(steps_kernel, levels=levels, width=width...  22.6 us
    ppermute x8, waiting for transfers between devices, shifted(): return lax.ppermute(x, axis, pairs)  13.2 us
    pallas_call x1, Pallas kernels, pack_v(): pl.pallas_call(functools.partial(pack_v_kernel, levels=levels, rows=rows)...  3.38 us
    unnamed x23, local copies, waits for them, and re-layouts  2.7 us
    pallas_call x1, Pallas kernels, pack_q(): pl.pallas_call(functools.partial(pack_q_kernel, levels=levels), out_shape...  2.61 us
    mul x2, other arithmetic, shards(): flux = exchange_rate[0] * sea * (regridded - surface)  2.4 us
    slice x2, local copies, waits for them, and re-layouts, halo_parts(): bot = shifted(x[:w], 'lat', -1, cyclic=False)  2.25 us
  transfers between devices with their start and end apart: 9, of which 3 were waited for; matrix products, arithmetic and copies ran while one was open for 8% of the time, Pallas kernels for 6%

profile of v9, /device:TPU:16, one launch (start us, length us, event | category | flops | bytes accessed | tf_op | source)
XLA Modules:
  0.0 95.3 jit_solution(14639867002190904549)
XLA Ops:
  0.6 1.3 %copy.11 = f32[1,2,60,16,128]{4,3,1,2,0:T(8,128)S(1)} copy(f32[1,2,60,16,128]{4,3,2,1,0:T(8,128)} %param.7) | data formatting | bytes 1966080 | tf_op args[0]
  2.0 1.9 %collective-permute-start = (f32[2,16,128]{2,1,0:T(8,128)S(1)}, f32[2,16,128]{2,1,0:T(8,128)S(1)}, u32[]{:S(2)}, u32[]{:S(2)}) collective-permute-start(f32[2,16,128]{2,1,0:T(8,128)S(1)} %slice_bitcast_fusion), channel_id=1, source_target_pairs={{0,256},{256,0},{1,257},{257,1},{2,258},{258,2},{3,259},{259,3},{4... | collective-permute-start | bytes 49160 | tf_op jit(solution)/shard_map/ppermute | solution.py:228
  3.9 0.0 copy-start.8
  3.9 0.0 copy-start.9
  3.9 0.0 copy-start.10
  3.9 3.4 %shard_map.87.xv_ref = f32[16,128,256]{2,1,0:T(8,128)} custom-call(f32[960,128]{1,0:T(8,128)} %bitcast.329, f32[960,128]{1,0:T(8,128)} %bitcast.330, f32[960,128]{1,0:T(8,128)} %bitcast.331), custom_call_target="tpu_custom_call" | custom-call | tf_op jit(solution)/shard_map/pallas_call | solution.py:198
  7.3 1.2 %fusion.79 = (f32[3,128,256]{2,1,0:T(8,128)S(1)}, f32[3,128,256]{2,1,0:T(8,128)S(1)}) fusion(f32[16,128,256]{2,1,0:T(8,128)} %shard_map.87.xv_ref), kind=kLoop, calls=%fused_computation.419 | loop fusion | bytes 1572864 | tf_op jit(solution)/shard_map/slice | solution.py:208
  8.5 4.4 %collective-permute-start.6 = (f32[3,128,256]{2,1,0:T(8,128)S(1)}, f32[3,128,256]{2,1,0:T(8,128)S(1)}, u32[]{:S(2)}, u32[]{:S(2)}) collective-permute-start(f32[3,128,256]{2,1,0:T(8,128)S(1)} %get-tuple-element.96), channel_id=1, source_target_pairs={{32,0},{64,32},{96,64},{128,96},{160,128},{192,160},{224,192},{33,... | collective-permute-start | bytes 1179656 | tf_op jit(solution)/shard_map/ppermute | solution.py:23
  13.0 1.9 %collective-permute-start.5 = (f32[3,128,256]{2,1,0:T(8,128)S(1)}, f32[3,128,256]{2,1,0:T(8,128)S(1)}, u32[]{:S(2)}, u32[]{:S(2)}) collective-permute-start(f32[3,128,256]{2,1,0:T(8,128)S(1)} %get-tuple-element.97), channel_id=1, source_target_pairs={{0,32},{32,64},{64,96},{96,128},{128,160},{160,192},{192,224},{1,3... | collective-permute-start | bytes 1179656 | tf_op jit(solution)/shard_map/ppermute | solution.py:23
  14.9 1.0 %fusion.78 = (f32[16,8,256]{2,1,0:T(8,128)S(1)}, f32[16,8,256]{2,1,0:T(8,128)S(1)}) fusion(f32[16,128,256]{2,1,0:T(8,128)} %shard_map.87.xv_ref), kind=kLoop, calls=%fused_computation.418 | loop fusion | bytes 524288 | tf_op jit(solution)/shard_map/slice | solution.py:214
  15.9 0.0 copy-done.8
  16.0 0.0 copy-done.9
  16.0 0.0 copy-done.10
  16.0 0.6 multiply_bitcast_fusion
  17.0 0.0 collective-permute-done
  17.0 0.1 fusion.6
  17.1 0.1 fusion.11
  17.2 0.1 fusion.10
  17.3 0.1 fusion.9
  17.4 0.1 fusion.8
  17.6 0.1 fusion.7
  17.7 1.8 %subtract_multiply_fusion.flux_ref = f32[2,16,128]{2,1,0:T(8,128)} fusion(f32[2,16,128]{2,1,0:T(8,128)S(1)} %collective-permute-done, f32[2,2,128]{2,1,0:T(2,128)S(1)} %reshape.27, f32[2,16,3]{2,1,0:T(8,128)S(1)} %get-tuple-element.231, f32[2,16,3]{2,1,0:T(8,128)S(1)} %get-tuple-element.290, f32[2,16,125]{2,1,0:T(8,128)S(1)} %get-tuple-element.286, ...), kind=kLoop, calls=%fused_computation.204 | loop fusion | flops 745472 | bytes 807680 | tf_op jit(solution)/shard_map/mul | solution.py:230
  19.4 2.6 %shard_map.86.xq_ref = f32[16,128,128]{2,1,0:T(8,128)} custom-call(f32[2,960,128]{2,1,0:T(8,128)} %bitcast.325, f32[16,128]{1,0:T(8,128)} %get-tuple-element.319.wet_ref, f32[2,16,128]{2,1,0:T(8,128)} %subtract_multiply_fusion.flux_ref), custom_call_target="tpu_custom_call" | custom-call | tf_op jit(solution)/shard_map/pallas_call | solution.py:188
  22.1 1.1 %fusion.81 = (f32[4,128,128]{2,1,0:T(8,128)S(1)}, f32[4,128,128]{2,1,0:T(8,128)S(1)}) fusion(f32[16,128,128]{2,1,0:T(8,128)} %shard_map.86.xq_ref), kind=kLoop, calls=%fused_computation.421 | loop fusion | bytes 1048576 | tf_op jit(solution)/shard_map/slice | solution.py:208
  23.1 7.5 %collective-permute-start.2 = (f32[4,128,128]{2,1,0:T(8,128)S(1)}, f32[4,128,128]{2,1,0:T(8,128)S(1)}, u32[]{:S(2)}, u32[]{:S(2)}) collective-permute-start(f32[4,128,128]{2,1,0:T(8,128)S(1)} %get-tuple-element.100), channel_id=1, source_target_pairs={{32,0},{64,32},{96,64},{128,96},{160,128},{192,160},{224,192},{33,... | collective-permute-start | bytes 786440 | tf_op jit(solution)/shard_map/ppermute | solution.py:23
  30.7 1.9 %collective-permute-start.1 = (f32[4,128,128]{2,1,0:T(8,128)S(1)}, f32[4,128,128]{2,1,0:T(8,128)S(1)}, u32[]{:S(2)}, u32[]{:S(2)}) collective-permute-start(f32[4,128,128]{2,1,0:T(8,128)S(1)} %get-tuple-element.101), channel_id=1, source_target_pairs={{0,32},{32,64},{64,96},{96,128},{128,160},{160,192},{192,224},{1,3... | collective-permute-start | bytes 786440 | tf_op jit(solution)/shard_map/ppermute | solution.py:23
  32.6 0.9 fusion.80
  33.5 2.8 %collective-permute-done.2 = f32[4,128,128]{2,1,0:T(8,128)S(1)} collective-permute-done((f32[4,128,128]{2,1,0:T(8,128)S(1)}, f32[4,128,128]{2,1,0:T(8,128)S(1)}, u32[]{:S(2)}, u32[]{:S(2)}) %collective-permute-start.2) | collective-permute-done | bytes 262176 | tf_op jit(solution)/shard_map/ppermute | solution.py:23
  36.3 0.0 copy-start
  36.4 7.8 %collective-permute-done.1 = f32[4,128,128]{2,1,0:T(8,128)S(1)} collective-permute-done((f32[4,128,128]{2,1,0:T(8,128)S(1)}, f32[4,128,128]{2,1,0:T(8,128)S(1)}, u32[]{:S(2)}, u32[]{:S(2)}) %collective-permute-start.1) | collective-permute-done | bytes 262176 | tf_op jit(solution)/shard_map/ppermute | solution.py:23
  44.2 0.0 copy-start.1
  44.2 4.0 %collective-permute-start.3 = (f32[24,8,128]{2,1,0:T(8,128)S(1)}, f32[24,8,128]{2,1,0:T(8,128)S(1)}, u32[]{:S(2)}, u32[]{:S(2)}) collective-permute-start(f32[24,8,128]{2,1,0:T(8,128)S(1)} %pad_maximum_fusion.2), channel_id=1, source_target_pairs={{0,1},{1,2},{2,3},{3,4},{4,5},{5,6},{6,7},{7,8},{8,9},{9,10},{10,1... | collective-permute-start | bytes 294920 | tf_op jit(solution)/shard_map/ppermute | solution.py:23
  48.2 0.0 collective-permute-done.6.botv_ref
  48.2 0.0 copy-start.2
  48.3 0.0 collective-permute-done.5.topv_ref
  48.3 0.0 copy-start.3
  48.3 3.2 %collective-permute-start.7 = (f32[22,8,256]{2,1,0:T(8,128)S(1)}, f32[22,8,256]{2,1,0:T(8,128)S(1)}, u32[]{:S(2)}, u32[]{:S(2)}) collective-permute-start(f32[22,8,256]{2,1,0:T(8,128)S(1)} %pad_maximum_fusion), channel_id=1, source_target_pairs={{0,1},{1,2},{2,3},{3,4},{4,5},{5,6},{6,7},{7,8},{8,9},{9,10},{10,1... | collective-permute-start | bytes 540680 | tf_op jit(solution)/shard_map/ppermute | solution.py:23
  51.6 13.2 %collective-permute-start.8 = (f32[22,8,256]{2,1,0:T(8,128)S(1)}, f32[22,8,256]{2,1,0:T(8,128)S(1)}, u32[]{:S(2)}, u32[]{:S(2)}) collective-permute-start(f32[22,8,256]{2,1,0:T(8,128)S(1)} %pad_maximum_fusion.1), channel_id=1, source_target_pairs={{0,31},{1,0},{2,1},{3,2},{4,3},{5,4},{6,5},{7,6},{8,7},{9,8},{10,9... | collective-permute-start | bytes 540680 | tf_op jit(solution)/shard_map/ppermute | solution.py:23
  64.8 3.9 %collective-permute-start.4 = (f32[24,8,128]{2,1,0:T(8,128)S(1)}, f32[24,8,128]{2,1,0:T(8,128)S(1)}, u32[]{:S(2)}, u32[]{:S(2)}) collective-permute-start(f32[24,8,128]{2,1,0:T(8,128)S(1)} %pad_maximum_fusion.3), channel_id=1, source_target_pairs={{0,31},{1,0},{2,1},{3,2},{4,3},{5,4},{6,5},{7,6},{8,7},{9,8},{10,9... | collective-permute-start | bytes 294920 | tf_op jit(solution)/shard_map/ppermute | solution.py:23
  68.7 0.0 collective-permute-done.3.leftq_ref
  68.7 0.0 copy-start.6
  68.7 2.6 %collective-permute-done.4.rightq_ref = f32[24,8,128]{2,1,0:T(8,128)S(1)} collective-permute-done((f32[24,8,128]{2,1,0:T(8,128)S(1)}, f32[24,8,128]{2,1,0:T(8,128)S(1)}, u32[]{:S(2)}, u32[]{:S(2)}) %collective-permute-start.4) | collective-permute-done | bytes 98336 | tf_op jit(solution)/shard_map/ppermute | solution.py:23
  71.3 0.0 collective-permute-done.7.leftv_ref
  71.3 0.0 collective-permute-done.8.rightv_ref
  71.3 0.6 copy-done.7
  71.9 0.1 copy-done.4
  72.0 0.7 copy-done.5
  72.7 22.6 %shard_map.88 = f32[2,960,128]{2,1,0:T(8,128)} custom-call(f32[16,128,128]{2,1,0:T(8,128)} %shard_map.86.xq_ref, f32[4,128,128]{2,1,0:T(8,128)} %copy-done.1, f32[4,128,128]{2,1,0:T(8,128)} %copy-done, f32[24,8,128]{2,1,0:T(8,128)} %copy-done.6, f32[24,8,128]{2,1,0:T(8,128)} %copy-done.7, f32[16,128,256]{2,1,0:T(8,128)} %shard_map.87.xv_ref, ...), custom_call_target="tpu_custom_call" | custom-call | tf_op jit(solution)/shard_map/pallas_call | solution.py:150
  (33 shorter events, 0.5 us)
Async XLA Ops:
  2.0 15.0 %collective-permute-start = (f32[2,16,128]{2,1,0:T(8,128)S(1)}, f32[2,16,128]{2,1,0:T(8,128)S(1)}, u32[]{:S(2)}, u32[]{:S(2)}) collective-permute-start(f32[2,16,128]{2,1,0:T(8,128)S(1)} %slice_bitcast_fusion), channel_id=1, source_target_pairs={{0,256},{256,0},{1,257},{257,1},{2,258},{258,2},{3,259},{259,3},{4... | collective-permute-start | bytes 49160 | tf_op jit(solution)/shard_map/ppermute | solution.py:228
  3.9 12.0 %copy-start.8 = (s32[1,4,16,128]{3,2,1,0:T(8,128)S(1)}, s32[1,4,16,128]{3,2,1,0:T(8,128)}, u32[]{:S(2)}) copy-start(s32[1,4,16,128]{3,2,1,0:T(8,128)} %param.13) | copy-start | bytes 98308
  3.9 12.1 %copy-start.9 = (f32[1,16,128]{2,1,0:T(8,128)S(1)}, f32[1,16,128]{2,1,0:T(8,128)}, u32[]{:S(2)}) copy-start(f32[1,16,128]{2,1,0:T(8,128)} %param.11) | copy-start | bytes 24580
  3.9 12.1 %copy-start.10 = (s32[1,16,128]{2,1,0:T(8,128)S(1)}, s32[1,16,128]{2,1,0:T(8,128)}, u32[]{:S(2)}) copy-start(s32[1,16,128]{2,1,0:T(8,128)} %param.12) | copy-start | bytes 24580
  8.5 39.7 %collective-permute-start.6 = (f32[3,128,256]{2,1,0:T(8,128)S(1)}, f32[3,128,256]{2,1,0:T(8,128)S(1)}, u32[]{:S(2)}, u32[]{:S(2)}) collective-permute-start(f32[3,128,256]{2,1,0:T(8,128)S(1)} %get-tuple-element.96), channel_id=1, source_target_pairs={{32,0},{64,32},{96,64},{128,96},{160,128},{192,160},{224,192},{33,... | collective-permute-start | bytes 1179656 | tf_op jit(solution)/shard_map/ppermute | solution.py:23
  13.0 35.3 %collective-permute-start.5 = (f32[3,128,256]{2,1,0:T(8,128)S(1)}, f32[3,128,256]{2,1,0:T(8,128)S(1)}, u32[]{:S(2)}, u32[]{:S(2)}) collective-permute-start(f32[3,128,256]{2,1,0:T(8,128)S(1)} %get-tuple-element.97), channel_id=1, source_target_pairs={{0,32},{32,64},{64,96},{96,128},{128,160},{160,192},{192,224},{1,3... | collective-permute-start | bytes 1179656 | tf_op jit(solution)/shard_map/ppermute | solution.py:23
  23.1 13.2 %collective-permute-start.2 = (f32[4,128,128]{2,1,0:T(8,128)S(1)}, f32[4,128,128]{2,1,0:T(8,128)S(1)}, u32[]{:S(2)}, u32[]{:S(2)}) collective-permute-start(f32[4,128,128]{2,1,0:T(8,128)S(1)} %get-tuple-element.100), channel_id=1, source_target_pairs={{32,0},{64,32},{96,64},{128,96},{160,128},{192,160},{224,192},{33,... | collective-permute-start | bytes 786440 | tf_op jit(solution)/shard_map/ppermute | solution.py:23
  30.7 13.5 %collective-permute-start.1 = (f32[4,128,128]{2,1,0:T(8,128)S(1)}, f32[4,128,128]{2,1,0:T(8,128)S(1)}, u32[]{:S(2)}, u32[]{:S(2)}) collective-permute-start(f32[4,128,128]{2,1,0:T(8,128)S(1)} %get-tuple-element.101), channel_id=1, source_target_pairs={{0,32},{32,64},{64,96},{96,128},{128,160},{160,192},{192,224},{1,3... | collective-permute-start | bytes 786440 | tf_op jit(solution)/shard_map/ppermute | solution.py:23
  36.3 35.0 %copy-start = (f32[4,128,128]{2,1,0:T(8,128)}, f32[4,128,128]{2,1,0:T(8,128)S(1)}, u32[]{:S(2)}) copy-start(f32[4,128,128]{2,1,0:T(8,128)S(1)} %broadcast_select_fusion.botq_ref) | copy-start | bytes 786436
  44.2 27.1 %copy-start.1 = (f32[4,128,128]{2,1,0:T(8,128)}, f32[4,128,128]{2,1,0:T(8,128)S(1)}, u32[]{:S(2)}) copy-start(f32[4,128,128]{2,1,0:T(8,128)S(1)} %broadcast_select_fusion.1.topq_ref) | copy-start | bytes 786436
  44.2 24.5 %collective-permute-start.3 = (f32[24,8,128]{2,1,0:T(8,128)S(1)}, f32[24,8,128]{2,1,0:T(8,128)S(1)}, u32[]{:S(2)}, u32[]{:S(2)}) collective-permute-start(f32[24,8,128]{2,1,0:T(8,128)S(1)} %pad_maximum_fusion.2), channel_id=1, source_target_pairs={{0,1},{1,2},{2,3},{3,4},{4,5},{5,6},{6,7},{7,8},{8,9},{9,10},{10,1... | collective-permute-start | bytes 294920 | tf_op jit(solution)/shard_map/ppermute | solution.py:23
  48.2 23.1 %copy-start.2 = (f32[3,128,256]{2,1,0:T(8,128)}, f32[3,128,256]{2,1,0:T(8,128)S(1)}, u32[]{:S(2)}) copy-start(f32[3,128,256]{2,1,0:T(8,128)S(1)} %collective-permute-done.6.botv_ref) | copy-start | bytes 1179652
  48.3 23.1 %copy-start.3 = (f32[3,128,256]{2,1,0:T(8,128)}, f32[3,128,256]{2,1,0:T(8,128)S(1)}, u32[]{:S(2)}) copy-start(f32[3,128,256]{2,1,0:T(8,128)S(1)} %collective-permute-done.5.topv_ref) | copy-start | bytes 1179652
  48.3 23.0 %collective-permute-start.7 = (f32[22,8,256]{2,1,0:T(8,128)S(1)}, f32[22,8,256]{2,1,0:T(8,128)S(1)}, u32[]{:S(2)}, u32[]{:S(2)}) collective-permute-start(f32[22,8,256]{2,1,0:T(8,128)S(1)} %pad_maximum_fusion), channel_id=1, source_target_pairs={{0,1},{1,2},{2,3},{3,4},{4,5},{5,6},{6,7},{7,8},{8,9},{9,10},{10,1... | collective-permute-start | bytes 540680 | tf_op jit(solution)/shard_map/ppermute | solution.py:23
  51.6 19.7 %collective-permute-start.8 = (f32[22,8,256]{2,1,0:T(8,128)S(1)}, f32[22,8,256]{2,1,0:T(8,128)S(1)}, u32[]{:S(2)}, u32[]{:S(2)}) collective-permute-start(f32[22,8,256]{2,1,0:T(8,128)S(1)} %pad_maximum_fusion.1), channel_id=1, source_target_pairs={{0,31},{1,0},{2,1},{3,2},{4,3},{5,4},{6,5},{7,6},{8,7},{9,8},{10,9... | collective-permute-start | bytes 540680 | tf_op jit(solution)/shard_map/ppermute | solution.py:23
  64.8 6.5 %collective-permute-start.4 = (f32[24,8,128]{2,1,0:T(8,128)S(1)}, f32[24,8,128]{2,1,0:T(8,128)S(1)}, u32[]{:S(2)}, u32[]{:S(2)}) collective-permute-start(f32[24,8,128]{2,1,0:T(8,128)S(1)} %pad_maximum_fusion.3), channel_id=1, source_target_pairs={{0,31},{1,0},{2,1},{3,2},{4,3},{5,4},{6,5},{7,6},{8,7},{9,8},{10,9... | collective-permute-start | bytes 294920 | tf_op jit(solution)/shard_map/ppermute | solution.py:23
  68.7 2.6 %copy-start.6 = (f32[24,8,128]{2,1,0:T(8,128)}, f32[24,8,128]{2,1,0:T(8,128)S(1)}, u32[]{:S(2)}) copy-start(f32[24,8,128]{2,1,0:T(8,128)S(1)} %collective-permute-done.3.leftq_ref) | copy-start | bytes 294916
  71.3 0.7 copy-start.7
  71.3 0.7 copy-start.4
  72.0 0.7 copy-start.5

commit v10 on v7

--- a/solution.py
+++ b/solution.py
@@ -208,14 +208,18 @@
     x = pack(tracers, zonal[0], meridional[0], mixing[0], wet, flux)
 
     width = SUB
-    top = shifted(x[-width:], "lat", 1, cyclic=False)
-    bot = shifted(x[:width], "lat", -1, cyclic=False)
     row_block = lax.axis_index("lat")
     wet_lane = lax.broadcasted_iota(jnp.int32, (1, 1, 3 * LANES), 2) >= 2 * LANES + HALF
-    top = jnp.where(jnp.logical_and(wet_lane, row_block == 0), 0.0, top)
-    bot = jnp.where(jnp.logical_and(wet_lane, row_block == lax.axis_size("lat") - 1), 0.0, bot)
-    left = shifted(jnp.concatenate([top[:, -COL_PAD:], x[:, -COL_PAD:], bot[:, -COL_PAD:]], axis=0), "lon", 1)
-    right = shifted(jnp.concatenate([top[:, :COL_PAD], x[:, :COL_PAD], bot[:, :COL_PAD]], axis=0), "lon", -1)
+    top_mask = jnp.logical_and(wet_lane, row_block == 0)
+    bot_mask = jnp.logical_and(wet_lane, row_block == lax.axis_size("lat") - 1)
+    top = jnp.where(top_mask, 0.0, shifted(x[-width:], "lat", 1, cyclic=False))
+    bot = jnp.where(bot_mask, 0.0, shifted(x[:width], "lat", -1, cyclic=False))
+    left = shifted(x[:, -COL_PAD:], "lon", 1)
+    right = shifted(x[:, :COL_PAD], "lon", -1)
+    upper = jnp.where(top_mask, 0.0, shifted(jnp.concatenate([left[-width:], right[-width:]], axis=1), "lat", 1, cyclic=False))
+    lower = jnp.where(bot_mask, 0.0, shifted(jnp.concatenate([left[:width], right[:width]], axis=1), "lat", -1, cyclic=False))
+    left = jnp.concatenate([upper[:, :COL_PAD], left, lower[:, :COL_PAD]], axis=0)
+    right = jnp.concatenate([upper[:, COL_PAD:], right, lower[:, COL_PAD:]], axis=0)
 
     out = run_steps(x, top, bot, left, right, levels, width)
     q = out.reshape(fields, levels, rows, cols)

time: 88.2 us -> 85.9 us (0.974)
  waiting for transfers between devices: 27 us -> 15.5 us
  starting transfers between devices: 25.5 us -> 32.1 us
  other arithmetic: 5.01 us -> 8.27 us
    ppermute x4 -> x6, waiting for transfers between devices: 27 us -> 15.5 us  [shifted(): return lax.ppermute(x, axis, pairs)]
    ppermute x4 -> x6, starting transfers between devices: 23.6 us -> 30.2 us  [shifted(): return lax.ppermute(x, axis, pairs)]
    select_n x2 -> x4, other arithmetic: 0.11 us -> 1.91 us  [the longest x1 0.95 us: shards(): bot = jnp.where(bot_mask, 0.0, shifted(x[:width], 'lat', -1, cyclic=False))]
    concatenate x2 -> x4, other arithmetic: 0.04 us -> 1.52 us  [the longest x1 0.76 us: shards(): jnp.concatenate([upper[:, COL_PAD:], right, lower[:, COL_PAD:]], axis=0)]
    unnamed x9 -> x1, local copies, waits for them, and re-layouts: 2.07 us -> 1.33 us
    slice x4 -> x6, local copies, waits for them, and re-layouts: 2.55 us -> 2.57 us  [the longest x1 1.49 us: shards(): bot = jnp.where(bot_mask, 0.0, shifted(x[:width], 'lat', -1, cyclic=False))]
  transfers between devices with their start and end apart: 5 -> 7, of which waited for: 4 -> 2; matrix products, arithmetic and copies ran while one was open for 4% -> 8% of each run, Pallas kernels for 0% -> 0%
where the time goes in v10:
time: 85.9 us; the launch traced here: 85.4 us
  starting transfers between devices  32.1 us (37%)
  Pallas kernels  24.7 us (29%)
  waiting for transfers between devices  15.5 us (18%)
  other arithmetic  8.27 us (10%)
  local copies, waits for them, and re-layouts  3.91 us (5%)
  between operations  0.94 us (1%)
    ppermute x6, starting transfers between devices, shifted(): return lax.ppermute(x, axis, pairs)  30.2 us
    pallas_call x1, Pallas kernels, run_steps(): pl.pallas_call(functools.partial(steps_kernel, levels=levels, width=width...  20.4 us
    ppermute x6, waiting for transfers between devices, shifted(): return lax.ppermute(x, axis, pairs)  15.5 us
    pallas_call x1, Pallas kernels, pack(): pl.pallas_call(functools.partial(pack_kernel, levels=levels), out_shape=j...  4.26 us
    mul x2, other arithmetic, shards(): flux = exchange_rate[0] * sea * (regridded - surface)  3.12 us
    ppermute x1, starting transfers between devices, shards(): partner = lax.ppermute(surface, 'sec', [(0, 1), (1, 0)])  1.92 us
  transfers between devices with their start and end apart: 7, of which 2 were waited for; matrix products, arithmetic and copies ran while one was open for 8% of the time, Pallas kernels for 0%

profile of v10, /device:TPU:16, one launch (start us, length us, event | category | flops | bytes accessed | tf_op | source)
XLA Modules:
  0.0 85.4 jit_solution(15621074983079526360)
XLA Ops:
  0.6 1.3 %copy.11 = f32[1,2,60,16,128]{4,3,1,2,0:T(8,128)S(1)} copy(f32[1,2,60,16,128]{4,3,2,1,0:T(8,128)} %param.7) | data formatting | bytes 1966080 | tf_op args[0]
  2.0 1.9 %collective-permute-start = (f32[2,16,128]{2,1,0:T(8,128)S(1)}, f32[2,16,128]{2,1,0:T(8,128)S(1)}, u32[]{:S(2)}, u32[]{:S(2)}) collective-permute-start(f32[2,16,128]{2,1,0:T(8,128)S(1)} %slice_bitcast_fusion), channel_id=1, source_target_pairs={{0,256},{256,0},{1,257},{257,1},{2,258},{258,2},{3,259},{259,3},{4... | collective-permute-start | bytes 49160 | tf_op jit(solution)/shard_map/ppermute | solution.py:203
  3.9 0.8 compare_select_fusion
  4.8 1.3 %multiply_bitcast_fusion = (f32[16,128]{1,0:T(8,128)S(1)}, f32[16,128]{1,0:T(8,128)}) fusion(f32[1,16,128]{2,1,0:T(8,128)} %param.11, s32[1,16,128]{2,1,0:T(8,128)} %param.12, pred[]{:T(512)S(6)} %eq.667), kind=kLoop, calls=%fused_computation.228 | loop fusion | flops 6144 | bytes 32769 | tf_op jit(solution)/shard_map/mul | solution.py:206
  6.4 0.0 collective-permute-done
  6.5 0.1 fusion.6
  6.6 0.1 fusion.11
  6.7 0.1 fusion.10
  6.8 0.1 fusion.9
  6.9 0.1 fusion.8
  7.0 0.1 fusion.7
  7.1 1.8 %subtract_multiply_fusion.flux_ref = f32[2,16,128]{2,1,0:T(8,128)} fusion(f32[2,16,128]{2,1,0:T(8,128)S(1)} %collective-permute-done, f32[2,2,128]{2,1,0:T(2,128)S(1)} %reshape.27, f32[2,16,3]{2,1,0:T(8,128)S(1)} %get-tuple-element.227, f32[2,16,3]{2,1,0:T(8,128)S(1)} %get-tuple-element.286, f32[2,16,125]{2,1,0:T(8,128)S(1)} %get-tuple-element.282, ...), kind=kLoop, calls=%fused_computation.206 | loop fusion | flops 745472 | bytes 807680 | tf_op jit(solution)/shard_map/mul | solution.py:206
  8.9 4.3 %shard_map.86.x_ref = f32[16,128,384]{2,1,0:T(8,128)} custom-call(f32[2,960,128]{2,1,0:T(8,128)} %bitcast.325, f32[960,128]{1,0:T(8,128)} %bitcast.329, f32[960,128]{1,0:T(8,128)} %bitcast.330, f32[960,128]{1,0:T(8,128)} %bitcast.331, f32[16,128]{1,0:T(8,128)} %get-tuple-element.315.wet_ref, f32[2,16,128]{2,1,0:T(8,128)} %subtract_multiply_fusion.flux_ref), custom_call_target="tpu_custom_call" | custom-call | tf_op jit(solution)/shard_map/pallas_call | solution.py:177
  13.2 1.0 %fusion.80 = (f32[16,8,384]{2,1,0:T(8,128)S(1)}, f32[16,8,384]{2,1,0:T(8,128)S(1)}) fusion(f32[16,128,384]{2,1,0:T(8,128)} %shard_map.86.x_ref), kind=kLoop, calls=%fused_computation.421 | loop fusion | bytes 786432 | tf_op jit(solution)/shard_map/slice | solution.py:217
  14.2 3.2 %collective-permute-start.3 = (f32[16,8,384]{2,1,0:T(8,128)S(1)}, f32[16,8,384]{2,1,0:T(8,128)S(1)}, u32[]{:S(2)}, u32[]{:S(2)}) collective-permute-start(f32[16,8,384]{2,1,0:T(8,128)S(1)} %get-tuple-element.94), channel_id=1, source_target_pairs={{0,1},{1,2},{2,3},{3,4},{4,5},{5,6},{6,7},{7,8},{8,9},{9,10},{10,1... | collective-permute-start | bytes 589832 | tf_op jit(solution)/shard_map/ppermute | solution.py:23
  17.4 10.9 %collective-permute-start.4 = (f32[16,8,384]{2,1,0:T(8,128)S(1)}, f32[16,8,384]{2,1,0:T(8,128)S(1)}, u32[]{:S(2)}, u32[]{:S(2)}) collective-permute-start(f32[16,8,384]{2,1,0:T(8,128)S(1)} %get-tuple-element.95), channel_id=1, source_target_pairs={{0,31},{1,0},{2,1},{3,2},{4,3},{5,4},{6,5},{7,6},{8,7},{9,8},{10,9... | collective-permute-start | bytes 589832 | tf_op jit(solution)/shard_map/ppermute | solution.py:23
  28.3 1.5 %fusion.81 = (f32[4,128,384]{2,1,0:T(8,128)S(1)}, f32[4,128,384]{2,1,0:T(8,128)S(1)}) fusion(f32[16,128,384]{2,1,0:T(8,128)} %shard_map.86.x_ref), kind=kLoop, calls=%fused_computation.422 | loop fusion | bytes 3145728 | tf_op jit(solution)/shard_map/slice | solution.py:216
  29.8 4.7 %collective-permute-start.2 = (f32[4,128,384]{2,1,0:T(8,128)S(1)}, f32[4,128,384]{2,1,0:T(8,128)S(1)}, u32[]{:S(2)}, u32[]{:S(2)}) collective-permute-start(f32[4,128,384]{2,1,0:T(8,128)S(1)} %get-tuple-element.96), channel_id=1, source_target_pairs={{32,0},{64,32},{96,64},{128,96},{160,128},{192,160},{224,192},{33,... | collective-permute-start | bytes 2359304 | tf_op jit(solution)/shard_map/ppermute | solution.py:23
  34.5 1.9 %collective-permute-start.1 = (f32[4,128,384]{2,1,0:T(8,128)S(1)}, f32[4,128,384]{2,1,0:T(8,128)S(1)}, u32[]{:S(2)}, u32[]{:S(2)}) collective-permute-start(f32[4,128,384]{2,1,0:T(8,128)S(1)} %get-tuple-element.97), channel_id=1, source_target_pairs={{0,32},{32,64},{64,96},{96,128},{128,160},{160,192},{192,224},{1,3... | collective-permute-start | bytes 2359304 | tf_op jit(solution)/shard_map/ppermute | solution.py:23
  36.5 0.0 collective-permute-done.3
  36.5 0.0 collective-permute-done.4
  36.5 7.5 %collective-permute-start.6 = (f32[4,16,384]{2,1,0:T(8,128)S(1)}, f32[4,16,384]{2,1,0:T(8,128)S(1)}, u32[]{:S(2)}, u32[]{:S(2)}) collective-permute-start(f32[4,16,384]{2,1,0:T(8,128)S(1)} %pad_maximum_fusion.3), channel_id=1, source_target_pairs={{32,0},{64,32},{96,64},{128,96},{160,128},{192,160},{224,192},{33,... | collective-permute-start | bytes 294920 | tf_op jit(solution)/shard_map/ppermute | solution.py:23
  44.1 1.9 %collective-permute-start.5 = (f32[4,16,384]{2,1,0:T(8,128)S(1)}, f32[4,16,384]{2,1,0:T(8,128)S(1)}, u32[]{:S(2)}, u32[]{:S(2)}) collective-permute-start(f32[4,16,384]{2,1,0:T(8,128)S(1)} %pad_maximum_fusion.2), channel_id=1, source_target_pairs={{0,32},{32,64},{64,96},{96,128},{128,160},{160,192},{192,224},{1,3... | collective-permute-start | bytes 294920 | tf_op jit(solution)/shard_map/ppermute | solution.py:23
  46.0 7.8 %collective-permute-done.6 = f32[4,16,384]{2,1,0:T(8,128)S(1)} collective-permute-done((f32[4,16,384]{2,1,0:T(8,128)S(1)}, f32[4,16,384]{2,1,0:T(8,128)S(1)}, u32[]{:S(2)}, u32[]{:S(2)}) %collective-permute-start.6) | collective-permute-done | bytes 98336 | tf_op jit(solution)/shard_map/ppermute | solution.py:23
  53.8 7.7 %collective-permute-done.5 = f32[4,16,384]{2,1,0:T(8,128)S(1)} collective-permute-done((f32[4,16,384]{2,1,0:T(8,128)S(1)}, f32[4,16,384]{2,1,0:T(8,128)S(1)}, u32[]{:S(2)}, u32[]{:S(2)}) %collective-permute-start.5) | collective-permute-done | bytes 98336 | tf_op jit(solution)/shard_map/ppermute | solution.py:23
  61.6 0.8 pad_maximum_fusion.1.right_ref
  62.3 0.7 pad_maximum_fusion.left_ref
  63.1 0.0 collective-permute-done.2
  63.1 0.9 %broadcast_select_fusion.bot_ref = f32[4,128,384]{2,1,0:T(8,128)} fusion(f32[4,128,384]{2,1,0:T(8,128)S(1)} %collective-permute-done.2, pred[384]{0:T(512)(128)(4,1)S(1)} %fusion.78), kind=kLoop, calls=%fused_computation.1 | loop fusion | flops 196608 | bytes 1573248 | tf_op jit(solution)/shard_map/jit(_where)/select_n | solution.py:216
  64.0 0.0 collective-permute-done.1
  64.0 0.9 %broadcast_select_fusion.1.top_ref = f32[4,128,384]{2,1,0:T(8,128)} fusion(f32[4,128,384]{2,1,0:T(8,128)S(1)} %collective-permute-done.1, pred[384]{0:T(512)(128)(4,1)S(1)} %fusion.79), kind=kLoop, calls=%fused_computation.2 | loop fusion | flops 196608 | bytes 1573248 | tf_op jit(solution)/shard_map/jit(_where)/select_n | solution.py:215
  65.0 20.4 %shard_map.87 = f32[2,960,128]{2,1,0:T(8,128)} custom-call(f32[16,128,384]{2,1,0:T(8,128)} %shard_map.86.x_ref, f32[4,128,384]{2,1,0:T(8,128)} %broadcast_select_fusion.1.top_ref, f32[4,128,384]{2,1,0:T(8,128)} %broadcast_select_fusion.bot_ref, f32[24,8,384]{2,1,0:T(8,128)} %pad_maximum_fusion.left_ref, f32[24,8,384]{2,1,0:T(8,128)} %pad_maximum_fusion.1.right_ref), custom_call_target="tpu_custom_call" | custom-call | tf_op jit(solution)/shard_map/pallas_call | solution.py:138
  (22 shorter events, 0.4 us)
Async XLA Ops:
  2.0 4.5 %collective-permute-start = (f32[2,16,128]{2,1,0:T(8,128)S(1)}, f32[2,16,128]{2,1,0:T(8,128)S(1)}, u32[]{:S(2)}, u32[]{:S(2)}) collective-permute-start(f32[2,16,128]{2,1,0:T(8,128)S(1)} %slice_bitcast_fusion), channel_id=1, source_target_pairs={{0,256},{256,0},{1,257},{257,1},{2,258},{258,2},{3,259},{259,3},{4... | collective-permute-start | bytes 49160 | tf_op jit(solution)/shard_map/ppermute | solution.py:203
  14.2 22.2 %collective-permute-start.3 = (f32[16,8,384]{2,1,0:T(8,128)S(1)}, f32[16,8,384]{2,1,0:T(8,128)S(1)}, u32[]{:S(2)}, u32[]{:S(2)}) collective-permute-start(f32[16,8,384]{2,1,0:T(8,128)S(1)} %get-tuple-element.94), channel_id=1, source_target_pairs={{0,1},{1,2},{2,3},{3,4},{4,5},{5,6},{6,7},{7,8},{8,9},{9,10},{10,1... | collective-permute-start | bytes 589832 | tf_op jit(solution)/shard_map/ppermute | solution.py:23
  17.4 19.1 %collective-permute-start.4 = (f32[16,8,384]{2,1,0:T(8,128)S(1)}, f32[16,8,384]{2,1,0:T(8,128)S(1)}, u32[]{:S(2)}, u32[]{:S(2)}) collective-permute-start(f32[16,8,384]{2,1,0:T(8,128)S(1)} %get-tuple-element.95), channel_id=1, source_target_pairs={{0,31},{1,0},{2,1},{3,2},{4,3},{5,4},{6,5},{7,6},{8,7},{9,8},{10,9... | collective-permute-start | bytes 589832 | tf_op jit(solution)/shard_map/ppermute | solution.py:23
  29.8 33.3 %collective-permute-start.2 = (f32[4,128,384]{2,1,0:T(8,128)S(1)}, f32[4,128,384]{2,1,0:T(8,128)S(1)}, u32[]{:S(2)}, u32[]{:S(2)}) collective-permute-start(f32[4,128,384]{2,1,0:T(8,128)S(1)} %get-tuple-element.96), channel_id=1, source_target_pairs={{32,0},{64,32},{96,64},{128,96},{160,128},{192,160},{224,192},{33,... | collective-permute-start | bytes 2359304 | tf_op jit(solution)/shard_map/ppermute | solution.py:23
  34.5 29.5 %collective-permute-start.1 = (f32[4,128,384]{2,1,0:T(8,128)S(1)}, f32[4,128,384]{2,1,0:T(8,128)S(1)}, u32[]{:S(2)}, u32[]{:S(2)}) collective-permute-start(f32[4,128,384]{2,1,0:T(8,128)S(1)} %get-tuple-element.97), channel_id=1, source_target_pairs={{0,32},{32,64},{64,96},{96,128},{128,160},{160,192},{192,224},{1,3... | collective-permute-start | bytes 2359304 | tf_op jit(solution)/shard_map/ppermute | solution.py:23
  36.5 17.3 %collective-permute-start.6 = (f32[4,16,384]{2,1,0:T(8,128)S(1)}, f32[4,16,384]{2,1,0:T(8,128)S(1)}, u32[]{:S(2)}, u32[]{:S(2)}) collective-permute-start(f32[4,16,384]{2,1,0:T(8,128)S(1)} %pad_maximum_fusion.3), channel_id=1, source_target_pairs={{32,0},{64,32},{96,64},{128,96},{160,128},{192,160},{224,192},{33,... | collective-permute-start | bytes 294920 | tf_op jit(solution)/shard_map/ppermute | solution.py:23
  44.1 17.4 %collective-permute-start.5 = (f32[4,16,384]{2,1,0:T(8,128)S(1)}, f32[4,16,384]{2,1,0:T(8,128)S(1)}, u32[]{:S(2)}, u32[]{:S(2)}) collective-permute-start(f32[4,16,384]{2,1,0:T(8,128)S(1)} %pad_maximum_fusion.2), channel_id=1, source_target_pairs={{0,32},{32,64},{64,96},{96,128},{128,160},{160,192},{192,224},{1,3... | collective-permute-start | bytes 294920 | tf_op jit(solution)/shard_map/ppermute | solution.py:23

commit v11 on v10

--- a/solution.py
+++ b/solution.py
@@ -144,7 +144,8 @@
     )(x, top, bot, left, right)
 
 
-def pack_kernel(st_ref, zon_ref, mer_ref, mix_ref, wet_ref, flux_ref, o_ref, t0_ref, t1_ref, t2_ref, *, levels):
+def pack_kernel(st_ref, zon_ref, mer_ref, mix_ref, wet_ref, flux_ref, o_ref, last_ref, first_ref, east_ref, west_ref,
+                t0_ref, t1_ref, t2_ref, *, levels, width):
     rows = wet_ref.shape[0]
     for t_ref in (t0_ref, t1_ref, t2_ref):
         t_ref[...] = jnp.zeros(t_ref.shape, jnp.float32)
@@ -163,20 +164,33 @@
         t0 = t0_ref[...]
         t0 = jnp.where(sub == levels, f0, t0)
         t0 = jnp.where(sub == HALF + levels, f1, t0)
-        o_ref[r, :, 0:LANES] = jnp.transpose(t0)
-        o_ref[r, :, LANES : 2 * LANES] = jnp.transpose(t1_ref[...])
-        o_ref[r, :, 2 * LANES : 3 * LANES] = jnp.transpose(t2_ref[...])
+        for b, tile in enumerate((t0, t1_ref[...], t2_ref[...])):
+            lanes = slice(b * LANES, (b + 1) * LANES)
+            cell = jnp.transpose(tile)
+            o_ref[r, :, lanes] = cell
+            if r >= rows - width:
+                last_ref[r - (rows - width), :, lanes] = cell
+            if r < width:
+                first_ref[r, :, lanes] = cell
+            east_ref[r, :, lanes] = cell[-COL_PAD:]
+            west_ref[r, :, lanes] = cell[:COL_PAD]
         return carry
 
     for r in range(rows):
         body(r, 0)
 
 
-def pack(tracers, zonal, meridional, mixing, wet, flux):
+def pack(tracers, zonal, meridional, mixing, wet, flux, width):
     fields, levels, rows, cols = tracers.shape
     return pl.pallas_call(
-        functools.partial(pack_kernel, levels=levels),
-        out_shape=jax.ShapeDtypeStruct((rows, cols, 3 * LANES), jnp.float32),
+        functools.partial(pack_kernel, levels=levels, width=width),
+        out_shape=(
+            jax.ShapeDtypeStruct((rows, cols, 3 * LANES), jnp.float32),
+            jax.ShapeDtypeStruct((width, cols, 3 * LANES), jnp.float32),
+            jax.ShapeDtypeStruct((width, cols, 3 * LANES), jnp.float32),
+            jax.ShapeDtypeStruct((rows, COL_PAD, 3 * LANES), jnp.float32),
+            jax.ShapeDtypeStruct((rows, COL_PAD, 3 * LANES), jnp.float32),
+        ),
         scratch_shapes=[pltpu.VMEM((LANES, LANES), jnp.float32) for _ in range(3)],
         interpret=INTERPRET,
     )(
@@ -205,17 +219,17 @@
     regridded = regrid(partner, regrid_map[0])
     flux = exchange_rate[0] * sea * (regridded - surface)
 
-    x = pack(tracers, zonal[0], meridional[0], mixing[0], wet, flux)
-
     width = SUB
+    x, last, first, east, west = pack(tracers, zonal[0], meridional[0], mixing[0], wet, flux, width)
+
     row_block = lax.axis_index("lat")
     wet_lane = lax.broadcasted_iota(jnp.int32, (1, 1, 3 * LANES), 2) >= 2 * LANES + HALF
     top_mask = jnp.logical_and(wet_lane, row_block == 0)
     bot_mask = jnp.logical_and(wet_lane, row_block == lax.axis_size("lat") - 1)
-    top = jnp.where(top_mask, 0.0, shifted(x[-width:], "lat", 1, cyclic=False))
-    bot = jnp.where(bot_mask, 0.0, shifted(x[:width], "lat", -1, cyclic=False))
-    left = shifted(x[:, -COL_PAD:], "lon", 1)
-    right = shifted(x[:, :COL_PAD], "lon", -1)
+    top = jnp.where(top_mask, 0.0, shifted(last, "lat", 1, cyclic=False))
+    bot = jnp.where(bot_mask, 0.0, shifted(first, "lat", -1, cyclic=False))
+    left = shifted(east, "lon", 1)
+    right = shifted(west, "lon", -1)
     upper = jnp.where(top_mask, 0.0, shifted(jnp.concatenate([left[-width:], right[-width:]], axis=1), "lat", 1, cyclic=False))
     lower = jnp.where(bot_mask, 0.0, shifted(jnp.concatenate([left[:width], right[:width]], axis=1), "lat", -1, cyclic=False))
     left = jnp.concatenate([upper[:, :COL_PAD], left, lower[:, :COL_PAD]], axis=0)

time: 85.9 us -> 87 us (1.013)
  the two profiles are of different devices: /device:TPU:16 before, /device:TPU:2 now
where the time goes in v11:
time: 87 us; the launch traced here: 86.6 us
  starting transfers between devices  46.1 us (53%)
  Pallas kernels  25.4 us (29%)
  other arithmetic  8.27 us (10%)
  waiting for transfers between devices  4.58 us (5%)
  local copies, waits for them, and re-layouts  1.38 us (2%)
  between operations  0.91 us (1%)
    ppermute x6, starting transfers between devices, shifted(): return lax.ppermute(x, axis, pairs)  44.1 us
    pallas_call x1, Pallas kernels, run_steps(): pl.pallas_call(functools.partial(steps_kernel, levels=levels, width=width...  20.4 us
    pallas_call x1, Pallas kernels, pack(): pl.pallas_call(functools.partial(pack_kernel, levels=levels, width=width)...  4.97 us
    ppermute x6, waiting for transfers between devices, shifted(): return lax.ppermute(x, axis, pairs)  4.58 us
    mul x2, other arithmetic, shards(): flux = exchange_rate[0] * sea * (regridded - surface)  3.11 us
    ppermute x1, starting transfers between devices, shards(): partner = lax.ppermute(surface, 'sec', [(0, 1), (1, 0)])  1.92 us
  transfers between devices with their start and end apart: 7, of which 2 were waited for; matrix products, arithmetic and copies ran while one was open for 6% of the time, Pallas kernels for 0%

profile of v11, /device:TPU:2, one launch (start us, length us, event | category | flops | bytes accessed | tf_op | source)
XLA Modules:
  0.0 86.6 jit_solution(6546140483340622923)
XLA Ops:
  0.6 1.3 %copy.11 = f32[1,2,60,16,128]{4,3,1,2,0:T(8,128)S(1)} copy(f32[1,2,60,16,128]{4,3,2,1,0:T(8,128)} %param.7) | data formatting | bytes 1966080 | tf_op args[0]
  2.0 1.9 %collective-permute-start = (f32[2,16,128]{2,1,0:T(8,128)S(1)}, f32[2,16,128]{2,1,0:T(8,128)S(1)}, u32[]{:S(2)}, u32[]{:S(2)}) collective-permute-start(f32[2,16,128]{2,1,0:T(8,128)S(1)} %slice_bitcast_fusion), channel_id=1, source_target_pairs={{0,256},{256,0},{1,257},{257,1},{2,258},{258,2},{3,259},{259,3},{4... | collective-permute-start | bytes 49160 | tf_op jit(solution)/shard_map/ppermute | solution.py:217
  3.9 0.8 compare_select_fusion
  4.8 0.1 and_bitcast_fusion.27
  5.1 1.3 %multiply_bitcast_fusion = (f32[16,128]{1,0:T(8,128)S(1)}, f32[16,128]{1,0:T(8,128)}) fusion(f32[1,16,128]{2,1,0:T(8,128)} %param.11, s32[1,16,128]{2,1,0:T(8,128)} %param.12, pred[]{:T(512)S(6)} %eq.667), kind=kLoop, calls=%fused_computation.228 | loop fusion | flops 6144 | bytes 32769 | tf_op jit(solution)/shard_map/mul | solution.py:220
  6.4 0.0 collective-permute-done
  6.5 0.1 fusion.6
  6.6 0.1 fusion.11
  6.7 0.1 fusion.10
  6.8 0.1 fusion.9
  6.9 0.1 fusion.8
  7.0 0.1 fusion.7
  7.1 1.8 %subtract_multiply_fusion.flux_ref = f32[2,16,128]{2,1,0:T(8,128)} fusion(f32[2,16,128]{2,1,0:T(8,128)S(1)} %collective-permute-done, f32[2,2,128]{2,1,0:T(2,128)S(1)} %reshape.27, f32[2,16,3]{2,1,0:T(8,128)S(1)} %get-tuple-element.233, f32[2,16,3]{2,1,0:T(8,128)S(1)} %get-tuple-element.292, f32[2,16,125]{2,1,0:T(8,128)S(1)} %get-tuple-element.288, ...), kind=kLoop, calls=%fused_computation.206 | loop fusion | flops 745472 | bytes 807680 | tf_op jit(solution)/shard_map/mul | solution.py:220
  8.9 5.0 %shard_map.86 = (f32[16,128,384]{2,1,0:T(8,128)}, f32[4,128,384]{2,1,0:T(8,128)}, f32[4,128,384]{2,1,0:T(8,128)}, f32[16,8,384]{2,1,0:T(8,128)}, f32[16,8,384]{2,1,0:T(8,128)}) custom-call(f32[2,960,128]{2,1,0:T(8,128)} %bitcast.325, f32[960,128]{1,0:T(8,128)} %bitcast.329, f32[960,128]{1,0:T(8,128)} %bitcast.330, f32[960,128]{1,0:T(8,128)} %bitcast.331, ...), custom_call_target="tpu_custom_call" | custom-call | tf_op jit(solution)/shard_map/pallas_call | solution.py:185
  13.9 3.5 %collective-permute-start.3 = (f32[16,8,384]{2,1,0:T(8,128)}, f32[16,8,384]{2,1,0:T(8,128)S(1)}, u32[]{:S(2)}, u32[]{:S(2)}) collective-permute-start(f32[16,8,384]{2,1,0:T(8,128)} %get-tuple-element.10), channel_id=1, source_target_pairs={{0,1},{1,2},{2,3},{3,4},{4,5},{5,6},{6,7},{7,8},{8,9},{9,10},{10,1... | collective-permute-start | bytes 589832 | tf_op jit(solution)/shard_map/ppermute | solution.py:23
  17.4 10.9 %collective-permute-start.4 = (f32[16,8,384]{2,1,0:T(8,128)}, f32[16,8,384]{2,1,0:T(8,128)S(1)}, u32[]{:S(2)}, u32[]{:S(2)}) collective-permute-start(f32[16,8,384]{2,1,0:T(8,128)} %get-tuple-element.11), channel_id=1, source_target_pairs={{0,31},{1,0},{2,1},{3,2},{4,3},{5,4},{6,5},{7,6},{8,7},{9,8},{10,9... | collective-permute-start | bytes 589832 | tf_op jit(solution)/shard_map/ppermute | solution.py:23
  28.2 3.4 %collective-permute-start.1 = (f32[4,128,384]{2,1,0:T(8,128)}, f32[4,128,384]{2,1,0:T(8,128)S(1)}, u32[]{:S(2)}, u32[]{:S(2)}) collective-permute-start(f32[4,128,384]{2,1,0:T(8,128)} %get-tuple-element.8), channel_id=1, source_target_pairs={{0,32},{32,64},{64,96},{96,128},{128,160},{160,192},{192,224},{1,3... | collective-permute-start | bytes 2359304 | tf_op jit(solution)/shard_map/ppermute | solution.py:23
  31.6 2.5 %collective-permute-start.2 = (f32[4,128,384]{2,1,0:T(8,128)}, f32[4,128,384]{2,1,0:T(8,128)S(1)}, u32[]{:S(2)}, u32[]{:S(2)}) collective-permute-start(f32[4,128,384]{2,1,0:T(8,128)} %get-tuple-element.9), channel_id=1, source_target_pairs={{32,0},{64,32},{96,64},{128,96},{160,128},{192,160},{224,192},{33,... | collective-permute-start | bytes 2359304 | tf_op jit(solution)/shard_map/ppermute | solution.py:23
  34.1 0.0 collective-permute-done.3
  34.1 0.0 collective-permute-done.4
  34.2 22.0 %collective-permute-start.6 = (f32[4,16,384]{2,1,0:T(8,128)S(1)}, f32[4,16,384]{2,1,0:T(8,128)S(1)}, u32[]{:S(2)}, u32[]{:S(2)}) collective-permute-start(f32[4,16,384]{2,1,0:T(8,128)S(1)} %pad_maximum_fusion.3), channel_id=1, source_target_pairs={{32,0},{64,32},{96,64},{128,96},{160,128},{192,160},{224,192},{33,... | collective-permute-start | bytes 294920 | tf_op jit(solution)/shard_map/ppermute | solution.py:23
  56.2 1.9 %collective-permute-start.5 = (f32[4,16,384]{2,1,0:T(8,128)S(1)}, f32[4,16,384]{2,1,0:T(8,128)S(1)}, u32[]{:S(2)}, u32[]{:S(2)}) collective-permute-start(f32[4,16,384]{2,1,0:T(8,128)S(1)} %pad_maximum_fusion.2), channel_id=1, source_target_pairs={{0,32},{32,64},{64,96},{96,128},{128,160},{160,192},{192,224},{1,3... | collective-permute-start | bytes 294920 | tf_op jit(solution)/shard_map/ppermute | solution.py:23
  58.1 0.2 collective-permute-done.6
  58.4 4.3 %collective-permute-done.5 = f32[4,16,384]{2,1,0:T(8,128)S(1)} collective-permute-done((f32[4,16,384]{2,1,0:T(8,128)S(1)}, f32[4,16,384]{2,1,0:T(8,128)S(1)}, u32[]{:S(2)}, u32[]{:S(2)}) %collective-permute-start.5) | collective-permute-done | bytes 98336 | tf_op jit(solution)/shard_map/ppermute | solution.py:23
  62.8 0.7 pad_maximum_fusion.1.right_ref
  63.5 0.7 pad_maximum_fusion.left_ref
  64.3 0.0 collective-permute-done.1
  64.3 0.9 %broadcast_select_fusion.1.top_ref = f32[4,128,384]{2,1,0:T(8,128)} fusion(f32[4,128,384]{2,1,0:T(8,128)S(1)} %collective-permute-done.1, pred[384]{0:T(512)(128)(4,1)S(1)} %fusion.79), kind=kLoop, calls=%fused_computation.2 | loop fusion | flops 196608 | bytes 1573248 | tf_op jit(solution)/shard_map/jit(_where)/select_n | solution.py:229
  65.2 0.0 collective-permute-done.2
  65.2 0.9 %broadcast_select_fusion.bot_ref = f32[4,128,384]{2,1,0:T(8,128)} fusion(f32[4,128,384]{2,1,0:T(8,128)S(1)} %collective-permute-done.2, pred[384]{0:T(512)(128)(4,1)S(1)} %fusion.78), kind=kLoop, calls=%fused_computation.1 | loop fusion | flops 196608 | bytes 1573248 | tf_op jit(solution)/shard_map/jit(_where)/select_n | solution.py:230
  66.2 20.4 %shard_map.87 = f32[2,960,128]{2,1,0:T(8,128)} custom-call(f32[16,128,384]{2,1,0:T(8,128)} %get-tuple-element.7.x_ref, f32[4,128,384]{2,1,0:T(8,128)} %broadcast_select_fusion.1.top_ref, f32[4,128,384]{2,1,0:T(8,128)} %broadcast_select_fusion.bot_ref, f32[24,8,384]{2,1,0:T(8,128)} %pad_maximum_fusion.left_ref, f32[24,8,384]{2,1,0:T(8,128)} %pad_maximum_fusion.1.right_ref), custom_call_target="tpu_custom_call" | custom-call | tf_op jit(solution)/shard_map/pallas_call | solution.py:138
  (21 shorter events, 0.4 us)
Async XLA Ops:
  2.0 4.5 %collective-permute-start = (f32[2,16,128]{2,1,0:T(8,128)S(1)}, f32[2,16,128]{2,1,0:T(8,128)S(1)}, u32[]{:S(2)}, u32[]{:S(2)}) collective-permute-start(f32[2,16,128]{2,1,0:T(8,128)S(1)} %slice_bitcast_fusion), channel_id=1, source_target_pairs={{0,256},{256,0},{1,257},{257,1},{2,258},{258,2},{3,259},{259,3},{4... | collective-permute-start | bytes 49160 | tf_op jit(solution)/shard_map/ppermute | solution.py:217
  13.9 20.3 %collective-permute-start.3 = (f32[16,8,384]{2,1,0:T(8,128)}, f32[16,8,384]{2,1,0:T(8,128)S(1)}, u32[]{:S(2)}, u32[]{:S(2)}) collective-permute-start(f32[16,8,384]{2,1,0:T(8,128)} %get-tuple-element.10), channel_id=1, source_target_pairs={{0,1},{1,2},{2,3},{3,4},{4,5},{5,6},{6,7},{7,8},{8,9},{9,10},{10,1... | collective-permute-start | bytes 589832 | tf_op jit(solution)/shard_map/ppermute | solution.py:23
  17.4 16.8 %collective-permute-start.4 = (f32[16,8,384]{2,1,0:T(8,128)}, f32[16,8,384]{2,1,0:T(8,128)S(1)}, u32[]{:S(2)}, u32[]{:S(2)}) collective-permute-start(f32[16,8,384]{2,1,0:T(8,128)} %get-tuple-element.11), channel_id=1, source_target_pairs={{0,31},{1,0},{2,1},{3,2},{4,3},{5,4},{6,5},{7,6},{8,7},{9,8},{10,9... | collective-permute-start | bytes 589832 | tf_op jit(solution)/shard_map/ppermute | solution.py:23
  28.2 36.0 %collective-permute-start.1 = (f32[4,128,384]{2,1,0:T(8,128)}, f32[4,128,384]{2,1,0:T(8,128)S(1)}, u32[]{:S(2)}, u32[]{:S(2)}) collective-permute-start(f32[4,128,384]{2,1,0:T(8,128)} %get-tuple-element.8), channel_id=1, source_target_pairs={{0,32},{32,64},{64,96},{96,128},{128,160},{160,192},{192,224},{1,3... | collective-permute-start | bytes 2359304 | tf_op jit(solution)/shard_map/ppermute | solution.py:23
  31.6 33.6 %collective-permute-start.2 = (f32[4,128,384]{2,1,0:T(8,128)}, f32[4,128,384]{2,1,0:T(8,128)S(1)}, u32[]{:S(2)}, u32[]{:S(2)}) collective-permute-start(f32[4,128,384]{2,1,0:T(8,128)} %get-tuple-element.9), channel_id=1, source_target_pairs={{32,0},{64,32},{96,64},{128,96},{160,128},{192,160},{224,192},{33,... | collective-permute-start | bytes 2359304 | tf_op jit(solution)/shard_map/ppermute | solution.py:23
  34.2 24.2 %collective-permute-start.6 = (f32[4,16,384]{2,1,0:T(8,128)S(1)}, f32[4,16,384]{2,1,0:T(8,128)S(1)}, u32[]{:S(2)}, u32[]{:S(2)}) collective-permute-start(f32[4,16,384]{2,1,0:T(8,128)S(1)} %pad_maximum_fusion.3), channel_id=1, source_target_pairs={{32,0},{64,32},{96,64},{128,96},{160,128},{192,160},{224,192},{33,... | collective-permute-start | bytes 294920 | tf_op jit(solution)/shard_map/ppermute | solution.py:23
  56.2 6.5 %collective-permute-start.5 = (f32[4,16,384]{2,1,0:T(8,128)S(1)}, f32[4,16,384]{2,1,0:T(8,128)S(1)}, u32[]{:S(2)}, u32[]{:S(2)}) collective-permute-start(f32[4,16,384]{2,1,0:T(8,128)S(1)} %pad_maximum_fusion.2), channel_id=1, source_target_pairs={{0,32},{32,64},{64,96},{96,128},{128,160},{160,192},{192,224},{1,3... | collective-permute-start | bytes 294920 | tf_op jit(solution)/shard_map/ppermute | solution.py:23

commit v12 on v10

--- a/solution.py
+++ b/solution.py
@@ -216,10 +216,10 @@
     bot = jnp.where(bot_mask, 0.0, shifted(x[:width], "lat", -1, cyclic=False))
     left = shifted(x[:, -COL_PAD:], "lon", 1)
     right = shifted(x[:, :COL_PAD], "lon", -1)
-    upper = jnp.where(top_mask, 0.0, shifted(jnp.concatenate([left[-width:], right[-width:]], axis=1), "lat", 1, cyclic=False))
-    lower = jnp.where(bot_mask, 0.0, shifted(jnp.concatenate([left[:width], right[:width]], axis=1), "lat", -1, cyclic=False))
-    left = jnp.concatenate([upper[:, :COL_PAD], left, lower[:, :COL_PAD]], axis=0)
-    right = jnp.concatenate([upper[:, COL_PAD:], right, lower[:, COL_PAD:]], axis=0)
+    east = shifted(jnp.concatenate([top[:, -COL_PAD:], bot[:, -COL_PAD:]], axis=0), "lon", 1)
+    west = shifted(jnp.concatenate([top[:, :COL_PAD], bot[:, :COL_PAD]], axis=0), "lon", -1)
+    left = jnp.concatenate([east[:width], left, east[width:]], axis=0)
+    right = jnp.concatenate([west[:width], right, west[width:]], axis=0)
 
     out = run_steps(x, top, bot, left, right, levels, width)
     q = out.reshape(fields, levels, rows, cols)

time: 85.9 us -> 89.7 us (1.044)
  starting transfers between devices: 32.1 us -> 39.6 us
  waiting for transfers between devices: 15.5 us -> 13.5 us
  other arithmetic: 8.27 us -> 6.5 us
    ppermute x6, starting transfers between devices: 30.2 us -> 37.7 us  [shifted(): return lax.ppermute(x, axis, pairs)]
    ppermute x6, waiting for transfers between devices: 15.5 us -> 13.5 us  [shifted(): return lax.ppermute(x, axis, pairs)]
  transfers between devices with their start and end apart: 7 -> 7, of which waited for: 2 -> 4; matrix products, arithmetic and copies ran while one was open for 8% -> 5% of each run, Pallas kernels for 0% -> 0%
where the time goes in v12:
time: 89.7 us; the launch traced here: 89.2 us
  starting transfers between devices  39.6 us (44%)
  Pallas kernels  24.7 us (28%)
  waiting for transfers between devices  13.5 us (15%)
  other arithmetic  6.5 us (7%)
  local copies, waits for them, and re-layouts  3.91 us (4%)
  between operations  0.94 us (1%)
    ppermute x6, starting transfers between devices, shifted(): return lax.ppermute(x, axis, pairs)  37.7 us
    pallas_call x1, Pallas kernels, run_steps(): pl.pallas_call(functools.partial(steps_kernel, levels=levels, width=width...  20.4 us
    ppermute x6, waiting for transfers between devices, shifted(): return lax.ppermute(x, axis, pairs)  13.5 us
    pallas_call x1, Pallas kernels, pack(): pl.pallas_call(functools.partial(pack_kernel, levels=levels), out_shape=j...  4.27 us
    mul x2, other arithmetic, shards(): flux = exchange_rate[0] * sea * (regridded - surface)  3.12 us
    ppermute x1, starting transfers between devices, shards(): partner = lax.ppermute(surface, 'sec', [(0, 1), (1, 0)])  1.92 us
  transfers between devices with their start and end apart: 7, of which 4 were waited for; matrix products, arithmetic and copies ran while one was open for 5% of the time, Pallas kernels for 0%

profile of v12, /device:TPU:16, one launch (start us, length us, event | category | flops | bytes accessed | tf_op | source)
XLA Modules:
  0.0 89.2 jit_solution(4141961988625689442)
XLA Ops:
  0.6 1.3 %copy.11 = f32[1,2,60,16,128]{4,3,1,2,0:T(8,128)S(1)} copy(f32[1,2,60,16,128]{4,3,2,1,0:T(8,128)} %param.7) | data formatting | bytes 1966080 | tf_op args[0]
  2.0 1.9 %collective-permute-start = (f32[2,16,128]{2,1,0:T(8,128)S(1)}, f32[2,16,128]{2,1,0:T(8,128)S(1)}, u32[]{:S(2)}, u32[]{:S(2)}) collective-permute-start(f32[2,16,128]{2,1,0:T(8,128)S(1)} %slice_bitcast_fusion), channel_id=1, source_target_pairs={{0,256},{256,0},{1,257},{257,1},{2,258},{258,2},{3,259},{259,3},{4... | collective-permute-start | bytes 49160 | tf_op jit(solution)/shard_map/ppermute | solution.py:203
  3.9 0.8 compare_select_fusion
  4.8 0.1 and_bitcast_fusion.27
  5.1 1.3 %multiply_bitcast_fusion = (f32[16,128]{1,0:T(8,128)S(1)}, f32[16,128]{1,0:T(8,128)}) fusion(f32[1,16,128]{2,1,0:T(8,128)} %param.11, s32[1,16,128]{2,1,0:T(8,128)} %param.12, pred[]{:T(512)S(6)} %eq.667), kind=kLoop, calls=%fused_computation.226 | loop fusion | flops 6144 | bytes 32769 | tf_op jit(solution)/shard_map/mul | solution.py:206
  6.4 0.0 collective-permute-done
  6.5 0.1 fusion.6
  6.6 0.1 fusion.11
  6.7 0.1 fusion.10
  6.8 0.1 fusion.9
  6.9 0.1 fusion.8
  7.0 0.1 fusion.7
  7.1 1.8 %subtract_multiply_fusion.flux_ref = f32[2,16,128]{2,1,0:T(8,128)} fusion(f32[2,16,128]{2,1,0:T(8,128)S(1)} %collective-permute-done, f32[2,2,128]{2,1,0:T(2,128)S(1)} %reshape.27, f32[2,16,3]{2,1,0:T(8,128)S(1)} %get-tuple-element.227, f32[2,16,3]{2,1,0:T(8,128)S(1)} %get-tuple-element.286, f32[2,16,125]{2,1,0:T(8,128)S(1)} %get-tuple-element.282, ...), kind=kLoop, calls=%fused_computation.204 | loop fusion | flops 745472 | bytes 807680 | tf_op jit(solution)/shard_map/mul | solution.py:206
  8.9 4.3 %shard_map.86.x_ref = f32[16,128,384]{2,1,0:T(8,128)} custom-call(f32[2,960,128]{2,1,0:T(8,128)} %bitcast.325, f32[960,128]{1,0:T(8,128)} %bitcast.329, f32[960,128]{1,0:T(8,128)} %bitcast.330, f32[960,128]{1,0:T(8,128)} %bitcast.331, f32[16,128]{1,0:T(8,128)} %get-tuple-element.315.wet_ref, f32[2,16,128]{2,1,0:T(8,128)} %subtract_multiply_fusion.flux_ref), custom_call_target="tpu_custom_call" | custom-call | tf_op jit(solution)/shard_map/pallas_call | solution.py:177
  13.2 1.5 %fusion.81 = (f32[4,128,384]{2,1,0:T(8,128)S(1)}, f32[4,128,384]{2,1,0:T(8,128)S(1)}) fusion(f32[16,128,384]{2,1,0:T(8,128)} %shard_map.86.x_ref), kind=kLoop, calls=%fused_computation.420 | loop fusion | bytes 3145728 | tf_op jit(solution)/shard_map/slice | solution.py:216
  14.6 4.4 %collective-permute-start.2 = (f32[4,128,384]{2,1,0:T(8,128)S(1)}, f32[4,128,384]{2,1,0:T(8,128)S(1)}, u32[]{:S(2)}, u32[]{:S(2)}) collective-permute-start(f32[4,128,384]{2,1,0:T(8,128)S(1)} %get-tuple-element.96), channel_id=1, source_target_pairs={{32,0},{64,32},{96,64},{128,96},{160,128},{192,160},{224,192},{33,... | collective-permute-start | bytes 2359304 | tf_op jit(solution)/shard_map/ppermute | solution.py:23
  19.1 1.9 %collective-permute-start.1 = (f32[4,128,384]{2,1,0:T(8,128)S(1)}, f32[4,128,384]{2,1,0:T(8,128)S(1)}, u32[]{:S(2)}, u32[]{:S(2)}) collective-permute-start(f32[4,128,384]{2,1,0:T(8,128)S(1)} %get-tuple-element.97), channel_id=1, source_target_pairs={{0,32},{32,64},{64,96},{96,128},{128,160},{160,192},{192,224},{1,3... | collective-permute-start | bytes 2359304 | tf_op jit(solution)/shard_map/ppermute | solution.py:23
  21.1 1.1 %fusion.80 = (f32[16,8,384]{2,1,0:T(8,128)S(1)}, f32[16,8,384]{2,1,0:T(8,128)S(1)}) fusion(f32[16,128,384]{2,1,0:T(8,128)} %shard_map.86.x_ref), kind=kLoop, calls=%fused_computation.419 | loop fusion | bytes 786432 | tf_op jit(solution)/shard_map/slice | solution.py:218
  22.1 13.0 %collective-permute-start.6 = (f32[16,8,384]{2,1,0:T(8,128)S(1)}, f32[16,8,384]{2,1,0:T(8,128)S(1)}, u32[]{:S(2)}, u32[]{:S(2)}) collective-permute-start(f32[16,8,384]{2,1,0:T(8,128)S(1)} %get-tuple-element.94), channel_id=1, source_target_pairs={{0,31},{1,0},{2,1},{3,2},{4,3},{5,4},{6,5},{7,6},{8,7},{9,8},{10,9... | collective-permute-start | bytes 589832 | tf_op jit(solution)/shard_map/ppermute | solution.py:23
  35.1 1.9 %collective-permute-start.4 = (f32[16,8,384]{2,1,0:T(8,128)S(1)}, f32[16,8,384]{2,1,0:T(8,128)S(1)}, u32[]{:S(2)}, u32[]{:S(2)}) collective-permute-start(f32[16,8,384]{2,1,0:T(8,128)S(1)} %get-tuple-element.95), channel_id=1, source_target_pairs={{0,1},{1,2},{2,3},{3,4},{4,5},{5,6},{6,7},{7,8},{8,9},{9,10},{10,1... | collective-permute-start | bytes 589832 | tf_op jit(solution)/shard_map/ppermute | solution.py:23
  37.1 3.7 %collective-permute-done.2 = f32[4,128,384]{2,1,0:T(8,128)S(1)} collective-permute-done((f32[4,128,384]{2,1,0:T(8,128)S(1)}, f32[4,128,384]{2,1,0:T(8,128)S(1)}, u32[]{:S(2)}, u32[]{:S(2)}) %collective-permute-start.2) | collective-permute-done | bytes 786464 | tf_op jit(solution)/shard_map/ppermute | solution.py:23
  40.8 0.1 broadcast_select_fusion.bot_ref
  40.9 0.0 copy-start
  40.9 8.4 %collective-permute-done.1 = f32[4,128,384]{2,1,0:T(8,128)S(1)} collective-permute-done((f32[4,128,384]{2,1,0:T(8,128)S(1)}, f32[4,128,384]{2,1,0:T(8,128)S(1)}, u32[]{:S(2)}, u32[]{:S(2)}) %collective-permute-start.1) | collective-permute-done | bytes 786464 | tf_op jit(solution)/shard_map/ppermute | solution.py:23
  49.2 0.1 broadcast_select_fusion.1.top_ref
  49.3 0.0 copy-start.1
  49.4 3.4 %collective-permute-start.3 = (f32[8,8,384]{2,1,0:T(8,128)S(1)}, f32[8,8,384]{2,1,0:T(8,128)S(1)}, u32[]{:S(2)}, u32[]{:S(2)}) collective-permute-start(f32[8,8,384]{2,1,0:T(8,128)S(1)} %pad_maximum_fusion.2), channel_id=1, source_target_pairs={{0,1},{1,2},{2,3},{3,4},{4,5},{5,6},{6,7},{7,8},{8,9},{9,10},{10,1... | collective-permute-start | bytes 294920 | tf_op jit(solution)/shard_map/ppermute | solution.py:23
  52.8 13.0 %collective-permute-start.5 = (f32[8,8,384]{2,1,0:T(8,128)S(1)}, f32[8,8,384]{2,1,0:T(8,128)S(1)}, u32[]{:S(2)}, u32[]{:S(2)}) collective-permute-start(f32[8,8,384]{2,1,0:T(8,128)S(1)} %pad_maximum_fusion.3), channel_id=1, source_target_pairs={{0,31},{1,0},{2,1},{3,2},{4,3},{5,4},{6,5},{7,6},{8,7},{9,8},{10,9... | collective-permute-start | bytes 294920 | tf_op jit(solution)/shard_map/ppermute | solution.py:23
  65.8 0.6 collective-permute-done.3
  66.4 0.0 collective-permute-done.4
  66.4 0.7 pad_maximum_fusion.left_ref
  67.2 0.8 collective-permute-done.5
  68.0 0.0 collective-permute-done.6
  68.0 0.8 pad_maximum_fusion.1.right_ref
  68.8 0.0 copy-done
  68.8 0.0 copy-done.1
  68.8 20.4 %shard_map.87 = f32[2,960,128]{2,1,0:T(8,128)} custom-call(f32[16,128,384]{2,1,0:T(8,128)} %shard_map.86.x_ref, f32[4,128,384]{2,1,0:T(8,128)} %copy-done.1, f32[4,128,384]{2,1,0:T(8,128)} %copy-done, f32[24,8,384]{2,1,0:T(8,128)} %pad_maximum_fusion.left_ref, f32[24,8,384]{2,1,0:T(8,128)} %pad_maximum_fusion.1.right_ref), custom_call_target="tpu_custom_call" | custom-call | tf_op jit(solution)/shard_map/pallas_call | solution.py:138
  (19 shorter events, 0.4 us)
Async XLA Ops:
  2.0 4.5 %collective-permute-start = (f32[2,16,128]{2,1,0:T(8,128)S(1)}, f32[2,16,128]{2,1,0:T(8,128)S(1)}, u32[]{:S(2)}, u32[]{:S(2)}) collective-permute-start(f32[2,16,128]{2,1,0:T(8,128)S(1)} %slice_bitcast_fusion), channel_id=1, source_target_pairs={{0,256},{256,0},{1,257},{257,1},{2,258},{258,2},{3,259},{259,3},{4... | collective-permute-start | bytes 49160 | tf_op jit(solution)/shard_map/ppermute | solution.py:203
  14.6 26.1 %collective-permute-start.2 = (f32[4,128,384]{2,1,0:T(8,128)S(1)}, f32[4,128,384]{2,1,0:T(8,128)S(1)}, u32[]{:S(2)}, u32[]{:S(2)}) collective-permute-start(f32[4,128,384]{2,1,0:T(8,128)S(1)} %get-tuple-element.96), channel_id=1, source_target_pairs={{32,0},{64,32},{96,64},{128,96},{160,128},{192,160},{224,192},{33,... | collective-permute-start | bytes 2359304 | tf_op jit(solution)/shard_map/ppermute | solution.py:23
  19.1 30.1 %collective-permute-start.1 = (f32[4,128,384]{2,1,0:T(8,128)S(1)}, f32[4,128,384]{2,1,0:T(8,128)S(1)}, u32[]{:S(2)}, u32[]{:S(2)}) collective-permute-start(f32[4,128,384]{2,1,0:T(8,128)S(1)} %get-tuple-element.97), channel_id=1, source_target_pairs={{0,32},{32,64},{64,96},{96,128},{128,160},{160,192},{192,224},{1,3... | collective-permute-start | bytes 2359304 | tf_op jit(solution)/shard_map/ppermute | solution.py:23
  22.1 45.9 %collective-permute-start.6 = (f32[16,8,384]{2,1,0:T(8,128)S(1)}, f32[16,8,384]{2,1,0:T(8,128)S(1)}, u32[]{:S(2)}, u32[]{:S(2)}) collective-permute-start(f32[16,8,384]{2,1,0:T(8,128)S(1)} %get-tuple-element.94), channel_id=1, source_target_pairs={{0,31},{1,0},{2,1},{3,2},{4,3},{5,4},{6,5},{7,6},{8,7},{9,8},{10,9... | collective-permute-start | bytes 589832 | tf_op jit(solution)/shard_map/ppermute | solution.py:23
  35.1 31.3 %collective-permute-start.4 = (f32[16,8,384]{2,1,0:T(8,128)S(1)}, f32[16,8,384]{2,1,0:T(8,128)S(1)}, u32[]{:S(2)}, u32[]{:S(2)}) collective-permute-start(f32[16,8,384]{2,1,0:T(8,128)S(1)} %get-tuple-element.95), channel_id=1, source_target_pairs={{0,1},{1,2},{2,3},{3,4},{4,5},{5,6},{6,7},{7,8},{8,9},{9,10},{10,1... | collective-permute-start | bytes 589832 | tf_op jit(solution)/shard_map/ppermute | solution.py:23
  40.9 27.9 %copy-start = (f32[4,128,384]{2,1,0:T(8,128)}, f32[4,128,384]{2,1,0:T(8,128)S(1)}, u32[]{:S(2)}) copy-start(f32[4,128,384]{2,1,0:T(8,128)S(1)} %broadcast_select_fusion.bot_ref) | copy-start | bytes 2359300
  49.3 19.4 %copy-start.1 = (f32[4,128,384]{2,1,0:T(8,128)}, f32[4,128,384]{2,1,0:T(8,128)S(1)}, u32[]{:S(2)}) copy-start(f32[4,128,384]{2,1,0:T(8,128)S(1)} %broadcast_select_fusion.1.top_ref) | copy-start | bytes 2359300
  49.4 17.1 %collective-permute-start.3 = (f32[8,8,384]{2,1,0:T(8,128)S(1)}, f32[8,8,384]{2,1,0:T(8,128)S(1)}, u32[]{:S(2)}, u32[]{:S(2)}) collective-permute-start(f32[8,8,384]{2,1,0:T(8,128)S(1)} %pad_maximum_fusion.2), channel_id=1, source_target_pairs={{0,1},{1,2},{2,3},{3,4},{4,5},{5,6},{6,7},{7,8},{8,9},{9,10},{10,1... | collective-permute-start | bytes 294920 | tf_op jit(solution)/shard_map/ppermute | solution.py:23
  52.8 15.2 %collective-permute-start.5 = (f32[8,8,384]{2,1,0:T(8,128)S(1)}, f32[8,8,384]{2,1,0:T(8,128)S(1)}, u32[]{:S(2)}, u32[]{:S(2)}) collective-permute-start(f32[8,8,384]{2,1,0:T(8,128)S(1)} %pad_maximum_fusion.3), channel_id=1, source_target_pairs={{0,31},{1,0},{2,1},{3,2},{4,3},{5,4},{6,5},{7,6},{8,7},{9,8},{10,9... | collective-permute-start | bytes 294920 | tf_op jit(solution)/shard_map/ppermute | solution.py:23

commit v13 on v10

--- a/solution.py
+++ b/solution.py
@@ -199,7 +199,7 @@
     section = lax.axis_index("sec")
     sea = sea_mask[0].astype(jnp.float32)
     wet = jnp.where(section == 1, sea, jnp.ones_like(sea))
-    surface = tracers[:, 0]
+    surface = jnp.stack([tracers[f, 0] for f in range(fields)])
     partner = lax.ppermute(surface, "sec", [(0, 1), (1, 0)])
 
     regridded = regrid(partner, regrid_map[0])

time: 85.9 us -> 85.4 us (level)
    unnamed x1 -> x0, local copies, waits for them, and re-layouts: 1.33 us -> none
where the time goes in v13:
time: 85.4 us; the launch traced here: 84.8 us
  starting transfers between devices  32.1 us (38%)
  Pallas kernels  24.7 us (29%)
  waiting for transfers between devices  15.5 us (18%)
  other arithmetic  8.31 us (10%)
  local copies, waits for them, and re-layouts  3.3 us (4%)
  between operations  0.93 us (1%)
    ppermute x6, starting transfers between devices, shifted(): return lax.ppermute(x, axis, pairs)  30.2 us
    pallas_call x1, Pallas kernels, run_steps(): pl.pallas_call(functools.partial(steps_kernel, levels=levels, width=width...  20.4 us
    ppermute x6, waiting for transfers between devices, shifted(): return lax.ppermute(x, axis, pairs)  15.5 us
    pallas_call x1, Pallas kernels, pack(): pl.pallas_call(functools.partial(pack_kernel, levels=levels), out_shape=j...  4.25 us
    mul x2, other arithmetic, shards(): flux = exchange_rate[0] * sea * (regridded - surface)  3.12 us
    ppermute x1, starting transfers between devices, shards(): partner = lax.ppermute(surface, 'sec', [(0, 1), (1, 0)])  1.91 us
  transfers between devices with their start and end apart: 7, of which 2 were waited for; matrix products, arithmetic and copies ran while one was open for 8% of the time, Pallas kernels for 0%

profile of v13, /device:TPU:16, one launch (start us, length us, event | category | flops | bytes accessed | tf_op | source)
XLA Modules:
  0.0 84.8 jit_solution(15034329000607239613)
XLA Ops:
  0.6 0.7 slice_bitcast_fusion.1
  1.4 1.9 %collective-permute-start = (f32[2,16,128]{2,1,0:T(8,128)S(1)}, f32[2,16,128]{2,1,0:T(8,128)S(1)}, u32[]{:S(2)}, u32[]{:S(2)}) collective-permute-start(f32[2,16,128]{2,1,0:T(8,128)S(1)} %pad_maximum_fusion.6), channel_id=1, source_target_pairs={{0,256},{256,0},{1,257},{257,1},{2,258},{258,2},{3,259},{259,3},{4... | collective-permute-start | bytes 49160 | tf_op jit(solution)/shard_map/ppermute | solution.py:203
  3.3 0.8 compare_select_fusion
  4.2 1.3 %multiply_bitcast_fusion = (f32[16,128]{1,0:T(8,128)S(1)}, f32[16,128]{1,0:T(8,128)}) fusion(f32[1,16,128]{2,1,0:T(8,128)} %param.11, s32[1,16,128]{2,1,0:T(8,128)} %param.12, pred[]{:T(512)S(6)} %eq.667), kind=kLoop, calls=%fused_computation.229 | loop fusion | flops 6144 | bytes 32769 | tf_op jit(solution)/shard_map/mul | solution.py:206
  5.8 0.0 collective-permute-done
  5.9 0.1 fusion.6
  6.0 0.1 fusion.11
  6.1 0.1 fusion.10
  6.2 0.1 fusion.9
  6.3 0.1 fusion.8
  6.4 0.1 fusion.7
  6.5 1.8 %subtract_multiply_fusion.flux_ref = f32[2,16,128]{2,1,0:T(8,128)} fusion(f32[2,16,128]{2,1,0:T(8,128)S(1)} %collective-permute-done, f32[2,2,128]{2,1,0:T(2,128)S(1)} %reshape.27, f32[2,16,3]{2,1,0:T(8,128)S(1)} %get-tuple-element.229, f32[2,16,3]{2,1,0:T(8,128)S(1)} %get-tuple-element.288, f32[2,16,125]{2,1,0:T(8,128)S(1)} %get-tuple-element.284, ...), kind=kLoop, calls=%fused_computation.205 | loop fusion | flops 749568 | bytes 807680 | tf_op jit(solution)/shard_map/mul | solution.py:206
  8.3 4.3 %shard_map.86.x_ref = f32[16,128,384]{2,1,0:T(8,128)} custom-call(f32[2,960,128]{2,1,0:T(8,128)} %bitcast.324, f32[960,128]{1,0:T(8,128)} %bitcast.326, f32[960,128]{1,0:T(8,128)} %bitcast.327, f32[960,128]{1,0:T(8,128)} %bitcast.328, f32[16,128]{1,0:T(8,128)} %get-tuple-element.317.wet_ref, f32[2,16,128]{2,1,0:T(8,128)} %subtract_multiply_fusion.flux_ref), custom_call_target="tpu_custom_call" | custom-call | tf_op jit(solution)/shard_map/pallas_call | solution.py:177
  12.5 1.0 %fusion.80 = (f32[16,8,384]{2,1,0:T(8,128)S(1)}, f32[16,8,384]{2,1,0:T(8,128)S(1)}) fusion(f32[16,128,384]{2,1,0:T(8,128)} %shard_map.86.x_ref), kind=kLoop, calls=%fused_computation.422 | loop fusion | bytes 786432 | tf_op jit(solution)/shard_map/slice | solution.py:217
  13.6 3.2 %collective-permute-start.3 = (f32[16,8,384]{2,1,0:T(8,128)S(1)}, f32[16,8,384]{2,1,0:T(8,128)S(1)}, u32[]{:S(2)}, u32[]{:S(2)}) collective-permute-start(f32[16,8,384]{2,1,0:T(8,128)S(1)} %get-tuple-element.94), channel_id=1, source_target_pairs={{0,1},{1,2},{2,3},{3,4},{4,5},{5,6},{6,7},{7,8},{8,9},{9,10},{10,1... | collective-permute-start | bytes 589832 | tf_op jit(solution)/shard_map/ppermute | solution.py:23
  16.8 10.9 %collective-permute-start.4 = (f32[16,8,384]{2,1,0:T(8,128)S(1)}, f32[16,8,384]{2,1,0:T(8,128)S(1)}, u32[]{:S(2)}, u32[]{:S(2)}) collective-permute-start(f32[16,8,384]{2,1,0:T(8,128)S(1)} %get-tuple-element.95), channel_id=1, source_target_pairs={{0,31},{1,0},{2,1},{3,2},{4,3},{5,4},{6,5},{7,6},{8,7},{9,8},{10,9... | collective-permute-start | bytes 589832 | tf_op jit(solution)/shard_map/ppermute | solution.py:23
  27.7 1.5 %fusion.81 = (f32[4,128,384]{2,1,0:T(8,128)S(1)}, f32[4,128,384]{2,1,0:T(8,128)S(1)}) fusion(f32[16,128,384]{2,1,0:T(8,128)} %shard_map.86.x_ref), kind=kLoop, calls=%fused_computation.423 | loop fusion | bytes 3145728 | tf_op jit(solution)/shard_map/slice | solution.py:216
  29.1 4.7 %collective-permute-start.2 = (f32[4,128,384]{2,1,0:T(8,128)S(1)}, f32[4,128,384]{2,1,0:T(8,128)S(1)}, u32[]{:S(2)}, u32[]{:S(2)}) collective-permute-start(f32[4,128,384]{2,1,0:T(8,128)S(1)} %get-tuple-element.96), channel_id=1, source_target_pairs={{32,0},{64,32},{96,64},{128,96},{160,128},{192,160},{224,192},{33,... | collective-permute-start | bytes 2359304 | tf_op jit(solution)/shard_map/ppermute | solution.py:23
  33.9 1.9 %collective-permute-start.1 = (f32[4,128,384]{2,1,0:T(8,128)S(1)}, f32[4,128,384]{2,1,0:T(8,128)S(1)}, u32[]{:S(2)}, u32[]{:S(2)}) collective-permute-start(f32[4,128,384]{2,1,0:T(8,128)S(1)} %get-tuple-element.97), channel_id=1, source_target_pairs={{0,32},{32,64},{64,96},{96,128},{128,160},{160,192},{192,224},{1,3... | collective-permute-start | bytes 2359304 | tf_op jit(solution)/shard_map/ppermute | solution.py:23
  35.8 0.0 collective-permute-done.3
  35.8 0.0 collective-permute-done.4
  35.9 7.5 %collective-permute-start.6 = (f32[4,16,384]{2,1,0:T(8,128)S(1)}, f32[4,16,384]{2,1,0:T(8,128)S(1)}, u32[]{:S(2)}, u32[]{:S(2)}) collective-permute-start(f32[4,16,384]{2,1,0:T(8,128)S(1)} %pad_maximum_fusion.3), channel_id=1, source_target_pairs={{32,0},{64,32},{96,64},{128,96},{160,128},{192,160},{224,192},{33,... | collective-permute-start | bytes 294920 | tf_op jit(solution)/shard_map/ppermute | solution.py:23
  43.4 1.9 %collective-permute-start.5 = (f32[4,16,384]{2,1,0:T(8,128)S(1)}, f32[4,16,384]{2,1,0:T(8,128)S(1)}, u32[]{:S(2)}, u32[]{:S(2)}) collective-permute-start(f32[4,16,384]{2,1,0:T(8,128)S(1)} %pad_maximum_fusion.2), channel_id=1, source_target_pairs={{0,32},{32,64},{64,96},{96,128},{128,160},{160,192},{192,224},{1,3... | collective-permute-start | bytes 294920 | tf_op jit(solution)/shard_map/ppermute | solution.py:23
  45.4 7.8 %collective-permute-done.6 = f32[4,16,384]{2,1,0:T(8,128)S(1)} collective-permute-done((f32[4,16,384]{2,1,0:T(8,128)S(1)}, f32[4,16,384]{2,1,0:T(8,128)S(1)}, u32[]{:S(2)}, u32[]{:S(2)}) %collective-permute-start.6) | collective-permute-done | bytes 98336 | tf_op jit(solution)/shard_map/ppermute | solution.py:23
  53.2 7.7 %collective-permute-done.5 = f32[4,16,384]{2,1,0:T(8,128)S(1)} collective-permute-done((f32[4,16,384]{2,1,0:T(8,128)S(1)}, f32[4,16,384]{2,1,0:T(8,128)S(1)}, u32[]{:S(2)}, u32[]{:S(2)}) %collective-permute-start.5) | collective-permute-done | bytes 98336 | tf_op jit(solution)/shard_map/ppermute | solution.py:23
  60.9 0.8 pad_maximum_fusion.1.right_ref
  61.7 0.8 pad_maximum_fusion.left_ref
  62.5 0.0 collective-permute-done.2
  62.5 1.0 %broadcast_select_fusion.bot_ref = f32[4,128,384]{2,1,0:T(8,128)} fusion(f32[4,128,384]{2,1,0:T(8,128)S(1)} %collective-permute-done.2, pred[384]{0:T(512)(128)(4,1)S(1)} %fusion.78), kind=kLoop, calls=%fused_computation | loop fusion | flops 196608 | bytes 1573248 | tf_op jit(solution)/shard_map/jit(_where)/select_n | solution.py:216
  63.4 0.0 collective-permute-done.1
  63.4 0.9 %broadcast_select_fusion.1.top_ref = f32[4,128,384]{2,1,0:T(8,128)} fusion(f32[4,128,384]{2,1,0:T(8,128)S(1)} %collective-permute-done.1, pred[384]{0:T(512)(128)(4,1)S(1)} %fusion.79), kind=kLoop, calls=%fused_computation.1 | loop fusion | flops 196608 | bytes 1573248 | tf_op jit(solution)/shard_map/jit(_where)/select_n | solution.py:215
  64.4 20.4 %shard_map.87 = f32[2,960,128]{2,1,0:T(8,128)} custom-call(f32[16,128,384]{2,1,0:T(8,128)} %shard_map.86.x_ref, f32[4,128,384]{2,1,0:T(8,128)} %broadcast_select_fusion.1.top_ref, f32[4,128,384]{2,1,0:T(8,128)} %broadcast_select_fusion.bot_ref, f32[24,8,384]{2,1,0:T(8,128)} %pad_maximum_fusion.left_ref, f32[24,8,384]{2,1,0:T(8,128)} %pad_maximum_fusion.1.right_ref), custom_call_target="tpu_custom_call" | custom-call | tf_op jit(solution)/shard_map/pallas_call | solution.py:138
  (22 shorter events, 0.4 us)
Async XLA Ops:
  1.4 4.5 %collective-permute-start = (f32[2,16,128]{2,1,0:T(8,128)S(1)}, f32[2,16,128]{2,1,0:T(8,128)S(1)}, u32[]{:S(2)}, u32[]{:S(2)}) collective-permute-start(f32[2,16,128]{2,1,0:T(8,128)S(1)} %pad_maximum_fusion.6), channel_id=1, source_target_pairs={{0,256},{256,0},{1,257},{257,1},{2,258},{258,2},{3,259},{259,3},{4... | collective-permute-start | bytes 49160 | tf_op jit(solution)/shard_map/ppermute | solution.py:203
  13.6 22.2 %collective-permute-start.3 = (f32[16,8,384]{2,1,0:T(8,128)S(1)}, f32[16,8,384]{2,1,0:T(8,128)S(1)}, u32[]{:S(2)}, u32[]{:S(2)}) collective-permute-start(f32[16,8,384]{2,1,0:T(8,128)S(1)} %get-tuple-element.94), channel_id=1, source_target_pairs={{0,1},{1,2},{2,3},{3,4},{4,5},{5,6},{6,7},{7,8},{8,9},{9,10},{10,1... | collective-permute-start | bytes 589832 | tf_op jit(solution)/shard_map/ppermute | solution.py:23
  16.8 19.1 %collective-permute-start.4 = (f32[16,8,384]{2,1,0:T(8,128)S(1)}, f32[16,8,384]{2,1,0:T(8,128)S(1)}, u32[]{:S(2)}, u32[]{:S(2)}) collective-permute-start(f32[16,8,384]{2,1,0:T(8,128)S(1)} %get-tuple-element.95), channel_id=1, source_target_pairs={{0,31},{1,0},{2,1},{3,2},{4,3},{5,4},{6,5},{7,6},{8,7},{9,8},{10,9... | collective-permute-start | bytes 589832 | tf_op jit(solution)/shard_map/ppermute | solution.py:23
  29.1 33.3 %collective-permute-start.2 = (f32[4,128,384]{2,1,0:T(8,128)S(1)}, f32[4,128,384]{2,1,0:T(8,128)S(1)}, u32[]{:S(2)}, u32[]{:S(2)}) collective-permute-start(f32[4,128,384]{2,1,0:T(8,128)S(1)} %get-tuple-element.96), channel_id=1, source_target_pairs={{32,0},{64,32},{96,64},{128,96},{160,128},{192,160},{224,192},{33,... | collective-permute-start | bytes 2359304 | tf_op jit(solution)/shard_map/ppermute | solution.py:23
  33.9 29.5 %collective-permute-start.1 = (f32[4,128,384]{2,1,0:T(8,128)S(1)}, f32[4,128,384]{2,1,0:T(8,128)S(1)}, u32[]{:S(2)}, u32[]{:S(2)}) collective-permute-start(f32[4,128,384]{2,1,0:T(8,128)S(1)} %get-tuple-element.97), channel_id=1, source_target_pairs={{0,32},{32,64},{64,96},{96,128},{128,160},{160,192},{192,224},{1,3... | collective-permute-start | bytes 2359304 | tf_op jit(solution)/shard_map/ppermute | solution.py:23
  35.9 17.3 %collective-permute-start.6 = (f32[4,16,384]{2,1,0:T(8,128)S(1)}, f32[4,16,384]{2,1,0:T(8,128)S(1)}, u32[]{:S(2)}, u32[]{:S(2)}) collective-permute-start(f32[4,16,384]{2,1,0:T(8,128)S(1)} %pad_maximum_fusion.3), channel_id=1, source_target_pairs={{32,0},{64,32},{96,64},{128,96},{160,128},{192,160},{224,192},{33,... | collective-permute-start | bytes 294920 | tf_op jit(solution)/shard_map/ppermute | solution.py:23
  43.4 17.4 %collective-permute-start.5 = (f32[4,16,384]{2,1,0:T(8,128)S(1)}, f32[4,16,384]{2,1,0:T(8,128)S(1)}, u32[]{:S(2)}, u32[]{:S(2)}) collective-permute-start(f32[4,16,384]{2,1,0:T(8,128)S(1)} %pad_maximum_fusion.2), channel_id=1, source_target_pairs={{0,32},{32,64},{64,96},{96,128},{128,160},{160,192},{192,224},{1,3... | collective-permute-start | bytes 294920 | tf_op jit(solution)/shard_map/ppermute | solution.py:23

commit v14 on v11

--- a/solution.py
+++ b/solution.py
@@ -213,15 +213,15 @@
     section = lax.axis_index("sec")
     sea = sea_mask[0].astype(jnp.float32)
     wet = jnp.where(section == 1, sea, jnp.ones_like(sea))
-    surface = tracers[:, 0]
+    surface = jnp.stack([tracers[f, 0] for f in range(fields)])
     partner = lax.ppermute(surface, "sec", [(0, 1), (1, 0)])
 
     regridded = regrid(partner, regrid_map[0])
     flux = exchange_rate[0] * sea * (regridded - surface)
 
+    x, last, first, east, west = pack(tracers, zonal[0], meridional[0], mixing[0], wet, flux, SUB)
+
     width = SUB
-    x, last, first, east, west = pack(tracers, zonal[0], meridional[0], mixing[0], wet, flux, width)
-
     row_block = lax.axis_index("lat")
     wet_lane = lax.broadcasted_iota(jnp.int32, (1, 1, 3 * LANES), 2) >= 2 * LANES + HALF
     top_mask = jnp.logical_and(wet_lane, row_block == 0)

time: 87 us -> 86.5 us (level)
    unnamed x1 -> x0, local copies, waits for them, and re-layouts: 1.33 us -> none
where the time goes in v14:
time: 86.5 us; the launch traced here: 85.9 us
  starting transfers between devices  46 us (53%)
  Pallas kernels  25.4 us (29%)
  other arithmetic  8.27 us (10%)
  waiting for transfers between devices  4.58 us (5%)
  between operations  0.9 us (1%)
    ppermute x6, starting transfers between devices, shifted(): return lax.ppermute(x, axis, pairs)  44.1 us
    pallas_call x1, Pallas kernels, run_steps(): pl.pallas_call(functools.partial(steps_kernel, levels=levels, width=width...  20.4 us
    pallas_call x1, Pallas kernels, pack(): pl.pallas_call(functools.partial(pack_kernel, levels=levels, width=width)...  4.96 us
    ppermute x6, waiting for transfers between devices, shifted(): return lax.ppermute(x, axis, pairs)  4.58 us
    mul x2, other arithmetic, shards(): flux = exchange_rate[0] * sea * (regridded - surface)  3.1 us
    ppermute x1, starting transfers between devices, shards(): partner = lax.ppermute(surface, 'sec', [(0, 1), (1, 0)])  1.91 us
  transfers between devices with their start and end apart: 7, of which 2 were waited for; matrix products, arithmetic and copies ran while one was open for 6% of the time, Pallas kernels for 0%

profile of v14, /device:TPU:2, one launch (start us, length us, event | category | flops | bytes accessed | tf_op | source)
XLA Modules:
  0.0 85.9 jit_solution(5100296048705674388)
XLA Ops:
  0.6 0.7 slice_bitcast_fusion.1
  1.4 1.9 %collective-permute-start = (f32[2,16,128]{2,1,0:T(8,128)S(1)}, f32[2,16,128]{2,1,0:T(8,128)S(1)}, u32[]{:S(2)}, u32[]{:S(2)}) collective-permute-start(f32[2,16,128]{2,1,0:T(8,128)S(1)} %pad_maximum_fusion.6), channel_id=1, source_target_pairs={{0,256},{256,0},{1,257},{257,1},{2,258},{258,2},{3,259},{259,3},{4... | collective-permute-start | bytes 49160 | tf_op jit(solution)/shard_map/ppermute | solution.py:217
  3.3 0.8 compare_select_fusion
  4.1 0.1 and_bitcast_fusion.27
  4.5 1.3 %multiply_bitcast_fusion = (f32[16,128]{1,0:T(8,128)S(1)}, f32[16,128]{1,0:T(8,128)}) fusion(f32[1,16,128]{2,1,0:T(8,128)} %param.11, s32[1,16,128]{2,1,0:T(8,128)} %param.12, pred[]{:T(512)S(6)} %eq.667), kind=kLoop, calls=%fused_computation.229 | loop fusion | flops 6144 | bytes 32769 | tf_op jit(solution)/shard_map/mul | solution.py:220
  5.8 0.0 collective-permute-done
  5.8 0.1 fusion.6
  5.9 0.1 fusion.11
  6.0 0.1 fusion.10
  6.1 0.1 fusion.9
  6.2 0.1 fusion.8
  6.3 0.1 fusion.7
  6.4 1.8 %subtract_multiply_fusion.flux_ref = f32[2,16,128]{2,1,0:T(8,128)} fusion(f32[2,16,128]{2,1,0:T(8,128)S(1)} %collective-permute-done, f32[2,2,128]{2,1,0:T(2,128)S(1)} %reshape.27, f32[2,16,3]{2,1,0:T(8,128)S(1)} %get-tuple-element.235, f32[2,16,3]{2,1,0:T(8,128)S(1)} %get-tuple-element.294, f32[2,16,125]{2,1,0:T(8,128)S(1)} %get-tuple-element.290, ...), kind=kLoop, calls=%fused_computation.205 | loop fusion | flops 749568 | bytes 807680 | tf_op jit(solution)/shard_map/mul | solution.py:220
  8.2 5.0 %shard_map.86 = (f32[16,128,384]{2,1,0:T(8,128)}, f32[4,128,384]{2,1,0:T(8,128)}, f32[4,128,384]{2,1,0:T(8,128)}, f32[16,8,384]{2,1,0:T(8,128)}, f32[16,8,384]{2,1,0:T(8,128)}) custom-call(f32[2,960,128]{2,1,0:T(8,128)} %bitcast.324, f32[960,128]{1,0:T(8,128)} %bitcast.326, f32[960,128]{1,0:T(8,128)} %bitcast.327, f32[960,128]{1,0:T(8,128)} %bitcast.328, ...), custom_call_target="tpu_custom_call" | custom-call | tf_op jit(solution)/shard_map/pallas_call | solution.py:185
  13.2 3.5 %collective-permute-start.3 = (f32[16,8,384]{2,1,0:T(8,128)}, f32[16,8,384]{2,1,0:T(8,128)S(1)}, u32[]{:S(2)}, u32[]{:S(2)}) collective-permute-start(f32[16,8,384]{2,1,0:T(8,128)} %get-tuple-element.10), channel_id=1, source_target_pairs={{0,1},{1,2},{2,3},{3,4},{4,5},{5,6},{6,7},{7,8},{8,9},{9,10},{10,1... | collective-permute-start | bytes 589832 | tf_op jit(solution)/shard_map/ppermute | solution.py:23
  16.7 10.9 %collective-permute-start.4 = (f32[16,8,384]{2,1,0:T(8,128)}, f32[16,8,384]{2,1,0:T(8,128)S(1)}, u32[]{:S(2)}, u32[]{:S(2)}) collective-permute-start(f32[16,8,384]{2,1,0:T(8,128)} %get-tuple-element.11), channel_id=1, source_target_pairs={{0,31},{1,0},{2,1},{3,2},{4,3},{5,4},{6,5},{7,6},{8,7},{9,8},{10,9... | collective-permute-start | bytes 589832 | tf_op jit(solution)/shard_map/ppermute | solution.py:23
  27.6 3.4 %collective-permute-start.1 = (f32[4,128,384]{2,1,0:T(8,128)}, f32[4,128,384]{2,1,0:T(8,128)S(1)}, u32[]{:S(2)}, u32[]{:S(2)}) collective-permute-start(f32[4,128,384]{2,1,0:T(8,128)} %get-tuple-element.8), channel_id=1, source_target_pairs={{0,32},{32,64},{64,96},{96,128},{128,160},{160,192},{192,224},{1,3... | collective-permute-start | bytes 2359304 | tf_op jit(solution)/shard_map/ppermute | solution.py:23
  31.0 2.5 %collective-permute-start.2 = (f32[4,128,384]{2,1,0:T(8,128)}, f32[4,128,384]{2,1,0:T(8,128)S(1)}, u32[]{:S(2)}, u32[]{:S(2)}) collective-permute-start(f32[4,128,384]{2,1,0:T(8,128)} %get-tuple-element.9), channel_id=1, source_target_pairs={{32,0},{64,32},{96,64},{128,96},{160,128},{192,160},{224,192},{33,... | collective-permute-start | bytes 2359304 | tf_op jit(solution)/shard_map/ppermute | solution.py:23
  33.5 0.0 collective-permute-done.3
  33.5 0.0 collective-permute-done.4
  33.5 22.0 %collective-permute-start.6 = (f32[4,16,384]{2,1,0:T(8,128)S(1)}, f32[4,16,384]{2,1,0:T(8,128)S(1)}, u32[]{:S(2)}, u32[]{:S(2)}) collective-permute-start(f32[4,16,384]{2,1,0:T(8,128)S(1)} %pad_maximum_fusion.3), channel_id=1, source_target_pairs={{32,0},{64,32},{96,64},{128,96},{160,128},{192,160},{224,192},{33,... | collective-permute-start | bytes 294920 | tf_op jit(solution)/shard_map/ppermute | solution.py:23
  55.6 1.9 %collective-permute-start.5 = (f32[4,16,384]{2,1,0:T(8,128)S(1)}, f32[4,16,384]{2,1,0:T(8,128)S(1)}, u32[]{:S(2)}, u32[]{:S(2)}) collective-permute-start(f32[4,16,384]{2,1,0:T(8,128)S(1)} %pad_maximum_fusion.2), channel_id=1, source_target_pairs={{0,32},{32,64},{64,96},{96,128},{128,160},{160,192},{192,224},{1,3... | collective-permute-start | bytes 294920 | tf_op jit(solution)/shard_map/ppermute | solution.py:23
  57.5 0.2 collective-permute-done.6
  57.8 4.3 %collective-permute-done.5 = f32[4,16,384]{2,1,0:T(8,128)S(1)} collective-permute-done((f32[4,16,384]{2,1,0:T(8,128)S(1)}, f32[4,16,384]{2,1,0:T(8,128)S(1)}, u32[]{:S(2)}, u32[]{:S(2)}) %collective-permute-start.5) | collective-permute-done | bytes 98336 | tf_op jit(solution)/shard_map/ppermute | solution.py:23
  62.1 0.8 pad_maximum_fusion.1.right_ref
  62.9 0.7 pad_maximum_fusion.left_ref
  63.6 0.0 collective-permute-done.1
  63.6 0.9 %broadcast_select_fusion.1.top_ref = f32[4,128,384]{2,1,0:T(8,128)} fusion(f32[4,128,384]{2,1,0:T(8,128)S(1)} %collective-permute-done.1, pred[384]{0:T(512)(128)(4,1)S(1)} %fusion.79), kind=kLoop, calls=%fused_computation.1 | loop fusion | flops 196608 | bytes 1573248 | tf_op jit(solution)/shard_map/jit(_where)/select_n | solution.py:229
  64.6 0.0 collective-permute-done.2
  64.6 0.9 %broadcast_select_fusion.bot_ref = f32[4,128,384]{2,1,0:T(8,128)} fusion(f32[4,128,384]{2,1,0:T(8,128)S(1)} %collective-permute-done.2, pred[384]{0:T(512)(128)(4,1)S(1)} %fusion.78), kind=kLoop, calls=%fused_computation | loop fusion | flops 196608 | bytes 1573248 | tf_op jit(solution)/shard_map/jit(_where)/select_n | solution.py:230
  65.5 20.4 %shard_map.87 = f32[2,960,128]{2,1,0:T(8,128)} custom-call(f32[16,128,384]{2,1,0:T(8,128)} %get-tuple-element.7.x_ref, f32[4,128,384]{2,1,0:T(8,128)} %broadcast_select_fusion.1.top_ref, f32[4,128,384]{2,1,0:T(8,128)} %broadcast_select_fusion.bot_ref, f32[24,8,384]{2,1,0:T(8,128)} %pad_maximum_fusion.left_ref, f32[24,8,384]{2,1,0:T(8,128)} %pad_maximum_fusion.1.right_ref), custom_call_target="tpu_custom_call" | custom-call | tf_op jit(solution)/shard_map/pallas_call | solution.py:138
  (21 shorter events, 0.4 us)
Async XLA Ops:
  1.4 4.4 %collective-permute-start = (f32[2,16,128]{2,1,0:T(8,128)S(1)}, f32[2,16,128]{2,1,0:T(8,128)S(1)}, u32[]{:S(2)}, u32[]{:S(2)}) collective-permute-start(f32[2,16,128]{2,1,0:T(8,128)S(1)} %pad_maximum_fusion.6), channel_id=1, source_target_pairs={{0,256},{256,0},{1,257},{257,1},{2,258},{258,2},{3,259},{259,3},{4... | collective-permute-start | bytes 49160 | tf_op jit(solution)/shard_map/ppermute | solution.py:217
  13.2 20.3 %collective-permute-start.3 = (f32[16,8,384]{2,1,0:T(8,128)}, f32[16,8,384]{2,1,0:T(8,128)S(1)}, u32[]{:S(2)}, u32[]{:S(2)}) collective-permute-start(f32[16,8,384]{2,1,0:T(8,128)} %get-tuple-element.10), channel_id=1, source_target_pairs={{0,1},{1,2},{2,3},{3,4},{4,5},{5,6},{6,7},{7,8},{8,9},{9,10},{10,1... | collective-permute-start | bytes 589832 | tf_op jit(solution)/shard_map/ppermute | solution.py:23
  16.7 16.8 %collective-permute-start.4 = (f32[16,8,384]{2,1,0:T(8,128)}, f32[16,8,384]{2,1,0:T(8,128)S(1)}, u32[]{:S(2)}, u32[]{:S(2)}) collective-permute-start(f32[16,8,384]{2,1,0:T(8,128)} %get-tuple-element.11), channel_id=1, source_target_pairs={{0,31},{1,0},{2,1},{3,2},{4,3},{5,4},{6,5},{7,6},{8,7},{9,8},{10,9... | collective-permute-start | bytes 589832 | tf_op jit(solution)/shard_map/ppermute | solution.py:23
  27.6 36.1 %collective-permute-start.1 = (f32[4,128,384]{2,1,0:T(8,128)}, f32[4,128,384]{2,1,0:T(8,128)S(1)}, u32[]{:S(2)}, u32[]{:S(2)}) collective-permute-start(f32[4,128,384]{2,1,0:T(8,128)} %get-tuple-element.8), channel_id=1, source_target_pairs={{0,32},{32,64},{64,96},{96,128},{128,160},{160,192},{192,224},{1,3... | collective-permute-start | bytes 2359304 | tf_op jit(solution)/shard_map/ppermute | solution.py:23
  31.0 33.6 %collective-permute-start.2 = (f32[4,128,384]{2,1,0:T(8,128)}, f32[4,128,384]{2,1,0:T(8,128)S(1)}, u32[]{:S(2)}, u32[]{:S(2)}) collective-permute-start(f32[4,128,384]{2,1,0:T(8,128)} %get-tuple-element.9), channel_id=1, source_target_pairs={{32,0},{64,32},{96,64},{128,96},{160,128},{192,160},{224,192},{33,... | collective-permute-start | bytes 2359304 | tf_op jit(solution)/shard_map/ppermute | solution.py:23
  33.5 24.2 %collective-permute-start.6 = (f32[4,16,384]{2,1,0:T(8,128)S(1)}, f32[4,16,384]{2,1,0:T(8,128)S(1)}, u32[]{:S(2)}, u32[]{:S(2)}) collective-permute-start(f32[4,16,384]{2,1,0:T(8,128)S(1)} %pad_maximum_fusion.3), channel_id=1, source_target_pairs={{32,0},{64,32},{96,64},{128,96},{160,128},{192,160},{224,192},{33,... | collective-permute-start | bytes 294920 | tf_op jit(solution)/shard_map/ppermute | solution.py:23
  55.6 6.5 %collective-permute-start.5 = (f32[4,16,384]{2,1,0:T(8,128)S(1)}, f32[4,16,384]{2,1,0:T(8,128)S(1)}, u32[]{:S(2)}, u32[]{:S(2)}) collective-permute-start(f32[4,16,384]{2,1,0:T(8,128)S(1)} %pad_maximum_fusion.2), channel_id=1, source_target_pairs={{0,32},{32,64},{64,96},{96,128},{128,160},{160,192},{192,224},{1,3... | collective-permute-start | bytes 294920 | tf_op jit(solution)/shard_map/ppermute | solution.py:23

commit v15 on v13

--- a/solution.py
+++ b/solution.py
@@ -116,7 +116,7 @@
             dst[r] = jnp.where(level0, updated + fl_ref[r], updated)
             return carry
 
-        lax.fori_loop(k + 1, ext_rows - 1 - k, body, 0)
+        lax.fori_loop(k + 1, ext_rows - 1 - k, body, 0, unroll=2)
 
     for k in range(SUB):
         if k % 2 == 0:

time: 85.4 us -> 80.3 us (0.940)
  Pallas kernels: 24.7 us -> 19.6 us
    pallas_call x1, Pallas kernels: 20.4 us -> 15.4 us  [run_steps(): pl.pallas_call(functools.partial(steps_kernel, levels=levels, width=width...]
where the time goes in v15:
time: 80.3 us; the launch traced here: 79.7 us
  starting transfers between devices  32.1 us (40%)
  Pallas kernels  19.6 us (24%)
  waiting for transfers between devices  15.5 us (19%)
  other arithmetic  8.31 us (10%)
  local copies, waits for them, and re-layouts  3.3 us (4%)
  between operations  0.93 us (1%)
    ppermute x6, starting transfers between devices, shifted(): return lax.ppermute(x, axis, pairs)  30.2 us
    ppermute x6, waiting for transfers between devices, shifted(): return lax.ppermute(x, axis, pairs)  15.5 us
    pallas_call x1, Pallas kernels, run_steps(): pl.pallas_call(functools.partial(steps_kernel, levels=levels, width=width...  15.4 us
    pallas_call x1, Pallas kernels, pack(): pl.pallas_call(functools.partial(pack_kernel, levels=levels), out_shape=j...  4.25 us
    mul x2, other arithmetic, shards(): flux = exchange_rate[0] * sea * (regridded - surface)  3.12 us
    ppermute x1, starting transfers between devices, shards(): partner = lax.ppermute(surface, 'sec', [(0, 1), (1, 0)])  1.91 us
  transfers between devices with their start and end apart: 7, of which 2 were waited for; matrix products, arithmetic and copies ran while one was open for 8% of the time, Pallas kernels for 0%

profile of v15, /device:TPU:16, one launch (start us, length us, event | category | flops | bytes accessed | tf_op | source)
XLA Modules:
  0.0 79.7 jit_solution(7908726100861379906)
XLA Ops:
  0.6 0.7 slice_bitcast_fusion.1
  1.4 1.9 %collective-permute-start = (f32[2,16,128]{2,1,0:T(8,128)S(1)}, f32[2,16,128]{2,1,0:T(8,128)S(1)}, u32[]{:S(2)}, u32[]{:S(2)}) collective-permute-start(f32[2,16,128]{2,1,0:T(8,128)S(1)} %pad_maximum_fusion.6), channel_id=1, source_target_pairs={{0,256},{256,0},{1,257},{257,1},{2,258},{258,2},{3,259},{259,3},{4... | collective-permute-start | bytes 49160 | tf_op jit(solution)/shard_map/ppermute | solution.py:203
  3.3 0.8 %compare_select_fusion = (s32[4,16,128]{2,1,0:T(8,128)S(1)}, s32[4,16,128]{2,1,0:T(8,128)S(1)}) fusion(s32[1,4,16,128]{3,2,1,0:T(8,128)} %param.13), kind=kLoop, calls=%fused_computation.56 | loop fusion | flops 221184 | bytes 98304 | tf_op jit(solution)/shard_map/jit(_where)/select_n | solution.py:33
  4.2 1.3 %multiply_bitcast_fusion = (f32[16,128]{1,0:T(8,128)S(1)}, f32[16,128]{1,0:T(8,128)}) fusion(f32[1,16,128]{2,1,0:T(8,128)} %param.11, s32[1,16,128]{2,1,0:T(8,128)} %param.12, pred[]{:T(512)S(6)} %eq.667), kind=kLoop, calls=%fused_computation.229 | loop fusion | flops 6144 | bytes 32769 | tf_op jit(solution)/shard_map/mul | solution.py:206
  5.8 0.0 collective-permute-done
  5.9 0.1 fusion.6
  6.0 0.1 fusion.11
  6.1 0.1 fusion.10
  6.2 0.1 fusion.9
  6.3 0.1 fusion.8
  6.4 0.1 fusion.7
  6.5 1.8 %subtract_multiply_fusion.flux_ref = f32[2,16,128]{2,1,0:T(8,128)} fusion(f32[2,16,128]{2,1,0:T(8,128)S(1)} %collective-permute-done, f32[2,2,128]{2,1,0:T(2,128)S(1)} %reshape.27, f32[2,16,3]{2,1,0:T(8,128)S(1)} %get-tuple-element.229, f32[2,16,3]{2,1,0:T(8,128)S(1)} %get-tuple-element.288, f32[2,16,125]{2,1,0:T(8,128)S(1)} %get-tuple-element.284, ...), kind=kLoop, calls=%fused_computation.205 | loop fusion | flops 749568 | bytes 807680 | tf_op jit(solution)/shard_map/mul | solution.py:206
  8.3 4.3 %shard_map.86.x_ref = f32[16,128,384]{2,1,0:T(8,128)} custom-call(f32[2,960,128]{2,1,0:T(8,128)} %bitcast.324, f32[960,128]{1,0:T(8,128)} %bitcast.326, f32[960,128]{1,0:T(8,128)} %bitcast.327, f32[960,128]{1,0:T(8,128)} %bitcast.328, f32[16,128]{1,0:T(8,128)} %get-tuple-element.317.wet_ref, f32[2,16,128]{2,1,0:T(8,128)} %subtract_multiply_fusion.flux_ref), custom_call_target="tpu_custom_call" | custom-call | tf_op jit(solution)/shard_map/pallas_call | solution.py:177
  12.5 1.0 %fusion.80 = (f32[16,8,384]{2,1,0:T(8,128)S(1)}, f32[16,8,384]{2,1,0:T(8,128)S(1)}) fusion(f32[16,128,384]{2,1,0:T(8,128)} %shard_map.86.x_ref), kind=kLoop, calls=%fused_computation.422 | loop fusion | bytes 786432 | tf_op jit(solution)/shard_map/slice | solution.py:217
  13.6 3.2 %collective-permute-start.3 = (f32[16,8,384]{2,1,0:T(8,128)S(1)}, f32[16,8,384]{2,1,0:T(8,128)S(1)}, u32[]{:S(2)}, u32[]{:S(2)}) collective-permute-start(f32[16,8,384]{2,1,0:T(8,128)S(1)} %get-tuple-element.94), channel_id=1, source_target_pairs={{0,1},{1,2},{2,3},{3,4},{4,5},{5,6},{6,7},{7,8},{8,9},{9,10},{10,1... | collective-permute-start | bytes 589832 | tf_op jit(solution)/shard_map/ppermute | solution.py:23
  16.8 10.9 %collective-permute-start.4 = (f32[16,8,384]{2,1,0:T(8,128)S(1)}, f32[16,8,384]{2,1,0:T(8,128)S(1)}, u32[]{:S(2)}, u32[]{:S(2)}) collective-permute-start(f32[16,8,384]{2,1,0:T(8,128)S(1)} %get-tuple-element.95), channel_id=1, source_target_pairs={{0,31},{1,0},{2,1},{3,2},{4,3},{5,4},{6,5},{7,6},{8,7},{9,8},{10,9... | collective-permute-start | bytes 589832 | tf_op jit(solution)/shard_map/ppermute | solution.py:23
  27.7 1.5 %fusion.81 = (f32[4,128,384]{2,1,0:T(8,128)S(1)}, f32[4,128,384]{2,1,0:T(8,128)S(1)}) fusion(f32[16,128,384]{2,1,0:T(8,128)} %shard_map.86.x_ref), kind=kLoop, calls=%fused_computation.423 | loop fusion | bytes 3145728 | tf_op jit(solution)/shard_map/slice | solution.py:216
  29.1 4.7 %collective-permute-start.2 = (f32[4,128,384]{2,1,0:T(8,128)S(1)}, f32[4,128,384]{2,1,0:T(8,128)S(1)}, u32[]{:S(2)}, u32[]{:S(2)}) collective-permute-start(f32[4,128,384]{2,1,0:T(8,128)S(1)} %get-tuple-element.96), channel_id=1, source_target_pairs={{32,0},{64,32},{96,64},{128,96},{160,128},{192,160},{224,192},{33,... | collective-permute-start | bytes 2359304 | tf_op jit(solution)/shard_map/ppermute | solution.py:23
  33.9 1.9 %collective-permute-start.1 = (f32[4,128,384]{2,1,0:T(8,128)S(1)}, f32[4,128,384]{2,1,0:T(8,128)S(1)}, u32[]{:S(2)}, u32[]{:S(2)}) collective-permute-start(f32[4,128,384]{2,1,0:T(8,128)S(1)} %get-tuple-element.97), channel_id=1, source_target_pairs={{0,32},{32,64},{64,96},{96,128},{128,160},{160,192},{192,224},{1,3... | collective-permute-start | bytes 2359304 | tf_op jit(solution)/shard_map/ppermute | solution.py:23
  35.8 0.0 collective-permute-done.3
  35.8 0.0 collective-permute-done.4
  35.9 7.5 %collective-permute-start.6 = (f32[4,16,384]{2,1,0:T(8,128)S(1)}, f32[4,16,384]{2,1,0:T(8,128)S(1)}, u32[]{:S(2)}, u32[]{:S(2)}) collective-permute-start(f32[4,16,384]{2,1,0:T(8,128)S(1)} %pad_maximum_fusion.3), channel_id=1, source_target_pairs={{32,0},{64,32},{96,64},{128,96},{160,128},{192,160},{224,192},{33,... | collective-permute-start | bytes 294920 | tf_op jit(solution)/shard_map/ppermute | solution.py:23
  43.4 1.9 %collective-permute-start.5 = (f32[4,16,384]{2,1,0:T(8,128)S(1)}, f32[4,16,384]{2,1,0:T(8,128)S(1)}, u32[]{:S(2)}, u32[]{:S(2)}) collective-permute-start(f32[4,16,384]{2,1,0:T(8,128)S(1)} %pad_maximum_fusion.2), channel_id=1, source_target_pairs={{0,32},{32,64},{64,96},{96,128},{128,160},{160,192},{192,224},{1,3... | collective-permute-start | bytes 294920 | tf_op jit(solution)/shard_map/ppermute | solution.py:23
  45.4 7.8 %collective-permute-done.6 = f32[4,16,384]{2,1,0:T(8,128)S(1)} collective-permute-done((f32[4,16,384]{2,1,0:T(8,128)S(1)}, f32[4,16,384]{2,1,0:T(8,128)S(1)}, u32[]{:S(2)}, u32[]{:S(2)}) %collective-permute-start.6) | collective-permute-done | bytes 98336 | tf_op jit(solution)/shard_map/ppermute | solution.py:23
  53.2 7.7 %collective-permute-done.5 = f32[4,16,384]{2,1,0:T(8,128)S(1)} collective-permute-done((f32[4,16,384]{2,1,0:T(8,128)S(1)}, f32[4,16,384]{2,1,0:T(8,128)S(1)}, u32[]{:S(2)}, u32[]{:S(2)}) %collective-permute-start.5) | collective-permute-done | bytes 98336 | tf_op jit(solution)/shard_map/ppermute | solution.py:23
  60.9 0.8 pad_maximum_fusion.1.right_ref
  61.7 0.8 pad_maximum_fusion.left_ref
  62.5 0.0 collective-permute-done.2
  62.5 1.0 %broadcast_select_fusion.bot_ref = f32[4,128,384]{2,1,0:T(8,128)} fusion(f32[4,128,384]{2,1,0:T(8,128)S(1)} %collective-permute-done.2, pred[384]{0:T(512)(128)(4,1)S(1)} %fusion.78), kind=kLoop, calls=%fused_computation | loop fusion | flops 196608 | bytes 1573248 | tf_op jit(solution)/shard_map/jit(_where)/select_n | solution.py:216
  63.4 0.0 collective-permute-done.1
  63.4 0.9 %broadcast_select_fusion.1.top_ref = f32[4,128,384]{2,1,0:T(8,128)} fusion(f32[4,128,384]{2,1,0:T(8,128)S(1)} %collective-permute-done.1, pred[384]{0:T(512)(128)(4,1)S(1)} %fusion.79), kind=kLoop, calls=%fused_computation.1 | loop fusion | flops 196608 | bytes 1573248 | tf_op jit(solution)/shard_map/jit(_where)/select_n | solution.py:215
  64.4 15.4 %shard_map.87 = f32[2,960,128]{2,1,0:T(8,128)} custom-call(f32[16,128,384]{2,1,0:T(8,128)} %shard_map.86.x_ref, f32[4,128,384]{2,1,0:T(8,128)} %broadcast_select_fusion.1.top_ref, f32[4,128,384]{2,1,0:T(8,128)} %broadcast_select_fusion.bot_ref, f32[24,8,384]{2,1,0:T(8,128)} %pad_maximum_fusion.left_ref, f32[24,8,384]{2,1,0:T(8,128)} %pad_maximum_fusion.1.right_ref), custom_call_target="tpu_custom_call" | custom-call | tf_op jit(solution)/shard_map/pallas_call | solution.py:138
  (22 shorter events, 0.4 us)
Async XLA Ops:
  1.4 4.5 %collective-permute-start = (f32[2,16,128]{2,1,0:T(8,128)S(1)}, f32[2,16,128]{2,1,0:T(8,128)S(1)}, u32[]{:S(2)}, u32[]{:S(2)}) collective-permute-start(f32[2,16,128]{2,1,0:T(8,128)S(1)} %pad_maximum_fusion.6), channel_id=1, source_target_pairs={{0,256},{256,0},{1,257},{257,1},{2,258},{258,2},{3,259},{259,3},{4... | collective-permute-start | bytes 49160 | tf_op jit(solution)/shard_map/ppermute | solution.py:203
  13.6 22.2 %collective-permute-start.3 = (f32[16,8,384]{2,1,0:T(8,128)S(1)}, f32[16,8,384]{2,1,0:T(8,128)S(1)}, u32[]{:S(2)}, u32[]{:S(2)}) collective-permute-start(f32[16,8,384]{2,1,0:T(8,128)S(1)} %get-tuple-element.94), channel_id=1, source_target_pairs={{0,1},{1,2},{2,3},{3,4},{4,5},{5,6},{6,7},{7,8},{8,9},{9,10},{10,1... | collective-permute-start | bytes 589832 | tf_op jit(solution)/shard_map/ppermute | solution.py:23
  16.8 19.1 %collective-permute-start.4 = (f32[16,8,384]{2,1,0:T(8,128)S(1)}, f32[16,8,384]{2,1,0:T(8,128)S(1)}, u32[]{:S(2)}, u32[]{:S(2)}) collective-permute-start(f32[16,8,384]{2,1,0:T(8,128)S(1)} %get-tuple-element.95), channel_id=1, source_target_pairs={{0,31},{1,0},{2,1},{3,2},{4,3},{5,4},{6,5},{7,6},{8,7},{9,8},{10,9... | collective-permute-start | bytes 589832 | tf_op jit(solution)/shard_map/ppermute | solution.py:23
  29.1 33.3 %collective-permute-start.2 = (f32[4,128,384]{2,1,0:T(8,128)S(1)}, f32[4,128,384]{2,1,0:T(8,128)S(1)}, u32[]{:S(2)}, u32[]{:S(2)}) collective-permute-start(f32[4,128,384]{2,1,0:T(8,128)S(1)} %get-tuple-element.96), channel_id=1, source_target_pairs={{32,0},{64,32},{96,64},{128,96},{160,128},{192,160},{224,192},{33,... | collective-permute-start | bytes 2359304 | tf_op jit(solution)/shard_map/ppermute | solution.py:23
  33.9 29.5 %collective-permute-start.1 = (f32[4,128,384]{2,1,0:T(8,128)S(1)}, f32[4,128,384]{2,1,0:T(8,128)S(1)}, u32[]{:S(2)}, u32[]{:S(2)}) collective-permute-start(f32[4,128,384]{2,1,0:T(8,128)S(1)} %get-tuple-element.97), channel_id=1, source_target_pairs={{0,32},{32,64},{64,96},{96,128},{128,160},{160,192},{192,224},{1,3... | collective-permute-start | bytes 2359304 | tf_op jit(solution)/shard_map/ppermute | solution.py:23
  35.9 17.3 %collective-permute-start.6 = (f32[4,16,384]{2,1,0:T(8,128)S(1)}, f32[4,16,384]{2,1,0:T(8,128)S(1)}, u32[]{:S(2)}, u32[]{:S(2)}) collective-permute-start(f32[4,16,384]{2,1,0:T(8,128)S(1)} %pad_maximum_fusion.3), channel_id=1, source_target_pairs={{32,0},{64,32},{96,64},{128,96},{160,128},{192,160},{224,192},{33,... | collective-permute-start | bytes 294920 | tf_op jit(solution)/shard_map/ppermute | solution.py:23
  43.4 17.4 %collective-permute-start.5 = (f32[4,16,384]{2,1,0:T(8,128)S(1)}, f32[4,16,384]{2,1,0:T(8,128)S(1)}, u32[]{:S(2)}, u32[]{:S(2)}) collective-permute-start(f32[4,16,384]{2,1,0:T(8,128)S(1)} %pad_maximum_fusion.2), channel_id=1, source_target_pairs={{0,32},{32,64},{64,96},{96,128},{128,160},{160,192},{192,224},{1,3... | collective-permute-start | bytes 294920 | tf_op jit(solution)/shard_map/ppermute | solution.py:23

commit v16 on v15

--- a/solution.py
+++ b/solution.py
@@ -116,7 +116,7 @@
             dst[r] = jnp.where(level0, updated + fl_ref[r], updated)
             return carry
 
-        lax.fori_loop(k + 1, ext_rows - 1 - k, body, 0, unroll=2)
+        lax.fori_loop(k + 1, ext_rows - 1 - k, body, 0, unroll=4)
 
     for k in range(SUB):
         if k % 2 == 0:

time: 80.3 us -> 79.2 us (0.986)
  Pallas kernels: 19.6 us -> 18.5 us
    pallas_call x1, Pallas kernels: 15.4 us -> 14.3 us  [run_steps(): pl.pallas_call(functools.partial(steps_kernel, levels=levels, width=width...]
where the time goes in v16:
time: 79.2 us; the launch traced here: 78.6 us
  starting transfers between devices  32.1 us (41%)
  Pallas kernels  18.5 us (23%)
  waiting for transfers between devices  15.5 us (20%)
  other arithmetic  8.31 us (10%)
  local copies, waits for them, and re-layouts  3.3 us (4%)
  between operations  0.93 us (1%)
    ppermute x6, starting transfers between devices, shifted(): return lax.ppermute(x, axis, pairs)  30.2 us
    ppermute x6, waiting for transfers between devices, shifted(): return lax.ppermute(x, axis, pairs)  15.5 us
    pallas_call x1, Pallas kernels, run_steps(): pl.pallas_call(functools.partial(steps_kernel, levels=levels, width=width...  14.3 us
    pallas_call x1, Pallas kernels, pack(): pl.pallas_call(functools.partial(pack_kernel, levels=levels), out_shape=j...  4.25 us
    mul x2, other arithmetic, shards(): flux = exchange_rate[0] * sea * (regridded - surface)  3.12 us
    ppermute x1, starting transfers between devices, shards(): partner = lax.ppermute(surface, 'sec', [(0, 1), (1, 0)])  1.91 us
  transfers between devices with their start and end apart: 7, of which 2 were waited for; matrix products, arithmetic and copies ran while one was open for 8% of the time, Pallas kernels for 0%

profile of v16, /device:TPU:16, one launch (start us, length us, event | category | flops | bytes accessed | tf_op | source)
XLA Modules:
  0.0 78.6 jit_solution(18120989161067648823)
XLA Ops:
  0.6 0.7 slice_bitcast_fusion.1
  1.4 1.9 %collective-permute-start = (f32[2,16,128]{2,1,0:T(8,128)S(1)}, f32[2,16,128]{2,1,0:T(8,128)S(1)}, u32[]{:S(2)}, u32[]{:S(2)}) collective-permute-start(f32[2,16,128]{2,1,0:T(8,128)S(1)} %pad_maximum_fusion.6), channel_id=1, source_target_pairs={{0,256},{256,0},{1,257},{257,1},{2,258},{258,2},{3,259},{259,3},{4... | collective-permute-start | bytes 49160 | tf_op jit(solution)/shard_map/ppermute | solution.py:203
  3.3 0.8 %compare_select_fusion = (s32[4,16,128]{2,1,0:T(8,128)S(1)}, s32[4,16,128]{2,1,0:T(8,128)S(1)}) fusion(s32[1,4,16,128]{3,2,1,0:T(8,128)} %param.13), kind=kLoop, calls=%fused_computation.56 | loop fusion | flops 221184 | bytes 98304 | tf_op jit(solution)/shard_map/jit(_where)/select_n | solution.py:33
  4.2 1.3 %multiply_bitcast_fusion = (f32[16,128]{1,0:T(8,128)S(1)}, f32[16,128]{1,0:T(8,128)}) fusion(f32[1,16,128]{2,1,0:T(8,128)} %param.11, s32[1,16,128]{2,1,0:T(8,128)} %param.12, pred[]{:T(512)S(6)} %eq.667), kind=kLoop, calls=%fused_computation.229 | loop fusion | flops 6144 | bytes 32769 | tf_op jit(solution)/shard_map/mul | solution.py:206
  5.8 0.0 collective-permute-done
  5.9 0.1 fusion.6
  6.0 0.1 fusion.11
  6.1 0.1 fusion.10
  6.2 0.1 fusion.9
  6.3 0.1 fusion.8
  6.4 0.1 fusion.7
  6.5 1.8 %subtract_multiply_fusion.flux_ref = f32[2,16,128]{2,1,0:T(8,128)} fusion(f32[2,16,128]{2,1,0:T(8,128)S(1)} %collective-permute-done, f32[2,2,128]{2,1,0:T(2,128)S(1)} %reshape.27, f32[2,16,3]{2,1,0:T(8,128)S(1)} %get-tuple-element.229, f32[2,16,3]{2,1,0:T(8,128)S(1)} %get-tuple-element.288, f32[2,16,125]{2,1,0:T(8,128)S(1)} %get-tuple-element.284, ...), kind=kLoop, calls=%fused_computation.205 | loop fusion | flops 749568 | bytes 807680 | tf_op jit(solution)/shard_map/mul | solution.py:206
  8.3 4.3 %shard_map.86.x_ref = f32[16,128,384]{2,1,0:T(8,128)} custom-call(f32[2,960,128]{2,1,0:T(8,128)} %bitcast.324, f32[960,128]{1,0:T(8,128)} %bitcast.326, f32[960,128]{1,0:T(8,128)} %bitcast.327, f32[960,128]{1,0:T(8,128)} %bitcast.328, f32[16,128]{1,0:T(8,128)} %get-tuple-element.317.wet_ref, f32[2,16,128]{2,1,0:T(8,128)} %subtract_multiply_fusion.flux_ref), custom_call_target="tpu_custom_call" | custom-call | tf_op jit(solution)/shard_map/pallas_call | solution.py:177
  12.5 1.0 %fusion.80 = (f32[16,8,384]{2,1,0:T(8,128)S(1)}, f32[16,8,384]{2,1,0:T(8,128)S(1)}) fusion(f32[16,128,384]{2,1,0:T(8,128)} %shard_map.86.x_ref), kind=kLoop, calls=%fused_computation.422 | loop fusion | bytes 786432 | tf_op jit(solution)/shard_map/slice | solution.py:217
  13.6 3.2 %collective-permute-start.3 = (f32[16,8,384]{2,1,0:T(8,128)S(1)}, f32[16,8,384]{2,1,0:T(8,128)S(1)}, u32[]{:S(2)}, u32[]{:S(2)}) collective-permute-start(f32[16,8,384]{2,1,0:T(8,128)S(1)} %get-tuple-element.94), channel_id=1, source_target_pairs={{0,1},{1,2},{2,3},{3,4},{4,5},{5,6},{6,7},{7,8},{8,9},{9,10},{10,1... | collective-permute-start | bytes 589832 | tf_op jit(solution)/shard_map/ppermute | solution.py:23
  16.8 10.9 %collective-permute-start.4 = (f32[16,8,384]{2,1,0:T(8,128)S(1)}, f32[16,8,384]{2,1,0:T(8,128)S(1)}, u32[]{:S(2)}, u32[]{:S(2)}) collective-permute-start(f32[16,8,384]{2,1,0:T(8,128)S(1)} %get-tuple-element.95), channel_id=1, source_target_pairs={{0,31},{1,0},{2,1},{3,2},{4,3},{5,4},{6,5},{7,6},{8,7},{9,8},{10,9... | collective-permute-start | bytes 589832 | tf_op jit(solution)/shard_map/ppermute | solution.py:23
  27.7 1.5 %fusion.81 = (f32[4,128,384]{2,1,0:T(8,128)S(1)}, f32[4,128,384]{2,1,0:T(8,128)S(1)}) fusion(f32[16,128,384]{2,1,0:T(8,128)} %shard_map.86.x_ref), kind=kLoop, calls=%fused_computation.423 | loop fusion | bytes 3145728 | tf_op jit(solution)/shard_map/slice | solution.py:216
  29.1 4.7 %collective-permute-start.2 = (f32[4,128,384]{2,1,0:T(8,128)S(1)}, f32[4,128,384]{2,1,0:T(8,128)S(1)}, u32[]{:S(2)}, u32[]{:S(2)}) collective-permute-start(f32[4,128,384]{2,1,0:T(8,128)S(1)} %get-tuple-element.96), channel_id=1, source_target_pairs={{32,0},{64,32},{96,64},{128,96},{160,128},{192,160},{224,192},{33,... | collective-permute-start | bytes 2359304 | tf_op jit(solution)/shard_map/ppermute | solution.py:23
  33.9 1.9 %collective-permute-start.1 = (f32[4,128,384]{2,1,0:T(8,128)S(1)}, f32[4,128,384]{2,1,0:T(8,128)S(1)}, u32[]{:S(2)}, u32[]{:S(2)}) collective-permute-start(f32[4,128,384]{2,1,0:T(8,128)S(1)} %get-tuple-element.97), channel_id=1, source_target_pairs={{0,32},{32,64},{64,96},{96,128},{128,160},{160,192},{192,224},{1,3... | collective-permute-start | bytes 2359304 | tf_op jit(solution)/shard_map/ppermute | solution.py:23
  35.8 0.0 collective-permute-done.3
  35.8 0.0 collective-permute-done.4
  35.9 7.5 %collective-permute-start.6 = (f32[4,16,384]{2,1,0:T(8,128)S(1)}, f32[4,16,384]{2,1,0:T(8,128)S(1)}, u32[]{:S(2)}, u32[]{:S(2)}) collective-permute-start(f32[4,16,384]{2,1,0:T(8,128)S(1)} %pad_maximum_fusion.3), channel_id=1, source_target_pairs={{32,0},{64,32},{96,64},{128,96},{160,128},{192,160},{224,192},{33,... | collective-permute-start | bytes 294920 | tf_op jit(solution)/shard_map/ppermute | solution.py:23
  43.4 1.9 %collective-permute-start.5 = (f32[4,16,384]{2,1,0:T(8,128)S(1)}, f32[4,16,384]{2,1,0:T(8,128)S(1)}, u32[]{:S(2)}, u32[]{:S(2)}) collective-permute-start(f32[4,16,384]{2,1,0:T(8,128)S(1)} %pad_maximum_fusion.2), channel_id=1, source_target_pairs={{0,32},{32,64},{64,96},{96,128},{128,160},{160,192},{192,224},{1,3... | collective-permute-start | bytes 294920 | tf_op jit(solution)/shard_map/ppermute | solution.py:23
  45.4 7.8 %collective-permute-done.6 = f32[4,16,384]{2,1,0:T(8,128)S(1)} collective-permute-done((f32[4,16,384]{2,1,0:T(8,128)S(1)}, f32[4,16,384]{2,1,0:T(8,128)S(1)}, u32[]{:S(2)}, u32[]{:S(2)}) %collective-permute-start.6) | collective-permute-done | bytes 98336 | tf_op jit(solution)/shard_map/ppermute | solution.py:23
  53.2 7.7 %collective-permute-done.5 = f32[4,16,384]{2,1,0:T(8,128)S(1)} collective-permute-done((f32[4,16,384]{2,1,0:T(8,128)S(1)}, f32[4,16,384]{2,1,0:T(8,128)S(1)}, u32[]{:S(2)}, u32[]{:S(2)}) %collective-permute-start.5) | collective-permute-done | bytes 98336 | tf_op jit(solution)/shard_map/ppermute | solution.py:23
  60.9 0.8 pad_maximum_fusion.1.right_ref
  61.7 0.8 pad_maximum_fusion.left_ref
  62.5 0.0 collective-permute-done.2
  62.5 1.0 %broadcast_select_fusion.bot_ref = f32[4,128,384]{2,1,0:T(8,128)} fusion(f32[4,128,384]{2,1,0:T(8,128)S(1)} %collective-permute-done.2, pred[384]{0:T(512)(128)(4,1)S(1)} %fusion.78), kind=kLoop, calls=%fused_computation | loop fusion | flops 196608 | bytes 1573248 | tf_op jit(solution)/shard_map/jit(_where)/select_n | solution.py:216
  63.4 0.0 collective-permute-done.1
  63.4 0.9 %broadcast_select_fusion.1.top_ref = f32[4,128,384]{2,1,0:T(8,128)} fusion(f32[4,128,384]{2,1,0:T(8,128)S(1)} %collective-permute-done.1, pred[384]{0:T(512)(128)(4,1)S(1)} %fusion.79), kind=kLoop, calls=%fused_computation.1 | loop fusion | flops 196608 | bytes 1573248 | tf_op jit(solution)/shard_map/jit(_where)/select_n | solution.py:215
  64.4 14.3 %shard_map.87 = f32[2,960,128]{2,1,0:T(8,128)} custom-call(f32[16,128,384]{2,1,0:T(8,128)} %shard_map.86.x_ref, f32[4,128,384]{2,1,0:T(8,128)} %broadcast_select_fusion.1.top_ref, f32[4,128,384]{2,1,0:T(8,128)} %broadcast_select_fusion.bot_ref, f32[24,8,384]{2,1,0:T(8,128)} %pad_maximum_fusion.left_ref, f32[24,8,384]{2,1,0:T(8,128)} %pad_maximum_fusion.1.right_ref), custom_call_target="tpu_custom_call" | custom-call | tf_op jit(solution)/shard_map/pallas_call | solution.py:138
  (22 shorter events, 0.4 us)
Async XLA Ops:
  1.4 4.5 %collective-permute-start = (f32[2,16,128]{2,1,0:T(8,128)S(1)}, f32[2,16,128]{2,1,0:T(8,128)S(1)}, u32[]{:S(2)}, u32[]{:S(2)}) collective-permute-start(f32[2,16,128]{2,1,0:T(8,128)S(1)} %pad_maximum_fusion.6), channel_id=1, source_target_pairs={{0,256},{256,0},{1,257},{257,1},{2,258},{258,2},{3,259},{259,3},{4... | collective-permute-start | bytes 49160 | tf_op jit(solution)/shard_map/ppermute | solution.py:203
  13.6 22.2 %collective-permute-start.3 = (f32[16,8,384]{2,1,0:T(8,128)S(1)}, f32[16,8,384]{2,1,0:T(8,128)S(1)}, u32[]{:S(2)}, u32[]{:S(2)}) collective-permute-start(f32[16,8,384]{2,1,0:T(8,128)S(1)} %get-tuple-element.94), channel_id=1, source_target_pairs={{0,1},{1,2},{2,3},{3,4},{4,5},{5,6},{6,7},{7,8},{8,9},{9,10},{10,1... | collective-permute-start | bytes 589832 | tf_op jit(solution)/shard_map/ppermute | solution.py:23
  16.8 19.1 %collective-permute-start.4 = (f32[16,8,384]{2,1,0:T(8,128)S(1)}, f32[16,8,384]{2,1,0:T(8,128)S(1)}, u32[]{:S(2)}, u32[]{:S(2)}) collective-permute-start(f32[16,8,384]{2,1,0:T(8,128)S(1)} %get-tuple-element.95), channel_id=1, source_target_pairs={{0,31},{1,0},{2,1},{3,2},{4,3},{5,4},{6,5},{7,6},{8,7},{9,8},{10,9... | collective-permute-start | bytes 589832 | tf_op jit(solution)/shard_map/ppermute | solution.py:23
  29.1 33.3 %collective-permute-start.2 = (f32[4,128,384]{2,1,0:T(8,128)S(1)}, f32[4,128,384]{2,1,0:T(8,128)S(1)}, u32[]{:S(2)}, u32[]{:S(2)}) collective-permute-start(f32[4,128,384]{2,1,0:T(8,128)S(1)} %get-tuple-element.96), channel_id=1, source_target_pairs={{32,0},{64,32},{96,64},{128,96},{160,128},{192,160},{224,192},{33,... | collective-permute-start | bytes 2359304 | tf_op jit(solution)/shard_map/ppermute | solution.py:23
  33.9 29.5 %collective-permute-start.1 = (f32[4,128,384]{2,1,0:T(8,128)S(1)}, f32[4,128,384]{2,1,0:T(8,128)S(1)}, u32[]{:S(2)}, u32[]{:S(2)}) collective-permute-start(f32[4,128,384]{2,1,0:T(8,128)S(1)} %get-tuple-element.97), channel_id=1, source_target_pairs={{0,32},{32,64},{64,96},{96,128},{128,160},{160,192},{192,224},{1,3... | collective-permute-start | bytes 2359304 | tf_op jit(solution)/shard_map/ppermute | solution.py:23
  35.9 17.3 %collective-permute-start.6 = (f32[4,16,384]{2,1,0:T(8,128)S(1)}, f32[4,16,384]{2,1,0:T(8,128)S(1)}, u32[]{:S(2)}, u32[]{:S(2)}) collective-permute-start(f32[4,16,384]{2,1,0:T(8,128)S(1)} %pad_maximum_fusion.3), channel_id=1, source_target_pairs={{32,0},{64,32},{96,64},{128,96},{160,128},{192,160},{224,192},{33,... | collective-permute-start | bytes 294920 | tf_op jit(solution)/shard_map/ppermute | solution.py:23
  43.4 17.4 %collective-permute-start.5 = (f32[4,16,384]{2,1,0:T(8,128)S(1)}, f32[4,16,384]{2,1,0:T(8,128)S(1)}, u32[]{:S(2)}, u32[]{:S(2)}) collective-permute-start(f32[4,16,384]{2,1,0:T(8,128)S(1)} %pad_maximum_fusion.2), channel_id=1, source_target_pairs={{0,32},{32,64},{64,96},{96,128},{128,160},{160,192},{192,224},{1,3... | collective-permute-start | bytes 294920 | tf_op jit(solution)/shard_map/ppermute | solution.py:23
